TPU v7x, 512 devices: a whole 4x8x8 slice. The times are simulated.
512 devices in a mesh: ctx: 64 (over y, z_lo, core), dp: 8 (over z_hi, x).
Axes of the slice: x: 4, y: 8, z: 8 (z_hi: 2, z_lo: 4; z = z_hi * 4 + z_lo), core: 2. Of those that a mesh axis runs over, the one named last changes fastest.
Arguments:
- features: bfloat16 [8, 12288, 1536], P('dp', 'ctx'), may hold values from -6 to 6
- bottleneck: bfloat16 [8, 12288, 384], P('dp', 'ctx'), may hold values from -6 to 6
- node_noise: bfloat16 [8, 12288, 1536], P('dp', 'ctx'), may hold values from -6 to 6
- targets: bfloat16 [8, 12288, 1536], P('dp', 'ctx'), may hold values from -15 to 15
- entry_weight: bfloat16 [384, 1536], P('ctx'), may hold values from -0.3125 to 0.3125
- conv_filters: bfloat16 [3, 1536, 384], P(None, None, 'ctx'), may hold values from -0.09375 to 0.09375
- exit_weight: bfloat16 [384, 1536], P('ctx'), may hold values from -0.3125 to 0.3125
Outputs:
- blended: bfloat16 [8, 12288, 1536], P('dp', 'ctx')
- estimate: float32 [384, 1536], P('ctx')
All inputs are finite; a program needn't handle non-finite values.
Results may differ from a plain program's by a relative error of at most 0.015.
The roundings to bfloat16 on the way count: a program that leaves them out, or rounds other values in their place, can miss the bound.
Values may be sent and summed in bfloat16 or wider, within the bound.
No kernel may reach another device: no remote copies, remote signals or barrier semaphores. Data moves between devices by JAX's collectives and lax.ppermute only.
A program may use at most 64 MiB of HBM per device.

v0:
```python
import jax
import jax.numpy as jnp
from jax import lax
from jax.sharding import PartitionSpec as P

DILATION = 32


NOISE_SCALE = 0.1


def padded_2(cells, sides, width):
    for axis, dim in sides:
        count = lax.axis_size(axis)
        ends = count - 1
        head = lax.slice_in_dim(cells, 0, width, axis=dim)
        tail = lax.slice_in_dim(cells, cells.shape[dim] - width, cells.shape[dim], axis=dim)
        cells = jnp.concatenate(
            [
                lax.ppermute(tail, axis, [(i, (i + 1) % count) for i in range(ends)]),
                cells,
                lax.ppermute(head, axis, [((i + 1) % count, i) for i in range(ends)]),
            ],
            axis=dim,
        )
    return cells


def taps_for(padded, row_count, spacing, portion):
    summed = jnp.dot(padded[..., 0:row_count, :], portion[0], preferred_element_type=jnp.float32)
    summed = summed + jnp.dot(
        padded[..., spacing : spacing + row_count, :],
        portion[1],
        preferred_element_type=jnp.float32,
    )
    summed = summed + jnp.dot(
        padded[..., 2 * spacing : 2 * spacing + row_count, :],
        portion[2],
        preferred_element_type=jnp.float32,
    )
    return summed


def rows_for(left_side, portion):
    return jnp.dot(left_side, portion, preferred_element_type=jnp.float32)


def body(features, bottleneck, node_noise, targets, entry_weight, conv_filters, exit_weight):
    feats = features[0]
    bottle = bottleneck[0]
    jitter = node_noise[0]
    goal = targets[0].astype(jnp.float32)
    row_count = feats.shape[0]
    chan_count = feats.shape[1]
    spacing = DILATION
    baseline = feats.astype(jnp.float32) + rows_for(
        bottle, lax.all_gather(entry_weight, "ctx", axis=0, tiled=True)
    )
    offset_field = jitter.astype(jnp.float32) * NOISE_SCALE
    results = []
    for polarity in (1.0, -1.0):
        state = baseline + polarity * offset_field
        activated = jax.nn.gelu(state).astype(jnp.bfloat16)
        padded = padded_2(activated, (("ctx", 0),), spacing)
        mixed = taps_for(
            padded, row_count, spacing, lax.all_gather(conv_filters, "ctx", axis=2, tiled=True)
        )
        inner = jax.nn.gelu(mixed).astype(jnp.bfloat16)
        results.append(
            state + rows_for(inner, lax.all_gather(exit_weight, "ctx", axis=0, tiled=True))
        )
    upper = results[0]
    lower = results[1]
    blended = ((upper + lower) * 0.5).astype(jnp.bfloat16)[None]
    local_gap = jnp.sum((upper - lower) * (upper + lower - 2.0 * goal)) / (
        row_count * lax.axis_size("ctx") * chan_count
    )
    factor = lax.psum(local_gap, "ctx") / (2.0 * NOISE_SCALE)
    local_term = factor * lax.dot_general(
        bottle, jitter, (((0,), (0,)), ((), ())), preferred_element_type=jnp.float32
    )
    grouped = lax.psum(local_term, "dp")
    estimate = lax.psum_scatter(grouped, "ctx", scatter_dimension=0, tiled=True)
    return (blended, estimate)


def solution(mesh):
    return jax.shard_map(
        body,
        mesh=mesh,
        in_specs=(
            P("dp", "ctx", None),
            P("dp", "ctx", None),
            P("dp", "ctx", None),
            P("dp", "ctx", None),
            P("ctx", None),
            P(None, None, "ctx"),
            P("ctx", None),
        ),
        out_specs=(P("dp", "ctx", None), P("ctx", None)),
        check_vma=False,
    )
```

profile of v0, /device:TPU:16, one launch (start us, length us, event | category | flops | bytes accessed | tf_op | source)
XLA Modules:
  0.0 813.7 jit_solution(17729310585328299950)
XLA Ops:
  10.3 120.4 %all-gather.8.cloned.1.call-done = bf16[64,6,1536]{2,1,0:T(8,128)(2,1)} async-done(((bf16[1,6,1536]{2,1,0:T(8,128)(2,1)}), bf16[64,6,1536]{2,1,0:T(8,128)(2,1)}) %all-gather.8.cloned.1.call-update) | async-done | bytes 1179664 | tf_op jit(solution)/shard_map/all_gather | solution.py:57
  130.7 2.3 reshape.11
  133.0 3.4 fusion.18
  137.2 5.5 collective-permute-start.3
  145.3 6.3 collective-permute-start.1
  153.6 95.0 %all-gather.10.cloned.1.call-done = bf16[64,6,1536]{2,1,0:T(8,128)(2,1)} async-done(((bf16[1,6,1536]{2,1,0:T(8,128)(2,1)}), bf16[64,6,1536]{2,1,0:T(8,128)(2,1)}) %all-gather.10.cloned.1.call-update) | async-done | bytes 1179664 | tf_op jit(solution)/shard_map/all_gather | solution.py:70
  248.6 3.1 reshape.13
  251.7 118.6 %all-gather.6.cloned.1.call-done = bf16[3,1536,384]{1,0,2:T(4,128)(2,1)} async-done(((bf16[3,1536,6]{1,0,2:T(4,128)(2,1)}), bf16[3,1536,384]{1,0,2:T(4,128)(2,1)}) %all-gather.6.cloned.1.call-update) | async-done | bytes 3538960 | tf_op jit(solution)/shard_map/all_gather | solution.py:66
  370.2 12.6 %fusion.103 = (bf16[1,1536,384]{1,0,2:T(2,128)(2,1)}, bf16[1,1536,384]{1,0,2:T(2,128)(2,1)}, bf16[1,1536,384]{1,0,2:T(2,128)(2,1)}) fusion(bf16[3,1536,384]{1,0,2:T(4,128)(2,1)} %all-gather.6.cloned.1.call-done), kind=kLoop, calls=%fused_computation.97 | loop fusion | bytes 7077888 | tf_op jit(solution)/shard_map/slice | solution.py:30
  382.9 5.6 copy.15
  388.9 6.5 copy.16
  395.5 2.5 fusion.21
  398.0 5.6 copy.14
  403.6 3.9 convolution_add_fusion
  411.4 4.6 fusion.20
  416.6 118.0 %psum.14 = f32[]{:T(128)} all-reduce(f32[]{:T(128)S(6)} %div.6), channel_id=1, replica_groups=mesh['ctx'=64,'dp'=8] {'ctx'}, use_global_device_ids=true, to_apply=%region_1.0 | all-reduce | flops 1 | bytes 8 | tf_op jit(solution)/shard_map/psum | solution.py:78
  535.8 132.1 %fusion = f32[8,1536]{1,0:T(8,128)S(1)} fusion(f32[384,1536]{1,0:T(8,128)S(1)} %convolution_multiply_fusion), kind=kCustom, calls=%all-reduce-scatter | all-reduce-scatter fusion | flops 786433 | bytes 2410496
  667.9 42.7 %collective-permute-start.19 = (f32[6,1536]{1,0:T(8,128)S(1)}, f32[6,1536]{1,0:T(8,128)S(1)}, u32[]{:S(2)}, u32[]{:S(2)}) collective-permute-start(f32[6,1536]{1,0:T(8,128)S(1)} %slice.58), channel_id=1, source_target_pairs={{0,128},{8,136},{16,144},{24,152},{32,160},{40,168},{48,176},{56,1... | collective-permute-start | bytes 110600
  720.6 5.3 collective-permute-start.15
  733.9 2.4 collective-permute-start.5
  736.3 2.6 collective-permute-start.6
  739.0 4.6 collective-permute-start.7
  745.5 4.1 collective-permute-start.9
  754.7 52.4 %psum.16 = f32[6,1536]{1,0:T(8,128)} all-reduce(f32[6,1536]{1,0:T(8,128)S(1)} %constant_dynamic-slice_fusion), channel_id=1, replica_groups=mesh['ctx'=64,'dp'=8] {'dp'}, use_global_device_ids=true, to_apply=%region_2.0 | all-reduce | flops 9216 | bytes 73728 | tf_op jit(solution)/shard_map/psum | solution.py:82
  (63 shorter events, 37.5 us)
Async XLA Ops:
  7.2 123.6 %all-gather.8.cloned.1.call-start = ((), (), s32[]{:S(2)}) async-start(), calls=%async_computation.1 | async-start | bytes 1597440 | tf_op jit(solution)/shard_map/all_gather | solution.py:57
  7.9 240.7 %all-gather.10.cloned.1.call-start = ((), (), s32[]{:S(2)}) async-start(), calls=%async_computation.2 | async-start | bytes 1597440 | tf_op jit(solution)/shard_map/all_gather | solution.py:70
  8.7 361.6 %all-gather.6.cloned.1.call-start = ((), (), s32[]{:S(2)}) async-start(), calls=%async_computation | async-start | bytes 4792320 | tf_op jit(solution)/shard_map/all_gather | solution.py:66
  136.4 259.0 %copy-start.3 = (bf16[192,1536]{1,0:T(8,128)(2,1)}, bf16[192,1536]{1,0:T(8,128)(2,1)S(1)}, u32[]{:S(2)}) copy-start(bf16[192,1536]{1,0:T(8,128)(2,1)S(1)} %get-tuple-element.7) | copy-start | bytes 1769476
  137.2 258.3 %collective-permute-start.3 = (bf16[32,1536]{1,0:T(8,128)(2,1)}, bf16[32,1536]{1,0:T(8,128)(2,1)}, u32[]{:S(2)}, u32[]{:S(2)}) collective-permute-start(bf16[32,1536]{1,0:T(8,128)(2,1)} %get-tuple-element.10), channel_id=1, source_target_pairs={{8,0},{16,8},{24,16},{32,24},{40,32},{48,40},{56,48},{64,56},{72,6... | collective-permute-start | bytes 294920 | tf_op jit(solution)/shard_map/ppermute | solution.py:22
  142.7 260.9 %collective-permute-start.2 = (bf16[32,1536]{1,0:T(8,128)(2,1)}, bf16[32,1536]{1,0:T(8,128)(2,1)}, u32[]{:S(2)}, u32[]{:S(2)}) collective-permute-start(bf16[32,1536]{1,0:T(8,128)(2,1)} %get-tuple-element.9), channel_id=1, source_target_pairs={{0,8},{8,16},{16,24},{24,32},{32,40},{40,48},{48,56},{56,64},{64,7... | collective-permute-start | bytes 294920 | tf_op jit(solution)/shard_map/ppermute | solution.py:20
  145.3 263.8 %collective-permute-start.1 = (bf16[32,1536]{1,0:T(8,128)(2,1)}, bf16[32,1536]{1,0:T(8,128)(2,1)}, u32[]{:S(2)}, u32[]{:S(2)}) collective-permute-start(bf16[32,1536]{1,0:T(8,128)(2,1)} %get-tuple-element.12), channel_id=1, source_target_pairs={{8,0},{16,8},{24,16},{32,24},{40,32},{48,40},{56,48},{64,56},{72,6... | collective-permute-start | bytes 294920 | tf_op jit(solution)/shard_map/ppermute | solution.py:22
  151.7 259.7 %collective-permute-start = (bf16[32,1536]{1,0:T(8,128)(2,1)}, bf16[32,1536]{1,0:T(8,128)(2,1)S(1)}, u32[]{:S(2)}, u32[]{:S(2)}) collective-permute-start(bf16[32,1536]{1,0:T(8,128)(2,1)} %get-tuple-element.11), channel_id=1, source_target_pairs={{0,8},{8,16},{16,24},{24,32},{32,40},{40,48},{48,56},{56,64},{64,7... | collective-permute-start | bytes 294920 | tf_op jit(solution)/shard_map/ppermute | solution.py:20
  667.9 50.8 %collective-permute-start.19 = (f32[6,1536]{1,0:T(8,128)S(1)}, f32[6,1536]{1,0:T(8,128)S(1)}, u32[]{:S(2)}, u32[]{:S(2)}) collective-permute-start(f32[6,1536]{1,0:T(8,128)S(1)} %slice.58), channel_id=1, source_target_pairs={{0,128},{8,136},{16,144},{24,152},{32,160},{40,168},{48,176},{56,1... | collective-permute-start | bytes 110600
  710.6 10.1 %collective-permute-start.10 = (f32[8,1536]{1,0:T(8,128)S(1)}, f32[8,1536]{1,0:T(8,128)S(1)}, u32[]{:S(2)}, u32[]{:S(2)}) collective-permute-start(f32[8,1536]{1,0:T(8,128)S(1)} %fusion), channel_id=1, source_target_pairs={{0,56},{8,64},{16,72},{24,80},{32,88},{40,96},{48,104},{56,112},{6... | collective-permute-start | bytes 147464
  712.5 13.4 %collective-permute-start.11 = (f32[8,1536]{1,0:T(8,128)S(1)}, f32[8,1536]{1,0:T(8,128)S(1)}, u32[]{:S(2)}, u32[]{:S(2)}) collective-permute-start(f32[8,1536]{1,0:T(8,128)S(1)} %fusion), channel_id=1, source_target_pairs={{0,64},{8,72},{16,80},{24,88},{32,96},{40,104},{48,112},{56,120},{... | collective-permute-start | bytes 147464
  714.4 13.4 %collective-permute-start.12 = (f32[8,1536]{1,0:T(8,128)S(1)}, f32[8,1536]{1,0:T(8,128)S(1)}, u32[]{:S(2)}, u32[]{:S(2)}) collective-permute-start(f32[8,1536]{1,0:T(8,128)S(1)} %fusion), channel_id=1, source_target_pairs={{0,72},{8,80},{16,88},{24,96},{32,104},{40,112},{48,120},{56,128},... | collective-permute-start | bytes 147464
  716.6 13.2 %collective-permute-start.13 = (f32[8,1536]{1,0:T(8,128)S(1)}, f32[8,1536]{1,0:T(8,128)S(1)}, u32[]{:S(2)}, u32[]{:S(2)}) collective-permute-start(f32[8,1536]{1,0:T(8,128)S(1)} %fusion), channel_id=1, source_target_pairs={{0,80},{8,88},{16,96},{24,104},{32,112},{40,120},{48,128},{56,136}... | collective-permute-start | bytes 147464
  718.7 13.1 %collective-permute-start.14 = (f32[8,1536]{1,0:T(8,128)S(1)}, f32[8,1536]{1,0:T(8,128)S(1)}, u32[]{:S(2)}, u32[]{:S(2)}) collective-permute-start(f32[8,1536]{1,0:T(8,128)S(1)} %fusion), channel_id=1, source_target_pairs={{0,88},{8,96},{16,104},{24,112},{32,120},{40,128},{48,136},{56,144... | collective-permute-start | bytes 147464
  720.6 13.2 %collective-permute-start.15 = (f32[8,1536]{1,0:T(8,128)S(1)}, f32[8,1536]{1,0:T(8,128)S(1)}, u32[]{:S(2)}, u32[]{:S(2)}) collective-permute-start(f32[8,1536]{1,0:T(8,128)S(1)} %fusion), channel_id=1, source_target_pairs={{0,96},{8,104},{16,112},{24,120},{32,128},{40,136},{48,144},{56,15... | collective-permute-start | bytes 147464
  725.9 10.4 %collective-permute-start.16 = (f32[8,1536]{1,0:T(8,128)S(1)}, f32[8,1536]{1,0:T(8,128)S(1)}, u32[]{:S(2)}, u32[]{:S(2)}) collective-permute-start(f32[8,1536]{1,0:T(8,128)S(1)} %fusion), channel_id=1, source_target_pairs={{0,104},{8,112},{16,120},{24,128},{32,136},{40,144},{48,152},{56,1... | collective-permute-start | bytes 147464
  727.8 11.1 %collective-permute-start.17 = (f32[8,1536]{1,0:T(8,128)S(1)}, f32[8,1536]{1,0:T(8,128)S(1)}, u32[]{:S(2)}, u32[]{:S(2)}) collective-permute-start(f32[8,1536]{1,0:T(8,128)S(1)} %fusion), channel_id=1, source_target_pairs={{0,112},{8,120},{16,128},{24,136},{32,144},{40,152},{48,160},{56,1... | collective-permute-start | bytes 147464
  729.9 13.7 %collective-permute-start.18 = (f32[8,1536]{1,0:T(8,128)S(1)}, f32[8,1536]{1,0:T(8,128)S(1)}, u32[]{:S(2)}, u32[]{:S(2)}) collective-permute-start(f32[8,1536]{1,0:T(8,128)S(1)} %fusion), channel_id=1, source_target_pairs={{0,120},{8,128},{16,136},{24,144},{32,152},{40,160},{48,168},{56,1... | collective-permute-start | bytes 147464
  731.8 13.7 %collective-permute-start.4 = (f32[8,1536]{1,0:T(8,128)S(1)}, f32[8,1536]{1,0:T(8,128)S(1)}, u32[]{:S(2)}, u32[]{:S(2)}) collective-permute-start(f32[8,1536]{1,0:T(8,128)S(1)} %fusion), channel_id=1, source_target_pairs={{0,8},{8,16},{16,24},{24,32},{32,40},{40,48},{48,56},{56,64},{64,7... | collective-permute-start | bytes 147464
  733.9 17.6 %collective-permute-start.5 = (f32[8,1536]{1,0:T(8,128)S(1)}, f32[8,1536]{1,0:T(8,128)S(1)}, u32[]{:S(2)}, u32[]{:S(2)}) collective-permute-start(f32[8,1536]{1,0:T(8,128)S(1)} %fusion), channel_id=1, source_target_pairs={{0,16},{8,24},{16,32},{24,40},{32,48},{40,56},{48,64},{56,72},{64,... | collective-permute-start | bytes 147464
  736.3 15.2 %collective-permute-start.6 = (f32[8,1536]{1,0:T(8,128)S(1)}, f32[8,1536]{1,0:T(8,128)S(1)}, u32[]{:S(2)}, u32[]{:S(2)}) collective-permute-start(f32[8,1536]{1,0:T(8,128)S(1)} %fusion), channel_id=1, source_target_pairs={{0,24},{8,32},{16,40},{24,48},{32,56},{40,64},{48,72},{56,80},{64,... | collective-permute-start | bytes 147464
  739.0 12.6 %collective-permute-start.7 = (f32[8,1536]{1,0:T(8,128)S(1)}, f32[8,1536]{1,0:T(8,128)S(1)}, u32[]{:S(2)}, u32[]{:S(2)}) collective-permute-start(f32[8,1536]{1,0:T(8,128)S(1)} %fusion), channel_id=1, source_target_pairs={{0,32},{8,40},{16,48},{24,56},{32,64},{40,72},{48,80},{56,88},{64,... | collective-permute-start | bytes 147464
  743.6 8.0 collective-permute-start.8
  745.5 7.3 collective-permute-start.9
  (6 other events, 369.4 us)
Sparse Core Ops, SparseCore 0:
  10.2 120.5 all-gather.7
  132.9 115.6 all-gather.9
  250.7 119.4 all-gather.5
where the time goes:
time: 816 us; the launch traced here: 814 us
  waiting for transfers between devices  337 us (41%)
  blocking collectives  303 us (37%)
  starting transfers between devices  97.3 us (12%)
  local copies, waits for them, and re-layouts  41.9 us (5%)
  matrix products  19.1 us (2%)
  between operations  16.1 us (2%)
    unnamed x1, blocking collectives  132 us
    all_gather x1, waiting for transfers between devices, body(): lax.all_gather(entry_weight, 'ctx', axis=0, tiled=True)  120 us
    all_gather x1, waiting for transfers between devices, body(): lax.all_gather(conv_filters, 'ctx', axis=2, tiled=True)  119 us
    psum x1, blocking collectives, body(): factor = lax.psum(local_gap, 'ctx') / (2.0 * NOISE_SCALE)  118 us
    all_gather x1, waiting for transfers between devices, body(): lax.all_gather(exit_weight, 'ctx', axis=0, tiled=True)  95 us
    unnamed x16, starting transfers between devices  81.5 us
    psum x1, blocking collectives, body(): grouped = lax.psum(local_term, 'dp')  52.4 us
    unnamed x24, local copies, waits for them, and re-layouts  27.9 us
  transfers between devices with their start and end apart: 23, of which 4 were waited for; matrix products, arithmetic and copies ran while one was open for 7% of the time, Pallas kernels for 0%

commit v1 on v0

v1 whole, which is shorter than its diff:
```python
import jax
import jax.numpy as jnp
from jax import lax
from jax.sharding import Mesh
from jax.sharding import PartitionSpec as P

DILATION = 32

NOISE_SCALE = 0.1

CTX = ("y", "zl", "c")
DP = ("zh", "x")


def _size(axes):
    n = 1
    for a in axes:
        n *= lax.axis_size(a)
    return n


def body(features, bottleneck, node_noise, targets, entry_weight, conv_filters, exit_weight):
    feats = features[0]
    bottle = bottleneck[0]
    jitter = node_noise[0]
    goal = targets[0].astype(jnp.float32)
    rows, chans = feats.shape
    bot = bottle.shape[1]
    n_ctx = _size(CTX)
    ny, nz, nc = (lax.axis_size(a) for a in CTX)
    shard = entry_weight.shape[0]

    bottle_perm = (
        bottle.reshape(rows, ny, nz, nc, shard).transpose(0, 3, 2, 1, 4).reshape(rows, bot)
    )
    summed = lax.dot_general(
        bottle_perm, jitter, (((0,), (0,)), ((), ())), preferred_element_type=jnp.float32
    )
    for axis in ("c", "zl", "y"):
        summed = lax.psum_scatter(summed, axis, scatter_dimension=0, tiled=True)

    conv_rows = conv_filters.transpose(2, 0, 1).reshape(shard, -1)
    packed = jnp.concatenate([entry_weight, conv_rows, exit_weight], axis=1)
    packed = lax.all_gather(packed, "y", axis=0, tiled=False)
    packed = lax.all_gather(packed, "zl", axis=1, tiled=False)
    packed = lax.all_gather(packed, "c", axis=2, tiled=False)
    packed = packed.reshape(n_ctx * shard, -1)
    w_entry = packed[:, :chans]
    w_conv = packed[:, chans : 4 * chans].reshape(bot, 3, chans)
    w_exit = packed[:, 4 * chans :]

    spacing = DILATION
    edge_in = jnp.concatenate([feats, bottle, jitter], axis=1)
    pairs_up = [(i, i + 1) for i in range(n_ctx - 1)]
    pairs_down = [(i + 1, i) for i in range(n_ctx - 1)]
    from_prev = lax.ppermute(edge_in[rows - spacing :], CTX, pairs_up)
    from_next = lax.ppermute(edge_in[:spacing], CTX, pairs_down)
    ext = jnp.concatenate([from_prev, edge_in, from_next], axis=0)
    ext_feats = ext[:, :chans]
    ext_bottle = ext[:, chans : chans + bot]
    ext_jitter = ext[:, chans + bot :]

    baseline = ext_feats.astype(jnp.float32) + jnp.dot(
        ext_bottle, w_entry, preferred_element_type=jnp.float32
    )
    offset = ext_jitter.astype(jnp.float32) * NOISE_SCALE
    state = jnp.stack([baseline + offset, baseline - offset])
    activated = jax.nn.gelu(state).astype(jnp.bfloat16)
    mixed = None
    for k in range(3):
        term = lax.dot_general(
            activated[:, k * spacing : k * spacing + rows],
            w_conv[:, k, :],
            (((2,), (1,)), ((), ())),
            preferred_element_type=jnp.float32,
        )
        mixed = term if mixed is None else mixed + term
    inner = jax.nn.gelu(mixed).astype(jnp.bfloat16)
    outs = state[:, spacing : spacing + rows] + jnp.dot(
        inner, w_exit, preferred_element_type=jnp.float32
    )
    upper = outs[0]
    lower = outs[1]
    blended = ((upper + lower) * 0.5).astype(jnp.bfloat16)[None]
    local_gap = jnp.sum((upper - lower) * (upper + lower - 2.0 * goal)) / (rows * n_ctx * chans)
    gap = local_gap
    for axis in ("c", "zl", "y"):
        gap = lax.psum(gap, axis)
    factor = gap / (2.0 * NOISE_SCALE)
    estimate = factor * summed
    for axis in ("x", "zh"):
        estimate = lax.psum(estimate, axis)
    return (blended, estimate)


def solution(mesh):
    ctx_n, dp_n = mesh.devices.shape
    devices = mesh.devices.reshape(8, ctx_n // 16, 2, dp_n // 4, 4)
    fine = Mesh(devices, CTX + DP)
    return jax.shard_map(
        body,
        mesh=fine,
        in_specs=(
            P(DP, CTX, None),
            P(DP, CTX, None),
            P(DP, CTX, None),
            P(DP, CTX, None),
            P(CTX, None),
            P(None, None, CTX),
            P(CTX, None),
        ),
        out_specs=(P(DP, CTX, None), P(CTX, None)),
        check_vma=False,
    )
```

time: 816 us -> 296 us (0.36)
  the two profiles are of different devices: /device:TPU:16 before, /device:TPU:4 now
where the time goes in v1:
time: 296 us; the launch traced here: 295 us
  blocking collectives  114 us (39%)
  waiting for transfers between devices  102 us (34%)
  local copies, waits for them, and re-layouts  33 us (11%)
  between operations  17.6 us (6%)
  matrix products  11.8 us (4%)
  starting transfers between devices  10.6 us (4%)
  other arithmetic  5.94 us (2%)
    all_gather x1, waiting for transfers between devices, body(): packed = lax.all_gather(packed, 'zl', axis=1, tiled=False)  69.2 us
    psum x2, blocking collectives, body(): estimate = lax.psum(estimate, axis)  33.3 us
    reduce_scatter x2, waiting for transfers between devices, body(): summed = lax.psum_scatter(summed, axis, scatter_dimension=0, tiled=True)  31.9 us
    psum x3, blocking collectives, body(): gap = lax.psum(gap, axis)  30.6 us
    all_gather x1, blocking collectives, body(): packed = lax.all_gather(packed, 'y', axis=0, tiled=False)  28.2 us
    unnamed x1, blocking collectives  22.1 us
    unnamed x24, local copies, waits for them, and re-layouts  9.79 us
    reshape x1, local copies, waits for them, and re-layouts, body(): packed = packed.reshape(n_ctx * shard, -1)  8.55 us
  transfers between devices with their start and end apart: 8, of which 2 were waited for; matrix products, arithmetic and copies ran while one was open for 21% of the time, Pallas kernels for 0%

profile of v1, /device:TPU:4, one launch (start us, length us, event | category | flops | bytes accessed | tf_op | source)
XLA Modules:
  0.0 294.6 jit_solution(6583239954696463793)
XLA Ops:
  9.4 1.9 fusion.46
  12.2 28.2 %all-gather.3 = bf16[8,6,7680]{2,1,0:T(8,128)(2,1)S(1)} all-gather(bf16[1,6,7680]{2,1,0:T(8,128)(2,1)S(1)} %maximum_bitcast_fusion), channel_id=2, replica_groups=mesh['y'=8,'zl'=4,'c'=2,'zh'=2,'x'=4] {'y'}, dimensions={0}, use_global_device_ids=true | all-gather | bytes 829440 | tf_op jit(solution)/shard_map/all_gather | solution.py:44
  42.2 69.2 %all-gather.7.cloned.1.call-done = bf16[8,24,7680]{2,0,1:T(8,128)(2,1)} async-done(((bf16[8,6,7680]{2,0,1:T(8,128)(2,1)}), bf16[8,24,7680]{2,0,1:T(8,128)(2,1)}) %all-gather.7.cloned.1.call-update) | async-done | bytes 2949136 | tf_op jit(solution)/shard_map/all_gather | solution.py:45
  112.7 3.0 %collective-permute-start = (bf16[32,3456]{1,0:T(8,128)(2,1)S(1)}, bf16[32,3456]{1,0:T(8,128)(2,1)S(1)}, u32[]{:S(2)}, u32[]{:S(2)}) collective-permute-start(bf16[32,3456]{1,0:T(8,128)(2,1)S(1)} %get-tuple-element.6), channel_id=1, source_target_pairs={{0,8},{8,16},{16,24},{24,32},{32,40},{40,48},{48,56},{56,64},{64,7... | collective-permute-start | bytes 663560 | tf_op jit(solution)/shard_map/ppermute | solution.py:56
  118.5 1.3 pad_maximum_fusion.1
  119.8 31.9 %reduce-scatter.7.cloned.1.call-done = f32[48,1536]{1,0:T(8,128)} async-done(((f32[192,1536]{1,0:T(8,128)}), f32[48,1536]{1,0:T(8,128)}) %reduce-scatter.7.cloned.1.call-update) | async-done | bytes 294928 | tf_op jit(solution)/shard_map/reduce_scatter | solution.py:40
  151.7 22.1 %fusion = f32[8,1536]{1,0:T(8,128)} fusion(f32[48,1536]{1,0:T(8,128)} %reduce-scatter.7.cloned.1.call-done), kind=kCustom, calls=%all-reduce-scatter | all-reduce-scatter fusion | flops 98305 | bytes 346112
  173.7 1.4 slice.82
  175.1 3.3 %collective-permute-start.2 = (f32[8,1536]{1,0:T(8,128)}, f32[8,1536]{1,0:T(8,128)}, u32[]{:S(2)}, u32[]{:S(2)}) collective-permute-start(f32[8,1536]{1,0:T(8,128)} %fusion), channel_id=1, source_target_pairs={{0,64},{64,128},{128,192},{192,256},{256,320},{320,384},{384,448},... | collective-permute-start | bytes 147464
  178.5 2.7 collective-permute-start.3
  181.2 7.7 %copy.25 = bf16[8,4,12,7680]{3,2,1,0:T(8,128)(2,1)} copy(bf16[8,4,12,7680]{3,0,2,1:T(8,128)(2,1)} %all-gather.9.cloned.1.call-done) | data formatting | bytes 11796480 | tf_op jit(solution)/shard_map/all_gather | solution.py:46
  188.9 8.6 %reshape.24 = bf16[384,7680]{1,0:T(8,128)(2,1)} reshape(bf16[8,4,12,7680]{3,2,1,0:T(8,128)(2,1)} %copy.25) | data formatting | bytes 11796480 | tf_op jit(solution)/shard_map/reshape | solution.py:47
  197.5 2.0 slice-done
  199.5 3.6 %copy.26 = bf16[384,4608]{0,1:T(8,128)(2,1)} copy(bf16[384,4608]{1,0:T(8,128)(2,1)S(1)} %slice-done) | data formatting | bytes 7077888 | tf_op jit(solution)/shard_map/slice | solution.py:49
  203.1 2.5 subtract_bitcast_fusion
  208.5 1.6 convolution_add_fusion.2
  210.1 5.1 %convolution_add_fusion = f32[2,192,1536]{2,1,0:T(8,128)} fusion(f32[1,256,1536]{2,1,0:T(8,128)S(1)} %get-tuple-element.3, f32[1,256,1536]{2,1,0:T(8,128)S(1)} %get-tuple-element.2, bf16[384,7680]{1,0:T(8,128)(2,1)} %reshape.24, f32[2,192,384]{2,1,0:T(8,128)} %convolution_add_fusion.2, bf16[384,3,1536]{0,2,1:T(8,128)(2,1)} %bitcast.58, ...), kind=kOutput, calls=%fused_computation.12 | convolution fusion | flops 908623872 | bytes 9633792 | tf_op jit(solution)/shard_map/dot_general | solution.py:79
  215.2 3.6 %multiply_reduce_fusion = (f32[]{:T(128)}, bf16[1,192,1536]{2,1,0:T(8,128)(2,1)}) fusion(bf16[1,192,1536]{2,1,0:T(8,128)(2,1)} %param.10, f32[2,192,1536]{2,1,0:T(8,128)} %convolution_add_fusion), kind=kLoop, calls=%fused_computation.31 | loop fusion | flops 2654207 | bytes 3538948 | tf_op jit(solution)/shard_map/reduce_sum | solution.py:85
  220.0 3.0 %psum.35 = f32[]{:T(128)} all-reduce(f32[]{:T(128)S(6)} %div.6), channel_id=1, replica_groups=mesh['y'=8,'zl'=4,'c'=2,'zh'=2,'x'=4] {'c'}, use_global_device_ids=true, to_apply=%region_1.0 | all-reduce | flops 1 | bytes 8 | tf_op jit(solution)/shard_map/psum | solution.py:88
  223.0 9.6 %psum.36 = f32[]{:T(128)} all-reduce(f32[]{:T(128)} %psum.35), channel_id=1, replica_groups=mesh['y'=8,'zl'=4,'c'=2,'zh'=2,'x'=4] {'zl'}, use_global_device_ids=true, to_apply=%region_2.0 | all-reduce | flops 1 | bytes 8 | tf_op jit(solution)/shard_map/psum | solution.py:88
  232.5 2.6 concatenate.12
  235.2 18.1 %psum.37 = f32[]{:T(128)} all-reduce(f32[]{:T(128)} %psum.36), channel_id=1, replica_groups=mesh['y'=8,'zl'=4,'c'=2,'zh'=2,'x'=4] {'y'}, use_global_device_ids=true, to_apply=%region_3.0 | all-reduce | flops 1 | bytes 8 | tf_op jit(solution)/shard_map/psum | solution.py:88
  253.9 15.7 %psum.38 = f32[6,1536]{1,0:T(8,128)S(1)} all-reduce(f32[6,1536]{1,0:T(8,128)S(1)} %dynamic-slice_multiply_fusion), channel_id=1, replica_groups=mesh['y'=8,'zl'=4,'c'=2,'zh'=2,'x'=4] {'x'}, use_global_device_ids=true, to_apply=%region_7.0 | all-reduce | flops 9216 | bytes 73728 | tf_op jit(solution)/shard_map/psum | solution.py:92
  269.7 17.6 %psum.39 = f32[6,1536]{1,0:T(8,128)} all-reduce(f32[6,1536]{1,0:T(8,128)S(1)} %psum.38), channel_id=1, replica_groups=mesh['y'=8,'zl'=4,'c'=2,'zh'=2,'x'=4] {'zh'}, use_global_device_ids=true, to_apply=%region_8.0 | all-reduce | flops 9216 | bytes 73728 | tf_op jit(solution)/shard_map/psum | solution.py:92
  (47 shorter events, 10.9 us)
Async XLA Ops:
  8.0 1.4 copy-start
  8.0 33.6 %reduce-scatter.5.cloned.1.call-start = ((), (), s32[]{:S(2)}) async-start(), calls=%async_computation.2 | async-start | bytes 3538944 | tf_op jit(solution)/shard_map/reduce_scatter | solution.py:40
  11.3 0.9 copy-start.7
  11.3 0.9 copy-start.8
  11.3 0.9 copy-start.9
  11.3 100.0 %all-gather.7.cloned.1.call-start = ((), (), s32[]{:S(2)}) async-start(), calls=%async_computation.4 | async-start | bytes 3686400 | tf_op jit(solution)/shard_map/all_gather | solution.py:45
  41.5 110.2 %reduce-scatter.7.cloned.1.call-start = ((), (), s32[]{:S(2)}) async-start(), calls=%async_computation.3 | async-start | bytes 1474560 | tf_op jit(solution)/shard_map/reduce_scatter | solution.py:40
  42.1 69.3 %copy-start.1 = (bf16[1,192,1536]{2,1,0:T(8,128)(2,1)S(1)}, bf16[1,192,1536]{2,1,0:T(8,128)(2,1)}, u32[]{:S(2)}) copy-start(bf16[1,192,1536]{2,1,0:T(8,128)(2,1)} %param.7) | copy-start | bytes 1769476
  42.1 69.3 %copy-start.2 = (bf16[1,192,384]{2,1,0:T(8,128)(2,1)S(1)}, bf16[1,192,384]{2,1,0:T(8,128)(2,1)}, u32[]{:S(2)}) copy-start(bf16[1,192,384]{2,1,0:T(8,128)(2,1)} %param.8) | copy-start | bytes 442372
  42.1 139.1 %all-gather.9.cloned.1.call-start = ((), (), s32[]{:S(2)}) async-start(), calls=%async_computation.5 | async-start | bytes 8847360 | tf_op jit(solution)/shard_map/all_gather | solution.py:46
  111.4 5.6 %collective-permute-start.1 = (bf16[32,3456]{1,0:T(8,128)(2,1)S(1)}, bf16[32,3456]{1,0:T(8,128)(2,1)S(1)}, u32[]{:S(2)}, u32[]{:S(2)}) collective-permute-start(bf16[32,3456]{1,0:T(8,128)(2,1)S(1)} %get-tuple-element.7), channel_id=1, source_target_pairs={{8,0},{16,8},{24,16},{32,24},{40,32},{48,40},{56,48},{64,56},{72,6... | collective-permute-start | bytes 663560 | tf_op jit(solution)/shard_map/ppermute | solution.py:57
  112.7 4.3 %collective-permute-start = (bf16[32,3456]{1,0:T(8,128)(2,1)S(1)}, bf16[32,3456]{1,0:T(8,128)(2,1)S(1)}, u32[]{:S(2)}, u32[]{:S(2)}) collective-permute-start(bf16[32,3456]{1,0:T(8,128)(2,1)S(1)} %get-tuple-element.6), channel_id=1, source_target_pairs={{0,8},{8,16},{16,24},{24,32},{32,40},{40,48},{48,56},{56,64},{64,7... | collective-permute-start | bytes 663560 | tf_op jit(solution)/shard_map/ppermute | solution.py:56
  117.1 0.7 copy-start.4
  117.8 0.7 copy-start.5
  175.1 57.4 %collective-permute-start.2 = (f32[8,1536]{1,0:T(8,128)}, f32[8,1536]{1,0:T(8,128)}, u32[]{:S(2)}, u32[]{:S(2)}) collective-permute-start(f32[8,1536]{1,0:T(8,128)} %fusion), channel_id=1, source_target_pairs={{0,64},{64,128},{128,192},{192,256},{256,320},{320,384},{384,448},... | collective-permute-start | bytes 147464
  178.5 54.1 %collective-permute-start.3 = (f32[6,1536]{1,0:T(8,128)}, f32[6,1536]{1,0:T(8,128)}, u32[]{:S(2)}, u32[]{:S(2)}) collective-permute-start(f32[6,1536]{1,0:T(8,128)} %slice.82), channel_id=1, source_target_pairs={{0,128},{64,192},{128,256},{192,320},{256,384},{320,448},{1,129},{... | collective-permute-start | bytes 110600
  197.5 2.0 slice-start
  205.6 2.1 copy-start.3
  206.5 1.9 copy-start.6
Sparse Core Ops, SparseCore 0:
  11.6 22.6 reduce-scatter.4
  111.5 24.0 all-gather.8
Sparse Core Ops, SparseCore 1:
  41.6 69.7 all-gather.6
  114.3 37.3 reduce-scatter.6

commit v2 on v1

--- a/solution.py
+++ b/solution.py
@@ -38,16 +38,22 @@
     )
     for axis in ("c", "zl", "y"):
         summed = lax.psum_scatter(summed, axis, scatter_dimension=0, tiled=True)
+    summed_all = lax.all_gather(summed, DP, axis=0, tiled=False)
 
+    n_dp = _size(DP)
+    me_dp = lax.axis_index("zh") * lax.axis_size("x") + lax.axis_index("x")
     conv_rows = conv_filters.transpose(2, 0, 1).reshape(shard, -1)
-    packed = jnp.concatenate([entry_weight, conv_rows, exit_weight], axis=1)
-    packed = lax.all_gather(packed, "y", axis=0, tiled=False)
-    packed = lax.all_gather(packed, "zl", axis=1, tiled=False)
-    packed = lax.all_gather(packed, "c", axis=2, tiled=False)
-    packed = packed.reshape(n_ctx * shard, -1)
-    w_entry = packed[:, :chans]
-    w_conv = packed[:, chans : 4 * chans].reshape(bot, 3, chans)
-    w_exit = packed[:, 4 * chans :]
+    parts = [
+        lax.dynamic_slice_in_dim(w.reshape(shard, n_dp, -1), me_dp, 1, axis=1)[:, 0]
+        for w in (entry_weight, conv_rows, exit_weight)
+    ]
+    piece = jnp.concatenate(parts, axis=1)
+    packed = lax.all_gather(piece, CTX + DP, axis=0, tiled=False)
+    packed = packed.reshape(n_ctx, n_dp, shard, -1)
+    cw = chans // n_dp
+    w_entry = packed[..., :cw].transpose(0, 2, 1, 3).reshape(n_ctx * shard, chans)
+    w_conv = packed[..., cw : 4 * cw].transpose(0, 2, 1, 3).reshape(bot, 3, chans)
+    w_exit = packed[..., 4 * cw :].transpose(0, 2, 1, 3).reshape(n_ctx * shard, chans)
 
     spacing = DILATION
     edge_in = jnp.concatenate([feats, bottle, jitter], axis=1)
@@ -83,13 +89,10 @@
     lower = outs[1]
     blended = ((upper + lower) * 0.5).astype(jnp.bfloat16)[None]
     local_gap = jnp.sum((upper - lower) * (upper + lower - 2.0 * goal)) / (rows * n_ctx * chans)
-    gap = local_gap
-    for axis in ("c", "zl", "y"):
-        gap = lax.psum(gap, axis)
-    factor = gap / (2.0 * NOISE_SCALE)
-    estimate = factor * summed
-    for axis in ("x", "zh"):
-        estimate = lax.psum(estimate, axis)
+    slots = jnp.zeros((n_dp,), jnp.float32).at[me_dp].set(local_gap)
+    gaps = lax.psum(slots, CTX + DP)
+    factors = gaps / (2.0 * NOISE_SCALE)
+    estimate = jnp.sum(factors[:, None, None] * summed_all, axis=0)
     return (blended, estimate)
 
 

time: 296 us -> 1670 us (5.64)
  the two profiles are of different devices: /device:TPU:4 before, /device:TPU:2 now
where the time goes in v2:
time: 1670 us
  waiting for transfers between devices  1410 us (84%)
  blocking collectives  165 us (10%)
  local copies, waits for them, and re-layouts  54.2 us (3%)
  between operations  17.1 us (1%)
    all_gather x1, waiting for transfers between devices, body(): packed = lax.all_gather(piece, CTX + DP, axis=0, tiled=False)  1350 us
    psum x1, blocking collectives, body(): gaps = lax.psum(slots, CTX + DP)  105 us
    reduce_scatter x2, waiting for transfers between devices, body(): summed = lax.psum_scatter(summed, axis, scatter_dimension=0, tiled=True)  57.3 us
    all_gather x1, blocking collectives, body(): summed_all = lax.all_gather(summed, DP, axis=0, tiled=False)  38.9 us
  transfers between devices with their start and end apart: 7, of which 4 were waited for; matrix products, arithmetic and copies ran while one was open for 2% of the time, Pallas kernels for 0%

profile of v2, /device:TPU:2, one launch (start us, length us, event | category | flops | bytes accessed | tf_op | source)
XLA Modules:
  0.0 1673.7 jit_solution(16459171354127405826)
XLA Ops:
  9.4 1.9 fusion.43
  11.4 22.9 %reduce-scatter.5.cloned.1.call-done = f32[192,1536]{1,0:T(8,128)} async-done(((f32[384,1536]{1,0:T(8,128)}), f32[192,1536]{1,0:T(8,128)}) %reduce-scatter.5.cloned.1.call-update) | async-done | bytes 1179664 | tf_op jit(solution)/shard_map/reduce_scatter | solution.py:40
  35.7 1.3 collective-permute-start.1
  37.0 3.0 collective-permute-start
  41.9 34.4 %reduce-scatter.7.cloned.1.call-done = f32[48,1536]{1,0:T(8,128)} async-done(((f32[192,1536]{1,0:T(8,128)}), f32[48,1536]{1,0:T(8,128)}) %reduce-scatter.7.cloned.1.call-update) | async-done | bytes 294928 | tf_op jit(solution)/shard_map/reduce_scatter | solution.py:40
  76.3 21.3 %fusion = f32[8,1536]{1,0:T(8,128)S(1)} fusion(f32[48,1536]{1,0:T(8,128)} %reduce-scatter.7.cloned.1.call-done), kind=kCustom, calls=%all-reduce-scatter | all-reduce-scatter fusion | flops 98305 | bytes 346112
  97.7 2.7 collective-permute-start.2
  100.3 2.9 collective-permute-start.3
  103.3 1.4 pad_maximum_fusion.1
  105.2 1351.0 %all-gather.6.cloned.1.call-done = bf16[512,6,960]{2,1,0:T(8,128)(2,1)} async-done(((bf16[1,6,960]{2,1,0:T(8,128)(2,1)}), bf16[512,6,960]{2,1,0:T(8,128)(2,1)}) %all-gather.6.cloned.1.call-update) | async-done | bytes 5898256 | tf_op jit(solution)/shard_map/all_gather | solution.py:51
  1456.2 6.9 copy.60
  1463.4 4.1 slice_bitcast_fusion
  1467.5 1.3 copy.35
  1468.8 3.8 reshape.88
  1473.8 3.8 reshape.71
  1477.6 4.4 copy.31
  1482.0 12.4 reshape.72
  1494.4 12.1 fusion.49
  1506.5 1.8 subtract_bitcast_fusion
  1510.6 1.6 convolution_add_fusion.2
  1512.3 5.6 convolution_add_fusion
  1517.8 3.4 multiply_reduce_fusion
  1522.0 38.9 %all-gather.3 = f32[8,6,1536]{2,1,0:T(8,128)S(1)} all-gather(f32[1,6,1536]{2,1,0:T(8,128)S(1)} %dynamic-slice_bitcast_fusion), channel_id=3, replica_groups=mesh['y'=8,'zl'=4,'c'=2,'zh'=2,'x'=4] {'zh','x'}, dimensions={0}, use_global_device_ids=true | all-gather | bytes 331776 | tf_op jit(solution)/shard_map/all_gather | solution.py:41
  1560.9 104.6 %psum.7 = f32[8]{0:T(128)S(1)} all-reduce(f32[8]{0:T(128)S(1)} %scatter.4), channel_id=1, replica_groups=mesh['y'=8,'zl'=4,'c'=2,'zh'=2,'x'=4] {'y','zl','c','zh','x'}, use_global_device_ids=true, to_apply=%region_1.0 | all-reduce | flops 8 | bytes 64 | tf_op jit(solution)/shard_map/psum | solution.py:93
  (59 shorter events, 9.3 us)
Async XLA Ops:
  8.0 1.4 copy-start
  8.0 26.3 %reduce-scatter.5.cloned.1.call-start = ((), (), s32[]{:S(2)}) async-start(), calls=%async_computation.2 | async-start | bytes 3538944 | tf_op jit(solution)/shard_map/reduce_scatter | solution.py:40
  11.3 23.1 %copy-start.9 = (bf16[6,1536]{1,0:T(8,128)(2,1)S(1)}, bf16[6,1536]{1,0:T(8,128)(2,1)}, u32[]{:S(2)}) copy-start(bf16[6,1536]{1,0:T(8,128)(2,1)} %param.15) | copy-start | bytes 55300
  11.3 23.2 %copy-start.10 = (bf16[6,1536]{1,0:T(8,128)(2,1)S(1)}, bf16[6,1536]{1,0:T(8,128)(2,1)}, u32[]{:S(2)}) copy-start(bf16[6,1536]{1,0:T(8,128)(2,1)} %param.13) | copy-start | bytes 55300
  11.3 23.4 %copy-start.8 = (bf16[3,1536,6]{1,2,0:T(8,128)(2,1)S(1)}, bf16[3,1536,6]{1,2,0:T(8,128)(2,1)}, u32[]{:S(2)}) copy-start(bf16[3,1536,6]{1,2,0:T(8,128)(2,1)} %param.14) | copy-start | bytes 165892
  11.3 24.3 %copy-start.1 = (bf16[1,192,1536]{2,1,0:T(8,128)(2,1)S(1)}, bf16[1,192,1536]{2,1,0:T(8,128)(2,1)}, u32[]{:S(2)}) copy-start(bf16[1,192,1536]{2,1,0:T(8,128)(2,1)} %param.9) | copy-start | bytes 1769476
  11.3 24.3 %copy-start.4 = (bf16[1,192,384]{2,1,0:T(8,128)(2,1)S(1)}, bf16[1,192,384]{2,1,0:T(8,128)(2,1)}, u32[]{:S(2)}) copy-start(bf16[1,192,384]{2,1,0:T(8,128)(2,1)} %param.10) | copy-start | bytes 442372
  11.3 65.0 %reduce-scatter.7.cloned.1.call-start = ((), (), s32[]{:S(2)}) async-start(), calls=%async_computation.3 | async-start | bytes 1474560 | tf_op jit(solution)/shard_map/reduce_scatter | solution.py:40
  34.3 1421.9 %all-gather.6.cloned.1.call-start = ((), (), s32[]{:S(2)}) async-start(), calls=%async_computation.4 | async-start | bytes 8404992 | tf_op jit(solution)/shard_map/all_gather | solution.py:51
  35.7 67.6 %collective-permute-start.1 = (bf16[32,3456]{1,0:T(8,128)(2,1)S(1)}, bf16[32,3456]{1,0:T(8,128)(2,1)S(1)}, u32[]{:S(2)}, u32[]{:S(2)}) collective-permute-start(bf16[32,3456]{1,0:T(8,128)(2,1)S(1)} %get-tuple-element.24), channel_id=1, source_target_pairs={{8,0},{16,8},{24,16},{32,24},{40,32},{48,40},{56,48},{64,56},{72,6... | collective-permute-start | bytes 663560 | tf_op jit(solution)/shard_map/ppermute | solution.py:63
  37.0 66.3 %collective-permute-start = (bf16[32,3456]{1,0:T(8,128)(2,1)S(1)}, bf16[32,3456]{1,0:T(8,128)(2,1)S(1)}, u32[]{:S(2)}, u32[]{:S(2)}) collective-permute-start(bf16[32,3456]{1,0:T(8,128)(2,1)S(1)} %get-tuple-element.23), channel_id=1, source_target_pairs={{0,8},{8,16},{16,24},{24,32},{32,40},{40,48},{48,56},{56,64},{64,7... | collective-permute-start | bytes 663560 | tf_op jit(solution)/shard_map/ppermute | solution.py:62
  97.7 7.3 collective-permute-start.2
  100.3 4.6 collective-permute-start.3
  1494.4 12.1 copy-start.3
  1508.2 1.1 copy-start.2
  1509.4 1.2 copy-start.5
  1510.6 1.6 copy-start.6
  1512.3 5.6 copy-start.7
Sparse Core Ops, SparseCore 0:
  11.6 22.6 reduce-scatter.4
  37.4 38.8 reduce-scatter.6
Sparse Core Ops, SparseCore 1:
  37.6 1418.6 all-gather.5

commit v3 on v1

--- a/solution.py
+++ b/solution.py
@@ -19,6 +19,46 @@
     return n
 
 
+def _swap(x, axis, d):
+    n = lax.axis_size(axis)
+    return lax.ppermute(x, axis, [(i, i ^ d) for i in range(n)])
+
+
+def _bit(axis, d):
+    return (lax.axis_index(axis) // d) % 2
+
+
+DIGITS = (("y", 4), ("y", 2), ("y", 1), ("zl", 2), ("zl", 1), ("c", 1))
+
+
+def _gather_rows(piece, order):
+    held = piece.reshape((1,) * len(DIGITS) + piece.shape)
+    for axis, d in order:
+        dim = DIGITS.index((axis, d))
+        theirs = _swap(held, axis, d)
+        low = jnp.concatenate([held, theirs], axis=dim)
+        high = jnp.concatenate([theirs, held], axis=dim)
+        held = jnp.where(_bit(axis, d) == 0, low, high)
+    return held.reshape((-1,) + piece.shape[1:])
+
+
+def _scatter_rows(full, order, shard):
+    held = full.reshape((2,) * len(DIGITS) + (shard,) + full.shape[1:])
+    for axis, d in order:
+        dim = DIGITS.index((axis, d))
+        mine = _bit(axis, d)
+        keep = lax.dynamic_index_in_dim(held, mine, axis=dim, keepdims=True)
+        give = lax.dynamic_index_in_dim(held, 1 - mine, axis=dim, keepdims=True)
+        held = keep + _swap(give, axis, d)
+    return held.reshape((shard,) + full.shape[1:])
+
+
+def _sum_all(x, steps):
+    for axis, d in steps:
+        x = x + _swap(x, axis, d)
+    return x
+
+
 def body(features, bottleneck, node_noise, targets, entry_weight, conv_filters, exit_weight):
     feats = features[0]
     bottle = bottleneck[0]
@@ -30,21 +70,18 @@
     ny, nz, nc = (lax.axis_size(a) for a in CTX)
     shard = entry_weight.shape[0]
 
-    bottle_perm = (
-        bottle.reshape(rows, ny, nz, nc, shard).transpose(0, 3, 2, 1, 4).reshape(rows, bot)
+    summed = lax.dot_general(
+        bottle, jitter, (((0,), (0,)), ((), ())), preferred_element_type=jnp.float32
     )
-    summed = lax.dot_general(
-        bottle_perm, jitter, (((0,), (0,)), ((), ())), preferred_element_type=jnp.float32
+    summed = _scatter_rows(
+        summed, (("c", 1), ("zl", 1), ("zl", 2), ("y", 1), ("y", 2), ("y", 4)), shard
     )
-    for axis in ("c", "zl", "y"):
-        summed = lax.psum_scatter(summed, axis, scatter_dimension=0, tiled=True)
 
     conv_rows = conv_filters.transpose(2, 0, 1).reshape(shard, -1)
     packed = jnp.concatenate([entry_weight, conv_rows, exit_weight], axis=1)
-    packed = lax.all_gather(packed, "y", axis=0, tiled=False)
-    packed = lax.all_gather(packed, "zl", axis=1, tiled=False)
-    packed = lax.all_gather(packed, "c", axis=2, tiled=False)
-    packed = packed.reshape(n_ctx * shard, -1)
+    packed = _gather_rows(
+        packed, (("y", 4), ("y", 2), ("zl", 2), ("y", 1), ("zl", 1), ("c", 1))
+    )
     w_entry = packed[:, :chans]
     w_conv = packed[:, chans : 4 * chans].reshape(bot, 3, chans)
     w_exit = packed[:, 4 * chans :]
@@ -83,13 +120,9 @@
     lower = outs[1]
     blended = ((upper + lower) * 0.5).astype(jnp.bfloat16)[None]
     local_gap = jnp.sum((upper - lower) * (upper + lower - 2.0 * goal)) / (rows * n_ctx * chans)
-    gap = local_gap
-    for axis in ("c", "zl", "y"):
-        gap = lax.psum(gap, axis)
+    gap = _sum_all(local_gap.reshape(1), (("c", 1), ("zl", 1), ("zl", 2), ("y", 1), ("y", 2), ("y", 4)))
     factor = gap / (2.0 * NOISE_SCALE)
-    estimate = factor * summed
-    for axis in ("x", "zh"):
-        estimate = lax.psum(estimate, axis)
+    estimate = _sum_all(factor * summed, (("x", 1), ("x", 2), ("zh", 1)))
     return (blended, estimate)
 
 

time: 296 us -> 290 us (0.980)
  the two profiles are of different devices: /device:TPU:4 before, /device:TPU:52 now
where the time goes in v3:
time: 290 us; the launch traced here: 289 us
  waiting for transfers between devices  97.8 us (34%)
  starting transfers between devices  97.4 us (34%)
  local copies, waits for them, and re-layouts  39.8 us (14%)
  other arithmetic  35.5 us (12%)
  matrix products  12 us (4%)
  between operations  6.05 us (2%)
    ppermute x21, waiting for transfers between devices, _swap(): return lax.ppermute(x, axis, [(i, i ^ d) for i in range(n)])  96.1 us
    ppermute x21, starting transfers between devices, _swap(): return lax.ppermute(x, axis, [(i, i ^ d) for i in range(n)])  91 us
    select_n x7, local copies, waits for them, and re-layouts, _gather_rows(): held = jnp.where(_bit(axis, d) == 0, low, high)  19.7 us
    select_n x8, other arithmetic, _gather_rows(): held = jnp.where(_bit(axis, d) == 0, low, high)  17.7 us
    ppermute x5, local copies, waits for them, and re-layouts, _swap(): return lax.ppermute(x, axis, [(i, i ^ d) for i in range(n)])  7.38 us
    concatenate x5, other arithmetic, _gather_rows(): low = jnp.concatenate([held, theirs], axis=dim)  6.58 us
  transfers between devices with their start and end apart: 23, of which 15 were waited for; matrix products, arithmetic and copies ran while one was open for 28% of the time, Pallas kernels for 0%

profile of v3, /device:TPU:52, one launch (start us, length us, event | category | flops | bytes accessed | tf_op | source)
XLA Modules:
  0.0 288.5 jit_solution(2120418993378781583)
XLA Ops:
  2.3 3.8 %collective-permute-start.2 = (bf16[1,1,1,1,1,1,6,7680]{7,6,5,4,3,2,1,0:T(8,128)(2,1)S(1)}, bf16[1,1,1,1,1,1,6,7680]{7,6,5,4,3,2,1,0:T(8,128)(2,1)S(1)}, u32[]{:S(2)}, u32[]{:S(2)}) collective-permute-start(bf16[1,1,1,1,1,1,6,7680]{7,6,5,4,3,2,1,0:T(8,128)(2,1)S(1)} %get-tuple-element.13), channel_id=1, source_target_pairs={{0,256},{64,320},{128,384},{192,448},{256,0},{320,64},{384,128},{4... | collective-permute-start | bytes 276488 | tf_op jit(solution)/shard_map/ppermute | solution.py:24
  15.7 4.2 %collective-permute-start.3 = (bf16[2,1,1,1,1,1,6,7680]{7,6,5,4,3,2,1,0:T(8,128)(2,1)S(1)}, bf16[2,1,1,1,1,1,6,7680]{7,6,5,4,3,2,1,0:T(8,128)(2,1)S(1)}, u32[]{:S(2)}, u32[]{:S(2)}) collective-permute-start(bf16[2,1,1,1,1,1,6,7680]{7,6,5,4,3,2,1,0:T(8,128)(2,1)S(1)} %maximum_select_fusion.3), channel_id=1, source_target_pairs={{0,128},{64,192},{128,0},{192,64},{256,384},{320,448},{384,256},{4... | collective-permute-start | bytes 552968 | tf_op jit(solution)/shard_map/ppermute | solution.py:24
  21.3 6.1 %collective-permute-done.3 = bf16[2,1,1,1,1,1,6,7680]{7,6,5,4,3,2,1,0:T(8,128)(2,1)S(1)} collective-permute-done((bf16[2,1,1,1,1,1,6,7680]{7,6,5,4,3,2,1,0:T(8,128)(2,1)S(1)}, bf16[2,1,1,1,1,1,6,7680]{7,6,5,4,3,2,1,0:T(8,128)(2,1)S(1)}, u32[]{:S(2)}, u32[]{:S(2)}) %collective-permute-start.3) | collective-permute-done | bytes 184352 | tf_op jit(solution)/shard_map/ppermute | solution.py:24
  27.5 6.1 %collective-permute-start.4 = (bf16[2,2,1,1,1,1,6,7680]{7,6,5,4,3,2,1,0:T(8,128)(2,1)S(1)}, bf16[2,2,1,1,1,1,6,7680]{7,6,5,4,3,2,1,0:T(8,128)(2,1)S(1)}, u32[]{:S(2)}, u32[]{:S(2)}) collective-permute-start(bf16[2,2,1,1,1,1,6,7680]{7,6,5,4,3,2,1,0:T(8,128)(2,1)S(1)} %maximum_select_fusion.1), channel_id=1, source_target_pairs={{0,32},{16,48},{32,0},{48,16},{1,33},{17,49},{33,1},{49,17},{2,34}... | collective-permute-start | bytes 1105928 | tf_op jit(solution)/shard_map/ppermute | solution.py:24
  35.2 18.9 %collective-permute-done.4 = bf16[2,2,1,1,1,1,6,7680]{7,6,5,4,3,2,1,0:T(8,128)(2,1)S(1)} collective-permute-done((bf16[2,2,1,1,1,1,6,7680]{7,6,5,4,3,2,1,0:T(8,128)(2,1)S(1)}, bf16[2,2,1,1,1,1,6,7680]{7,6,5,4,3,2,1,0:T(8,128)(2,1)S(1)}, u32[]{:S(2)}, u32[]{:S(2)}) %collective-permute-start.4) | collective-permute-done | bytes 368672 | tf_op jit(solution)/shard_map/ppermute | solution.py:24
  55.0 7.9 %collective-permute-start.5 = (bf16[2,2,1,2,1,1,6,7680]{7,3,6,5,4,2,1,0:T(2,128)(2,1)S(1)}, bf16[2,2,1,2,1,1,6,7680]{7,3,6,5,4,2,1,0:T(2,128)(2,1)S(1)}, u32[]{:S(2)}, u32[]{:S(2)}) collective-permute-start(bf16[2,2,1,2,1,1,6,7680]{7,3,6,5,4,2,1,0:T(2,128)(2,1)S(1)} %copy.104), channel_id=1, source_target_pairs={{0,64},{64,0},{128,192},{192,128},{256,320},{320,256},{384,448},{4... | collective-permute-start | bytes 2211848 | tf_op jit(solution)/shard_map/ppermute | solution.py:24
  69.3 9.7 %collective-permute-done.5 = bf16[2,2,1,2,1,1,6,7680]{7,3,6,5,4,2,1,0:T(2,128)(2,1)S(1)} collective-permute-done((bf16[2,2,1,2,1,1,6,7680]{7,3,6,5,4,2,1,0:T(2,128)(2,1)S(1)}, bf16[2,2,1,2,1,1,6,7680]{7,3,6,5,4,2,1,0:T(2,128)(2,1)S(1)}, u32[]{:S(2)}, u32[]{:S(2)}) %collective-permute-start.5) | collective-permute-done | bytes 737312 | tf_op jit(solution)/shard_map/ppermute | solution.py:24
  88.7 5.3 %collective-permute-start.16 = (f32[2,2,2,1,1,1,6,1536]{7,6,5,4,3,2,1,0:T(8,128)S(1)}, f32[2,2,2,1,1,1,6,1536]{7,6,5,4,3,2,1,0:T(8,128)S(1)}, u32[]{:S(2)}, u32[]{:S(2)}) collective-permute-start(f32[2,2,2,1,1,1,6,1536]{7,6,5,4,3,2,1,0:T(8,128)S(1)} %constant_dynamic-slice_fusion.3), channel_id=1, source_target_pairs={{0,32},{16,48},{32,0},{48,16},{1,33},{17,49},{33,1},{49,17},{2,34}... | collective-permute-start | bytes 884744 | tf_op jit(solution)/shard_map/ppermute | solution.py:24
  94.0 32.4 %collective-permute-done.6 = bf16[2,2,2,2,1,1,6,7680]{7,3,6,5,4,2,1,0:T(2,128)(2,1)S(1)} collective-permute-done((bf16[2,2,2,2,1,1,6,7680]{7,3,6,5,4,2,1,0:T(2,128)(2,1)S(1)}, bf16[2,2,2,2,1,1,6,7680]{7,3,6,5,4,2,1,0:T(2,128)(2,1)S(1)}, u32[]{:S(2)}, u32[]{:S(2)}) %collective-permute-start.6) | collective-permute-done | bytes 1474592 | tf_op jit(solution)/shard_map/ppermute | solution.py:24
  128.0 4.4 %broadcast_select_fusion.1 = bf16[2,2,2,2,2,1,6,7680]{7,0,6,1,3,2,5,4:T(2,128)(2,1)S(1)} fusion(pred[]{:T(512)S(6)} %eq.32, bf16[2,2,2,2,1,1,6,7680]{7,0,6,1,3,2,5,4:T(2,128)(2,1)S(1)} %copy.109, bf16[2,2,2,2,1,1,6,7680]{7,0,6,1,3,2,5,4:T(2,128)(2,1)S(1)} %fusion.9), kind=kLoop, calls=%fused_computation.1 | loop fusion | flops 4423680 | bytes 5898241 | tf_op jit(solution)/shard_map/jit(_where)/select_n | solution.py:41
  132.3 4.6 %copy.111 = bf16[2,2,2,2,2,1,6,7680]{7,4,6,5,3,2,1,0:T(2,128)(2,1)} copy(bf16[2,2,2,2,2,1,6,7680]{7,0,6,1,3,2,5,4:T(2,128)(2,1)S(1)} %broadcast_select_fusion.1) | data formatting | bytes 5898240 | tf_op jit(solution)/shard_map/jit(_where)/select_n | solution.py:41
  144.0 4.4 %collective-permute-start.1 = (bf16[32,3456]{1,0:T(8,128)(2,1)}, bf16[32,3456]{1,0:T(8,128)(2,1)}, u32[]{:S(2)}, u32[]{:S(2)}) collective-permute-start(bf16[32,3456]{1,0:T(8,128)(2,1)} %get-tuple-element.7), channel_id=1, source_target_pairs={{8,0},{16,8},{24,16},{32,24},{40,32},{48,40},{56,48},{64,56},{72,6... | collective-permute-start | bytes 663560 | tf_op jit(solution)/shard_map/ppermute | solution.py:94
  151.5 5.5 %collective-permute-start.18 = (f32[2,1,1,1,1,1,6,1536]{7,6,5,4,3,2,1,0:T(8,128)S(1)}, f32[2,1,1,1,1,1,6,1536]{7,6,5,4,3,2,1,0:T(8,128)S(1)}, u32[]{:S(2)}, u32[]{:S(2)}) collective-permute-start(f32[2,1,1,1,1,1,6,1536]{7,6,5,4,3,2,1,0:T(8,128)S(1)} %constant_dynamic-slice_fusion.1), channel_id=1, source_target_pairs={{0,128},{64,192},{128,0},{192,64},{256,384},{320,448},{384,256},{4... | collective-permute-start | bytes 221192 | tf_op jit(solution)/shard_map/ppermute | solution.py:24
  162.0 11.7 %collective-permute-start.19 = (f32[1,1,1,1,1,1,6,1536]{7,6,5,4,3,2,1,0:T(8,128)}, f32[1,1,1,1,1,1,6,1536]{7,6,5,4,3,2,1,0:T(8,128)}, u32[]{:S(2)}, u32[]{:S(2)}) collective-permute-start(f32[1,1,1,1,1,1,6,1536]{7,6,5,4,3,2,1,0:T(8,128)} %constant_dynamic-slice_fusion), channel_id=1, source_target_pairs={{0,256},{64,320},{128,384},{192,448},{256,0},{320,64},{384,128},{4... | collective-permute-start | bytes 110600 | tf_op jit(solution)/shard_map/ppermute | solution.py:24
  173.8 4.9 %copy.112 = bf16[2,2,2,2,2,1,6,7680]{7,0,6,1,3,2,5,4:T(2,128)(2,1)S(1)} copy(bf16[2,2,2,2,2,1,6,7680]{7,4,6,5,3,2,1,0:T(2,128)(2,1)} %collective-permute-done.7) | data formatting | bytes 5898240 | tf_op jit(solution)/shard_map/ppermute | solution.py:24
  178.6 8.8 %broadcast_select_fusion = bf16[2,2,2,2,2,2,6,7680]{7,0,6,1,3,2,5,4:T(2,128)(2,1)S(1)} fusion(pred[]{:T(512)S(6)} %eq.31, bf16[2,2,2,2,2,1,6,7680]{7,0,6,1,3,2,5,4:T(2,128)(2,1)S(1)} %copy.112, bf16[2,2,2,2,2,1,6,7680]{7,0,6,1,3,2,5,4:T(2,128)(2,1)S(1)} %broadcast_select_fusion.1), kind=kLoop, calls=%fused_computation | loop fusion | flops 8847360 | bytes 11796481 | tf_op jit(solution)/shard_map/jit(_where)/select_n | solution.py:41
  187.4 4.2 %copy.114 = bf16[2,2,2,2,2,2,6,7680]{7,6,5,4,3,2,1,0:T(8,128)(2,1)} copy(bf16[2,2,2,2,2,2,6,7680]{7,0,6,1,3,2,5,4:T(2,128)(2,1)S(1)} %broadcast_select_fusion) | data formatting | bytes 11796480 | tf_op jit(solution)/shard_map/jit(_where)/select_n | solution.py:41
  191.7 8.8 %select_n.332 = bf16[384,7680]{1,0:T(8,128)(2,1)} reshape(bf16[2,2,2,2,2,2,6,7680]{7,6,5,4,3,2,1,0:T(8,128)(2,1)} %copy.114) | data formatting | bytes 11796480 | tf_op jit(solution)/shard_map/jit(_where)/select_n | solution.py:41
  202.4 3.6 %copy.115 = bf16[384,4608]{0,1:T(8,128)(2,1)} copy(bf16[384,4608]{1,0:T(8,128)(2,1)S(1)} %slice-done) | data formatting | bytes 7077888 | tf_op jit(solution)/shard_map/slice | solution.py:86
  213.0 5.1 %convolution_add_fusion = f32[2,192,1536]{2,1,0:T(8,128)} fusion(f32[1,256,1536]{2,1,0:T(8,128)S(1)} %get-tuple-element.3, f32[1,256,1536]{2,1,0:T(8,128)S(1)} %get-tuple-element.2, bf16[384,7680]{1,0:T(8,128)(2,1)} %select_n.332, f32[2,192,384]{2,1,0:T(8,128)} %convolution_add_fusion.2, bf16[384,3,1536]{0,2,1:T(8,128)(2,1)} %bitcast.89, ...), kind=kOutput, calls=%fused_computation.14 | convolution fusion | flops 908623872 | bytes 9633792 | tf_op jit(solution)/shard_map/dot_general | solution.py:116
  218.1 3.7 %multiply_reduce_fusion = (f32[]{:T(128)}, bf16[1,192,1536]{2,1,0:T(8,128)(2,1)}) fusion(bf16[1,192,1536]{2,1,0:T(8,128)(2,1)} %param.10, f32[2,192,1536]{2,1,0:T(8,128)} %convolution_add_fusion), kind=kLoop, calls=%fused_computation.38 | loop fusion | flops 2654207 | bytes 3538948 | tf_op jit(solution)/shard_map/reduce_sum | solution.py:122
  255.5 6.1 %collective-permute-done.13 = f32[1]{0:T(128)} collective-permute-done((f32[1]{0:T(128)}, f32[1]{0:T(128)}, u32[]{:S(2)}, u32[]{:S(2)}) %collective-permute-start.13) | collective-permute-done | bytes 36 | tf_op jit(solution)/shard_map/ppermute | solution.py:24
  271.5 5.3 %collective-permute-done.21 = f32[6,1536]{1,0:T(8,128)S(1)} collective-permute-done((f32[6,1536]{1,0:T(8,128)S(1)}, f32[6,1536]{1,0:T(8,128)S(1)}, u32[]{:S(2)}, u32[]{:S(2)}) %collective-permute-start.21) | collective-permute-done | bytes 36896 | tf_op jit(solution)/shard_map/ppermute | solution.py:24
  276.7 9.1 %collective-permute-start.22 = (f32[6,1536]{1,0:T(8,128)S(1)}, f32[6,1536]{1,0:T(8,128)S(1)}, u32[]{:S(2)}, u32[]{:S(2)}) collective-permute-start(f32[6,1536]{1,0:T(8,128)S(1)} %add.206), channel_id=1, source_target_pairs={{0,4},{4,0},{1,5},{5,1},{2,6},{6,2},{3,7},{7,3},{8,12},{12,8},{9,1... | collective-permute-start | bytes 110600 | tf_op jit(solution)/shard_map/ppermute | solution.py:24
  (101 shorter events, 98.1 us)
Async XLA Ops:
  2.3 13.3 %collective-permute-start.2 = (bf16[1,1,1,1,1,1,6,7680]{7,6,5,4,3,2,1,0:T(8,128)(2,1)S(1)}, bf16[1,1,1,1,1,1,6,7680]{7,6,5,4,3,2,1,0:T(8,128)(2,1)S(1)}, u32[]{:S(2)}, u32[]{:S(2)}) collective-permute-start(bf16[1,1,1,1,1,1,6,7680]{7,6,5,4,3,2,1,0:T(8,128)(2,1)S(1)} %get-tuple-element.13), channel_id=1, source_target_pairs={{0,256},{64,320},{128,384},{192,448},{256,0},{320,64},{384,128},{4... | collective-permute-start | bytes 276488 | tf_op jit(solution)/shard_map/ppermute | solution.py:24
  11.8 53.9 %collective-permute-start.14 = (f32[2,2,2,2,2,1,6,1536]{7,4,6,5,3,2,1,0:T(2,128)S(1)}, f32[2,2,2,2,2,1,6,1536]{7,4,6,5,3,2,1,0:T(2,128)S(1)}, u32[]{:S(2)}, u32[]{:S(2)}) collective-permute-start(f32[2,2,2,2,2,1,6,1536]{7,4,6,5,3,2,1,0:T(2,128)S(1)} %copy.120), channel_id=1, source_target_pairs={{0,8},{8,0},{1,9},{9,1},{2,10},{10,2},{3,11},{11,3},{4,12},{12,4},... | collective-permute-start | bytes 3538952 | tf_op jit(solution)/shard_map/ppermute | solution.py:24
  15.7 11.7 %collective-permute-start.3 = (bf16[2,1,1,1,1,1,6,7680]{7,6,5,4,3,2,1,0:T(8,128)(2,1)S(1)}, bf16[2,1,1,1,1,1,6,7680]{7,6,5,4,3,2,1,0:T(8,128)(2,1)S(1)}, u32[]{:S(2)}, u32[]{:S(2)}) collective-permute-start(bf16[2,1,1,1,1,1,6,7680]{7,6,5,4,3,2,1,0:T(8,128)(2,1)S(1)} %maximum_select_fusion.3), channel_id=1, source_target_pairs={{0,128},{64,192},{128,0},{192,64},{256,384},{320,448},{384,256},{4... | collective-permute-start | bytes 552968 | tf_op jit(solution)/shard_map/ppermute | solution.py:24
  27.5 26.6 %collective-permute-start.4 = (bf16[2,2,1,1,1,1,6,7680]{7,6,5,4,3,2,1,0:T(8,128)(2,1)S(1)}, bf16[2,2,1,1,1,1,6,7680]{7,6,5,4,3,2,1,0:T(8,128)(2,1)S(1)}, u32[]{:S(2)}, u32[]{:S(2)}) collective-permute-start(bf16[2,2,1,1,1,1,6,7680]{7,6,5,4,3,2,1,0:T(8,128)(2,1)S(1)} %maximum_select_fusion.1), channel_id=1, source_target_pairs={{0,32},{16,48},{32,0},{48,16},{1,33},{17,49},{33,1},{49,17},{2,34}... | collective-permute-start | bytes 1105928 | tf_op jit(solution)/shard_map/ppermute | solution.py:24
  55.0 24.0 %collective-permute-start.5 = (bf16[2,2,1,2,1,1,6,7680]{7,3,6,5,4,2,1,0:T(2,128)(2,1)S(1)}, bf16[2,2,1,2,1,1,6,7680]{7,3,6,5,4,2,1,0:T(2,128)(2,1)S(1)}, u32[]{:S(2)}, u32[]{:S(2)}) collective-permute-start(bf16[2,2,1,2,1,1,6,7680]{7,3,6,5,4,2,1,0:T(2,128)(2,1)S(1)} %copy.104), channel_id=1, source_target_pairs={{0,64},{64,0},{128,192},{192,128},{256,320},{320,256},{384,448},{4... | collective-permute-start | bytes 2211848 | tf_op jit(solution)/shard_map/ppermute | solution.py:24
  66.7 21.8 %collective-permute-start.15 = (f32[2,2,2,2,1,1,6,1536]{7,3,6,5,4,2,1,0:T(2,128)S(1)}, f32[2,2,2,2,1,1,6,1536]{7,3,6,5,4,2,1,0:T(2,128)S(1)}, u32[]{:S(2)}, u32[]{:S(2)}) collective-permute-start(f32[2,2,2,2,1,1,6,1536]{7,3,6,5,4,2,1,0:T(2,128)S(1)} %copy.122), channel_id=1, source_target_pairs={{0,16},{16,0},{32,48},{48,32},{1,17},{17,1},{33,49},{49,33},{2,18}... | collective-permute-start | bytes 1769480 | tf_op jit(solution)/shard_map/ppermute | solution.py:24
  82.9 43.5 %collective-permute-start.6 = (bf16[2,2,2,2,1,1,6,7680]{7,3,6,5,4,2,1,0:T(2,128)(2,1)S(1)}, bf16[2,2,2,2,1,1,6,7680]{7,3,6,5,4,2,1,0:T(2,128)(2,1)S(1)}, u32[]{:S(2)}, u32[]{:S(2)}) collective-permute-start(bf16[2,2,2,2,1,1,6,7680]{7,3,6,5,4,2,1,0:T(2,128)(2,1)S(1)} %copy.108), channel_id=1, source_target_pairs={{0,16},{16,0},{32,48},{48,32},{1,17},{17,1},{33,49},{49,33},{2,18}... | collective-permute-start | bytes 4423688 | tf_op jit(solution)/shard_map/ppermute | solution.py:24
  88.7 50.3 %collective-permute-start.16 = (f32[2,2,2,1,1,1,6,1536]{7,6,5,4,3,2,1,0:T(8,128)S(1)}, f32[2,2,2,1,1,1,6,1536]{7,6,5,4,3,2,1,0:T(8,128)S(1)}, u32[]{:S(2)}, u32[]{:S(2)}) collective-permute-start(f32[2,2,2,1,1,1,6,1536]{7,6,5,4,3,2,1,0:T(8,128)S(1)} %constant_dynamic-slice_fusion.3), channel_id=1, source_target_pairs={{0,32},{16,48},{32,0},{48,16},{1,33},{17,49},{33,1},{49,17},{2,34}... | collective-permute-start | bytes 884744 | tf_op jit(solution)/shard_map/ppermute | solution.py:24
  136.9 36.8 %collective-permute-start.7 = (bf16[2,2,2,2,2,1,6,7680]{7,4,6,5,3,2,1,0:T(2,128)(2,1)}, bf16[2,2,2,2,2,1,6,7680]{7,4,6,5,3,2,1,0:T(2,128)(2,1)}, u32[]{:S(2)}, u32[]{:S(2)}) collective-permute-start(bf16[2,2,2,2,2,1,6,7680]{7,4,6,5,3,2,1,0:T(2,128)(2,1)} %copy.111), channel_id=1, source_target_pairs={{0,8},{8,0},{1,9},{9,1},{2,10},{10,2},{3,11},{11,3},{4,12},{12,4},... | collective-permute-start | bytes 8847368 | tf_op jit(solution)/shard_map/ppermute | solution.py:24
  139.8 10.5 %collective-permute-start.17 = (f32[2,2,1,1,1,1,6,1536]{7,6,5,4,3,2,1,0:T(8,128)}, f32[2,2,1,1,1,1,6,1536]{7,6,5,4,3,2,1,0:T(8,128)}, u32[]{:S(2)}, u32[]{:S(2)}) collective-permute-start(f32[2,2,1,1,1,1,6,1536]{7,6,5,4,3,2,1,0:T(8,128)} %constant_dynamic-slice_fusion.2), channel_id=1, source_target_pairs={{0,64},{64,0},{128,192},{192,128},{256,320},{320,256},{384,448},{4... | collective-permute-start | bytes 442376 | tf_op jit(solution)/shard_map/ppermute | solution.py:24
  144.0 13.0 %collective-permute-start.1 = (bf16[32,3456]{1,0:T(8,128)(2,1)}, bf16[32,3456]{1,0:T(8,128)(2,1)}, u32[]{:S(2)}, u32[]{:S(2)}) collective-permute-start(bf16[32,3456]{1,0:T(8,128)(2,1)} %get-tuple-element.7), channel_id=1, source_target_pairs={{8,0},{16,8},{24,16},{32,24},{40,32},{48,40},{56,48},{64,56},{72,6... | collective-permute-start | bytes 663560 | tf_op jit(solution)/shard_map/ppermute | solution.py:94
  148.4 10.3 %collective-permute-start = (bf16[32,3456]{1,0:T(8,128)(2,1)}, bf16[32,3456]{1,0:T(8,128)(2,1)}, u32[]{:S(2)}, u32[]{:S(2)}) collective-permute-start(bf16[32,3456]{1,0:T(8,128)(2,1)} %get-tuple-element.6), channel_id=1, source_target_pairs={{0,8},{8,16},{16,24},{24,32},{32,40},{40,48},{48,56},{56,64},{64,7... | collective-permute-start | bytes 663560 | tf_op jit(solution)/shard_map/ppermute | solution.py:93
  151.5 9.9 %collective-permute-start.18 = (f32[2,1,1,1,1,1,6,1536]{7,6,5,4,3,2,1,0:T(8,128)S(1)}, f32[2,1,1,1,1,1,6,1536]{7,6,5,4,3,2,1,0:T(8,128)S(1)}, u32[]{:S(2)}, u32[]{:S(2)}) collective-permute-start(f32[2,1,1,1,1,1,6,1536]{7,6,5,4,3,2,1,0:T(8,128)S(1)} %constant_dynamic-slice_fusion.1), channel_id=1, source_target_pairs={{0,128},{64,192},{128,0},{192,64},{256,384},{320,448},{384,256},{4... | collective-permute-start | bytes 221192 | tf_op jit(solution)/shard_map/ppermute | solution.py:24
  162.0 100.2 %collective-permute-start.19 = (f32[1,1,1,1,1,1,6,1536]{7,6,5,4,3,2,1,0:T(8,128)}, f32[1,1,1,1,1,1,6,1536]{7,6,5,4,3,2,1,0:T(8,128)}, u32[]{:S(2)}, u32[]{:S(2)}) collective-permute-start(f32[1,1,1,1,1,1,6,1536]{7,6,5,4,3,2,1,0:T(8,128)} %constant_dynamic-slice_fusion), channel_id=1, source_target_pairs={{0,256},{64,320},{128,384},{192,448},{256,0},{320,64},{384,128},{4... | collective-permute-start | bytes 110600 | tf_op jit(solution)/shard_map/ppermute | solution.py:24
  218.1 44.1 %copy-start.9 = (f32[2,1,1,1,1,1,6,1536]{7,6,5,4,3,2,1,0:T(8,128)S(1)}, f32[2,1,1,1,1,1,6,1536]{7,6,5,4,3,2,1,0:T(8,128)}, u32[]{:S(2)}) copy-start(f32[2,1,1,1,1,1,6,1536]{7,6,5,4,3,2,1,0:T(8,128)} %copy-done.8) | copy-start | bytes 221188
  222.5 3.1 %collective-permute-start.8 = (f32[1]{0:T(128)}, f32[1]{0:T(128)}, u32[]{:S(2)}, u32[]{:S(2)}) collective-permute-start(f32[1]{0:T(128)} %bitcast.28), channel_id=1, source_target_pairs={{0,8},{8,0},{1,9},{9,1},{2,10},{10,2},{3,11},{11,3},{4,12},{12,4},... | collective-permute-start | bytes 20 | tf_op jit(solution)/shard_map/ppermute | solution.py:24
  226.2 5.4 %collective-permute-start.9 = (f32[1]{0:T(128)}, f32[1]{0:T(128)}, u32[]{:S(2)}, u32[]{:S(2)}) collective-permute-start(f32[1]{0:T(128)} %add.181), channel_id=1, source_target_pairs={{0,16},{16,0},{32,48},{48,32},{1,17},{17,1},{33,49},{49,33},{2,18}... | collective-permute-start | bytes 20 | tf_op jit(solution)/shard_map/ppermute | solution.py:24
  232.3 6.3 %collective-permute-start.10 = (f32[1]{0:T(128)}, f32[1]{0:T(128)}, u32[]{:S(2)}, u32[]{:S(2)}) collective-permute-start(f32[1]{0:T(128)} %add.182), channel_id=1, source_target_pairs={{0,32},{16,48},{32,0},{48,16},{1,33},{17,49},{33,1},{49,17},{2,34}... | collective-permute-start | bytes 20 | tf_op jit(solution)/shard_map/ppermute | solution.py:24
  239.2 5.4 %collective-permute-start.11 = (f32[1]{0:T(128)}, f32[1]{0:T(128)}, u32[]{:S(2)}, u32[]{:S(2)}) collective-permute-start(f32[1]{0:T(128)} %add.183), channel_id=1, source_target_pairs={{0,64},{64,0},{128,192},{192,128},{256,320},{320,256},{384,448},{4... | collective-permute-start | bytes 20 | tf_op jit(solution)/shard_map/ppermute | solution.py:24
  245.3 6.3 %collective-permute-start.12 = (f32[1]{0:T(128)}, f32[1]{0:T(128)}, u32[]{:S(2)}, u32[]{:S(2)}) collective-permute-start(f32[1]{0:T(128)} %add.184), channel_id=1, source_target_pairs={{0,128},{64,192},{128,0},{192,64},{256,384},{320,448},{384,256},{4... | collective-permute-start | bytes 20 | tf_op jit(solution)/shard_map/ppermute | solution.py:24
  252.3 9.3 %collective-permute-start.13 = (f32[1]{0:T(128)}, f32[1]{0:T(128)}, u32[]{:S(2)}, u32[]{:S(2)}) collective-permute-start(f32[1]{0:T(128)} %add.185), channel_id=1, source_target_pairs={{0,256},{64,320},{128,384},{192,448},{256,0},{320,64},{384,128},{4... | collective-permute-start | bytes 20 | tf_op jit(solution)/shard_map/ppermute | solution.py:24
  263.1 6.2 %collective-permute-start.20 = (f32[6,1536]{1,0:T(8,128)S(1)}, f32[6,1536]{1,0:T(8,128)S(1)}, u32[]{:S(2)}, u32[]{:S(2)}) collective-permute-start(f32[6,1536]{1,0:T(8,128)S(1)} %multiply_bitcast_fusion), channel_id=1, source_target_pairs={{0,1},{1,0},{2,3},{3,2},{4,5},{5,4},{6,7},{7,6},{8,9},{9,8},{10,11... | collective-permute-start | bytes 110600 | tf_op jit(solution)/shard_map/ppermute | solution.py:24
  269.3 7.5 %collective-permute-start.21 = (f32[6,1536]{1,0:T(8,128)S(1)}, f32[6,1536]{1,0:T(8,128)S(1)}, u32[]{:S(2)}, u32[]{:S(2)}) collective-permute-start(f32[6,1536]{1,0:T(8,128)S(1)} %add.205), channel_id=1, source_target_pairs={{0,2},{1,3},{2,0},{3,1},{4,6},{5,7},{6,4},{7,5},{8,10},{9,11},{10,... | collective-permute-start | bytes 110600 | tf_op jit(solution)/shard_map/ppermute | solution.py:24
  276.7 11.2 %collective-permute-start.22 = (f32[6,1536]{1,0:T(8,128)S(1)}, f32[6,1536]{1,0:T(8,128)S(1)}, u32[]{:S(2)}, u32[]{:S(2)}) collective-permute-start(f32[6,1536]{1,0:T(8,128)S(1)} %add.206), channel_id=1, source_target_pairs={{0,4},{4,0},{1,5},{5,1},{2,6},{6,2},{3,7},{7,3},{8,12},{12,8},{9,1... | collective-permute-start | bytes 110600 | tf_op jit(solution)/shard_map/ppermute | solution.py:24
  (10 other events, 49.3 us)

commit v4 on v3

--- a/solution.py
+++ b/solution.py
@@ -79,9 +79,8 @@
 
     conv_rows = conv_filters.transpose(2, 0, 1).reshape(shard, -1)
     packed = jnp.concatenate([entry_weight, conv_rows, exit_weight], axis=1)
-    packed = _gather_rows(
-        packed, (("y", 4), ("y", 2), ("zl", 2), ("y", 1), ("zl", 1), ("c", 1))
-    )
+    for axis in ("y", "zl", "c"):
+        packed = lax.all_gather(packed, axis, axis=0, tiled=True)
     w_entry = packed[:, :chans]
     w_conv = packed[:, chans : 4 * chans].reshape(bot, 3, chans)
     w_exit = packed[:, 4 * chans :]
@@ -94,7 +93,13 @@
     from_next = lax.ppermute(edge_in[:spacing], CTX, pairs_down)
     ext = jnp.concatenate([from_prev, edge_in, from_next], axis=0)
     ext_feats = ext[:, :chans]
-    ext_bottle = ext[:, chans : chans + bot]
+    ny, nz, nc = (lax.axis_size(a) for a in CTX)
+    ext_bottle = (
+        ext[:, chans : chans + bot]
+        .reshape(-1, ny, nz, nc, shard)
+        .transpose(0, 3, 2, 1, 4)
+        .reshape(-1, bot)
+    )
     ext_jitter = ext[:, chans + bot :]
 
     baseline = ext_feats.astype(jnp.float32) + jnp.dot(
@@ -120,7 +125,9 @@
     lower = outs[1]
     blended = ((upper + lower) * 0.5).astype(jnp.bfloat16)[None]
     local_gap = jnp.sum((upper - lower) * (upper + lower - 2.0 * goal)) / (rows * n_ctx * chans)
-    gap = _sum_all(local_gap.reshape(1), (("c", 1), ("zl", 1), ("zl", 2), ("y", 1), ("y", 2), ("y", 4)))
+    gap = local_gap
+    for axis in ("c", "zl", "y"):
+        gap = lax.psum(gap, axis)
     factor = gap / (2.0 * NOISE_SCALE)
     estimate = _sum_all(factor * summed, (("x", 1), ("x", 2), ("zh", 1)))
     return (blended, estimate)

time: 290 us -> 267 us (0.921)
  the two profiles are of different devices: /device:TPU:52 before, /device:TPU:2 now
where the time goes in v4:
time: 267 us; the launch traced here: 266 us
  waiting for transfers between devices  105 us (39%)
  blocking collectives  59 us (22%)
  starting transfers between devices  46.5 us (17%)
  between operations  15.9 us (6%)
  local copies, waits for them, and re-layouts  15.7 us (6%)
  other arithmetic  12.6 us (5%)
  matrix products  11.8 us (4%)
    all_gather x2, waiting for transfers between devices, body(): packed = lax.all_gather(packed, axis, axis=0, tiled=True)  64.2 us
    ppermute x9, starting transfers between devices, _swap(): return lax.ppermute(x, axis, [(i, i ^ d) for i in range(n)])  42.1 us
    ppermute x9, waiting for transfers between devices, _swap(): return lax.ppermute(x, axis, [(i, i ^ d) for i in range(n)])  40.6 us
    psum x3, blocking collectives, body(): gap = lax.psum(gap, axis)  30.7 us
    all_gather x1, blocking collectives, body(): packed = lax.all_gather(packed, axis, axis=0, tiled=True)  28.3 us
    slice x3, local copies, waits for them, and re-layouts, body(): w_conv = packed[:, chans:4 * chans].reshape(bot, 3, chans)  5.61 us
    unnamed x25, local copies, waits for them, and re-layouts  5.59 us
    dot_general x1, matrix products, body(): jnp.dot(inner, w_exit, preferred_element_type=jnp.float32)  5.49 us
  transfers between devices with their start and end apart: 13, of which 8 were waited for; matrix products, arithmetic and copies ran while one was open for 11% of the time, Pallas kernels for 0%

profile of v4, /device:TPU:2, one launch (start us, length us, event | category | flops | bytes accessed | tf_op | source)
XLA Modules:
  0.0 266.3 jit_solution(2195391306737188750)
XLA Ops:
  8.2 28.3 %all-gather = bf16[8,6,7680]{2,1,0:T(8,128)(2,1)S(1)} all-gather(bf16[1,6,7680]{2,1,0:T(8,128)(2,1)S(1)} %maximum_bitcast_fusion), channel_id=1, replica_groups=mesh['y'=8,'zl'=4,'c'=2,'zh'=2,'x'=4] {'y'}, dimensions={0}, use_global_device_ids=true | all-gather | bytes 829440 | tf_op jit(solution)/shard_map/all_gather | solution.py:83
  43.4 64.2 %all-gather.4.cloned.1.call-done = bf16[192,7680]{1,0:T(8,128)(2,1)} async-done(((bf16[48,7680]{1,0:T(8,128)(2,1)}), bf16[192,7680]{1,0:T(8,128)(2,1)}) %all-gather.4.cloned.1.call-update) | async-done | bytes 2949136 | tf_op jit(solution)/shard_map/all_gather | solution.py:83
  110.9 3.2 %collective-permute-start.3 = (f32[2,2,2,2,1,1,6,1536]{7,3,6,5,4,2,1,0:T(2,128)S(1)}, f32[2,2,2,2,1,1,6,1536]{7,3,6,5,4,2,1,0:T(2,128)S(1)}, u32[]{:S(2)}, u32[]{:S(2)}) collective-permute-start(f32[2,2,2,2,1,1,6,1536]{7,3,6,5,4,2,1,0:T(2,128)S(1)} %copy.26), channel_id=1, source_target_pairs={{0,16},{16,0},{32,48},{48,32},{1,17},{17,1},{33,49},{49,33},{2,18}... | collective-permute-start | bytes 1769480 | tf_op jit(solution)/shard_map/ppermute | solution.py:24
  114.2 13.7 %collective-permute-done.3 = f32[2,2,2,2,1,1,6,1536]{7,3,6,5,4,2,1,0:T(2,128)S(1)} collective-permute-done((f32[2,2,2,2,1,1,6,1536]{7,3,6,5,4,2,1,0:T(2,128)S(1)}, f32[2,2,2,2,1,1,6,1536]{7,3,6,5,4,2,1,0:T(2,128)S(1)}, u32[]{:S(2)}, u32[]{:S(2)}) %collective-permute-start.3) | collective-permute-done | bytes 589856 | tf_op jit(solution)/shard_map/ppermute | solution.py:24
  129.4 4.5 %collective-permute-start.4 = (f32[2,2,2,1,1,1,6,1536]{7,6,5,4,3,2,1,0:T(8,128)S(1)}, f32[2,2,2,1,1,1,6,1536]{7,6,5,4,3,2,1,0:T(8,128)}, u32[]{:S(2)}, u32[]{:S(2)}) collective-permute-start(f32[2,2,2,1,1,1,6,1536]{7,6,5,4,3,2,1,0:T(8,128)S(1)} %constant_dynamic-slice_fusion.3), channel_id=1, source_target_pairs={{0,32},{16,48},{32,0},{48,16},{1,33},{17,49},{33,1},{49,17},{2,34}... | collective-permute-start | bytes 884744 | tf_op jit(solution)/shard_map/ppermute | solution.py:24
  135.2 3.0 %collective-permute-start = (bf16[32,3456]{1,0:T(8,128)(2,1)S(1)}, bf16[32,3456]{1,0:T(8,128)(2,1)S(1)}, u32[]{:S(2)}, u32[]{:S(2)}) collective-permute-start(bf16[32,3456]{1,0:T(8,128)(2,1)S(1)} %get-tuple-element.6), channel_id=1, source_target_pairs={{0,8},{8,16},{16,24},{24,32},{32,40},{40,48},{48,56},{56,64},{64,7... | collective-permute-start | bytes 663560 | tf_op jit(solution)/shard_map/ppermute | solution.py:92
  138.3 12.2 %collective-permute-done.4 = f32[2,2,2,1,1,1,6,1536]{7,6,5,4,3,2,1,0:T(8,128)} collective-permute-done((f32[2,2,2,1,1,1,6,1536]{7,6,5,4,3,2,1,0:T(8,128)S(1)}, f32[2,2,2,1,1,1,6,1536]{7,6,5,4,3,2,1,0:T(8,128)}, u32[]{:S(2)}, u32[]{:S(2)}) %collective-permute-start.4) | collective-permute-done | bytes 294944 | tf_op jit(solution)/shard_map/ppermute | solution.py:24
  151.6 5.8 %collective-permute-start.5 = (f32[2,2,1,1,1,1,6,1536]{7,6,5,4,3,2,1,0:T(8,128)S(1)}, f32[2,2,1,1,1,1,6,1536]{7,6,5,4,3,2,1,0:T(8,128)S(1)}, u32[]{:S(2)}, u32[]{:S(2)}) collective-permute-start(f32[2,2,1,1,1,1,6,1536]{7,6,5,4,3,2,1,0:T(8,128)S(1)} %constant_dynamic-slice_fusion.2), channel_id=1, source_target_pairs={{0,64},{64,0},{128,192},{192,128},{256,320},{320,256},{384,448},{4... | collective-permute-start | bytes 442376 | tf_op jit(solution)/shard_map/ppermute | solution.py:24
  158.8 2.8 %collective-permute-done.5 = f32[2,2,1,1,1,1,6,1536]{7,6,5,4,3,2,1,0:T(8,128)S(1)} collective-permute-done((f32[2,2,1,1,1,1,6,1536]{7,6,5,4,3,2,1,0:T(8,128)S(1)}, f32[2,2,1,1,1,1,6,1536]{7,6,5,4,3,2,1,0:T(8,128)S(1)}, u32[]{:S(2)}, u32[]{:S(2)}) %collective-permute-start.5) | collective-permute-done | bytes 147488 | tf_op jit(solution)/shard_map/ppermute | solution.py:24
  161.6 4.6 %collective-permute-start.6 = (f32[2,1,1,1,1,1,6,1536]{7,6,5,4,3,2,1,0:T(8,128)S(1)}, f32[2,1,1,1,1,1,6,1536]{7,6,5,4,3,2,1,0:T(8,128)S(1)}, u32[]{:S(2)}, u32[]{:S(2)}) collective-permute-start(f32[2,1,1,1,1,1,6,1536]{7,6,5,4,3,2,1,0:T(8,128)S(1)} %constant_dynamic-slice_fusion.1), channel_id=1, source_target_pairs={{0,128},{64,192},{128,0},{192,64},{256,384},{320,448},{384,256},{4... | collective-permute-start | bytes 221192 | tf_op jit(solution)/shard_map/ppermute | solution.py:24
  170.3 8.7 %collective-permute-start.7 = (f32[1,1,1,1,1,1,6,1536]{7,6,5,4,3,2,1,0:T(8,128)}, f32[1,1,1,1,1,1,6,1536]{7,6,5,4,3,2,1,0:T(8,128)}, u32[]{:S(2)}, u32[]{:S(2)}) collective-permute-start(f32[1,1,1,1,1,1,6,1536]{7,6,5,4,3,2,1,0:T(8,128)} %constant_dynamic-slice_fusion), channel_id=1, source_target_pairs={{0,256},{64,320},{128,384},{192,448},{256,0},{320,64},{384,128},{4... | collective-permute-start | bytes 110600 | tf_op jit(solution)/shard_map/ppermute | solution.py:24
  181.0 3.6 %copy.19 = bf16[384,4608]{0,1:T(8,128)(2,1)} copy(bf16[384,4608]{1,0:T(8,128)(2,1)S(1)} %slice-done) | data formatting | bytes 7077888 | tf_op jit(solution)/shard_map/slice | solution.py:85
  184.6 2.4 subtract_bitcast_fusion
  193.2 5.5 %convolution_add_fusion = f32[2,192,1536]{2,1,0:T(8,128)} fusion(f32[1,256,1536]{2,1,0:T(8,128)} %copy-done.6, f32[1,256,1536]{2,1,0:T(8,128)} %copy-done.5, bf16[384,7680]{1,0:T(8,128)(2,1)} %all-gather.6.cloned.1.call-done, f32[2,192,384]{2,1,0:T(8,128)} %convolution_add_fusion.2, bf16[384,3,1536]{0,2,1:T(8,128)(2,1)S(1)} %bitcast.64, ...), kind=kOutput, calls=%fused_computation.12 | convolution fusion | flops 908623872 | bytes 9633792 | tf_op jit(solution)/shard_map/dot_general | solution.py:121
  198.7 3.6 %multiply_reduce_fusion = (f32[]{:T(128)}, bf16[1,192,1536]{2,1,0:T(8,128)(2,1)}) fusion(bf16[1,192,1536]{2,1,0:T(8,128)(2,1)} %param.10, f32[2,192,1536]{2,1,0:T(8,128)} %convolution_add_fusion), kind=kLoop, calls=%fused_computation.32 | loop fusion | flops 2654207 | bytes 3538948 | tf_op jit(solution)/shard_map/reduce_sum | solution.py:127
  202.9 3.0 %psum.21 = f32[]{:T(128)} all-reduce(f32[]{:T(128)S(6)} %div.31), channel_id=1, replica_groups=mesh['y'=8,'zl'=4,'c'=2,'zh'=2,'x'=4] {'c'}, use_global_device_ids=true, to_apply=%region_1.2 | all-reduce | flops 1 | bytes 8 | tf_op jit(solution)/shard_map/psum | solution.py:130
  205.9 12.5 %psum.22 = f32[]{:T(128)} all-reduce(f32[]{:T(128)} %psum.21), channel_id=1, replica_groups=mesh['y'=8,'zl'=4,'c'=2,'zh'=2,'x'=4] {'zl'}, use_global_device_ids=true, to_apply=%region_2.3 | all-reduce | flops 1 | bytes 8 | tf_op jit(solution)/shard_map/psum | solution.py:130
  218.4 15.3 %psum.23 = f32[]{:T(128)} all-reduce(f32[]{:T(128)} %psum.22), channel_id=1, replica_groups=mesh['y'=8,'zl'=4,'c'=2,'zh'=2,'x'=4] {'y'}, use_global_device_ids=true, to_apply=%region_3.4 | all-reduce | flops 1 | bytes 8 | tf_op jit(solution)/shard_map/psum | solution.py:130
  235.1 2.5 collective-permute-start.8
  237.6 3.8 %collective-permute-done.8 = f32[6,1536]{1,0:T(8,128)S(1)} collective-permute-done((f32[6,1536]{1,0:T(8,128)S(1)}, f32[6,1536]{1,0:T(8,128)S(1)}, u32[]{:S(2)}, u32[]{:S(2)}) %collective-permute-start.8) | collective-permute-done | bytes 36896 | tf_op jit(solution)/shard_map/ppermute | solution.py:24
  241.4 3.7 %collective-permute-start.9 = (f32[6,1536]{1,0:T(8,128)S(1)}, f32[6,1536]{1,0:T(8,128)S(1)}, u32[]{:S(2)}, u32[]{:S(2)}) collective-permute-start(f32[6,1536]{1,0:T(8,128)S(1)} %add.181), channel_id=1, source_target_pairs={{0,2},{1,3},{2,0},{3,1},{4,6},{5,7},{6,4},{7,5},{8,10},{9,11},{10,... | collective-permute-start | bytes 110600 | tf_op jit(solution)/shard_map/ppermute | solution.py:24
  245.1 3.8 %collective-permute-done.9 = f32[6,1536]{1,0:T(8,128)S(1)} collective-permute-done((f32[6,1536]{1,0:T(8,128)S(1)}, f32[6,1536]{1,0:T(8,128)S(1)}, u32[]{:S(2)}, u32[]{:S(2)}) %collective-permute-start.9) | collective-permute-done | bytes 36896 | tf_op jit(solution)/shard_map/ppermute | solution.py:24
  248.9 7.4 %collective-permute-start.10 = (f32[6,1536]{1,0:T(8,128)S(1)}, f32[6,1536]{1,0:T(8,128)S(1)}, u32[]{:S(2)}, u32[]{:S(2)}) collective-permute-start(f32[6,1536]{1,0:T(8,128)S(1)} %add.182), channel_id=1, source_target_pairs={{0,4},{4,0},{1,5},{5,1},{2,6},{6,2},{3,7},{7,3},{8,12},{12,8},{9,1... | collective-permute-start | bytes 110600 | tf_op jit(solution)/shard_map/ppermute | solution.py:24
  256.3 2.5 collective-permute-done.10
  (70 shorter events, 30.0 us)
Async XLA Ops:
  7.2 100.4 %all-gather.4.cloned.1.call-start = ((), (), s32[]{:S(2)}) async-start(), calls=%async_computation | async-start | bytes 3686400 | tf_op jit(solution)/shard_map/all_gather | solution.py:83
  8.1 29.5 %copy-start.4 = (bf16[1,192,384]{2,1,0:T(8,128)(2,1)S(1)}, bf16[1,192,384]{2,1,0:T(8,128)(2,1)}, u32[]{:S(2)}) copy-start(bf16[1,192,384]{2,1,0:T(8,128)(2,1)} %param.8) | copy-start | bytes 442372
  37.6 141.4 %all-gather.6.cloned.1.call-start = ((), (), s32[]{:S(2)}) async-start(), calls=%async_computation.1 | async-start | bytes 8847360 | tf_op jit(solution)/shard_map/all_gather | solution.py:83
  41.5 66.1 %collective-permute-start.2 = (f32[2,2,2,2,2,1,6,1536]{7,4,6,5,3,2,1,0:T(2,128)}, f32[2,2,2,2,2,1,6,1536]{7,4,6,5,3,2,1,0:T(2,128)}, u32[]{:S(2)}, u32[]{:S(2)}) collective-permute-start(f32[2,2,2,2,2,1,6,1536]{7,4,6,5,3,2,1,0:T(2,128)} %copy.24), channel_id=1, source_target_pairs={{0,8},{8,0},{1,9},{9,1},{2,10},{10,2},{3,11},{11,3},{4,12},{12,4},... | collective-permute-start | bytes 3538952 | tf_op jit(solution)/shard_map/ppermute | solution.py:24
  110.9 22.9 %copy-start = (bf16[1,192,1536]{2,1,0:T(8,128)(2,1)S(1)}, bf16[1,192,1536]{2,1,0:T(8,128)(2,1)}, u32[]{:S(2)}) copy-start(bf16[1,192,1536]{2,1,0:T(8,128)(2,1)} %param.9) | copy-start | bytes 1769476
  110.9 22.9 %copy-start.2 = (bf16[1,192,1536]{2,1,0:T(8,128)(2,1)S(1)}, bf16[1,192,1536]{2,1,0:T(8,128)(2,1)}, u32[]{:S(2)}) copy-start(bf16[1,192,1536]{2,1,0:T(8,128)(2,1)} %param.7) | copy-start | bytes 1769476
  110.9 16.9 %collective-permute-start.3 = (f32[2,2,2,2,1,1,6,1536]{7,3,6,5,4,2,1,0:T(2,128)S(1)}, f32[2,2,2,2,1,1,6,1536]{7,3,6,5,4,2,1,0:T(2,128)S(1)}, u32[]{:S(2)}, u32[]{:S(2)}) collective-permute-start(f32[2,2,2,2,1,1,6,1536]{7,3,6,5,4,2,1,0:T(2,128)S(1)} %copy.26), channel_id=1, source_target_pairs={{0,16},{16,0},{32,48},{48,32},{1,17},{17,1},{33,49},{49,33},{2,18}... | collective-permute-start | bytes 1769480 | tf_op jit(solution)/shard_map/ppermute | solution.py:24
  129.4 21.2 %collective-permute-start.4 = (f32[2,2,2,1,1,1,6,1536]{7,6,5,4,3,2,1,0:T(8,128)S(1)}, f32[2,2,2,1,1,1,6,1536]{7,6,5,4,3,2,1,0:T(8,128)}, u32[]{:S(2)}, u32[]{:S(2)}) collective-permute-start(f32[2,2,2,1,1,1,6,1536]{7,6,5,4,3,2,1,0:T(8,128)S(1)} %constant_dynamic-slice_fusion.3), channel_id=1, source_target_pairs={{0,32},{16,48},{32,0},{48,16},{1,33},{17,49},{33,1},{49,17},{2,34}... | collective-permute-start | bytes 884744 | tf_op jit(solution)/shard_map/ppermute | solution.py:24
  133.9 23.5 %collective-permute-start.1 = (bf16[32,3456]{1,0:T(8,128)(2,1)S(1)}, bf16[32,3456]{1,0:T(8,128)(2,1)S(1)}, u32[]{:S(2)}, u32[]{:S(2)}) collective-permute-start(bf16[32,3456]{1,0:T(8,128)(2,1)S(1)} %get-tuple-element.7), channel_id=1, source_target_pairs={{8,0},{16,8},{24,16},{32,24},{40,32},{48,40},{56,48},{64,56},{72,6... | collective-permute-start | bytes 663560 | tf_op jit(solution)/shard_map/ppermute | solution.py:93
  135.2 22.2 %collective-permute-start = (bf16[32,3456]{1,0:T(8,128)(2,1)S(1)}, bf16[32,3456]{1,0:T(8,128)(2,1)S(1)}, u32[]{:S(2)}, u32[]{:S(2)}) collective-permute-start(bf16[32,3456]{1,0:T(8,128)(2,1)S(1)} %get-tuple-element.6), channel_id=1, source_target_pairs={{0,8},{8,16},{16,24},{24,32},{32,40},{40,48},{48,56},{56,64},{64,7... | collective-permute-start | bytes 663560 | tf_op jit(solution)/shard_map/ppermute | solution.py:92
  151.6 10.0 %collective-permute-start.5 = (f32[2,2,1,1,1,1,6,1536]{7,6,5,4,3,2,1,0:T(8,128)S(1)}, f32[2,2,1,1,1,1,6,1536]{7,6,5,4,3,2,1,0:T(8,128)S(1)}, u32[]{:S(2)}, u32[]{:S(2)}) collective-permute-start(f32[2,2,1,1,1,1,6,1536]{7,6,5,4,3,2,1,0:T(8,128)S(1)} %constant_dynamic-slice_fusion.2), channel_id=1, source_target_pairs={{0,64},{64,0},{128,192},{192,128},{256,320},{320,256},{384,448},{4... | collective-permute-start | bytes 442376 | tf_op jit(solution)/shard_map/ppermute | solution.py:24
  157.4 8.8 %copy-start.8 = (bf16[32,3456]{1,0:T(8,128)(2,1)}, bf16[32,3456]{1,0:T(8,128)(2,1)S(1)}, u32[]{:S(2)}) copy-start(bf16[32,3456]{1,0:T(8,128)(2,1)S(1)} %collective-permute-done.1) | copy-start | bytes 663556
  157.4 8.8 %copy-start.9 = (bf16[32,3456]{1,0:T(8,128)(2,1)}, bf16[32,3456]{1,0:T(8,128)(2,1)S(1)}, u32[]{:S(2)}) copy-start(bf16[32,3456]{1,0:T(8,128)(2,1)S(1)} %collective-permute-done) | copy-start | bytes 663556
  161.6 7.4 %collective-permute-start.6 = (f32[2,1,1,1,1,1,6,1536]{7,6,5,4,3,2,1,0:T(8,128)S(1)}, f32[2,1,1,1,1,1,6,1536]{7,6,5,4,3,2,1,0:T(8,128)S(1)}, u32[]{:S(2)}, u32[]{:S(2)}) collective-permute-start(f32[2,1,1,1,1,1,6,1536]{7,6,5,4,3,2,1,0:T(8,128)S(1)} %constant_dynamic-slice_fusion.1), channel_id=1, source_target_pairs={{0,128},{64,192},{128,0},{192,64},{256,384},{320,448},{384,256},{4... | collective-permute-start | bytes 221192 | tf_op jit(solution)/shard_map/ppermute | solution.py:24
  170.3 64.0 %collective-permute-start.7 = (f32[1,1,1,1,1,1,6,1536]{7,6,5,4,3,2,1,0:T(8,128)}, f32[1,1,1,1,1,1,6,1536]{7,6,5,4,3,2,1,0:T(8,128)}, u32[]{:S(2)}, u32[]{:S(2)}) collective-permute-start(f32[1,1,1,1,1,1,6,1536]{7,6,5,4,3,2,1,0:T(8,128)} %constant_dynamic-slice_fusion), channel_id=1, source_target_pairs={{0,256},{64,320},{128,384},{192,448},{256,0},{320,64},{384,128},{4... | collective-permute-start | bytes 110600 | tf_op jit(solution)/shard_map/ppermute | solution.py:24
  179.0 2.0 slice-start
  187.1 1.2 copy-start.5
  187.1 1.7 copy-start.6
  187.1 3.7 %copy-start.3 = (bf16[384,4608]{0,1:T(8,128)(2,1)S(1)}, bf16[384,4608]{0,1:T(8,128)(2,1)}, u32[]{:S(2)}) copy-start(bf16[384,4608]{0,1:T(8,128)(2,1)} %copy.19) | copy-start | bytes 10616836
  188.7 2.8 %copy-start.7 = (bf16[2,256,1536]{2,1,0:T(8,128)(2,1)}, bf16[2,256,1536]{2,1,0:T(8,128)(2,1)S(1)}, u32[]{:S(2)}) copy-start(bf16[2,256,1536]{2,1,0:T(8,128)(2,1)S(1)} %fusion.7) | copy-start | bytes 4718596
  198.7 35.6 %copy-start.11 = (f32[2,1,1,1,1,1,6,1536]{7,6,5,4,3,2,1,0:T(8,128)S(1)}, f32[2,1,1,1,1,1,6,1536]{7,6,5,4,3,2,1,0:T(8,128)}, u32[]{:S(2)}) copy-start(f32[2,1,1,1,1,1,6,1536]{7,6,5,4,3,2,1,0:T(8,128)} %copy-done.10) | copy-start | bytes 221188
  235.1 6.3 %collective-permute-start.8 = (f32[6,1536]{1,0:T(8,128)S(1)}, f32[6,1536]{1,0:T(8,128)S(1)}, u32[]{:S(2)}, u32[]{:S(2)}) collective-permute-start(f32[6,1536]{1,0:T(8,128)S(1)} %multiply_bitcast_fusion), channel_id=1, source_target_pairs={{0,1},{1,0},{2,3},{3,2},{4,5},{5,4},{6,7},{7,6},{8,9},{9,8},{10,11... | collective-permute-start | bytes 110600 | tf_op jit(solution)/shard_map/ppermute | solution.py:24
  241.4 7.5 %collective-permute-start.9 = (f32[6,1536]{1,0:T(8,128)S(1)}, f32[6,1536]{1,0:T(8,128)S(1)}, u32[]{:S(2)}, u32[]{:S(2)}) collective-permute-start(f32[6,1536]{1,0:T(8,128)S(1)} %add.181), channel_id=1, source_target_pairs={{0,2},{1,3},{2,0},{3,1},{4,6},{5,7},{6,4},{7,5},{8,10},{9,11},{10,... | collective-permute-start | bytes 110600 | tf_op jit(solution)/shard_map/ppermute | solution.py:24
  248.9 9.9 %collective-permute-start.10 = (f32[6,1536]{1,0:T(8,128)S(1)}, f32[6,1536]{1,0:T(8,128)S(1)}, u32[]{:S(2)}, u32[]{:S(2)}) collective-permute-start(f32[6,1536]{1,0:T(8,128)S(1)} %add.182), channel_id=1, source_target_pairs={{0,4},{4,0},{1,5},{5,1},{2,6},{6,2},{3,7},{7,3},{8,12},{12,8},{9,1... | collective-permute-start | bytes 110600 | tf_op jit(solution)/shard_map/ppermute | solution.py:24
  (2 other events, 1.8 us)
Sparse Core Ops, SparseCore 0:
  37.7 69.8 all-gather.3
  109.7 24.1 all-gather.5

commit v5 on v4

--- a/solution.py
+++ b/solution.py
@@ -73,9 +73,6 @@
     summed = lax.dot_general(
         bottle, jitter, (((0,), (0,)), ((), ())), preferred_element_type=jnp.float32
     )
-    summed = _scatter_rows(
-        summed, (("c", 1), ("zl", 1), ("zl", 2), ("y", 1), ("y", 2), ("y", 4)), shard
-    )
 
     conv_rows = conv_filters.transpose(2, 0, 1).reshape(shard, -1)
     packed = jnp.concatenate([entry_weight, conv_rows, exit_weight], axis=1)
@@ -93,7 +90,6 @@
     from_next = lax.ppermute(edge_in[:spacing], CTX, pairs_down)
     ext = jnp.concatenate([from_prev, edge_in, from_next], axis=0)
     ext_feats = ext[:, :chans]
-    ny, nz, nc = (lax.axis_size(a) for a in CTX)
     ext_bottle = (
         ext[:, chans : chans + bot]
         .reshape(-1, ny, nz, nc, shard)
@@ -125,9 +121,15 @@
     lower = outs[1]
     blended = ((upper + lower) * 0.5).astype(jnp.bfloat16)[None]
     local_gap = jnp.sum((upper - lower) * (upper + lower - 2.0 * goal)) / (rows * n_ctx * chans)
-    gap = local_gap
-    for axis in ("c", "zl", "y"):
-        gap = lax.psum(gap, axis)
+    lanes = 128
+    with_gap = jnp.concatenate(
+        [summed, jnp.broadcast_to(local_gap, (summed.shape[0], lanes))], axis=1
+    )
+    with_gap = _scatter_rows(
+        with_gap, (("c", 1), ("zl", 1), ("zl", 2), ("y", 1), ("y", 2), ("y", 4)), shard
+    )
+    summed = with_gap[:, :chans]
+    gap = with_gap[0, chans]
     factor = gap / (2.0 * NOISE_SCALE)
     estimate = _sum_all(factor * summed, (("x", 1), ("x", 2), ("zh", 1)))
     return (blended, estimate)

time: 267 us -> 276 us (1.034)
  the two profiles are of different devices: /device:TPU:2 before, /device:TPU:62 now
where the time goes in v5:
time: 276 us
  waiting for transfers between devices  147 us (53%)
  starting transfers between devices  44.7 us (16%)
  blocking collectives  26.7 us (10%)
  local copies, waits for them, and re-layouts  18.8 us (7%)
  between operations  15.9 us (6%)
  matrix products  12.2 us (4%)
  other arithmetic  10.7 us (4%)
    all_gather x2, waiting for transfers between devices, body(): packed = lax.all_gather(packed, axis, axis=0, tiled=True)  80.5 us
    ppermute x9, waiting for transfers between devices, _swap(): return lax.ppermute(x, axis, [(i, i ^ d) for i in range(n)])  59.9 us
    ppermute x9, starting transfers between devices, _swap(): return lax.ppermute(x, axis, [(i, i ^ d) for i in range(n)])  38.7 us
    all_gather x1, blocking collectives, body(): packed = lax.all_gather(packed, axis, axis=0, tiled=True)  26.7 us
    ppermute x1, waiting for transfers between devices, body(): from_prev = lax.ppermute(edge_in[rows - spacing:], CTX, pairs_up)  6.11 us
    slice x3, local copies, waits for them, and re-layouts, body(): w_conv = packed[:, chans:4 * chans].reshape(bot, 3, chans)  5.66 us
  transfers between devices with their start and end apart: 13, of which 12 were waited for; matrix products, arithmetic and copies ran while one was open for 2% of the time, Pallas kernels for 0%

profile of v5, /device:TPU:62, one launch (start us, length us, event | category | flops | bytes accessed | tf_op | source)
XLA Modules:
  0.0 275.6 jit_solution(9441245739731622)
XLA Ops:
  8.1 26.7 %all-gather = bf16[8,6,7680]{2,1,0:T(8,128)(2,1)S(1)} all-gather(bf16[1,6,7680]{2,1,0:T(8,128)(2,1)S(1)} %maximum_bitcast_fusion), channel_id=1, replica_groups=mesh['y'=8,'zl'=4,'c'=2,'zh'=2,'x'=4] {'y'}, dimensions={0}, use_global_device_ids=true | all-gather | bytes 829440 | tf_op jit(solution)/shard_map/all_gather | solution.py:80
  36.1 70.7 %all-gather.4.cloned.1.call-done = bf16[192,7680]{1,0:T(8,128)(2,1)} async-done(((bf16[48,7680]{1,0:T(8,128)(2,1)}), bf16[192,7680]{1,0:T(8,128)(2,1)}) %all-gather.4.cloned.1.call-update) | async-done | bytes 2949136 | tf_op jit(solution)/shard_map/all_gather | solution.py:80
  106.9 4.0 %collective-permute-start.1 = (bf16[32,3456]{1,0:T(8,128)(2,1)S(1)}, bf16[32,3456]{1,0:T(8,128)(2,1)S(1)}, u32[]{:S(2)}, u32[]{:S(2)}) collective-permute-start(bf16[32,3456]{1,0:T(8,128)(2,1)S(1)} %get-tuple-element.7), channel_id=1, source_target_pairs={{8,0},{16,8},{24,16},{32,24},{40,32},{48,40},{56,48},{64,56},{72,6... | collective-permute-start | bytes 663560 | tf_op jit(solution)/shard_map/ppermute | solution.py:90
  114.7 6.1 %collective-permute-done = bf16[32,3456]{1,0:T(8,128)(2,1)S(1)} collective-permute-done((bf16[32,3456]{1,0:T(8,128)(2,1)S(1)}, bf16[32,3456]{1,0:T(8,128)(2,1)S(1)}, u32[]{:S(2)}, u32[]{:S(2)}) %collective-permute-start) | collective-permute-done | bytes 221216 | tf_op jit(solution)/shard_map/ppermute | solution.py:89
  123.3 9.8 %all-gather.6.cloned.1.call-done = bf16[384,7680]{1,0:T(8,128)(2,1)} async-done(((bf16[192,7680]{1,0:T(8,128)(2,1)}), bf16[384,7680]{1,0:T(8,128)(2,1)}) %all-gather.6.cloned.1.call-update) | async-done | bytes 5898256 | tf_op jit(solution)/shard_map/all_gather | solution.py:80
  135.1 3.7 %copy.17 = bf16[384,4608]{0,1:T(8,128)(2,1)} copy(bf16[384,4608]{1,0:T(8,128)(2,1)S(1)} %slice-done) | data formatting | bytes 7077888 | tf_op jit(solution)/shard_map/slice | solution.py:82
  147.3 5.5 %convolution_add_fusion = f32[2,192,1536]{2,1,0:T(8,128)} fusion(f32[1,256,1536]{2,1,0:T(8,128)} %copy-done.7, f32[1,256,1536]{2,1,0:T(8,128)} %copy-done.6, bf16[384,7680]{1,0:T(8,128)(2,1)} %all-gather.6.cloned.1.call-done, f32[2,192,384]{2,1,0:T(8,128)} %convolution_add_fusion.2, bf16[384,3,1536]{0,2,1:T(8,128)(2,1)S(1)} %bitcast.60, ...), kind=kOutput, calls=%fused_computation.12 | convolution fusion | flops 908623872 | bytes 9633792 | tf_op jit(solution)/shard_map/dot_general | solution.py:117
  152.8 3.7 %multiply_reduce_fusion = (f32[]{:T(128)}, bf16[1,192,1536]{2,1,0:T(8,128)(2,1)}) fusion(bf16[1,192,1536]{2,1,0:T(8,128)(2,1)} %param.10, f32[2,192,1536]{2,1,0:T(8,128)} %convolution_add_fusion), kind=kLoop, calls=%fused_computation.32 | loop fusion | flops 2654207 | bytes 3538948 | tf_op jit(solution)/shard_map/reduce_sum | solution.py:123
  165.5 3.0 %collective-permute-done.2 = f32[2,2,2,2,2,1,6,1664]{7,4,6,5,3,2,1,0:T(2,128)} collective-permute-done((f32[2,2,2,2,2,1,6,1664]{7,4,6,5,3,2,1,0:T(2,128)}, f32[2,2,2,2,2,1,6,1664]{7,4,6,5,3,2,1,0:T(2,128)}, u32[]{:S(2)}, u32[]{:S(2)}) %collective-permute-start.2) | collective-permute-done | bytes 1277984 | tf_op jit(solution)/shard_map/ppermute | solution.py:24
  171.7 3.6 %collective-permute-start.3 = (f32[2,2,2,2,1,1,6,1664]{7,3,6,5,4,2,1,0:T(2,128)S(1)}, f32[2,2,2,2,1,1,6,1664]{7,3,6,5,4,2,1,0:T(2,128)S(1)}, u32[]{:S(2)}, u32[]{:S(2)}) collective-permute-start(f32[2,2,2,2,1,1,6,1664]{7,3,6,5,4,2,1,0:T(2,128)S(1)} %copy.23), channel_id=1, source_target_pairs={{0,16},{16,0},{32,48},{48,32},{1,17},{17,1},{33,49},{49,33},{2,18}... | collective-permute-start | bytes 1916936 | tf_op jit(solution)/shard_map/ppermute | solution.py:24
  175.3 14.9 %collective-permute-done.3 = f32[2,2,2,2,1,1,6,1664]{7,3,6,5,4,2,1,0:T(2,128)S(1)} collective-permute-done((f32[2,2,2,2,1,1,6,1664]{7,3,6,5,4,2,1,0:T(2,128)S(1)}, f32[2,2,2,2,1,1,6,1664]{7,3,6,5,4,2,1,0:T(2,128)S(1)}, u32[]{:S(2)}, u32[]{:S(2)}) %collective-permute-start.3) | collective-permute-done | bytes 639008 | tf_op jit(solution)/shard_map/ppermute | solution.py:24
  191.5 4.6 %collective-permute-start.4 = (f32[2,2,2,1,1,1,6,1664]{7,6,5,4,3,2,1,0:T(8,128)S(1)}, f32[2,2,2,1,1,1,6,1664]{7,6,5,4,3,2,1,0:T(8,128)S(1)}, u32[]{:S(2)}, u32[]{:S(2)}) collective-permute-start(f32[2,2,2,1,1,1,6,1664]{7,6,5,4,3,2,1,0:T(8,128)S(1)} %constant_dynamic-slice_fusion.3), channel_id=1, source_target_pairs={{0,32},{16,48},{32,0},{48,16},{1,33},{17,49},{33,1},{49,17},{2,34}... | collective-permute-start | bytes 958472 | tf_op jit(solution)/shard_map/ppermute | solution.py:24
  196.2 18.6 %collective-permute-done.4 = f32[2,2,2,1,1,1,6,1664]{7,6,5,4,3,2,1,0:T(8,128)S(1)} collective-permute-done((f32[2,2,2,1,1,1,6,1664]{7,6,5,4,3,2,1,0:T(8,128)S(1)}, f32[2,2,2,1,1,1,6,1664]{7,6,5,4,3,2,1,0:T(8,128)S(1)}, u32[]{:S(2)}, u32[]{:S(2)}) %collective-permute-start.4) | collective-permute-done | bytes 319520 | tf_op jit(solution)/shard_map/ppermute | solution.py:24
  214.8 3.3 %collective-permute-start.5 = (f32[2,2,1,1,1,1,6,1664]{7,6,5,4,3,2,1,0:T(8,128)S(1)}, f32[2,2,1,1,1,1,6,1664]{7,6,5,4,3,2,1,0:T(8,128)S(1)}, u32[]{:S(2)}, u32[]{:S(2)}) collective-permute-start(f32[2,2,1,1,1,1,6,1664]{7,6,5,4,3,2,1,0:T(8,128)S(1)} %constant_dynamic-slice_fusion.2), channel_id=1, source_target_pairs={{0,64},{64,0},{128,192},{192,128},{256,320},{320,256},{384,448},{4... | collective-permute-start | bytes 479240 | tf_op jit(solution)/shard_map/ppermute | solution.py:24
  218.2 4.5 %collective-permute-done.5 = f32[2,2,1,1,1,1,6,1664]{7,6,5,4,3,2,1,0:T(8,128)S(1)} collective-permute-done((f32[2,2,1,1,1,1,6,1664]{7,6,5,4,3,2,1,0:T(8,128)S(1)}, f32[2,2,1,1,1,1,6,1664]{7,6,5,4,3,2,1,0:T(8,128)S(1)}, u32[]{:S(2)}, u32[]{:S(2)}) %collective-permute-start.5) | collective-permute-done | bytes 159776 | tf_op jit(solution)/shard_map/ppermute | solution.py:24
  222.8 4.2 %collective-permute-start.6 = (f32[2,1,1,1,1,1,6,1664]{7,6,5,4,3,2,1,0:T(8,128)S(1)}, f32[2,1,1,1,1,1,6,1664]{7,6,5,4,3,2,1,0:T(8,128)S(1)}, u32[]{:S(2)}, u32[]{:S(2)}) collective-permute-start(f32[2,1,1,1,1,1,6,1664]{7,6,5,4,3,2,1,0:T(8,128)S(1)} %constant_dynamic-slice_fusion.1), channel_id=1, source_target_pairs={{0,128},{64,192},{128,0},{192,64},{256,384},{320,448},{384,256},{4... | collective-permute-start | bytes 239624 | tf_op jit(solution)/shard_map/ppermute | solution.py:24
  227.1 4.4 %collective-permute-done.6 = f32[2,1,1,1,1,1,6,1664]{7,6,5,4,3,2,1,0:T(8,128)S(1)} collective-permute-done((f32[2,1,1,1,1,1,6,1664]{7,6,5,4,3,2,1,0:T(8,128)S(1)}, f32[2,1,1,1,1,1,6,1664]{7,6,5,4,3,2,1,0:T(8,128)S(1)}, u32[]{:S(2)}, u32[]{:S(2)}) %collective-permute-start.6) | collective-permute-done | bytes 79904 | tf_op jit(solution)/shard_map/ppermute | solution.py:24
  231.5 5.1 %collective-permute-start.7 = (f32[1,1,1,1,1,1,6,1664]{7,6,5,4,3,2,1,0:T(8,128)S(1)}, f32[1,1,1,1,1,1,6,1664]{7,6,5,4,3,2,1,0:T(8,128)S(1)}, u32[]{:S(2)}, u32[]{:S(2)}) collective-permute-start(f32[1,1,1,1,1,1,6,1664]{7,6,5,4,3,2,1,0:T(8,128)S(1)} %constant_dynamic-slice_fusion), channel_id=1, source_target_pairs={{0,256},{64,320},{128,384},{192,448},{256,0},{320,64},{384,128},{4... | collective-permute-start | bytes 119816 | tf_op jit(solution)/shard_map/ppermute | solution.py:24
  236.5 5.2 %collective-permute-done.7 = f32[1,1,1,1,1,1,6,1664]{7,6,5,4,3,2,1,0:T(8,128)S(1)} collective-permute-done((f32[1,1,1,1,1,1,6,1664]{7,6,5,4,3,2,1,0:T(8,128)S(1)}, f32[1,1,1,1,1,1,6,1664]{7,6,5,4,3,2,1,0:T(8,128)S(1)}, u32[]{:S(2)}, u32[]{:S(2)}) %collective-permute-start.7) | collective-permute-done | bytes 39968 | tf_op jit(solution)/shard_map/ppermute | solution.py:24
  242.9 2.8 %collective-permute-start.8 = (f32[6,1536]{1,0:T(8,128)S(1)}, f32[6,1536]{1,0:T(8,128)S(1)}, u32[]{:S(2)}, u32[]{:S(2)}) collective-permute-start(f32[6,1536]{1,0:T(8,128)S(1)} %slice_multiply_fusion), channel_id=1, source_target_pairs={{0,1},{1,0},{2,3},{3,2},{4,5},{5,4},{6,7},{7,6},{8,9},{9,8},{10,11... | collective-permute-start | bytes 110600 | tf_op jit(solution)/shard_map/ppermute | solution.py:24
  245.7 3.2 %collective-permute-done.8 = f32[6,1536]{1,0:T(8,128)S(1)} collective-permute-done((f32[6,1536]{1,0:T(8,128)S(1)}, f32[6,1536]{1,0:T(8,128)S(1)}, u32[]{:S(2)}, u32[]{:S(2)}) %collective-permute-start.8) | collective-permute-done | bytes 36896 | tf_op jit(solution)/shard_map/ppermute | solution.py:24
  248.9 3.4 %collective-permute-start.9 = (f32[6,1536]{1,0:T(8,128)S(1)}, f32[6,1536]{1,0:T(8,128)S(1)}, u32[]{:S(2)}, u32[]{:S(2)}) collective-permute-start(f32[6,1536]{1,0:T(8,128)S(1)} %fusion.43), channel_id=1, source_target_pairs={{0,2},{1,3},{2,0},{3,1},{4,6},{5,7},{6,4},{7,5},{8,10},{9,11},{10,... | collective-permute-start | bytes 110600 | tf_op jit(solution)/shard_map/ppermute | solution.py:24
  252.3 4.1 %collective-permute-done.9 = f32[6,1536]{1,0:T(8,128)S(1)} collective-permute-done((f32[6,1536]{1,0:T(8,128)S(1)}, f32[6,1536]{1,0:T(8,128)S(1)}, u32[]{:S(2)}, u32[]{:S(2)}) %collective-permute-start.9) | collective-permute-done | bytes 36896 | tf_op jit(solution)/shard_map/ppermute | solution.py:24
  256.4 9.6 %collective-permute-start.10 = (f32[6,1536]{1,0:T(8,128)S(1)}, f32[6,1536]{1,0:T(8,128)S(1)}, u32[]{:S(2)}, u32[]{:S(2)}) collective-permute-start(f32[6,1536]{1,0:T(8,128)S(1)} %add.178), channel_id=1, source_target_pairs={{0,4},{4,0},{1,5},{5,1},{2,6},{6,2},{3,7},{7,3},{8,12},{12,8},{9,1... | collective-permute-start | bytes 110600 | tf_op jit(solution)/shard_map/ppermute | solution.py:24
  (67 shorter events, 35.1 us)
Async XLA Ops:
  7.2 99.6 %all-gather.4.cloned.1.call-start = ((), (), s32[]{:S(2)}) async-start(), calls=%async_computation | async-start | bytes 3686400 | tf_op jit(solution)/shard_map/all_gather | solution.py:80
  36.0 70.8 %copy-start.1 = (bf16[1,192,1536]{2,1,0:T(8,128)(2,1)S(1)}, bf16[1,192,1536]{2,1,0:T(8,128)(2,1)}, u32[]{:S(2)}) copy-start(bf16[1,192,1536]{2,1,0:T(8,128)(2,1)} %param.9) | copy-start | bytes 1769476
  36.0 70.8 %copy-start.3 = (bf16[1,192,1536]{2,1,0:T(8,128)(2,1)S(1)}, bf16[1,192,1536]{2,1,0:T(8,128)(2,1)}, u32[]{:S(2)}) copy-start(bf16[1,192,1536]{2,1,0:T(8,128)(2,1)} %param.7) | copy-start | bytes 1769476
  36.0 70.8 %copy-start.5 = (bf16[1,192,384]{2,1,0:T(8,128)(2,1)S(1)}, bf16[1,192,384]{2,1,0:T(8,128)(2,1)}, u32[]{:S(2)}) copy-start(bf16[1,192,384]{2,1,0:T(8,128)(2,1)} %param.8) | copy-start | bytes 442372
  36.0 97.0 %all-gather.6.cloned.1.call-start = ((), (), s32[]{:S(2)}) async-start(), calls=%async_computation.1 | async-start | bytes 8847360 | tf_op jit(solution)/shard_map/all_gather | solution.py:80
  106.9 7.8 %collective-permute-start.1 = (bf16[32,3456]{1,0:T(8,128)(2,1)S(1)}, bf16[32,3456]{1,0:T(8,128)(2,1)S(1)}, u32[]{:S(2)}, u32[]{:S(2)}) collective-permute-start(bf16[32,3456]{1,0:T(8,128)(2,1)S(1)} %get-tuple-element.7), channel_id=1, source_target_pairs={{8,0},{16,8},{24,16},{32,24},{40,32},{48,40},{56,48},{64,56},{72,6... | collective-permute-start | bytes 663560 | tf_op jit(solution)/shard_map/ppermute | solution.py:90
  110.9 9.9 %collective-permute-start = (bf16[32,3456]{1,0:T(8,128)(2,1)S(1)}, bf16[32,3456]{1,0:T(8,128)(2,1)S(1)}, u32[]{:S(2)}, u32[]{:S(2)}) collective-permute-start(bf16[32,3456]{1,0:T(8,128)(2,1)S(1)} %get-tuple-element.6), channel_id=1, source_target_pairs={{0,8},{8,16},{16,24},{24,32},{32,40},{40,48},{48,56},{56,64},{64,7... | collective-permute-start | bytes 663560 | tf_op jit(solution)/shard_map/ppermute | solution.py:89
  114.7 7.1 %copy-start.9 = (bf16[32,3456]{1,0:T(8,128)(2,1)}, bf16[32,3456]{1,0:T(8,128)(2,1)S(1)}, u32[]{:S(2)}) copy-start(bf16[32,3456]{1,0:T(8,128)(2,1)S(1)} %collective-permute-done.1) | copy-start | bytes 663556
  133.1 2.0 slice-start
  141.2 1.1 copy-start.6
  141.2 1.7 copy-start.7
  141.2 3.7 %copy-start.4 = (bf16[384,4608]{0,1:T(8,128)(2,1)S(1)}, bf16[384,4608]{0,1:T(8,128)(2,1)}, u32[]{:S(2)}) copy-start(bf16[384,4608]{0,1:T(8,128)(2,1)} %copy.17) | copy-start | bytes 10616836
  142.9 2.8 %copy-start.8 = (bf16[2,256,1536]{2,1,0:T(8,128)(2,1)}, bf16[2,256,1536]{2,1,0:T(8,128)(2,1)S(1)}, u32[]{:S(2)}) copy-start(bf16[2,256,1536]{2,1,0:T(8,128)(2,1)S(1)} %fusion.7) | copy-start | bytes 4718596
  152.8 4.4 %copy-start = (f32[384,1536]{1,0:T(8,128)S(1)}, f32[384,1536]{1,0:T(8,128)}, u32[]{:S(2)}) copy-start(f32[384,1536]{1,0:T(8,128)} %fusion.33) | copy-start | bytes 7077892
  163.2 5.2 %collective-permute-start.2 = (f32[2,2,2,2,2,1,6,1664]{7,4,6,5,3,2,1,0:T(2,128)}, f32[2,2,2,2,2,1,6,1664]{7,4,6,5,3,2,1,0:T(2,128)}, u32[]{:S(2)}, u32[]{:S(2)}) collective-permute-start(f32[2,2,2,2,2,1,6,1664]{7,4,6,5,3,2,1,0:T(2,128)} %copy.21), channel_id=1, source_target_pairs={{0,8},{8,0},{1,9},{9,1},{2,10},{10,2},{3,11},{11,3},{4,12},{12,4},... | collective-permute-start | bytes 3833864 | tf_op jit(solution)/shard_map/ppermute | solution.py:24
  170.0 1.2 copy-start.2
  171.7 18.5 %collective-permute-start.3 = (f32[2,2,2,2,1,1,6,1664]{7,3,6,5,4,2,1,0:T(2,128)S(1)}, f32[2,2,2,2,1,1,6,1664]{7,3,6,5,4,2,1,0:T(2,128)S(1)}, u32[]{:S(2)}, u32[]{:S(2)}) collective-permute-start(f32[2,2,2,2,1,1,6,1664]{7,3,6,5,4,2,1,0:T(2,128)S(1)} %copy.23), channel_id=1, source_target_pairs={{0,16},{16,0},{32,48},{48,32},{1,17},{17,1},{33,49},{49,33},{2,18}... | collective-permute-start | bytes 1916936 | tf_op jit(solution)/shard_map/ppermute | solution.py:24
  191.5 23.2 %collective-permute-start.4 = (f32[2,2,2,1,1,1,6,1664]{7,6,5,4,3,2,1,0:T(8,128)S(1)}, f32[2,2,2,1,1,1,6,1664]{7,6,5,4,3,2,1,0:T(8,128)S(1)}, u32[]{:S(2)}, u32[]{:S(2)}) collective-permute-start(f32[2,2,2,1,1,1,6,1664]{7,6,5,4,3,2,1,0:T(8,128)S(1)} %constant_dynamic-slice_fusion.3), channel_id=1, source_target_pairs={{0,32},{16,48},{32,0},{48,16},{1,33},{17,49},{33,1},{49,17},{2,34}... | collective-permute-start | bytes 958472 | tf_op jit(solution)/shard_map/ppermute | solution.py:24
  214.8 7.9 %collective-permute-start.5 = (f32[2,2,1,1,1,1,6,1664]{7,6,5,4,3,2,1,0:T(8,128)S(1)}, f32[2,2,1,1,1,1,6,1664]{7,6,5,4,3,2,1,0:T(8,128)S(1)}, u32[]{:S(2)}, u32[]{:S(2)}) collective-permute-start(f32[2,2,1,1,1,1,6,1664]{7,6,5,4,3,2,1,0:T(8,128)S(1)} %constant_dynamic-slice_fusion.2), channel_id=1, source_target_pairs={{0,64},{64,0},{128,192},{192,128},{256,320},{320,256},{384,448},{4... | collective-permute-start | bytes 479240 | tf_op jit(solution)/shard_map/ppermute | solution.py:24
  222.8 8.6 %collective-permute-start.6 = (f32[2,1,1,1,1,1,6,1664]{7,6,5,4,3,2,1,0:T(8,128)S(1)}, f32[2,1,1,1,1,1,6,1664]{7,6,5,4,3,2,1,0:T(8,128)S(1)}, u32[]{:S(2)}, u32[]{:S(2)}) collective-permute-start(f32[2,1,1,1,1,1,6,1664]{7,6,5,4,3,2,1,0:T(8,128)S(1)} %constant_dynamic-slice_fusion.1), channel_id=1, source_target_pairs={{0,128},{64,192},{128,0},{192,64},{256,384},{320,448},{384,256},{4... | collective-permute-start | bytes 239624 | tf_op jit(solution)/shard_map/ppermute | solution.py:24
  231.5 10.3 %collective-permute-start.7 = (f32[1,1,1,1,1,1,6,1664]{7,6,5,4,3,2,1,0:T(8,128)S(1)}, f32[1,1,1,1,1,1,6,1664]{7,6,5,4,3,2,1,0:T(8,128)S(1)}, u32[]{:S(2)}, u32[]{:S(2)}) collective-permute-start(f32[1,1,1,1,1,1,6,1664]{7,6,5,4,3,2,1,0:T(8,128)S(1)} %constant_dynamic-slice_fusion), channel_id=1, source_target_pairs={{0,256},{64,320},{128,384},{192,448},{256,0},{320,64},{384,128},{4... | collective-permute-start | bytes 119816 | tf_op jit(solution)/shard_map/ppermute | solution.py:24
  242.9 6.0 %collective-permute-start.8 = (f32[6,1536]{1,0:T(8,128)S(1)}, f32[6,1536]{1,0:T(8,128)S(1)}, u32[]{:S(2)}, u32[]{:S(2)}) collective-permute-start(f32[6,1536]{1,0:T(8,128)S(1)} %slice_multiply_fusion), channel_id=1, source_target_pairs={{0,1},{1,0},{2,3},{3,2},{4,5},{5,4},{6,7},{7,6},{8,9},{9,8},{10,11... | collective-permute-start | bytes 110600 | tf_op jit(solution)/shard_map/ppermute | solution.py:24
  248.9 7.5 %collective-permute-start.9 = (f32[6,1536]{1,0:T(8,128)S(1)}, f32[6,1536]{1,0:T(8,128)S(1)}, u32[]{:S(2)}, u32[]{:S(2)}) collective-permute-start(f32[6,1536]{1,0:T(8,128)S(1)} %fusion.43), channel_id=1, source_target_pairs={{0,2},{1,3},{2,0},{3,1},{4,6},{5,7},{6,4},{7,5},{8,10},{9,11},{10,... | collective-permute-start | bytes 110600 | tf_op jit(solution)/shard_map/ppermute | solution.py:24
  256.4 11.7 %collective-permute-start.10 = (f32[6,1536]{1,0:T(8,128)S(1)}, f32[6,1536]{1,0:T(8,128)S(1)}, u32[]{:S(2)}, u32[]{:S(2)}) collective-permute-start(f32[6,1536]{1,0:T(8,128)S(1)} %add.178), channel_id=1, source_target_pairs={{0,4},{4,0},{1,5},{5,1},{2,6},{6,2},{3,7},{7,3},{8,12},{12,8},{9,1... | collective-permute-start | bytes 110600 | tf_op jit(solution)/shard_map/ppermute | solution.py:24
  (1 other events, 1.0 us)
Sparse Core Ops, SparseCore 0:
  36.2 70.5 all-gather.3
  108.9 24.1 all-gather.5

commit v6 on v4

--- a/solution.py
+++ b/solution.py
@@ -79,7 +79,7 @@
 
     conv_rows = conv_filters.transpose(2, 0, 1).reshape(shard, -1)
     packed = jnp.concatenate([entry_weight, conv_rows, exit_weight], axis=1)
-    for axis in ("y", "zl", "c"):
+    for axis in ("zl", "y", "c"):
         packed = lax.all_gather(packed, axis, axis=0, tiled=True)
     w_entry = packed[:, :chans]
     w_conv = packed[:, chans : 4 * chans].reshape(bot, 3, chans)
@@ -93,11 +93,10 @@
     from_next = lax.ppermute(edge_in[:spacing], CTX, pairs_down)
     ext = jnp.concatenate([from_prev, edge_in, from_next], axis=0)
     ext_feats = ext[:, :chans]
-    ny, nz, nc = (lax.axis_size(a) for a in CTX)
     ext_bottle = (
         ext[:, chans : chans + bot]
         .reshape(-1, ny, nz, nc, shard)
-        .transpose(0, 3, 2, 1, 4)
+        .transpose(0, 3, 1, 2, 4)
         .reshape(-1, bot)
     )
     ext_jitter = ext[:, chans + bot :]

time: 267 us -> 236 us (0.88)
  waiting for transfers between devices: 105 us -> 83.3 us
  blocking collectives: 59 us -> 53.5 us
  starting transfers between devices: 46.5 us -> 42.3 us
    all_gather x2, waiting for transfers between devices: 64.2 us -> 43.5 us  [body(): packed = lax.all_gather(packed, axis, axis=0, tiled=True)]
    all_gather x1, blocking collectives: 28.3 us -> 17.9 us  [body(): packed = lax.all_gather(packed, axis, axis=0, tiled=True)]
    psum x3, blocking collectives: 30.7 us -> 35.6 us  [body(): gap = lax.psum(gap, axis)]
    ppermute x9, starting transfers between devices: 42.1 us -> 37.9 us  [_swap(): return lax.ppermute(x, axis, [(i, i ^ d) for i in range(n)])]
  transfers between devices with their start and end apart: 13 -> 13, of which waited for: 8 -> 8; matrix products, arithmetic and copies ran while one was open for 11% -> 13% of each run, Pallas kernels for 0% -> 0%
where the time goes in v6:
time: 236 us; the launch traced here: 235 us
  waiting for transfers between devices  83.3 us (35%)
  blocking collectives  53.5 us (23%)
  starting transfers between devices  42.3 us (18%)
  between operations  15.9 us (7%)
  local copies, waits for them, and re-layouts  15.4 us (7%)
  other arithmetic  12.5 us (5%)
  matrix products  11.8 us (5%)
    all_gather x2, waiting for transfers between devices, body(): packed = lax.all_gather(packed, axis, axis=0, tiled=True)  43.5 us
    ppermute x9, waiting for transfers between devices, _swap(): return lax.ppermute(x, axis, [(i, i ^ d) for i in range(n)])  39.8 us
    ppermute x9, starting transfers between devices, _swap(): return lax.ppermute(x, axis, [(i, i ^ d) for i in range(n)])  37.9 us
    psum x3, blocking collectives, body(): gap = lax.psum(gap, axis)  35.6 us
    all_gather x1, blocking collectives, body(): packed = lax.all_gather(packed, axis, axis=0, tiled=True)  17.9 us
    slice x3, local copies, waits for them, and re-layouts, body(): w_conv = packed[:, chans:4 * chans].reshape(bot, 3, chans)  5.61 us
    dot_general x1, matrix products, body(): jnp.dot(inner, w_exit, preferred_element_type=jnp.float32)  5.49 us
    unnamed x25, local copies, waits for them, and re-layouts  5.32 us
  transfers between devices with their start and end apart: 13, of which 8 were waited for; matrix products, arithmetic and copies ran while one was open for 13% of the time, Pallas kernels for 0%

profile of v6, /device:TPU:2, one launch (start us, length us, event | category | flops | bytes accessed | tf_op | source)
XLA Modules:
  0.0 234.8 jit_solution(12637944600069657359)
XLA Ops:
  8.2 17.9 %all-gather = bf16[4,6,7680]{2,1,0:T(8,128)(2,1)S(1)} all-gather(bf16[1,6,7680]{2,1,0:T(8,128)(2,1)S(1)} %maximum_bitcast_fusion), channel_id=1, replica_groups=mesh['y'=8,'zl'=4,'c'=2,'zh'=2,'x'=4] {'zl'}, dimensions={0}, use_global_device_ids=true | all-gather | bytes 460800 | tf_op jit(solution)/shard_map/all_gather | solution.py:83
  32.8 43.5 %all-gather.4.cloned.1.call-done = bf16[192,7680]{1,0:T(8,128)(2,1)} async-done(((bf16[24,7680]{1,0:T(8,128)(2,1)}), bf16[192,7680]{1,0:T(8,128)(2,1)}) %all-gather.4.cloned.1.call-update) | async-done | bytes 2949136 | tf_op jit(solution)/shard_map/all_gather | solution.py:83
  79.6 3.7 %collective-permute-start.3 = (f32[2,2,2,2,1,1,6,1536]{7,3,6,5,4,2,1,0:T(2,128)S(1)}, f32[2,2,2,2,1,1,6,1536]{7,3,6,5,4,2,1,0:T(2,128)S(1)}, u32[]{:S(2)}, u32[]{:S(2)}) collective-permute-start(f32[2,2,2,2,1,1,6,1536]{7,3,6,5,4,2,1,0:T(2,128)S(1)} %copy.26), channel_id=1, source_target_pairs={{0,16},{16,0},{32,48},{48,32},{1,17},{17,1},{33,49},{49,33},{2,18}... | collective-permute-start | bytes 1769480 | tf_op jit(solution)/shard_map/ppermute | solution.py:24
  83.4 11.6 %collective-permute-done.3 = f32[2,2,2,2,1,1,6,1536]{7,3,6,5,4,2,1,0:T(2,128)S(1)} collective-permute-done((f32[2,2,2,2,1,1,6,1536]{7,3,6,5,4,2,1,0:T(2,128)S(1)}, f32[2,2,2,2,1,1,6,1536]{7,3,6,5,4,2,1,0:T(2,128)S(1)}, u32[]{:S(2)}, u32[]{:S(2)}) %collective-permute-start.3) | collective-permute-done | bytes 589856 | tf_op jit(solution)/shard_map/ppermute | solution.py:24
  96.4 4.6 %collective-permute-start.4 = (f32[2,2,2,1,1,1,6,1536]{7,6,5,4,3,2,1,0:T(8,128)S(1)}, f32[2,2,2,1,1,1,6,1536]{7,6,5,4,3,2,1,0:T(8,128)}, u32[]{:S(2)}, u32[]{:S(2)}) collective-permute-start(f32[2,2,2,1,1,1,6,1536]{7,6,5,4,3,2,1,0:T(8,128)S(1)} %constant_dynamic-slice_fusion.3), channel_id=1, source_target_pairs={{0,32},{16,48},{32,0},{48,16},{1,33},{17,49},{33,1},{49,17},{2,34}... | collective-permute-start | bytes 884744 | tf_op jit(solution)/shard_map/ppermute | solution.py:24
  102.4 3.0 %collective-permute-start = (bf16[32,3456]{1,0:T(8,128)(2,1)S(1)}, bf16[32,3456]{1,0:T(8,128)(2,1)S(1)}, u32[]{:S(2)}, u32[]{:S(2)}) collective-permute-start(bf16[32,3456]{1,0:T(8,128)(2,1)S(1)} %get-tuple-element.6), channel_id=1, source_target_pairs={{0,8},{8,16},{16,24},{24,32},{32,40},{40,48},{48,56},{56,64},{64,7... | collective-permute-start | bytes 663560 | tf_op jit(solution)/shard_map/ppermute | solution.py:92
  105.6 10.5 %collective-permute-done.4 = f32[2,2,2,1,1,1,6,1536]{7,6,5,4,3,2,1,0:T(8,128)} collective-permute-done((f32[2,2,2,1,1,1,6,1536]{7,6,5,4,3,2,1,0:T(8,128)S(1)}, f32[2,2,2,1,1,1,6,1536]{7,6,5,4,3,2,1,0:T(8,128)}, u32[]{:S(2)}, u32[]{:S(2)}) %collective-permute-start.4) | collective-permute-done | bytes 294944 | tf_op jit(solution)/shard_map/ppermute | solution.py:24
  117.2 6.2 %collective-permute-start.5 = (f32[2,2,1,1,1,1,6,1536]{7,6,5,4,3,2,1,0:T(8,128)S(1)}, f32[2,2,1,1,1,1,6,1536]{7,6,5,4,3,2,1,0:T(8,128)S(1)}, u32[]{:S(2)}, u32[]{:S(2)}) collective-permute-start(f32[2,2,1,1,1,1,6,1536]{7,6,5,4,3,2,1,0:T(8,128)S(1)} %constant_dynamic-slice_fusion.2), channel_id=1, source_target_pairs={{0,64},{64,0},{128,192},{192,128},{256,320},{320,256},{384,448},{4... | collective-permute-start | bytes 442376 | tf_op jit(solution)/shard_map/ppermute | solution.py:24
  124.8 2.6 %collective-permute-done.5 = f32[2,2,1,1,1,1,6,1536]{7,6,5,4,3,2,1,0:T(8,128)S(1)} collective-permute-done((f32[2,2,1,1,1,1,6,1536]{7,6,5,4,3,2,1,0:T(8,128)S(1)}, f32[2,2,1,1,1,1,6,1536]{7,6,5,4,3,2,1,0:T(8,128)S(1)}, u32[]{:S(2)}, u32[]{:S(2)}) %collective-permute-start.5) | collective-permute-done | bytes 147488 | tf_op jit(solution)/shard_map/ppermute | solution.py:24
  127.4 5.6 %collective-permute-start.6 = (f32[2,1,1,1,1,1,6,1536]{7,6,5,4,3,2,1,0:T(8,128)S(1)}, f32[2,1,1,1,1,1,6,1536]{7,6,5,4,3,2,1,0:T(8,128)S(1)}, u32[]{:S(2)}, u32[]{:S(2)}) collective-permute-start(f32[2,1,1,1,1,1,6,1536]{7,6,5,4,3,2,1,0:T(8,128)S(1)} %constant_dynamic-slice_fusion.1), channel_id=1, source_target_pairs={{0,128},{64,192},{128,0},{192,64},{256,384},{320,448},{384,256},{4... | collective-permute-start | bytes 221192 | tf_op jit(solution)/shard_map/ppermute | solution.py:24
  136.9 5.6 %collective-permute-start.7 = (f32[1,1,1,1,1,1,6,1536]{7,6,5,4,3,2,1,0:T(8,128)}, f32[1,1,1,1,1,1,6,1536]{7,6,5,4,3,2,1,0:T(8,128)}, u32[]{:S(2)}, u32[]{:S(2)}) collective-permute-start(f32[1,1,1,1,1,1,6,1536]{7,6,5,4,3,2,1,0:T(8,128)} %constant_dynamic-slice_fusion), channel_id=1, source_target_pairs={{0,256},{64,320},{128,384},{192,448},{256,0},{320,64},{384,128},{4... | collective-permute-start | bytes 110600 | tf_op jit(solution)/shard_map/ppermute | solution.py:24
  144.6 3.6 %copy.19 = bf16[384,4608]{0,1:T(8,128)(2,1)} copy(bf16[384,4608]{1,0:T(8,128)(2,1)S(1)} %slice-done) | data formatting | bytes 7077888 | tf_op jit(solution)/shard_map/slice | solution.py:85
  148.2 2.4 %subtract_bitcast_fusion = (f32[1,256,1536]{2,1,0:T(8,128)S(1)}, f32[1,256,1536]{2,1,0:T(8,128)S(1)}) fusion(bf16[256,3456]{1,0:T(8,128)(2,1)} %pad_maximum_fusion.1, bf16[32,3456]{1,0:T(8,128)(2,1)} %copy-done.8, bf16[192,1536]{1,0:T(8,128)(2,1)} %bitcast.54, bf16[192,384]{1,0:T(8,128)(2,1)} %bitcast.65, bf16[192,1536]{1,0:T(8,128)(2,1)} %bitcast.58, ...), kind=kOutput, calls=%fused_computation.16 | convolution fusion | flops 307888128 | bytes 7077888 | tf_op jit(solution)/shard_map/dot_general | solution.py:104
  156.7 5.5 %convolution_add_fusion = f32[2,192,1536]{2,1,0:T(8,128)} fusion(f32[1,256,1536]{2,1,0:T(8,128)} %copy-done.6, f32[1,256,1536]{2,1,0:T(8,128)} %copy-done.5, bf16[384,7680]{1,0:T(8,128)(2,1)} %all-gather.6.cloned.1.call-done, f32[2,192,384]{2,1,0:T(8,128)} %convolution_add_fusion.2, bf16[384,3,1536]{0,2,1:T(8,128)(2,1)S(1)} %bitcast.64, ...), kind=kOutput, calls=%fused_computation.12 | convolution fusion | flops 908623872 | bytes 9633792 | tf_op jit(solution)/shard_map/dot_general | solution.py:120
  162.2 3.6 %multiply_reduce_fusion = (f32[]{:T(128)}, bf16[1,192,1536]{2,1,0:T(8,128)(2,1)}) fusion(bf16[1,192,1536]{2,1,0:T(8,128)(2,1)} %param.10, f32[2,192,1536]{2,1,0:T(8,128)} %convolution_add_fusion), kind=kLoop, calls=%fused_computation.32 | loop fusion | flops 2654207 | bytes 3538948 | tf_op jit(solution)/shard_map/reduce_sum | solution.py:126
  166.5 3.0 %psum.21 = f32[]{:T(128)} all-reduce(f32[]{:T(128)S(6)} %div.31), channel_id=1, replica_groups=mesh['y'=8,'zl'=4,'c'=2,'zh'=2,'x'=4] {'c'}, use_global_device_ids=true, to_apply=%region_1.2 | all-reduce | flops 1 | bytes 8 | tf_op jit(solution)/shard_map/psum | solution.py:129
  169.5 14.9 %psum.22 = f32[]{:T(128)} all-reduce(f32[]{:T(128)} %psum.21), channel_id=1, replica_groups=mesh['y'=8,'zl'=4,'c'=2,'zh'=2,'x'=4] {'zl'}, use_global_device_ids=true, to_apply=%region_2.3 | all-reduce | flops 1 | bytes 8 | tf_op jit(solution)/shard_map/psum | solution.py:129
  184.4 17.7 %psum.23 = f32[]{:T(128)} all-reduce(f32[]{:T(128)} %psum.22), channel_id=1, replica_groups=mesh['y'=8,'zl'=4,'c'=2,'zh'=2,'x'=4] {'y'}, use_global_device_ids=true, to_apply=%region_3.4 | all-reduce | flops 1 | bytes 8 | tf_op jit(solution)/shard_map/psum | solution.py:129
  203.6 2.1 collective-permute-start.8
  205.7 4.3 %collective-permute-done.8 = f32[6,1536]{1,0:T(8,128)S(1)} collective-permute-done((f32[6,1536]{1,0:T(8,128)S(1)}, f32[6,1536]{1,0:T(8,128)S(1)}, u32[]{:S(2)}, u32[]{:S(2)}) %collective-permute-start.8) | collective-permute-done | bytes 36896 | tf_op jit(solution)/shard_map/ppermute | solution.py:24
  210.0 3.5 %collective-permute-start.9 = (f32[6,1536]{1,0:T(8,128)S(1)}, f32[6,1536]{1,0:T(8,128)S(1)}, u32[]{:S(2)}, u32[]{:S(2)}) collective-permute-start(f32[6,1536]{1,0:T(8,128)S(1)} %add.181), channel_id=1, source_target_pairs={{0,2},{1,3},{2,0},{3,1},{4,6},{5,7},{6,4},{7,5},{8,10},{9,11},{10,... | collective-permute-start | bytes 110600 | tf_op jit(solution)/shard_map/ppermute | solution.py:24
  213.5 3.9 %collective-permute-done.9 = f32[6,1536]{1,0:T(8,128)S(1)} collective-permute-done((f32[6,1536]{1,0:T(8,128)S(1)}, f32[6,1536]{1,0:T(8,128)S(1)}, u32[]{:S(2)}, u32[]{:S(2)}) %collective-permute-start.9) | collective-permute-done | bytes 36896 | tf_op jit(solution)/shard_map/ppermute | solution.py:24
  217.5 4.6 %collective-permute-start.10 = (f32[6,1536]{1,0:T(8,128)S(1)}, f32[6,1536]{1,0:T(8,128)S(1)}, u32[]{:S(2)}, u32[]{:S(2)}) collective-permute-start(f32[6,1536]{1,0:T(8,128)S(1)} %add.182), channel_id=1, source_target_pairs={{0,4},{4,0},{1,5},{5,1},{2,6},{6,2},{3,7},{7,3},{8,12},{12,8},{9,1... | collective-permute-start | bytes 110600 | tf_op jit(solution)/shard_map/ppermute | solution.py:24
  222.1 5.3 %collective-permute-done.10 = f32[6,1536]{1,0:T(8,128)S(1)} collective-permute-done((f32[6,1536]{1,0:T(8,128)S(1)}, f32[6,1536]{1,0:T(8,128)S(1)}, u32[]{:S(2)}, u32[]{:S(2)}) %collective-permute-start.10) | collective-permute-done | bytes 36896 | tf_op jit(solution)/shard_map/ppermute | solution.py:24
  (70 shorter events, 29.5 us)
Async XLA Ops:
  7.2 19.9 %copy-start.4 = (bf16[1,192,384]{2,1,0:T(8,128)(2,1)S(1)}, bf16[1,192,384]{2,1,0:T(8,128)(2,1)}, u32[]{:S(2)}) copy-start(bf16[1,192,384]{2,1,0:T(8,128)(2,1)} %param.8) | copy-start | bytes 442372
  7.2 69.1 %all-gather.4.cloned.1.call-start = ((), (), s32[]{:S(2)}) async-start(), calls=%async_computation | async-start | bytes 3317760 | tf_op jit(solution)/shard_map/all_gather | solution.py:83
  27.0 115.5 %all-gather.6.cloned.1.call-start = ((), (), s32[]{:S(2)}) async-start(), calls=%async_computation.1 | async-start | bytes 8847360 | tf_op jit(solution)/shard_map/all_gather | solution.py:83
  30.9 45.4 %collective-permute-start.2 = (f32[2,2,2,2,2,1,6,1536]{7,4,6,5,3,2,1,0:T(2,128)}, f32[2,2,2,2,2,1,6,1536]{7,4,6,5,3,2,1,0:T(2,128)}, u32[]{:S(2)}, u32[]{:S(2)}) collective-permute-start(f32[2,2,2,2,2,1,6,1536]{7,4,6,5,3,2,1,0:T(2,128)} %copy.24), channel_id=1, source_target_pairs={{0,8},{8,0},{1,9},{9,1},{2,10},{10,2},{3,11},{11,3},{4,12},{12,4},... | collective-permute-start | bytes 3538952 | tf_op jit(solution)/shard_map/ppermute | solution.py:24
  79.6 21.5 %copy-start = (bf16[1,192,1536]{2,1,0:T(8,128)(2,1)S(1)}, bf16[1,192,1536]{2,1,0:T(8,128)(2,1)}, u32[]{:S(2)}) copy-start(bf16[1,192,1536]{2,1,0:T(8,128)(2,1)} %param.9) | copy-start | bytes 1769476
  79.6 21.5 %copy-start.2 = (bf16[1,192,1536]{2,1,0:T(8,128)(2,1)S(1)}, bf16[1,192,1536]{2,1,0:T(8,128)(2,1)}, u32[]{:S(2)}) copy-start(bf16[1,192,1536]{2,1,0:T(8,128)(2,1)} %param.7) | copy-start | bytes 1769476
  79.6 15.4 %collective-permute-start.3 = (f32[2,2,2,2,1,1,6,1536]{7,3,6,5,4,2,1,0:T(2,128)S(1)}, f32[2,2,2,2,1,1,6,1536]{7,3,6,5,4,2,1,0:T(2,128)S(1)}, u32[]{:S(2)}, u32[]{:S(2)}) collective-permute-start(f32[2,2,2,2,1,1,6,1536]{7,3,6,5,4,2,1,0:T(2,128)S(1)} %copy.26), channel_id=1, source_target_pairs={{0,16},{16,0},{32,48},{48,32},{1,17},{17,1},{33,49},{49,33},{2,18}... | collective-permute-start | bytes 1769480 | tf_op jit(solution)/shard_map/ppermute | solution.py:24
  96.4 19.7 %collective-permute-start.4 = (f32[2,2,2,1,1,1,6,1536]{7,6,5,4,3,2,1,0:T(8,128)S(1)}, f32[2,2,2,1,1,1,6,1536]{7,6,5,4,3,2,1,0:T(8,128)}, u32[]{:S(2)}, u32[]{:S(2)}) collective-permute-start(f32[2,2,2,1,1,1,6,1536]{7,6,5,4,3,2,1,0:T(8,128)S(1)} %constant_dynamic-slice_fusion.3), channel_id=1, source_target_pairs={{0,32},{16,48},{32,0},{48,16},{1,33},{17,49},{33,1},{49,17},{2,34}... | collective-permute-start | bytes 884744 | tf_op jit(solution)/shard_map/ppermute | solution.py:24
  101.1 22.3 %collective-permute-start.1 = (bf16[32,3456]{1,0:T(8,128)(2,1)S(1)}, bf16[32,3456]{1,0:T(8,128)(2,1)S(1)}, u32[]{:S(2)}, u32[]{:S(2)}) collective-permute-start(bf16[32,3456]{1,0:T(8,128)(2,1)S(1)} %get-tuple-element.7), channel_id=1, source_target_pairs={{8,0},{16,8},{24,16},{32,24},{40,32},{48,40},{56,48},{64,56},{72,6... | collective-permute-start | bytes 663560 | tf_op jit(solution)/shard_map/ppermute | solution.py:93
  102.4 21.0 %collective-permute-start = (bf16[32,3456]{1,0:T(8,128)(2,1)S(1)}, bf16[32,3456]{1,0:T(8,128)(2,1)S(1)}, u32[]{:S(2)}, u32[]{:S(2)}) collective-permute-start(bf16[32,3456]{1,0:T(8,128)(2,1)S(1)} %get-tuple-element.6), channel_id=1, source_target_pairs={{0,8},{8,16},{16,24},{24,32},{32,40},{40,48},{48,56},{56,64},{64,7... | collective-permute-start | bytes 663560 | tf_op jit(solution)/shard_map/ppermute | solution.py:92
  117.2 10.2 %collective-permute-start.5 = (f32[2,2,1,1,1,1,6,1536]{7,6,5,4,3,2,1,0:T(8,128)S(1)}, f32[2,2,1,1,1,1,6,1536]{7,6,5,4,3,2,1,0:T(8,128)S(1)}, u32[]{:S(2)}, u32[]{:S(2)}) collective-permute-start(f32[2,2,1,1,1,1,6,1536]{7,6,5,4,3,2,1,0:T(8,128)S(1)} %constant_dynamic-slice_fusion.2), channel_id=1, source_target_pairs={{0,64},{64,0},{128,192},{192,128},{256,320},{320,256},{384,448},{4... | collective-permute-start | bytes 442376 | tf_op jit(solution)/shard_map/ppermute | solution.py:24
  123.4 9.7 %copy-start.8 = (bf16[32,3456]{1,0:T(8,128)(2,1)}, bf16[32,3456]{1,0:T(8,128)(2,1)S(1)}, u32[]{:S(2)}) copy-start(bf16[32,3456]{1,0:T(8,128)(2,1)S(1)} %collective-permute-done.1) | copy-start | bytes 663556
  123.4 9.7 %copy-start.9 = (bf16[32,3456]{1,0:T(8,128)(2,1)}, bf16[32,3456]{1,0:T(8,128)(2,1)S(1)}, u32[]{:S(2)}) copy-start(bf16[32,3456]{1,0:T(8,128)(2,1)S(1)} %collective-permute-done) | copy-start | bytes 663556
  127.4 8.2 %collective-permute-start.6 = (f32[2,1,1,1,1,1,6,1536]{7,6,5,4,3,2,1,0:T(8,128)S(1)}, f32[2,1,1,1,1,1,6,1536]{7,6,5,4,3,2,1,0:T(8,128)S(1)}, u32[]{:S(2)}, u32[]{:S(2)}) collective-permute-start(f32[2,1,1,1,1,1,6,1536]{7,6,5,4,3,2,1,0:T(8,128)S(1)} %constant_dynamic-slice_fusion.1), channel_id=1, source_target_pairs={{0,128},{64,192},{128,0},{192,64},{256,384},{320,448},{384,256},{4... | collective-permute-start | bytes 221192 | tf_op jit(solution)/shard_map/ppermute | solution.py:24
  136.9 65.8 %collective-permute-start.7 = (f32[1,1,1,1,1,1,6,1536]{7,6,5,4,3,2,1,0:T(8,128)}, f32[1,1,1,1,1,1,6,1536]{7,6,5,4,3,2,1,0:T(8,128)}, u32[]{:S(2)}, u32[]{:S(2)}) collective-permute-start(f32[1,1,1,1,1,1,6,1536]{7,6,5,4,3,2,1,0:T(8,128)} %constant_dynamic-slice_fusion), channel_id=1, source_target_pairs={{0,256},{64,320},{128,384},{192,448},{256,0},{320,64},{384,128},{4... | collective-permute-start | bytes 110600 | tf_op jit(solution)/shard_map/ppermute | solution.py:24
  142.6 2.0 slice-start
  150.6 1.2 copy-start.5
  150.6 1.7 copy-start.6
  150.6 3.7 %copy-start.3 = (bf16[384,4608]{0,1:T(8,128)(2,1)S(1)}, bf16[384,4608]{0,1:T(8,128)(2,1)}, u32[]{:S(2)}) copy-start(bf16[384,4608]{0,1:T(8,128)(2,1)} %copy.19) | copy-start | bytes 10616836
  152.3 2.8 %copy-start.7 = (bf16[2,256,1536]{2,1,0:T(8,128)(2,1)}, bf16[2,256,1536]{2,1,0:T(8,128)(2,1)S(1)}, u32[]{:S(2)}) copy-start(bf16[2,256,1536]{2,1,0:T(8,128)(2,1)S(1)} %fusion.7) | copy-start | bytes 4718596
  162.2 40.5 %copy-start.11 = (f32[2,1,1,1,1,1,6,1536]{7,6,5,4,3,2,1,0:T(8,128)S(1)}, f32[2,1,1,1,1,1,6,1536]{7,6,5,4,3,2,1,0:T(8,128)}, u32[]{:S(2)}) copy-start(f32[2,1,1,1,1,1,6,1536]{7,6,5,4,3,2,1,0:T(8,128)} %copy-done.10) | copy-start | bytes 221188
  203.6 6.4 %collective-permute-start.8 = (f32[6,1536]{1,0:T(8,128)S(1)}, f32[6,1536]{1,0:T(8,128)S(1)}, u32[]{:S(2)}, u32[]{:S(2)}) collective-permute-start(f32[6,1536]{1,0:T(8,128)S(1)} %multiply_bitcast_fusion), channel_id=1, source_target_pairs={{0,1},{1,0},{2,3},{3,2},{4,5},{5,4},{6,7},{7,6},{8,9},{9,8},{10,11... | collective-permute-start | bytes 110600 | tf_op jit(solution)/shard_map/ppermute | solution.py:24
  210.0 7.5 %collective-permute-start.9 = (f32[6,1536]{1,0:T(8,128)S(1)}, f32[6,1536]{1,0:T(8,128)S(1)}, u32[]{:S(2)}, u32[]{:S(2)}) collective-permute-start(f32[6,1536]{1,0:T(8,128)S(1)} %add.181), channel_id=1, source_target_pairs={{0,2},{1,3},{2,0},{3,1},{4,6},{5,7},{6,4},{7,5},{8,10},{9,11},{10,... | collective-permute-start | bytes 110600 | tf_op jit(solution)/shard_map/ppermute | solution.py:24
  217.5 9.9 %collective-permute-start.10 = (f32[6,1536]{1,0:T(8,128)S(1)}, f32[6,1536]{1,0:T(8,128)S(1)}, u32[]{:S(2)}, u32[]{:S(2)}) collective-permute-start(f32[6,1536]{1,0:T(8,128)S(1)} %add.182), channel_id=1, source_target_pairs={{0,4},{4,0},{1,5},{5,1},{2,6},{6,2},{3,7},{7,3},{8,12},{12,8},{9,1... | collective-permute-start | bytes 110600 | tf_op jit(solution)/shard_map/ppermute | solution.py:24
  (2 other events, 1.8 us)
Sparse Core Ops, SparseCore 0:
  27.1 49.1 all-gather.3
  78.4 23.0 all-gather.5

commit v7 on v6

--- a/solution.py
+++ b/solution.py
@@ -73,14 +73,16 @@
     summed = lax.dot_general(
         bottle, jitter, (((0,), (0,)), ((), ())), preferred_element_type=jnp.float32
     )
+
+    conv_rows = conv_filters.transpose(2, 0, 1).reshape(shard, -1)
+    packed = jnp.concatenate([entry_weight, conv_rows, exit_weight], axis=1)
+    for axis in ("zl", "y"):
+        packed = lax.all_gather(packed, axis, axis=0, tiled=True)
     summed = _scatter_rows(
         summed, (("c", 1), ("zl", 1), ("zl", 2), ("y", 1), ("y", 2), ("y", 4)), shard
     )
-
-    conv_rows = conv_filters.transpose(2, 0, 1).reshape(shard, -1)
-    packed = jnp.concatenate([entry_weight, conv_rows, exit_weight], axis=1)
-    for axis in ("zl", "y", "c"):
-        packed = lax.all_gather(packed, axis, axis=0, tiled=True)
+    packed, summed = lax.optimization_barrier((packed, summed))
+    packed = lax.all_gather(packed, "c", axis=0, tiled=True)
     w_entry = packed[:, :chans]
     w_conv = packed[:, chans : 4 * chans].reshape(bot, 3, chans)
     w_exit = packed[:, 4 * chans :]

time: 236 us -> 221 us (0.936)
  waiting for transfers between devices: 83.3 us -> 75 us
  starting transfers between devices: 42.3 us -> 38.6 us
    all_gather x2 -> x1, waiting for transfers between devices: 43.5 us -> 0.01 us  [body(): packed = lax.all_gather(packed, axis, axis=0, tiled=True)]
    ppermute x9, waiting for transfers between devices: 39.8 us -> 58.8 us  [_swap(): return lax.ppermute(x, axis, [(i, i ^ d) for i in range(n)])]
    all_gather x0 -> x1, waiting for transfers between devices: none -> 15.2 us  [body(): packed = lax.all_gather(packed, 'c', axis=0, tiled=True)]
    ppermute x9, starting transfers between devices: 37.9 us -> 34.2 us  [_swap(): return lax.ppermute(x, axis, [(i, i ^ d) for i in range(n)])]
    unnamed x25 -> x29, local copies, waits for them, and re-layouts: 5.32 us -> 5.82 us
  transfers between devices with their start and end apart: 13 -> 13, of which waited for: 8 -> 10; matrix products, arithmetic and copies ran while one was open for 13% -> 4% of each run, Pallas kernels for 0% -> 0%
where the time goes in v7:
time: 221 us; the launch traced here: 220 us
  waiting for transfers between devices  75 us (34%)
  blocking collectives  52.3 us (24%)
  starting transfers between devices  38.6 us (17%)
  local copies, waits for them, and re-layouts  16.2 us (7%)
  between operations  15.9 us (7%)
  matrix products  11.8 us (5%)
  other arithmetic  10.3 us (5%)
    ppermute x9, waiting for transfers between devices, _swap(): return lax.ppermute(x, axis, [(i, i ^ d) for i in range(n)])  58.8 us
    ppermute x9, starting transfers between devices, _swap(): return lax.ppermute(x, axis, [(i, i ^ d) for i in range(n)])  34.2 us
    psum x3, blocking collectives, body(): gap = lax.psum(gap, axis)  33.4 us
    all_gather x1, blocking collectives, body(): packed = lax.all_gather(packed, axis, axis=0, tiled=True)  19 us
    all_gather x1, waiting for transfers between devices, body(): packed = lax.all_gather(packed, 'c', axis=0, tiled=True)  15.2 us
    unnamed x29, local copies, waits for them, and re-layouts  5.82 us
    slice x3, local copies, waits for them, and re-layouts, body(): w_conv = packed[:, chans:4 * chans].reshape(bot, 3, chans)  5.65 us
    dot_general x1, matrix products, body(): jnp.dot(inner, w_exit, preferred_element_type=jnp.float32)  5.5 us
  transfers between devices with their start and end apart: 13, of which 10 were waited for; matrix products, arithmetic and copies ran while one was open for 4% of the time, Pallas kernels for 0%

profile of v7, /device:TPU:2, one launch (start us, length us, event | category | flops | bytes accessed | tf_op | source)
XLA Modules:
  0.0 220.3 jit_solution(2754065165041499918)
XLA Ops:
  14.0 19.0 %all-gather = bf16[4,6,7680]{2,1,0:T(8,128)(2,1)} all-gather(bf16[1,6,7680]{2,1,0:T(8,128)(2,1)S(1)} %maximum_bitcast_fusion), channel_id=1, replica_groups=mesh['y'=8,'zl'=4,'c'=2,'zh'=2,'x'=4] {'zl'}, dimensions={0}, use_global_device_ids=true | all-gather | bytes 460800 | tf_op jit(solution)/shard_map/all_gather | solution.py:80
  38.3 3.9 %collective-permute-start.3 = (f32[2,2,2,2,1,1,6,1536]{7,3,6,5,4,2,1,0:T(2,128)S(1)}, f32[2,2,2,2,1,1,6,1536]{7,3,6,5,4,2,1,0:T(2,128)S(1)}, u32[]{:S(2)}, u32[]{:S(2)}) collective-permute-start(f32[2,2,2,2,1,1,6,1536]{7,3,6,5,4,2,1,0:T(2,128)S(1)} %copy.22), channel_id=1, source_target_pairs={{0,16},{16,0},{32,48},{48,32},{1,17},{17,1},{33,49},{49,33},{2,18}... | collective-permute-start | bytes 1769480 | tf_op jit(solution)/shard_map/ppermute | solution.py:24
  42.2 12.4 %collective-permute-done.3 = f32[2,2,2,2,1,1,6,1536]{7,3,6,5,4,2,1,0:T(2,128)S(1)} collective-permute-done((f32[2,2,2,2,1,1,6,1536]{7,3,6,5,4,2,1,0:T(2,128)S(1)}, f32[2,2,2,2,1,1,6,1536]{7,3,6,5,4,2,1,0:T(2,128)S(1)}, u32[]{:S(2)}, u32[]{:S(2)}) %collective-permute-start.3) | collective-permute-done | bytes 589856 | tf_op jit(solution)/shard_map/ppermute | solution.py:24
  56.0 3.8 %collective-permute-start.4 = (f32[2,2,2,1,1,1,6,1536]{7,6,5,4,3,2,1,0:T(8,128)S(1)}, f32[2,2,2,1,1,1,6,1536]{7,6,5,4,3,2,1,0:T(8,128)S(1)}, u32[]{:S(2)}, u32[]{:S(2)}) collective-permute-start(f32[2,2,2,1,1,1,6,1536]{7,6,5,4,3,2,1,0:T(8,128)S(1)} %constant_dynamic-slice_fusion.3), channel_id=1, source_target_pairs={{0,32},{16,48},{32,0},{48,16},{1,33},{17,49},{33,1},{49,17},{2,34}... | collective-permute-start | bytes 884744 | tf_op jit(solution)/shard_map/ppermute | solution.py:24
  59.8 16.4 %collective-permute-done.4 = f32[2,2,2,1,1,1,6,1536]{7,6,5,4,3,2,1,0:T(8,128)S(1)} collective-permute-done((f32[2,2,2,1,1,1,6,1536]{7,6,5,4,3,2,1,0:T(8,128)S(1)}, f32[2,2,2,1,1,1,6,1536]{7,6,5,4,3,2,1,0:T(8,128)S(1)}, u32[]{:S(2)}, u32[]{:S(2)}) %collective-permute-start.4) | collective-permute-done | bytes 294944 | tf_op jit(solution)/shard_map/ppermute | solution.py:24
  76.3 3.5 %collective-permute-start.5 = (f32[2,2,1,1,1,1,6,1536]{7,6,5,4,3,2,1,0:T(8,128)S(1)}, f32[2,2,1,1,1,1,6,1536]{7,6,5,4,3,2,1,0:T(8,128)S(1)}, u32[]{:S(2)}, u32[]{:S(2)}) collective-permute-start(f32[2,2,1,1,1,1,6,1536]{7,6,5,4,3,2,1,0:T(8,128)S(1)} %constant_dynamic-slice_fusion.2), channel_id=1, source_target_pairs={{0,64},{64,0},{128,192},{192,128},{256,320},{320,256},{384,448},{4... | collective-permute-start | bytes 442376 | tf_op jit(solution)/shard_map/ppermute | solution.py:24
  79.8 6.9 %collective-permute-done.5 = f32[2,2,1,1,1,1,6,1536]{7,6,5,4,3,2,1,0:T(8,128)S(1)} collective-permute-done((f32[2,2,1,1,1,1,6,1536]{7,6,5,4,3,2,1,0:T(8,128)S(1)}, f32[2,2,1,1,1,1,6,1536]{7,6,5,4,3,2,1,0:T(8,128)S(1)}, u32[]{:S(2)}, u32[]{:S(2)}) %collective-permute-start.5) | collective-permute-done | bytes 147488 | tf_op jit(solution)/shard_map/ppermute | solution.py:24
  86.7 4.3 %collective-permute-start.6 = (f32[2,1,1,1,1,1,6,1536]{7,6,5,4,3,2,1,0:T(8,128)S(1)}, f32[2,1,1,1,1,1,6,1536]{7,6,5,4,3,2,1,0:T(8,128)S(1)}, u32[]{:S(2)}, u32[]{:S(2)}) collective-permute-start(f32[2,1,1,1,1,1,6,1536]{7,6,5,4,3,2,1,0:T(8,128)S(1)} %constant_dynamic-slice_fusion.1), channel_id=1, source_target_pairs={{0,128},{64,192},{128,0},{192,64},{256,384},{320,448},{384,256},{4... | collective-permute-start | bytes 221192 | tf_op jit(solution)/shard_map/ppermute | solution.py:24
  91.1 5.1 %collective-permute-done.6 = f32[2,1,1,1,1,1,6,1536]{7,6,5,4,3,2,1,0:T(8,128)S(1)} collective-permute-done((f32[2,1,1,1,1,1,6,1536]{7,6,5,4,3,2,1,0:T(8,128)S(1)}, f32[2,1,1,1,1,1,6,1536]{7,6,5,4,3,2,1,0:T(8,128)S(1)}, u32[]{:S(2)}, u32[]{:S(2)}) %collective-permute-start.6) | collective-permute-done | bytes 73760 | tf_op jit(solution)/shard_map/ppermute | solution.py:24
  96.3 5.5 %collective-permute-start.7 = (f32[1,1,1,1,1,1,6,1536]{7,6,5,4,3,2,1,0:T(8,128)S(1)}, f32[1,1,1,1,1,1,6,1536]{7,6,5,4,3,2,1,0:T(8,128)S(1)}, u32[]{:S(2)}, u32[]{:S(2)}) collective-permute-start(f32[1,1,1,1,1,1,6,1536]{7,6,5,4,3,2,1,0:T(8,128)S(1)} %constant_dynamic-slice_fusion), channel_id=1, source_target_pairs={{0,256},{64,320},{128,384},{192,448},{256,0},{320,64},{384,128},{4... | collective-permute-start | bytes 110600 | tf_op jit(solution)/shard_map/ppermute | solution.py:24
  101.8 5.0 %collective-permute-done.7 = f32[1,1,1,1,1,1,6,1536]{7,6,5,4,3,2,1,0:T(8,128)S(1)} collective-permute-done((f32[1,1,1,1,1,1,6,1536]{7,6,5,4,3,2,1,0:T(8,128)S(1)}, f32[1,1,1,1,1,1,6,1536]{7,6,5,4,3,2,1,0:T(8,128)S(1)}, u32[]{:S(2)}, u32[]{:S(2)}) %collective-permute-start.7) | collective-permute-done | bytes 36896 | tf_op jit(solution)/shard_map/ppermute | solution.py:24
  108.8 3.0 %collective-permute-start = (bf16[32,3456]{1,0:T(8,128)(2,1)S(1)}, bf16[32,3456]{1,0:T(8,128)(2,1)S(1)}, u32[]{:S(2)}, u32[]{:S(2)}) collective-permute-start(bf16[32,3456]{1,0:T(8,128)(2,1)S(1)} %get-tuple-element.10), channel_id=1, source_target_pairs={{0,8},{8,16},{16,24},{24,32},{32,40},{40,48},{48,56},{56,64},{64,7... | collective-permute-start | bytes 663560 | tf_op jit(solution)/shard_map/ppermute | solution.py:94
  115.3 15.2 %all-gather.6.cloned.1.call-done = bf16[384,7680]{1,0:T(8,128)(2,1)} async-done(((bf16[192,7680]{1,0:T(8,128)(2,1)}), bf16[384,7680]{1,0:T(8,128)(2,1)}) %all-gather.6.cloned.1.call-update) | async-done | bytes 5898256 | tf_op jit(solution)/shard_map/all_gather | solution.py:85
  132.5 3.7 %copy.24 = bf16[384,4608]{0,1:T(8,128)(2,1)} copy(bf16[384,4608]{1,0:T(8,128)(2,1)S(1)} %slice-done) | data formatting | bytes 7077888 | tf_op jit(solution)/shard_map/slice | solution.py:87
  144.7 5.5 %convolution_add_fusion = f32[2,192,1536]{2,1,0:T(8,128)} fusion(f32[1,256,1536]{2,1,0:T(8,128)} %copy-done.6, f32[1,256,1536]{2,1,0:T(8,128)} %copy-done.5, bf16[384,7680]{1,0:T(8,128)(2,1)} %all-gather.6.cloned.1.call-done, f32[2,192,384]{2,1,0:T(8,128)} %convolution_add_fusion.2, bf16[384,3,1536]{0,2,1:T(8,128)(2,1)S(1)} %bitcast.64, ...), kind=kOutput, calls=%fused_computation.12 | convolution fusion | flops 908623872 | bytes 9633792 | tf_op jit(solution)/shard_map/dot_general | solution.py:122
  150.2 3.6 %multiply_reduce_fusion = (f32[]{:T(128)}, bf16[1,192,1536]{2,1,0:T(8,128)(2,1)}) fusion(bf16[1,192,1536]{2,1,0:T(8,128)(2,1)} %param.10, f32[2,192,1536]{2,1,0:T(8,128)} %convolution_add_fusion), kind=kLoop, calls=%fused_computation.32 | loop fusion | flops 2654207 | bytes 3538948 | tf_op jit(solution)/shard_map/reduce_sum | solution.py:128
  154.4 3.0 %psum.21 = f32[]{:T(128)} all-reduce(f32[]{:T(128)S(6)} %div.40), channel_id=1, replica_groups=mesh['y'=8,'zl'=4,'c'=2,'zh'=2,'x'=4] {'c'}, use_global_device_ids=true, to_apply=%region_1.2 | all-reduce | flops 1 | bytes 8 | tf_op jit(solution)/shard_map/psum | solution.py:131
  157.4 12.8 %psum.22 = f32[]{:T(128)} all-reduce(f32[]{:T(128)} %psum.21), channel_id=1, replica_groups=mesh['y'=8,'zl'=4,'c'=2,'zh'=2,'x'=4] {'zl'}, use_global_device_ids=true, to_apply=%region_2.3 | all-reduce | flops 1 | bytes 8 | tf_op jit(solution)/shard_map/psum | solution.py:131
  170.2 17.6 %psum.23 = f32[]{:T(128)} all-reduce(f32[]{:T(128)} %psum.22), channel_id=1, replica_groups=mesh['y'=8,'zl'=4,'c'=2,'zh'=2,'x'=4] {'y'}, use_global_device_ids=true, to_apply=%region_3.4 | all-reduce | flops 1 | bytes 8 | tf_op jit(solution)/shard_map/psum | solution.py:131
  190.9 4.0 %collective-permute-done.8 = f32[6,1536]{1,0:T(8,128)S(1)} collective-permute-done((f32[6,1536]{1,0:T(8,128)S(1)}, f32[6,1536]{1,0:T(8,128)S(1)}, u32[]{:S(2)}, u32[]{:S(2)}) %collective-permute-start.8) | collective-permute-done | bytes 36896 | tf_op jit(solution)/shard_map/ppermute | solution.py:24
  194.9 3.5 %collective-permute-start.9 = (f32[6,1536]{1,0:T(8,128)S(1)}, f32[6,1536]{1,0:T(8,128)S(1)}, u32[]{:S(2)}, u32[]{:S(2)}) collective-permute-start(f32[6,1536]{1,0:T(8,128)S(1)} %fusion.43), channel_id=1, source_target_pairs={{0,2},{1,3},{2,0},{3,1},{4,6},{5,7},{6,4},{7,5},{8,10},{9,11},{10,... | collective-permute-start | bytes 110600 | tf_op jit(solution)/shard_map/ppermute | solution.py:24
  198.4 3.9 %collective-permute-done.9 = f32[6,1536]{1,0:T(8,128)S(1)} collective-permute-done((f32[6,1536]{1,0:T(8,128)S(1)}, f32[6,1536]{1,0:T(8,128)S(1)}, u32[]{:S(2)}, u32[]{:S(2)}) %collective-permute-start.9) | collective-permute-done | bytes 36896 | tf_op jit(solution)/shard_map/ppermute | solution.py:24
  202.4 5.3 %collective-permute-start.10 = (f32[6,1536]{1,0:T(8,128)S(1)}, f32[6,1536]{1,0:T(8,128)S(1)}, u32[]{:S(2)}, u32[]{:S(2)}) collective-permute-start(f32[6,1536]{1,0:T(8,128)S(1)} %add.182), channel_id=1, source_target_pairs={{0,4},{4,0},{1,5},{5,1},{2,6},{6,2},{3,7},{7,3},{8,12},{12,8},{9,1... | collective-permute-start | bytes 110600 | tf_op jit(solution)/shard_map/ppermute | solution.py:24
  207.7 5.1 %collective-permute-done.10 = f32[6,1536]{1,0:T(8,128)S(1)} collective-permute-done((f32[6,1536]{1,0:T(8,128)S(1)}, f32[6,1536]{1,0:T(8,128)S(1)}, u32[]{:S(2)}, u32[]{:S(2)}) %collective-permute-start.10) | collective-permute-done | bytes 36896 | tf_op jit(solution)/shard_map/ppermute | solution.py:24
  (75 shorter events, 32.5 us)
Async XLA Ops:
  7.2 100.3 %all-gather.4.cloned.1.call-start = ((), (), s32[]{:S(2)}) async-start(), calls=%async_computation | async-start | bytes 3317760 | tf_op jit(solution)/shard_map/all_gather | solution.py:80
  10.0 3.9 %copy-start.11 = (bf16[3,1536,6]{1,2,0:T(8,128)(2,1)S(1)}, bf16[3,1536,6]{1,2,0:T(8,128)(2,1)}, u32[]{:S(2)}) copy-start(bf16[3,1536,6]{1,2,0:T(8,128)(2,1)} %param.12) | copy-start | bytes 165892
  10.0 3.9 %copy-start.12 = (bf16[6,1536]{1,0:T(8,128)(2,1)S(1)}, bf16[6,1536]{1,0:T(8,128)(2,1)}, u32[]{:S(2)}) copy-start(bf16[6,1536]{1,0:T(8,128)(2,1)} %param.13) | copy-start | bytes 55300
  10.1 3.9 %copy-start.13 = (bf16[6,1536]{1,0:T(8,128)(2,1)S(1)}, bf16[6,1536]{1,0:T(8,128)(2,1)}, u32[]{:S(2)}) copy-start(bf16[6,1536]{1,0:T(8,128)(2,1)} %param.11) | copy-start | bytes 55300
  12.0 22.9 %collective-permute-start.2 = (f32[2,2,2,2,2,1,6,1536]{7,4,6,5,3,2,1,0:T(2,128)}, f32[2,2,2,2,2,1,6,1536]{7,4,6,5,3,2,1,0:T(2,128)}, u32[]{:S(2)}, u32[]{:S(2)}) collective-permute-start(f32[2,2,2,2,2,1,6,1536]{7,4,6,5,3,2,1,0:T(2,128)} %copy.20), channel_id=1, source_target_pairs={{0,8},{8,0},{1,9},{9,1},{2,10},{10,2},{3,11},{11,3},{4,12},{12,4},... | collective-permute-start | bytes 3538952 | tf_op jit(solution)/shard_map/ppermute | solution.py:24
  34.9 95.6 %all-gather.6.cloned.1.call-start = ((), (), s32[]{:S(2)}) async-start(), calls=%async_computation.1 | async-start | bytes 8847360 | tf_op jit(solution)/shard_map/all_gather | solution.py:85
  38.3 16.3 %collective-permute-start.3 = (f32[2,2,2,2,1,1,6,1536]{7,3,6,5,4,2,1,0:T(2,128)S(1)}, f32[2,2,2,2,1,1,6,1536]{7,3,6,5,4,2,1,0:T(2,128)S(1)}, u32[]{:S(2)}, u32[]{:S(2)}) collective-permute-start(f32[2,2,2,2,1,1,6,1536]{7,3,6,5,4,2,1,0:T(2,128)S(1)} %copy.22), channel_id=1, source_target_pairs={{0,16},{16,0},{32,48},{48,32},{1,17},{17,1},{33,49},{49,33},{2,18}... | collective-permute-start | bytes 1769480 | tf_op jit(solution)/shard_map/ppermute | solution.py:24
  56.0 20.3 %collective-permute-start.4 = (f32[2,2,2,1,1,1,6,1536]{7,6,5,4,3,2,1,0:T(8,128)S(1)}, f32[2,2,2,1,1,1,6,1536]{7,6,5,4,3,2,1,0:T(8,128)S(1)}, u32[]{:S(2)}, u32[]{:S(2)}) collective-permute-start(f32[2,2,2,1,1,1,6,1536]{7,6,5,4,3,2,1,0:T(8,128)S(1)} %constant_dynamic-slice_fusion.3), channel_id=1, source_target_pairs={{0,32},{16,48},{32,0},{48,16},{1,33},{17,49},{33,1},{49,17},{2,34}... | collective-permute-start | bytes 884744 | tf_op jit(solution)/shard_map/ppermute | solution.py:24
  76.3 10.4 %collective-permute-start.5 = (f32[2,2,1,1,1,1,6,1536]{7,6,5,4,3,2,1,0:T(8,128)S(1)}, f32[2,2,1,1,1,1,6,1536]{7,6,5,4,3,2,1,0:T(8,128)S(1)}, u32[]{:S(2)}, u32[]{:S(2)}) collective-permute-start(f32[2,2,1,1,1,1,6,1536]{7,6,5,4,3,2,1,0:T(8,128)S(1)} %constant_dynamic-slice_fusion.2), channel_id=1, source_target_pairs={{0,64},{64,0},{128,192},{192,128},{256,320},{320,256},{384,448},{4... | collective-permute-start | bytes 442376 | tf_op jit(solution)/shard_map/ppermute | solution.py:24
  86.7 9.4 %collective-permute-start.6 = (f32[2,1,1,1,1,1,6,1536]{7,6,5,4,3,2,1,0:T(8,128)S(1)}, f32[2,1,1,1,1,1,6,1536]{7,6,5,4,3,2,1,0:T(8,128)S(1)}, u32[]{:S(2)}, u32[]{:S(2)}) collective-permute-start(f32[2,1,1,1,1,1,6,1536]{7,6,5,4,3,2,1,0:T(8,128)S(1)} %constant_dynamic-slice_fusion.1), channel_id=1, source_target_pairs={{0,128},{64,192},{128,0},{192,64},{256,384},{320,448},{384,256},{4... | collective-permute-start | bytes 221192 | tf_op jit(solution)/shard_map/ppermute | solution.py:24
  96.2 11.2 %copy-start = (bf16[1,192,1536]{2,1,0:T(8,128)(2,1)S(1)}, bf16[1,192,1536]{2,1,0:T(8,128)(2,1)}, u32[]{:S(2)}) copy-start(bf16[1,192,1536]{2,1,0:T(8,128)(2,1)} %param.9) | copy-start | bytes 1769476
  96.2 11.2 %copy-start.2 = (bf16[1,192,1536]{2,1,0:T(8,128)(2,1)S(1)}, bf16[1,192,1536]{2,1,0:T(8,128)(2,1)}, u32[]{:S(2)}) copy-start(bf16[1,192,1536]{2,1,0:T(8,128)(2,1)} %param.7) | copy-start | bytes 1769476
  96.2 11.2 %copy-start.4 = (bf16[1,192,384]{2,1,0:T(8,128)(2,1)S(1)}, bf16[1,192,384]{2,1,0:T(8,128)(2,1)}, u32[]{:S(2)}) copy-start(bf16[1,192,384]{2,1,0:T(8,128)(2,1)} %param.8) | copy-start | bytes 442372
  96.3 10.5 %collective-permute-start.7 = (f32[1,1,1,1,1,1,6,1536]{7,6,5,4,3,2,1,0:T(8,128)S(1)}, f32[1,1,1,1,1,1,6,1536]{7,6,5,4,3,2,1,0:T(8,128)S(1)}, u32[]{:S(2)}, u32[]{:S(2)}) collective-permute-start(f32[1,1,1,1,1,1,6,1536]{7,6,5,4,3,2,1,0:T(8,128)S(1)} %constant_dynamic-slice_fusion), channel_id=1, source_target_pairs={{0,256},{64,320},{128,384},{192,448},{256,0},{320,64},{384,128},{4... | collective-permute-start | bytes 110600 | tf_op jit(solution)/shard_map/ppermute | solution.py:24
  107.5 4.4 %collective-permute-start.1 = (bf16[32,3456]{1,0:T(8,128)(2,1)S(1)}, bf16[32,3456]{1,0:T(8,128)(2,1)S(1)}, u32[]{:S(2)}, u32[]{:S(2)}) collective-permute-start(bf16[32,3456]{1,0:T(8,128)(2,1)S(1)} %get-tuple-element.11), channel_id=1, source_target_pairs={{8,0},{16,8},{24,16},{32,24},{40,32},{48,40},{56,48},{64,56},{72,6... | collective-permute-start | bytes 663560 | tf_op jit(solution)/shard_map/ppermute | solution.py:95
  108.8 4.1 %collective-permute-start = (bf16[32,3456]{1,0:T(8,128)(2,1)S(1)}, bf16[32,3456]{1,0:T(8,128)(2,1)S(1)}, u32[]{:S(2)}, u32[]{:S(2)}) collective-permute-start(bf16[32,3456]{1,0:T(8,128)(2,1)S(1)} %get-tuple-element.10), channel_id=1, source_target_pairs={{0,8},{8,16},{16,24},{24,32},{32,40},{40,48},{48,56},{56,64},{64,7... | collective-permute-start | bytes 663560 | tf_op jit(solution)/shard_map/ppermute | solution.py:94
  111.9 2.1 copy-start.8
  130.5 2.0 slice-start
  138.6 3.7 %copy-start.3 = (bf16[384,4608]{0,1:T(8,128)(2,1)S(1)}, bf16[384,4608]{0,1:T(8,128)(2,1)}, u32[]{:S(2)}) copy-start(bf16[384,4608]{0,1:T(8,128)(2,1)} %copy.24) | copy-start | bytes 10616836
  140.2 2.9 %copy-start.7 = (bf16[2,256,1536]{2,1,0:T(8,128)(2,1)}, bf16[2,256,1536]{2,1,0:T(8,128)(2,1)S(1)}, u32[]{:S(2)}) copy-start(bf16[2,256,1536]{2,1,0:T(8,128)(2,1)S(1)} %fusion.7) | copy-start | bytes 4718596
  150.2 38.2 %copy-start.10 = (f32[6,1536]{1,0:T(8,128)S(1)}, f32[6,1536]{1,0:T(8,128)}, u32[]{:S(2)}) copy-start(f32[6,1536]{1,0:T(8,128)} %add_bitcast_fusion.1) | copy-start | bytes 110596
  188.4 6.4 %collective-permute-start.8 = (f32[6,1536]{1,0:T(8,128)S(1)}, f32[6,1536]{1,0:T(8,128)S(1)}, u32[]{:S(2)}, u32[]{:S(2)}) collective-permute-start(f32[6,1536]{1,0:T(8,128)S(1)} %broadcast_multiply_fusion), channel_id=1, source_target_pairs={{0,1},{1,0},{2,3},{3,2},{4,5},{5,4},{6,7},{7,6},{8,9},{9,8},{10,11... | collective-permute-start | bytes 110600 | tf_op jit(solution)/shard_map/ppermute | solution.py:24
  194.9 7.5 %collective-permute-start.9 = (f32[6,1536]{1,0:T(8,128)S(1)}, f32[6,1536]{1,0:T(8,128)S(1)}, u32[]{:S(2)}, u32[]{:S(2)}) collective-permute-start(f32[6,1536]{1,0:T(8,128)S(1)} %fusion.43), channel_id=1, source_target_pairs={{0,2},{1,3},{2,0},{3,1},{4,6},{5,7},{6,4},{7,5},{8,10},{9,11},{10,... | collective-permute-start | bytes 110600 | tf_op jit(solution)/shard_map/ppermute | solution.py:24
  202.4 10.4 %collective-permute-start.10 = (f32[6,1536]{1,0:T(8,128)S(1)}, f32[6,1536]{1,0:T(8,128)S(1)}, u32[]{:S(2)}, u32[]{:S(2)}) collective-permute-start(f32[6,1536]{1,0:T(8,128)S(1)} %add.182), channel_id=1, source_target_pairs={{0,4},{4,0},{1,5},{5,1},{2,6},{6,2},{3,7},{7,3},{8,12},{12,8},{9,1... | collective-permute-start | bytes 110600 | tf_op jit(solution)/shard_map/ppermute | solution.py:24
  (4 other events, 5.0 us)
Sparse Core Ops, SparseCore 0:
  35.0 50.7 all-gather.3
  107.6 22.8 all-gather.5

commit v8 on v7

--- a/solution.py
+++ b/solution.py
@@ -49,7 +49,7 @@
         mine = _bit(axis, d)
         keep = lax.dynamic_index_in_dim(held, mine, axis=dim, keepdims=True)
         give = lax.dynamic_index_in_dim(held, 1 - mine, axis=dim, keepdims=True)
-        held = keep + _swap(give, axis, d)
+        held = keep + _swap(give.astype(jnp.bfloat16), axis, d).astype(full.dtype)
     return held.reshape((shard,) + full.shape[1:])
 
 

time: 221 us -> 208 us (0.941)
  waiting for transfers between devices: 75 us -> 62.4 us
  starting transfers between devices: 38.6 us -> 42 us
  local copies, waits for them, and re-layouts: 16.2 us -> 13.2 us
    ppermute x9, waiting for transfers between devices: 58.8 us -> 43.4 us  [_swap(): return lax.ppermute(x, axis, [(i, i ^ d) for i in range(n)])]
    ppermute x9, starting transfers between devices: 34.2 us -> 37.6 us  [_swap(): return lax.ppermute(x, axis, [(i, i ^ d) for i in range(n)])]
    all_gather x1, waiting for transfers between devices: 15.2 us -> 17.9 us  [body(): packed = lax.all_gather(packed, 'c', axis=0, tiled=True)]
    dynamic_slice x8 -> x1, local copies, waits for them, and re-layouts: 2.65 us -> 0.11 us  [_scatter_rows(): give = lax.dynamic_index_in_dim(held, 1 - mine, axis=dim, keepdims=True)]
    unnamed x29 -> x24, local copies, waits for them, and re-layouts: 5.82 us -> 6.06 us
  transfers between devices with their start and end apart: 13 -> 13, of which waited for: 10 -> 11; matrix products, arithmetic and copies ran while one was open for 4% -> 4% of each run, Pallas kernels for 0% -> 0%
where the time goes in v8:
time: 208 us; the launch traced here: 207 us
  waiting for transfers between devices  62.4 us (30%)
  blocking collectives  51.3 us (25%)
  starting transfers between devices  42 us (20%)
  between operations  15.9 us (8%)
  local copies, waits for them, and re-layouts  13.2 us (6%)
  matrix products  11.8 us (6%)
  other arithmetic  10.8 us (5%)
    ppermute x9, waiting for transfers between devices, _swap(): return lax.ppermute(x, axis, [(i, i ^ d) for i in range(n)])  43.4 us
    ppermute x9, starting transfers between devices, _swap(): return lax.ppermute(x, axis, [(i, i ^ d) for i in range(n)])  37.6 us
    psum x3, blocking collectives, body(): gap = lax.psum(gap, axis)  33.4 us
    all_gather x1, blocking collectives, body(): packed = lax.all_gather(packed, axis, axis=0, tiled=True)  17.9 us
    all_gather x1, waiting for transfers between devices, body(): packed = lax.all_gather(packed, 'c', axis=0, tiled=True)  17.9 us
    unnamed x24, local copies, waits for them, and re-layouts  6.06 us
    slice x3, local copies, waits for them, and re-layouts, body(): w_conv = packed[:, chans:4 * chans].reshape(bot, 3, chans)  5.63 us
    dot_general x1, matrix products, body(): jnp.dot(inner, w_exit, preferred_element_type=jnp.float32)  5.49 us
  transfers between devices with their start and end apart: 13, of which 11 were waited for; matrix products, arithmetic and copies ran while one was open for 4% of the time, Pallas kernels for 0%

profile of v8, /device:TPU:2, one launch (start us, length us, event | category | flops | bytes accessed | tf_op | source)
XLA Modules:
  0.0 207.4 jit_solution(5239717958573454475)
XLA Ops:
  8.2 17.9 %all-gather = bf16[4,6,7680]{2,1,0:T(8,128)(2,1)S(1)} all-gather(bf16[1,6,7680]{2,1,0:T(8,128)(2,1)S(1)} %maximum_bitcast_fusion), channel_id=1, replica_groups=mesh['y'=8,'zl'=4,'c'=2,'zh'=2,'x'=4] {'zl'}, dimensions={0}, use_global_device_ids=true | all-gather | bytes 460800 | tf_op jit(solution)/shard_map/all_gather | solution.py:80
  37.0 4.1 %collective-permute-start.3 = (bf16[2,2,2,2,1,1,6,1536]{7,6,5,4,3,2,1,0:T(8,128)(2,1)S(1)}, bf16[2,2,2,2,1,1,6,1536]{7,6,5,4,3,2,1,0:T(8,128)(2,1)S(1)}, u32[]{:S(2)}, u32[]{:S(2)}) collective-permute-start(bf16[2,2,2,2,1,1,6,1536]{7,6,5,4,3,2,1,0:T(8,128)(2,1)S(1)} %dynamic-slice_convert_fusion), channel_id=1, source_target_pairs={{0,16},{16,0},{32,48},{48,32},{1,17},{17,1},{33,49},{49,33},{2,18}... | collective-permute-start | bytes 884744 | tf_op jit(solution)/shard_map/ppermute | solution.py:24
  41.1 9.4 %collective-permute-done.3 = bf16[2,2,2,2,1,1,6,1536]{7,6,5,4,3,2,1,0:T(8,128)(2,1)S(1)} collective-permute-done((bf16[2,2,2,2,1,1,6,1536]{7,6,5,4,3,2,1,0:T(8,128)(2,1)S(1)}, bf16[2,2,2,2,1,1,6,1536]{7,6,5,4,3,2,1,0:T(8,128)(2,1)S(1)}, u32[]{:S(2)}, u32[]{:S(2)}) %collective-permute-start.3) | collective-permute-done | bytes 294944 | tf_op jit(solution)/shard_map/ppermute | solution.py:24
  51.8 4.4 %collective-permute-start.4 = (bf16[2,2,2,1,1,1,6,1536]{7,6,5,4,3,2,1,0:T(8,128)(2,1)S(1)}, bf16[2,2,2,1,1,1,6,1536]{7,6,5,4,3,2,1,0:T(8,128)(2,1)S(1)}, u32[]{:S(2)}, u32[]{:S(2)}) collective-permute-start(bf16[2,2,2,1,1,1,6,1536]{7,6,5,4,3,2,1,0:T(8,128)(2,1)S(1)} %dynamic-slice_convert_fusion.1), channel_id=1, source_target_pairs={{0,32},{16,48},{32,0},{48,16},{1,33},{17,49},{33,1},{49,17},{2,34}... | collective-permute-start | bytes 442376 | tf_op jit(solution)/shard_map/ppermute | solution.py:24
  56.2 9.1 %collective-permute-done.4 = bf16[2,2,2,1,1,1,6,1536]{7,6,5,4,3,2,1,0:T(8,128)(2,1)S(1)} collective-permute-done((bf16[2,2,2,1,1,1,6,1536]{7,6,5,4,3,2,1,0:T(8,128)(2,1)S(1)}, bf16[2,2,2,1,1,1,6,1536]{7,6,5,4,3,2,1,0:T(8,128)(2,1)S(1)}, u32[]{:S(2)}, u32[]{:S(2)}) %collective-permute-start.4) | collective-permute-done | bytes 147488 | tf_op jit(solution)/shard_map/ppermute | solution.py:24
  65.4 3.4 %collective-permute-start.5 = (bf16[2,2,1,1,1,1,6,1536]{7,6,5,4,3,2,1,0:T(8,128)(2,1)S(1)}, bf16[2,2,1,1,1,1,6,1536]{7,6,5,4,3,2,1,0:T(8,128)(2,1)S(1)}, u32[]{:S(2)}, u32[]{:S(2)}) collective-permute-start(bf16[2,2,1,1,1,1,6,1536]{7,6,5,4,3,2,1,0:T(8,128)(2,1)S(1)} %dynamic-slice_convert_fusion.2), channel_id=1, source_target_pairs={{0,64},{64,0},{128,192},{192,128},{256,320},{320,256},{384,448},{4... | collective-permute-start | bytes 221192 | tf_op jit(solution)/shard_map/ppermute | solution.py:24
  68.9 5.5 %collective-permute-done.5 = bf16[2,2,1,1,1,1,6,1536]{7,6,5,4,3,2,1,0:T(8,128)(2,1)S(1)} collective-permute-done((bf16[2,2,1,1,1,1,6,1536]{7,6,5,4,3,2,1,0:T(8,128)(2,1)S(1)}, bf16[2,2,1,1,1,1,6,1536]{7,6,5,4,3,2,1,0:T(8,128)(2,1)S(1)}, u32[]{:S(2)}, u32[]{:S(2)}) %collective-permute-start.5) | collective-permute-done | bytes 73760 | tf_op jit(solution)/shard_map/ppermute | solution.py:24
  74.5 4.4 %collective-permute-start.6 = (bf16[2,1,1,1,1,1,6,1536]{7,6,5,4,3,2,1,0:T(8,128)(2,1)S(1)}, bf16[2,1,1,1,1,1,6,1536]{7,6,5,4,3,2,1,0:T(8,128)(2,1)S(1)}, u32[]{:S(2)}, u32[]{:S(2)}) collective-permute-start(bf16[2,1,1,1,1,1,6,1536]{7,6,5,4,3,2,1,0:T(8,128)(2,1)S(1)} %dynamic-slice_convert_fusion.3), channel_id=1, source_target_pairs={{0,128},{64,192},{128,0},{192,64},{256,384},{320,448},{384,256},{4... | collective-permute-start | bytes 110600 | tf_op jit(solution)/shard_map/ppermute | solution.py:24
  81.4 8.0 %collective-permute-start.7 = (bf16[1,1,1,1,1,1,6,1536]{7,6,5,4,3,2,1,0:T(8,128)(2,1)S(1)}, bf16[1,1,1,1,1,1,6,1536]{7,6,5,4,3,2,1,0:T(8,128)(2,1)S(1)}, u32[]{:S(2)}, u32[]{:S(2)}) collective-permute-start(bf16[1,1,1,1,1,1,6,1536]{7,6,5,4,3,2,1,0:T(8,128)(2,1)S(1)} %dynamic-slice_convert_fusion.4), channel_id=1, source_target_pairs={{0,256},{64,320},{128,384},{192,448},{256,0},{320,64},{384,128},{4... | collective-permute-start | bytes 55304 | tf_op jit(solution)/shard_map/ppermute | solution.py:24
  93.3 3.0 %collective-permute-start = (bf16[32,3456]{1,0:T(8,128)(2,1)S(1)}, bf16[32,3456]{1,0:T(8,128)(2,1)S(1)}, u32[]{:S(2)}, u32[]{:S(2)}) collective-permute-start(bf16[32,3456]{1,0:T(8,128)(2,1)S(1)} %get-tuple-element.10), channel_id=1, source_target_pairs={{0,8},{8,16},{16,24},{24,32},{32,40},{40,48},{48,56},{56,64},{64,7... | collective-permute-start | bytes 663560 | tf_op jit(solution)/shard_map/ppermute | solution.py:94
  99.8 17.9 %all-gather.6.cloned.1.call-done = bf16[384,7680]{1,0:T(8,128)(2,1)} async-done(((bf16[192,7680]{1,0:T(8,128)(2,1)}), bf16[384,7680]{1,0:T(8,128)(2,1)}) %all-gather.6.cloned.1.call-update) | async-done | bytes 5898256 | tf_op jit(solution)/shard_map/all_gather | solution.py:85
  119.7 3.6 %copy.31 = bf16[384,4608]{0,1:T(8,128)(2,1)} copy(bf16[384,4608]{1,0:T(8,128)(2,1)S(1)} %slice-done) | data formatting | bytes 7077888 | tf_op jit(solution)/shard_map/slice | solution.py:87
  123.3 2.4 %subtract_bitcast_fusion = (f32[1,256,1536]{2,1,0:T(8,128)S(1)}, f32[1,256,1536]{2,1,0:T(8,128)S(1)}) fusion(bf16[256,3456]{1,0:T(8,128)(2,1)} %pad_maximum_fusion.1, bf16[32,3456]{1,0:T(8,128)(2,1)} %copy-done.8, bf16[192,1536]{1,0:T(8,128)(2,1)} %bitcast.54, bf16[192,384]{1,0:T(8,128)(2,1)} %bitcast.65, bf16[192,1536]{1,0:T(8,128)(2,1)} %bitcast.58, ...), kind=kOutput, calls=%fused_computation.15 | convolution fusion | flops 307888128 | bytes 7077888 | tf_op jit(solution)/shard_map/dot_general | solution.py:106
  131.9 5.5 %convolution_add_fusion = f32[2,192,1536]{2,1,0:T(8,128)} fusion(f32[1,256,1536]{2,1,0:T(8,128)} %copy-done.6, f32[1,256,1536]{2,1,0:T(8,128)} %copy-done.5, bf16[384,7680]{1,0:T(8,128)(2,1)} %all-gather.6.cloned.1.call-done, f32[2,192,384]{2,1,0:T(8,128)} %convolution_add_fusion.2, bf16[384,3,1536]{0,2,1:T(8,128)(2,1)S(1)} %bitcast.64, ...), kind=kOutput, calls=%fused_computation.12 | convolution fusion | flops 908623872 | bytes 9633792 | tf_op jit(solution)/shard_map/dot_general | solution.py:122
  137.4 3.6 %multiply_reduce_fusion = (f32[]{:T(128)}, bf16[1,192,1536]{2,1,0:T(8,128)(2,1)}) fusion(bf16[1,192,1536]{2,1,0:T(8,128)(2,1)} %param.10, f32[2,192,1536]{2,1,0:T(8,128)} %convolution_add_fusion), kind=kLoop, calls=%fused_computation.33 | loop fusion | flops 2654207 | bytes 3538948 | tf_op jit(solution)/shard_map/reduce_sum | solution.py:128
  141.6 3.0 %psum.21 = f32[]{:T(128)} all-reduce(f32[]{:T(128)S(6)} %div.40), channel_id=1, replica_groups=mesh['y'=8,'zl'=4,'c'=2,'zh'=2,'x'=4] {'c'}, use_global_device_ids=true, to_apply=%region_1.2 | all-reduce | flops 1 | bytes 8 | tf_op jit(solution)/shard_map/psum | solution.py:131
  144.6 12.8 %psum.22 = f32[]{:T(128)} all-reduce(f32[]{:T(128)} %psum.21), channel_id=1, replica_groups=mesh['y'=8,'zl'=4,'c'=2,'zh'=2,'x'=4] {'zl'}, use_global_device_ids=true, to_apply=%region_2.3 | all-reduce | flops 1 | bytes 8 | tf_op jit(solution)/shard_map/psum | solution.py:131
  157.4 17.6 %psum.23 = f32[]{:T(128)} all-reduce(f32[]{:T(128)} %psum.22), channel_id=1, replica_groups=mesh['y'=8,'zl'=4,'c'=2,'zh'=2,'x'=4] {'y'}, use_global_device_ids=true, to_apply=%region_3.4 | all-reduce | flops 1 | bytes 8 | tf_op jit(solution)/shard_map/psum | solution.py:131
  175.6 2.5 %collective-permute-start.8 = (f32[6,1536]{1,0:T(8,128)S(1)}, f32[6,1536]{1,0:T(8,128)S(1)}, u32[]{:S(2)}, u32[]{:S(2)}) collective-permute-start(f32[6,1536]{1,0:T(8,128)S(1)} %broadcast_multiply_fusion), channel_id=1, source_target_pairs={{0,1},{1,0},{2,3},{3,2},{4,5},{5,4},{6,7},{7,6},{8,9},{9,8},{10,11... | collective-permute-start | bytes 110600 | tf_op jit(solution)/shard_map/ppermute | solution.py:24
  178.1 4.0 %collective-permute-done.8 = f32[6,1536]{1,0:T(8,128)S(1)} collective-permute-done((f32[6,1536]{1,0:T(8,128)S(1)}, f32[6,1536]{1,0:T(8,128)S(1)}, u32[]{:S(2)}, u32[]{:S(2)}) %collective-permute-start.8) | collective-permute-done | bytes 36896 | tf_op jit(solution)/shard_map/ppermute | solution.py:24
  182.1 3.5 %collective-permute-start.9 = (f32[6,1536]{1,0:T(8,128)S(1)}, f32[6,1536]{1,0:T(8,128)S(1)}, u32[]{:S(2)}, u32[]{:S(2)}) collective-permute-start(f32[6,1536]{1,0:T(8,128)S(1)} %fusion.43), channel_id=1, source_target_pairs={{0,2},{1,3},{2,0},{3,1},{4,6},{5,7},{6,4},{7,5},{8,10},{9,11},{10,... | collective-permute-start | bytes 110600 | tf_op jit(solution)/shard_map/ppermute | solution.py:24
  185.6 3.9 %collective-permute-done.9 = f32[6,1536]{1,0:T(8,128)S(1)} collective-permute-done((f32[6,1536]{1,0:T(8,128)S(1)}, f32[6,1536]{1,0:T(8,128)S(1)}, u32[]{:S(2)}, u32[]{:S(2)}) %collective-permute-start.9) | collective-permute-done | bytes 36896 | tf_op jit(solution)/shard_map/ppermute | solution.py:24
  189.5 5.3 %collective-permute-start.10 = (f32[6,1536]{1,0:T(8,128)S(1)}, f32[6,1536]{1,0:T(8,128)S(1)}, u32[]{:S(2)}, u32[]{:S(2)}) collective-permute-start(f32[6,1536]{1,0:T(8,128)S(1)} %add.182), channel_id=1, source_target_pairs={{0,4},{4,0},{1,5},{5,1},{2,6},{6,2},{3,7},{7,3},{8,12},{12,8},{9,1... | collective-permute-start | bytes 110600 | tf_op jit(solution)/shard_map/ppermute | solution.py:24
  194.9 5.1 %collective-permute-done.10 = f32[6,1536]{1,0:T(8,128)S(1)} collective-permute-done((f32[6,1536]{1,0:T(8,128)S(1)}, f32[6,1536]{1,0:T(8,128)S(1)}, u32[]{:S(2)}, u32[]{:S(2)}) %collective-permute-start.10) | collective-permute-done | bytes 36896 | tf_op jit(solution)/shard_map/ppermute | solution.py:24
  (68 shorter events, 31.5 us)
Async XLA Ops:
  7.2 19.9 %copy-start.4 = (bf16[1,192,384]{2,1,0:T(8,128)(2,1)S(1)}, bf16[1,192,384]{2,1,0:T(8,128)(2,1)}, u32[]{:S(2)}) copy-start(bf16[1,192,384]{2,1,0:T(8,128)(2,1)} %param.8) | copy-start | bytes 442372
  7.2 84.7 %all-gather.4.cloned.1.call-start = ((), (), s32[]{:S(2)}) async-start(), calls=%async_computation | async-start | bytes 3317760 | tf_op jit(solution)/shard_map/all_gather | solution.py:80
  27.0 90.7 %all-gather.6.cloned.1.call-start = ((), (), s32[]{:S(2)}) async-start(), calls=%async_computation.1 | async-start | bytes 8847360 | tf_op jit(solution)/shard_map/all_gather | solution.py:85
  30.3 4.2 %collective-permute-start.2 = (bf16[2,2,2,2,2,1,6,1536]{7,4,6,5,3,2,1,0:T(2,128)(2,1)}, bf16[2,2,2,2,2,1,6,1536]{7,4,6,5,3,2,1,0:T(2,128)(2,1)}, u32[]{:S(2)}, u32[]{:S(2)}) collective-permute-start(bf16[2,2,2,2,2,1,6,1536]{7,4,6,5,3,2,1,0:T(2,128)(2,1)} %copy.42), channel_id=1, source_target_pairs={{0,8},{8,0},{1,9},{9,1},{2,10},{10,2},{3,11},{11,3},{4,12},{12,4},... | collective-permute-start | bytes 1769480 | tf_op jit(solution)/shard_map/ppermute | solution.py:24
  35.8 1.2 copy-start.2
  37.0 13.5 %collective-permute-start.3 = (bf16[2,2,2,2,1,1,6,1536]{7,6,5,4,3,2,1,0:T(8,128)(2,1)S(1)}, bf16[2,2,2,2,1,1,6,1536]{7,6,5,4,3,2,1,0:T(8,128)(2,1)S(1)}, u32[]{:S(2)}, u32[]{:S(2)}) collective-permute-start(bf16[2,2,2,2,1,1,6,1536]{7,6,5,4,3,2,1,0:T(8,128)(2,1)S(1)} %dynamic-slice_convert_fusion), channel_id=1, source_target_pairs={{0,16},{16,0},{32,48},{48,32},{1,17},{17,1},{33,49},{49,33},{2,18}... | collective-permute-start | bytes 884744 | tf_op jit(solution)/shard_map/ppermute | solution.py:24
  51.8 13.6 %collective-permute-start.4 = (bf16[2,2,2,1,1,1,6,1536]{7,6,5,4,3,2,1,0:T(8,128)(2,1)S(1)}, bf16[2,2,2,1,1,1,6,1536]{7,6,5,4,3,2,1,0:T(8,128)(2,1)S(1)}, u32[]{:S(2)}, u32[]{:S(2)}) collective-permute-start(bf16[2,2,2,1,1,1,6,1536]{7,6,5,4,3,2,1,0:T(8,128)(2,1)S(1)} %dynamic-slice_convert_fusion.1), channel_id=1, source_target_pairs={{0,32},{16,48},{32,0},{48,16},{1,33},{17,49},{33,1},{49,17},{2,34}... | collective-permute-start | bytes 442376 | tf_op jit(solution)/shard_map/ppermute | solution.py:24
  65.4 9.0 %collective-permute-start.5 = (bf16[2,2,1,1,1,1,6,1536]{7,6,5,4,3,2,1,0:T(8,128)(2,1)S(1)}, bf16[2,2,1,1,1,1,6,1536]{7,6,5,4,3,2,1,0:T(8,128)(2,1)S(1)}, u32[]{:S(2)}, u32[]{:S(2)}) collective-permute-start(bf16[2,2,1,1,1,1,6,1536]{7,6,5,4,3,2,1,0:T(8,128)(2,1)S(1)} %dynamic-slice_convert_fusion.2), channel_id=1, source_target_pairs={{0,64},{64,0},{128,192},{192,128},{256,320},{320,256},{384,448},{4... | collective-permute-start | bytes 221192 | tf_op jit(solution)/shard_map/ppermute | solution.py:24
  74.5 6.9 %collective-permute-start.6 = (bf16[2,1,1,1,1,1,6,1536]{7,6,5,4,3,2,1,0:T(8,128)(2,1)S(1)}, bf16[2,1,1,1,1,1,6,1536]{7,6,5,4,3,2,1,0:T(8,128)(2,1)S(1)}, u32[]{:S(2)}, u32[]{:S(2)}) collective-permute-start(bf16[2,1,1,1,1,1,6,1536]{7,6,5,4,3,2,1,0:T(8,128)(2,1)S(1)} %dynamic-slice_convert_fusion.3), channel_id=1, source_target_pairs={{0,128},{64,192},{128,0},{192,64},{256,384},{320,448},{384,256},{4... | collective-permute-start | bytes 110600 | tf_op jit(solution)/shard_map/ppermute | solution.py:24
  81.4 10.5 %copy-start = (bf16[1,192,1536]{2,1,0:T(8,128)(2,1)S(1)}, bf16[1,192,1536]{2,1,0:T(8,128)(2,1)}, u32[]{:S(2)}) copy-start(bf16[1,192,1536]{2,1,0:T(8,128)(2,1)} %param.9) | copy-start | bytes 1769476
  81.4 10.5 %copy-start.1 = (bf16[1,192,1536]{2,1,0:T(8,128)(2,1)S(1)}, bf16[1,192,1536]{2,1,0:T(8,128)(2,1)}, u32[]{:S(2)}) copy-start(bf16[1,192,1536]{2,1,0:T(8,128)(2,1)} %param.7) | copy-start | bytes 1769476
  81.4 9.8 %collective-permute-start.7 = (bf16[1,1,1,1,1,1,6,1536]{7,6,5,4,3,2,1,0:T(8,128)(2,1)S(1)}, bf16[1,1,1,1,1,1,6,1536]{7,6,5,4,3,2,1,0:T(8,128)(2,1)S(1)}, u32[]{:S(2)}, u32[]{:S(2)}) collective-permute-start(bf16[1,1,1,1,1,1,6,1536]{7,6,5,4,3,2,1,0:T(8,128)(2,1)S(1)} %dynamic-slice_convert_fusion.4), channel_id=1, source_target_pairs={{0,256},{64,320},{128,384},{192,448},{256,0},{320,64},{384,128},{4... | collective-permute-start | bytes 55304 | tf_op jit(solution)/shard_map/ppermute | solution.py:24
  92.0 4.4 %collective-permute-start.1 = (bf16[32,3456]{1,0:T(8,128)(2,1)S(1)}, bf16[32,3456]{1,0:T(8,128)(2,1)S(1)}, u32[]{:S(2)}, u32[]{:S(2)}) collective-permute-start(bf16[32,3456]{1,0:T(8,128)(2,1)S(1)} %get-tuple-element.11), channel_id=1, source_target_pairs={{8,0},{16,8},{24,16},{32,24},{40,32},{48,40},{56,48},{64,56},{72,6... | collective-permute-start | bytes 663560 | tf_op jit(solution)/shard_map/ppermute | solution.py:95
  93.3 4.1 %collective-permute-start = (bf16[32,3456]{1,0:T(8,128)(2,1)S(1)}, bf16[32,3456]{1,0:T(8,128)(2,1)S(1)}, u32[]{:S(2)}, u32[]{:S(2)}) collective-permute-start(bf16[32,3456]{1,0:T(8,128)(2,1)S(1)} %get-tuple-element.10), channel_id=1, source_target_pairs={{0,8},{8,16},{16,24},{24,32},{32,40},{40,48},{48,56},{56,64},{64,7... | collective-permute-start | bytes 663560 | tf_op jit(solution)/shard_map/ppermute | solution.py:94
  96.3 2.1 %copy-start.8 = (bf16[32,3456]{1,0:T(8,128)(2,1)}, bf16[32,3456]{1,0:T(8,128)(2,1)S(1)}, u32[]{:S(2)}) copy-start(bf16[32,3456]{1,0:T(8,128)(2,1)S(1)} %collective-permute-done.1) | copy-start | bytes 663556
  117.7 2.0 slice-start
  125.8 1.2 copy-start.5
  125.8 1.6 copy-start.6
  125.8 3.7 %copy-start.3 = (bf16[384,4608]{0,1:T(8,128)(2,1)S(1)}, bf16[384,4608]{0,1:T(8,128)(2,1)}, u32[]{:S(2)}) copy-start(bf16[384,4608]{0,1:T(8,128)(2,1)} %copy.31) | copy-start | bytes 10616836
  127.4 2.9 %copy-start.7 = (bf16[2,256,1536]{2,1,0:T(8,128)(2,1)}, bf16[2,256,1536]{2,1,0:T(8,128)(2,1)S(1)}, u32[]{:S(2)}) copy-start(bf16[2,256,1536]{2,1,0:T(8,128)(2,1)S(1)} %fusion.7) | copy-start | bytes 4718596
  137.4 38.2 %copy-start.10 = (f32[6,1536]{1,0:T(8,128)S(1)}, f32[6,1536]{1,0:T(8,128)}, u32[]{:S(2)}) copy-start(f32[6,1536]{1,0:T(8,128)} %add_bitcast_fusion.1) | copy-start | bytes 110596
  175.6 6.4 %collective-permute-start.8 = (f32[6,1536]{1,0:T(8,128)S(1)}, f32[6,1536]{1,0:T(8,128)S(1)}, u32[]{:S(2)}, u32[]{:S(2)}) collective-permute-start(f32[6,1536]{1,0:T(8,128)S(1)} %broadcast_multiply_fusion), channel_id=1, source_target_pairs={{0,1},{1,0},{2,3},{3,2},{4,5},{5,4},{6,7},{7,6},{8,9},{9,8},{10,11... | collective-permute-start | bytes 110600 | tf_op jit(solution)/shard_map/ppermute | solution.py:24
  182.1 7.5 %collective-permute-start.9 = (f32[6,1536]{1,0:T(8,128)S(1)}, f32[6,1536]{1,0:T(8,128)S(1)}, u32[]{:S(2)}, u32[]{:S(2)}) collective-permute-start(f32[6,1536]{1,0:T(8,128)S(1)} %fusion.43), channel_id=1, source_target_pairs={{0,2},{1,3},{2,0},{3,1},{4,6},{5,7},{6,4},{7,5},{8,10},{9,11},{10,... | collective-permute-start | bytes 110600 | tf_op jit(solution)/shard_map/ppermute | solution.py:24
  189.5 10.4 %collective-permute-start.10 = (f32[6,1536]{1,0:T(8,128)S(1)}, f32[6,1536]{1,0:T(8,128)S(1)}, u32[]{:S(2)}, u32[]{:S(2)}) collective-permute-start(f32[6,1536]{1,0:T(8,128)S(1)} %add.182), channel_id=1, source_target_pairs={{0,4},{4,0},{1,5},{5,1},{2,6},{6,2},{3,7},{7,3},{8,12},{12,8},{9,1... | collective-permute-start | bytes 110600 | tf_op jit(solution)/shard_map/ppermute | solution.py:24
  (1 other events, 1.0 us)
Sparse Core Ops, SparseCore 0:
  27.1 50.4 all-gather.3
  92.0 25.6 all-gather.5

commit v9 on v8

--- a/solution.py
+++ b/solution.py
@@ -42,15 +42,14 @@
     return held.reshape((-1,) + piece.shape[1:])
 
 
-def _scatter_rows(full, order, shard):
-    held = full.reshape((2,) * len(DIGITS) + (shard,) + full.shape[1:])
+def _halve(held, order):
     for axis, d in order:
         dim = DIGITS.index((axis, d))
         mine = _bit(axis, d)
         keep = lax.dynamic_index_in_dim(held, mine, axis=dim, keepdims=True)
         give = lax.dynamic_index_in_dim(held, 1 - mine, axis=dim, keepdims=True)
-        held = keep + _swap(give.astype(jnp.bfloat16), axis, d).astype(full.dtype)
-    return held.reshape((shard,) + full.shape[1:])
+        held = keep + _swap(give.astype(jnp.bfloat16), axis, d).astype(held.dtype)
+    return held
 
 
 def _sum_all(x, steps):
@@ -78,14 +77,6 @@
     packed = jnp.concatenate([entry_weight, conv_rows, exit_weight], axis=1)
     for axis in ("zl", "y"):
         packed = lax.all_gather(packed, axis, axis=0, tiled=True)
-    summed = _scatter_rows(
-        summed, (("c", 1), ("zl", 1), ("zl", 2), ("y", 1), ("y", 2), ("y", 4)), shard
-    )
-    packed, summed = lax.optimization_barrier((packed, summed))
-    packed = lax.all_gather(packed, "c", axis=0, tiled=True)
-    w_entry = packed[:, :chans]
-    w_conv = packed[:, chans : 4 * chans].reshape(bot, 3, chans)
-    w_exit = packed[:, 4 * chans :]
 
     spacing = DILATION
     edge_in = jnp.concatenate([feats, bottle, jitter], axis=1)
@@ -93,6 +84,20 @@
     pairs_down = [(i + 1, i) for i in range(n_ctx - 1)]
     from_prev = lax.ppermute(edge_in[rows - spacing :], CTX, pairs_up)
     from_next = lax.ppermute(edge_in[:spacing], CTX, pairs_down)
+
+    summed = summed.reshape((2,) * len(DIGITS) + (shard, chans))
+    summed = _halve(summed, (("c", 1), ("zl", 1), ("zl", 2)))
+    packed, summed, from_prev, from_next = lax.optimization_barrier(
+        (packed, summed, from_prev, from_next)
+    )
+    packed = lax.all_gather(packed, "c", axis=0, tiled=True)
+    summed = _halve(summed, (("y", 1), ("y", 2), ("y", 4)))
+    packed, summed = lax.optimization_barrier((packed, summed))
+    summed = summed.reshape(shard, chans)
+    w_entry = packed[:, :chans]
+    w_conv = packed[:, chans : 4 * chans].reshape(bot, 3, chans)
+    w_exit = packed[:, 4 * chans :]
+
     ext = jnp.concatenate([from_prev, edge_in, from_next], axis=0)
     ext_feats = ext[:, :chans]
     ext_bottle = (

time: 208 us -> 194 us (0.933)
  waiting for transfers between devices: 62.4 us -> 54.3 us
  starting transfers between devices: 42 us -> 34.9 us
    all_gather x1, waiting for transfers between devices: 17.9 us -> 0.53 us  [body(): packed = lax.all_gather(packed, 'c', axis=0, tiled=True)]
    all_gather x1, waiting for transfers between devices: 0.01 us -> 11.9 us  [body(): packed = lax.all_gather(packed, axis, axis=0, tiled=True)]
    ppermute x9, starting transfers between devices: 37.6 us -> 32.1 us  [_swap(): return lax.ppermute(x, axis, [(i, i ^ d) for i in range(n)])]
  transfers between devices with their start and end apart: 13 -> 13, of which waited for: 11 -> 11; matrix products, arithmetic and copies ran while one was open for 4% -> 5% of each run, Pallas kernels for 0% -> 0%
where the time goes in v9:
time: 194 us; the launch traced here: 193 us
  waiting for transfers between devices  54.3 us (28%)
  blocking collectives  51.3 us (26%)
  starting transfers between devices  34.9 us (18%)
  between operations  15.9 us (8%)
  local copies, waits for them, and re-layouts  13.1 us (7%)
  matrix products  11.9 us (6%)
  other arithmetic  11.7 us (6%)
    ppermute x9, waiting for transfers between devices, _swap(): return lax.ppermute(x, axis, [(i, i ^ d) for i in range(n)])  41.9 us
    psum x3, blocking collectives, body(): gap = lax.psum(gap, axis)  33.4 us
    ppermute x9, starting transfers between devices, _swap(): return lax.ppermute(x, axis, [(i, i ^ d) for i in range(n)])  32.1 us
    all_gather x1, blocking collectives, body(): packed = lax.all_gather(packed, axis, axis=0, tiled=True)  17.9 us
    all_gather x1, waiting for transfers between devices, body(): packed = lax.all_gather(packed, axis, axis=0, tiled=True)  11.9 us
    unnamed x24, local copies, waits for them, and re-layouts  6.06 us
    slice x3, local copies, waits for them, and re-layouts, body(): w_conv = packed[:, chans:4 * chans].reshape(bot, 3, chans)  5.63 us
    dot_general x1, matrix products, body(): jnp.dot(inner, w_exit, preferred_element_type=jnp.float32)  5.49 us
  transfers between devices with their start and end apart: 13, of which 11 were waited for; matrix products, arithmetic and copies ran while one was open for 5% of the time, Pallas kernels for 0%

profile of v9, /device:TPU:2, one launch (start us, length us, event | category | flops | bytes accessed | tf_op | source)
XLA Modules:
  0.0 193.2 jit_solution(8328863281527535028)
XLA Ops:
  8.2 17.9 %all-gather = bf16[4,6,7680]{2,1,0:T(8,128)(2,1)S(1)} all-gather(bf16[1,6,7680]{2,1,0:T(8,128)(2,1)S(1)} %maximum_bitcast_fusion), channel_id=1, replica_groups=mesh['y'=8,'zl'=4,'c'=2,'zh'=2,'x'=4] {'zl'}, dimensions={0}, use_global_device_ids=true | all-gather | bytes 460800 | tf_op jit(solution)/shard_map/all_gather | solution.py:79
  37.0 4.2 %collective-permute-start.1 = (bf16[2,2,2,2,1,1,6,1536]{7,6,5,4,3,2,1,0:T(8,128)(2,1)S(1)}, bf16[2,2,2,2,1,1,6,1536]{7,6,5,4,3,2,1,0:T(8,128)(2,1)S(1)}, u32[]{:S(2)}, u32[]{:S(2)}) collective-permute-start(bf16[2,2,2,2,1,1,6,1536]{7,6,5,4,3,2,1,0:T(8,128)(2,1)S(1)} %dynamic-slice_convert_fusion), channel_id=1, source_target_pairs={{0,16},{16,0},{32,48},{48,32},{1,17},{17,1},{33,49},{49,33},{2,18}... | collective-permute-start | bytes 884744 | tf_op jit(solution)/shard_map/ppermute | solution.py:24
  41.2 9.4 %collective-permute-done.1 = bf16[2,2,2,2,1,1,6,1536]{7,6,5,4,3,2,1,0:T(8,128)(2,1)S(1)} collective-permute-done((bf16[2,2,2,2,1,1,6,1536]{7,6,5,4,3,2,1,0:T(8,128)(2,1)S(1)}, bf16[2,2,2,2,1,1,6,1536]{7,6,5,4,3,2,1,0:T(8,128)(2,1)S(1)}, u32[]{:S(2)}, u32[]{:S(2)}) %collective-permute-start.1) | collective-permute-done | bytes 294944 | tf_op jit(solution)/shard_map/ppermute | solution.py:24
  51.9 4.4 %collective-permute-start.2 = (bf16[2,2,2,1,1,1,6,1536]{7,6,5,4,3,2,1,0:T(8,128)(2,1)S(1)}, bf16[2,2,2,1,1,1,6,1536]{7,6,5,4,3,2,1,0:T(8,128)(2,1)}, u32[]{:S(2)}, u32[]{:S(2)}) collective-permute-start(bf16[2,2,2,1,1,1,6,1536]{7,6,5,4,3,2,1,0:T(8,128)(2,1)S(1)} %dynamic-slice_convert_fusion.1), channel_id=1, source_target_pairs={{0,32},{16,48},{32,0},{48,16},{1,33},{17,49},{33,1},{49,17},{2,34}... | collective-permute-start | bytes 442376 | tf_op jit(solution)/shard_map/ppermute | solution.py:24
  59.1 6.5 %collective-permute-done.2 = bf16[2,2,2,1,1,1,6,1536]{7,6,5,4,3,2,1,0:T(8,128)(2,1)} collective-permute-done((bf16[2,2,2,1,1,1,6,1536]{7,6,5,4,3,2,1,0:T(8,128)(2,1)S(1)}, bf16[2,2,2,1,1,1,6,1536]{7,6,5,4,3,2,1,0:T(8,128)(2,1)}, u32[]{:S(2)}, u32[]{:S(2)}) %collective-permute-start.2) | collective-permute-done | bytes 147488 | tf_op jit(solution)/shard_map/ppermute | solution.py:24
  66.6 11.9 %all-gather.4.cloned.1.call-done = bf16[192,7680]{1,0:T(8,128)(2,1)} async-done(((bf16[24,7680]{1,0:T(8,128)(2,1)}), bf16[192,7680]{1,0:T(8,128)(2,1)}) %all-gather.4.cloned.1.call-update) | async-done | bytes 2949136 | tf_op jit(solution)/shard_map/all_gather | solution.py:79
  78.5 2.7 %collective-permute-start.5 = (bf16[2,2,1,1,1,1,6,1536]{7,6,5,4,3,2,1,0:T(8,128)(2,1)S(1)}, bf16[2,2,1,1,1,1,6,1536]{7,6,5,4,3,2,1,0:T(8,128)(2,1)S(1)}, u32[]{:S(2)}, u32[]{:S(2)}) collective-permute-start(bf16[2,2,1,1,1,1,6,1536]{7,6,5,4,3,2,1,0:T(8,128)(2,1)S(1)} %dynamic-slice_convert_fusion.2), channel_id=1, source_target_pairs={{0,64},{64,0},{128,192},{192,128},{256,320},{320,256},{384,448},{4... | collective-permute-start | bytes 221192 | tf_op jit(solution)/shard_map/ppermute | solution.py:24
  81.4 3.7 %collective-permute-done.5 = bf16[2,2,1,1,1,1,6,1536]{7,6,5,4,3,2,1,0:T(8,128)(2,1)S(1)} collective-permute-done((bf16[2,2,1,1,1,1,6,1536]{7,6,5,4,3,2,1,0:T(8,128)(2,1)S(1)}, bf16[2,2,1,1,1,1,6,1536]{7,6,5,4,3,2,1,0:T(8,128)(2,1)S(1)}, u32[]{:S(2)}, u32[]{:S(2)}) %collective-permute-start.5) | collective-permute-done | bytes 73760 | tf_op jit(solution)/shard_map/ppermute | solution.py:24
  85.1 3.6 %collective-permute-start.6 = (bf16[2,1,1,1,1,1,6,1536]{7,6,5,4,3,2,1,0:T(8,128)(2,1)S(1)}, bf16[2,1,1,1,1,1,6,1536]{7,6,5,4,3,2,1,0:T(8,128)(2,1)S(1)}, u32[]{:S(2)}, u32[]{:S(2)}) collective-permute-start(bf16[2,1,1,1,1,1,6,1536]{7,6,5,4,3,2,1,0:T(8,128)(2,1)S(1)} %dynamic-slice_convert_fusion.3), channel_id=1, source_target_pairs={{0,128},{64,192},{128,0},{192,64},{256,384},{320,448},{384,256},{4... | collective-permute-start | bytes 110600 | tf_op jit(solution)/shard_map/ppermute | solution.py:24
  90.0 2.5 %collective-permute-done.6 = bf16[2,1,1,1,1,1,6,1536]{7,6,5,4,3,2,1,0:T(8,128)(2,1)S(1)} collective-permute-done((bf16[2,1,1,1,1,1,6,1536]{7,6,5,4,3,2,1,0:T(8,128)(2,1)S(1)}, bf16[2,1,1,1,1,1,6,1536]{7,6,5,4,3,2,1,0:T(8,128)(2,1)S(1)}, u32[]{:S(2)}, u32[]{:S(2)}) %collective-permute-start.6) | collective-permute-done | bytes 36896 | tf_op jit(solution)/shard_map/ppermute | solution.py:24
  92.5 4.0 %collective-permute-start.7 = (bf16[1,1,1,1,1,1,6,1536]{7,6,5,4,3,2,1,0:T(8,128)(2,1)S(1)}, bf16[1,1,1,1,1,1,6,1536]{7,6,5,4,3,2,1,0:T(8,128)(2,1)S(1)}, u32[]{:S(2)}, u32[]{:S(2)}) collective-permute-start(bf16[1,1,1,1,1,1,6,1536]{7,6,5,4,3,2,1,0:T(8,128)(2,1)S(1)} %dynamic-slice_convert_fusion.4), channel_id=1, source_target_pairs={{0,256},{64,320},{128,384},{192,448},{256,0},{320,64},{384,128},{4... | collective-permute-start | bytes 55304 | tf_op jit(solution)/shard_map/ppermute | solution.py:24
  97.6 4.6 %collective-permute-done.7 = bf16[1,1,1,1,1,1,6,1536]{7,6,5,4,3,2,1,0:T(8,128)(2,1)S(1)} collective-permute-done((bf16[1,1,1,1,1,1,6,1536]{7,6,5,4,3,2,1,0:T(8,128)(2,1)S(1)}, bf16[1,1,1,1,1,1,6,1536]{7,6,5,4,3,2,1,0:T(8,128)(2,1)S(1)}, u32[]{:S(2)}, u32[]{:S(2)}) %collective-permute-start.7) | collective-permute-done | bytes 18464 | tf_op jit(solution)/shard_map/ppermute | solution.py:24
  105.3 3.6 %copy.31 = bf16[384,4608]{0,1:T(8,128)(2,1)} copy(bf16[384,4608]{1,0:T(8,128)(2,1)S(1)} %slice-done) | data formatting | bytes 7077888 | tf_op jit(solution)/shard_map/slice | solution.py:98
  109.0 2.5 %subtract_bitcast_fusion = (f32[1,256,1536]{2,1,0:T(8,128)S(1)}, f32[1,256,1536]{2,1,0:T(8,128)S(1)}) fusion(bf16[32,3456]{1,0:T(8,128)(2,1)} %copy-done.9, bf16[192,1536]{1,0:T(8,128)(2,1)} %bitcast.56, bf16[192,384]{1,0:T(8,128)(2,1)} %bitcast.67, bf16[192,1536]{1,0:T(8,128)(2,1)} %bitcast.60, bf16[32,3456]{1,0:T(8,128)(2,1)} %copy-done.8, ...), kind=kOutput, calls=%fused_computation.16 | convolution fusion | flops 307888128 | bytes 7077888 | tf_op jit(solution)/shard_map/dot_general | solution.py:111
  117.6 5.5 %convolution_add_fusion = f32[2,192,1536]{2,1,0:T(8,128)} fusion(f32[1,256,1536]{2,1,0:T(8,128)} %copy-done.6, f32[1,256,1536]{2,1,0:T(8,128)} %copy-done.5, bf16[384,7680]{1,0:T(8,128)(2,1)} %all-gather.6.cloned.1.call-done, f32[2,192,384]{2,1,0:T(8,128)} %convolution_add_fusion.3, bf16[384,3,1536]{0,2,1:T(8,128)(2,1)S(1)} %bitcast.66, ...), kind=kOutput, calls=%fused_computation.12 | convolution fusion | flops 908623872 | bytes 9633792 | tf_op jit(solution)/shard_map/dot_general | solution.py:127
  123.1 3.6 %multiply_reduce_fusion = (f32[]{:T(128)}, bf16[1,192,1536]{2,1,0:T(8,128)(2,1)}) fusion(bf16[1,192,1536]{2,1,0:T(8,128)(2,1)} %param.10, f32[2,192,1536]{2,1,0:T(8,128)} %convolution_add_fusion), kind=kLoop, calls=%fused_computation.31 | loop fusion | flops 2654207 | bytes 3538948 | tf_op jit(solution)/shard_map/reduce_sum | solution.py:133
  127.3 3.0 %psum.21 = f32[]{:T(128)} all-reduce(f32[]{:T(128)S(6)} %div.40), channel_id=1, replica_groups=mesh['y'=8,'zl'=4,'c'=2,'zh'=2,'x'=4] {'c'}, use_global_device_ids=true, to_apply=%region_1.2 | all-reduce | flops 1 | bytes 8 | tf_op jit(solution)/shard_map/psum | solution.py:136
  130.3 12.8 %psum.22 = f32[]{:T(128)} all-reduce(f32[]{:T(128)} %psum.21), channel_id=1, replica_groups=mesh['y'=8,'zl'=4,'c'=2,'zh'=2,'x'=4] {'zl'}, use_global_device_ids=true, to_apply=%region_2.3 | all-reduce | flops 1 | bytes 8 | tf_op jit(solution)/shard_map/psum | solution.py:136
  143.1 17.6 %psum.23 = f32[]{:T(128)} all-reduce(f32[]{:T(128)} %psum.22), channel_id=1, replica_groups=mesh['y'=8,'zl'=4,'c'=2,'zh'=2,'x'=4] {'y'}, use_global_device_ids=true, to_apply=%region_3.4 | all-reduce | flops 1 | bytes 8 | tf_op jit(solution)/shard_map/psum | solution.py:136
  163.8 4.0 %collective-permute-done.8 = f32[6,1536]{1,0:T(8,128)S(1)} collective-permute-done((f32[6,1536]{1,0:T(8,128)S(1)}, f32[6,1536]{1,0:T(8,128)S(1)}, u32[]{:S(2)}, u32[]{:S(2)}) %collective-permute-start.8) | collective-permute-done | bytes 36896 | tf_op jit(solution)/shard_map/ppermute | solution.py:24
  167.8 3.5 %collective-permute-start.9 = (f32[6,1536]{1,0:T(8,128)S(1)}, f32[6,1536]{1,0:T(8,128)S(1)}, u32[]{:S(2)}, u32[]{:S(2)}) collective-permute-start(f32[6,1536]{1,0:T(8,128)S(1)} %fusion.44), channel_id=1, source_target_pairs={{0,2},{1,3},{2,0},{3,1},{4,6},{5,7},{6,4},{7,5},{8,10},{9,11},{10,... | collective-permute-start | bytes 110600 | tf_op jit(solution)/shard_map/ppermute | solution.py:24
  171.4 3.9 %collective-permute-done.9 = f32[6,1536]{1,0:T(8,128)S(1)} collective-permute-done((f32[6,1536]{1,0:T(8,128)S(1)}, f32[6,1536]{1,0:T(8,128)S(1)}, u32[]{:S(2)}, u32[]{:S(2)}) %collective-permute-start.9) | collective-permute-done | bytes 36896 | tf_op jit(solution)/shard_map/ppermute | solution.py:24
  175.3 5.3 %collective-permute-start.10 = (f32[6,1536]{1,0:T(8,128)S(1)}, f32[6,1536]{1,0:T(8,128)S(1)}, u32[]{:S(2)}, u32[]{:S(2)}) collective-permute-start(f32[6,1536]{1,0:T(8,128)S(1)} %add.182), channel_id=1, source_target_pairs={{0,4},{4,0},{1,5},{5,1},{2,6},{6,2},{3,7},{7,3},{8,12},{12,8},{9,1... | collective-permute-start | bytes 110600 | tf_op jit(solution)/shard_map/ppermute | solution.py:24
  180.6 5.1 %collective-permute-done.10 = f32[6,1536]{1,0:T(8,128)S(1)} collective-permute-done((f32[6,1536]{1,0:T(8,128)S(1)}, f32[6,1536]{1,0:T(8,128)S(1)}, u32[]{:S(2)}, u32[]{:S(2)}) %collective-permute-start.10) | collective-permute-done | bytes 36896 | tf_op jit(solution)/shard_map/ppermute | solution.py:24
  (68 shorter events, 31.5 us)
Async XLA Ops:
  7.2 19.9 %copy-start.4 = (bf16[1,192,384]{2,1,0:T(8,128)(2,1)S(1)}, bf16[1,192,384]{2,1,0:T(8,128)(2,1)}, u32[]{:S(2)}) copy-start(bf16[1,192,384]{2,1,0:T(8,128)(2,1)} %param.8) | copy-start | bytes 442372
  7.2 71.3 %all-gather.4.cloned.1.call-start = ((), (), s32[]{:S(2)}) async-start(), calls=%async_computation | async-start | bytes 3317760 | tf_op jit(solution)/shard_map/all_gather | solution.py:79
  27.0 76.3 %all-gather.6.cloned.1.call-start = ((), (), s32[]{:S(2)}) async-start(), calls=%async_computation.1 | async-start | bytes 8847360 | tf_op jit(solution)/shard_map/all_gather | solution.py:93
  30.3 4.2 %collective-permute-start = (bf16[2,2,2,2,2,1,6,1536]{7,4,6,5,3,2,1,0:T(2,128)(2,1)}, bf16[2,2,2,2,2,1,6,1536]{7,4,6,5,3,2,1,0:T(2,128)(2,1)}, u32[]{:S(2)}, u32[]{:S(2)}) collective-permute-start(bf16[2,2,2,2,2,1,6,1536]{7,4,6,5,3,2,1,0:T(2,128)(2,1)} %copy.42), channel_id=1, source_target_pairs={{0,8},{8,0},{1,9},{9,1},{2,10},{10,2},{3,11},{11,3},{4,12},{12,4},... | collective-permute-start | bytes 1769480 | tf_op jit(solution)/shard_map/ppermute | solution.py:24
  35.8 1.2 copy-start.2
  36.9 19.4 %copy-start = (bf16[1,192,1536]{2,1,0:T(8,128)(2,1)S(1)}, bf16[1,192,1536]{2,1,0:T(8,128)(2,1)}, u32[]{:S(2)}) copy-start(bf16[1,192,1536]{2,1,0:T(8,128)(2,1)} %param.9) | copy-start | bytes 1769476
  36.9 19.4 %copy-start.1 = (bf16[1,192,1536]{2,1,0:T(8,128)(2,1)S(1)}, bf16[1,192,1536]{2,1,0:T(8,128)(2,1)}, u32[]{:S(2)}) copy-start(bf16[1,192,1536]{2,1,0:T(8,128)(2,1)} %param.7) | copy-start | bytes 1769476
  37.0 13.6 %collective-permute-start.1 = (bf16[2,2,2,2,1,1,6,1536]{7,6,5,4,3,2,1,0:T(8,128)(2,1)S(1)}, bf16[2,2,2,2,1,1,6,1536]{7,6,5,4,3,2,1,0:T(8,128)(2,1)S(1)}, u32[]{:S(2)}, u32[]{:S(2)}) collective-permute-start(bf16[2,2,2,2,1,1,6,1536]{7,6,5,4,3,2,1,0:T(8,128)(2,1)S(1)} %dynamic-slice_convert_fusion), channel_id=1, source_target_pairs={{0,16},{16,0},{32,48},{48,32},{1,17},{17,1},{33,49},{49,33},{2,18}... | collective-permute-start | bytes 884744 | tf_op jit(solution)/shard_map/ppermute | solution.py:24
  51.9 13.7 %collective-permute-start.2 = (bf16[2,2,2,1,1,1,6,1536]{7,6,5,4,3,2,1,0:T(8,128)(2,1)S(1)}, bf16[2,2,2,1,1,1,6,1536]{7,6,5,4,3,2,1,0:T(8,128)(2,1)}, u32[]{:S(2)}, u32[]{:S(2)}) collective-permute-start(bf16[2,2,2,1,1,1,6,1536]{7,6,5,4,3,2,1,0:T(8,128)(2,1)S(1)} %dynamic-slice_convert_fusion.1), channel_id=1, source_target_pairs={{0,32},{16,48},{32,0},{48,16},{1,33},{17,49},{33,1},{49,17},{2,34}... | collective-permute-start | bytes 442376 | tf_op jit(solution)/shard_map/ppermute | solution.py:24
  56.4 10.2 %collective-permute-start.3 = (bf16[32,3456]{1,0:T(8,128)(2,1)S(1)}, bf16[32,3456]{1,0:T(8,128)(2,1)S(1)}, u32[]{:S(2)}, u32[]{:S(2)}) collective-permute-start(bf16[32,3456]{1,0:T(8,128)(2,1)S(1)} %get-tuple-element.19), channel_id=1, source_target_pairs={{0,8},{8,16},{16,24},{24,32},{32,40},{40,48},{48,56},{56,64},{64,7... | collective-permute-start | bytes 663560 | tf_op jit(solution)/shard_map/ppermute | solution.py:85
  57.8 8.8 %collective-permute-start.4 = (bf16[32,3456]{1,0:T(8,128)(2,1)S(1)}, bf16[32,3456]{1,0:T(8,128)(2,1)S(1)}, u32[]{:S(2)}, u32[]{:S(2)}) collective-permute-start(bf16[32,3456]{1,0:T(8,128)(2,1)S(1)} %get-tuple-element.18), channel_id=1, source_target_pairs={{8,0},{16,8},{24,16},{32,24},{40,32},{48,40},{56,48},{64,56},{72,6... | collective-permute-start | bytes 663560 | tf_op jit(solution)/shard_map/ppermute | solution.py:86
  66.6 30.0 %copy-start.8 = (bf16[32,3456]{1,0:T(8,128)(2,1)}, bf16[32,3456]{1,0:T(8,128)(2,1)S(1)}, u32[]{:S(2)}) copy-start(bf16[32,3456]{1,0:T(8,128)(2,1)S(1)} %collective-permute-done.3) | copy-start | bytes 663556
  66.6 29.9 %copy-start.9 = (bf16[32,3456]{1,0:T(8,128)(2,1)}, bf16[32,3456]{1,0:T(8,128)(2,1)S(1)}, u32[]{:S(2)}) copy-start(bf16[32,3456]{1,0:T(8,128)(2,1)S(1)} %collective-permute-done.4) | copy-start | bytes 663556
  78.5 6.5 %collective-permute-start.5 = (bf16[2,2,1,1,1,1,6,1536]{7,6,5,4,3,2,1,0:T(8,128)(2,1)S(1)}, bf16[2,2,1,1,1,1,6,1536]{7,6,5,4,3,2,1,0:T(8,128)(2,1)S(1)}, u32[]{:S(2)}, u32[]{:S(2)}) collective-permute-start(bf16[2,2,1,1,1,1,6,1536]{7,6,5,4,3,2,1,0:T(8,128)(2,1)S(1)} %dynamic-slice_convert_fusion.2), channel_id=1, source_target_pairs={{0,64},{64,0},{128,192},{192,128},{256,320},{320,256},{384,448},{4... | collective-permute-start | bytes 221192 | tf_op jit(solution)/shard_map/ppermute | solution.py:24
  85.1 7.4 %collective-permute-start.6 = (bf16[2,1,1,1,1,1,6,1536]{7,6,5,4,3,2,1,0:T(8,128)(2,1)S(1)}, bf16[2,1,1,1,1,1,6,1536]{7,6,5,4,3,2,1,0:T(8,128)(2,1)S(1)}, u32[]{:S(2)}, u32[]{:S(2)}) collective-permute-start(bf16[2,1,1,1,1,1,6,1536]{7,6,5,4,3,2,1,0:T(8,128)(2,1)S(1)} %dynamic-slice_convert_fusion.3), channel_id=1, source_target_pairs={{0,128},{64,192},{128,0},{192,64},{256,384},{320,448},{384,256},{4... | collective-permute-start | bytes 110600 | tf_op jit(solution)/shard_map/ppermute | solution.py:24
  92.5 9.6 %collective-permute-start.7 = (bf16[1,1,1,1,1,1,6,1536]{7,6,5,4,3,2,1,0:T(8,128)(2,1)S(1)}, bf16[1,1,1,1,1,1,6,1536]{7,6,5,4,3,2,1,0:T(8,128)(2,1)S(1)}, u32[]{:S(2)}, u32[]{:S(2)}) collective-permute-start(bf16[1,1,1,1,1,1,6,1536]{7,6,5,4,3,2,1,0:T(8,128)(2,1)S(1)} %dynamic-slice_convert_fusion.4), channel_id=1, source_target_pairs={{0,256},{64,320},{128,384},{192,448},{256,0},{320,64},{384,128},{4... | collective-permute-start | bytes 55304 | tf_op jit(solution)/shard_map/ppermute | solution.py:24
  103.3 2.0 %slice-start = ((bf16[384,7680]{1,0:T(8,128)(2,1)}), bf16[384,4608]{1,0:T(8,128)(2,1)S(1)}, s32[]{:S(2)}) async-start(bf16[384,7680]{1,0:T(8,128)(2,1)} %all-gather.6.cloned.1.call-done), calls=%async_computation.2 | async-start | bytes 7077888 | tf_op jit(solution)/shard_map/slice | solution.py:98
  111.5 1.6 copy-start.6
  111.5 3.7 %copy-start.3 = (bf16[384,4608]{0,1:T(8,128)(2,1)S(1)}, bf16[384,4608]{0,1:T(8,128)(2,1)}, u32[]{:S(2)}) copy-start(bf16[384,4608]{0,1:T(8,128)(2,1)} %copy.31) | copy-start | bytes 10616836
  113.2 2.9 %copy-start.7 = (bf16[2,256,1536]{2,1,0:T(8,128)(2,1)}, bf16[2,256,1536]{2,1,0:T(8,128)(2,1)S(1)}, u32[]{:S(2)}) copy-start(bf16[2,256,1536]{2,1,0:T(8,128)(2,1)S(1)} %fusion.7) | copy-start | bytes 4718596
  123.1 38.2 %copy-start.10 = (f32[1,1,1,1,1,1,6,1536]{7,6,5,4,3,2,1,0:T(8,128)S(1)}, f32[1,1,1,1,1,1,6,1536]{7,6,5,4,3,2,1,0:T(8,128)}, u32[]{:S(2)}) copy-start(f32[1,1,1,1,1,1,6,1536]{7,6,5,4,3,2,1,0:T(8,128)} %convert_add_fusion.5) | copy-start | bytes 110596
  161.4 6.4 %collective-permute-start.8 = (f32[6,1536]{1,0:T(8,128)S(1)}, f32[6,1536]{1,0:T(8,128)S(1)}, u32[]{:S(2)}, u32[]{:S(2)}) collective-permute-start(f32[6,1536]{1,0:T(8,128)S(1)} %multiply_bitcast_fusion), channel_id=1, source_target_pairs={{0,1},{1,0},{2,3},{3,2},{4,5},{5,4},{6,7},{7,6},{8,9},{9,8},{10,11... | collective-permute-start | bytes 110600 | tf_op jit(solution)/shard_map/ppermute | solution.py:24
  167.8 7.5 %collective-permute-start.9 = (f32[6,1536]{1,0:T(8,128)S(1)}, f32[6,1536]{1,0:T(8,128)S(1)}, u32[]{:S(2)}, u32[]{:S(2)}) collective-permute-start(f32[6,1536]{1,0:T(8,128)S(1)} %fusion.44), channel_id=1, source_target_pairs={{0,2},{1,3},{2,0},{3,1},{4,6},{5,7},{6,4},{7,5},{8,10},{9,11},{10,... | collective-permute-start | bytes 110600 | tf_op jit(solution)/shard_map/ppermute | solution.py:24
  175.3 10.4 %collective-permute-start.10 = (f32[6,1536]{1,0:T(8,128)S(1)}, f32[6,1536]{1,0:T(8,128)S(1)}, u32[]{:S(2)}, u32[]{:S(2)}) collective-permute-start(f32[6,1536]{1,0:T(8,128)S(1)} %add.182), channel_id=1, source_target_pairs={{0,4},{4,0},{1,5},{5,1},{2,6},{6,2},{3,7},{7,3},{8,12},{12,8},{9,1... | collective-permute-start | bytes 110600 | tf_op jit(solution)/shard_map/ppermute | solution.py:24
  (1 other events, 1.2 us)
Sparse Core Ops, SparseCore 0:
  27.1 51.2 all-gather.3
  80.5 22.7 all-gather.5

commit v10 on v9

--- a/solution.py
+++ b/solution.py
@@ -56,6 +56,14 @@
     for axis, d in steps:
         x = x + _swap(x, axis, d)
     return x
+
+
+def _sum_group(x, axes):
+    n = _size(axes)
+    vals = [x] + [lax.ppermute(x, axes, [(i, i ^ k) for i in range(n)]) for k in range(1, n)]
+    while len(vals) > 1:
+        vals = [vals[i] + vals[i + 1] for i in range(0, len(vals), 2)]
+    return vals[0]
 
 
 def body(features, bottleneck, node_noise, targets, entry_weight, conv_filters, exit_weight):
@@ -131,11 +139,9 @@
     lower = outs[1]
     blended = ((upper + lower) * 0.5).astype(jnp.bfloat16)[None]
     local_gap = jnp.sum((upper - lower) * (upper + lower - 2.0 * goal)) / (rows * n_ctx * chans)
-    gap = local_gap
-    for axis in ("c", "zl", "y"):
-        gap = lax.psum(gap, axis)
+    gap = _sum_group(_sum_group(local_gap.reshape(1), ("zl", "c")), ("y",))
     factor = gap / (2.0 * NOISE_SCALE)
-    estimate = _sum_all(factor * summed, (("x", 1), ("x", 2), ("zh", 1)))
+    estimate = _sum_group(factor * summed, DP)
     return (blended, estimate)
 
 

time: 194 us -> 249 us (1.28)
  the two profiles are of different devices: /device:TPU:2 before, /device:TPU:8 now
where the time goes in v10:
time: 249 us; the launch traced here: 248 us
  starting transfers between devices  129 us (52%)
  waiting for transfers between devices  40 us (16%)
  between operations  24.2 us (10%)
  blocking collectives  17.9 us (7%)
  local copies, waits for them, and re-layouts  13.2 us (5%)
  matrix products  12 us (5%)
  other arithmetic  11.7 us (5%)
    ppermute x21, starting transfers between devices, _sum_group(): lax.ppermute(x, axes, [(i, i ^ k) for i in range(n)])  97.8 us
    ppermute x6, starting transfers between devices, _swap(): return lax.ppermute(x, axis, [(i, i ^ d) for i in range(n)])  22.5 us
    ppermute x6, waiting for transfers between devices, _swap(): return lax.ppermute(x, axis, [(i, i ^ d) for i in range(n)])  22 us
    all_gather x1, blocking collectives, body(): packed = lax.all_gather(packed, axis, axis=0, tiled=True)  17.9 us
    ppermute x1, starting transfers between devices, body(): from_next = lax.ppermute(edge_in[:spacing], CTX, pairs_down)  6.34 us
    unnamed x24, local copies, waits for them, and re-layouts  6.05 us
    ppermute x21, waiting for transfers between devices, _sum_group(): lax.ppermute(x, axes, [(i, i ^ k) for i in range(n)])  5.96 us
    slice x3, local copies, waits for them, and re-layouts, body(): w_conv = packed[:, chans:4 * chans].reshape(bot, 3, chans)  5.67 us
  transfers between devices with their start and end apart: 31, of which 14 were waited for; matrix products, arithmetic and copies ran while one was open for 4% of the time, Pallas kernels for 0%

profile of v10, /device:TPU:8, one launch (start us, length us, event | category | flops | bytes accessed | tf_op | source)
XLA Modules:
  0.0 247.7 jit_solution(16122438158209815367)
XLA Ops:
  8.2 17.9 %all-gather = bf16[4,6,7680]{2,1,0:T(8,128)(2,1)S(1)} all-gather(bf16[1,6,7680]{2,1,0:T(8,128)(2,1)S(1)} %maximum_bitcast_fusion), channel_id=1, replica_groups=mesh['y'=8,'zl'=4,'c'=2,'zh'=2,'x'=4] {'zl'}, dimensions={0}, use_global_device_ids=true | all-gather | bytes 460800 | tf_op jit(solution)/shard_map/all_gather | solution.py:87
  37.0 4.2 %collective-permute-start.1 = (bf16[2,2,2,2,1,1,6,1536]{7,6,5,4,3,2,1,0:T(8,128)(2,1)S(1)}, bf16[2,2,2,2,1,1,6,1536]{7,6,5,4,3,2,1,0:T(8,128)(2,1)S(1)}, u32[]{:S(2)}, u32[]{:S(2)}) collective-permute-start(bf16[2,2,2,2,1,1,6,1536]{7,6,5,4,3,2,1,0:T(8,128)(2,1)S(1)} %dynamic-slice_convert_fusion), channel_id=1, source_target_pairs={{0,16},{16,0},{32,48},{48,32},{1,17},{17,1},{33,49},{49,33},{2,18}... | collective-permute-start | bytes 884744 | tf_op jit(solution)/shard_map/ppermute | solution.py:24
  41.2 9.4 %collective-permute-done.1 = bf16[2,2,2,2,1,1,6,1536]{7,6,5,4,3,2,1,0:T(8,128)(2,1)S(1)} collective-permute-done((bf16[2,2,2,2,1,1,6,1536]{7,6,5,4,3,2,1,0:T(8,128)(2,1)S(1)}, bf16[2,2,2,2,1,1,6,1536]{7,6,5,4,3,2,1,0:T(8,128)(2,1)S(1)}, u32[]{:S(2)}, u32[]{:S(2)}) %collective-permute-start.1) | collective-permute-done | bytes 294944 | tf_op jit(solution)/shard_map/ppermute | solution.py:24
  51.9 4.4 %collective-permute-start.2 = (bf16[2,2,2,1,1,1,6,1536]{7,6,5,4,3,2,1,0:T(8,128)(2,1)S(1)}, bf16[2,2,2,1,1,1,6,1536]{7,6,5,4,3,2,1,0:T(8,128)(2,1)}, u32[]{:S(2)}, u32[]{:S(2)}) collective-permute-start(bf16[2,2,2,1,1,1,6,1536]{7,6,5,4,3,2,1,0:T(8,128)(2,1)S(1)} %dynamic-slice_convert_fusion.1), channel_id=1, source_target_pairs={{0,32},{16,48},{32,0},{48,16},{1,33},{17,49},{33,1},{49,17},{2,34}... | collective-permute-start | bytes 442376 | tf_op jit(solution)/shard_map/ppermute | solution.py:24
  58.3 6.3 %collective-permute-start.4 = (bf16[32,3456]{1,0:T(8,128)(2,1)S(1)}, bf16[32,3456]{1,0:T(8,128)(2,1)S(1)}, u32[]{:S(2)}, u32[]{:S(2)}) collective-permute-start(bf16[32,3456]{1,0:T(8,128)(2,1)S(1)} %get-tuple-element.18), channel_id=1, source_target_pairs={{8,0},{16,8},{24,16},{32,24},{40,32},{48,40},{56,48},{64,56},{72,6... | collective-permute-start | bytes 663560 | tf_op jit(solution)/shard_map/ppermute | solution.py:94
  72.6 5.1 %all-gather.4.cloned.1.call-done = bf16[192,7680]{1,0:T(8,128)(2,1)} async-done(((bf16[24,7680]{1,0:T(8,128)(2,1)}), bf16[192,7680]{1,0:T(8,128)(2,1)}) %all-gather.4.cloned.1.call-update) | async-done | bytes 2949136 | tf_op jit(solution)/shard_map/all_gather | solution.py:87
  84.4 4.1 %collective-permute-start.6 = (bf16[2,1,1,1,1,1,6,1536]{7,6,5,4,3,2,1,0:T(8,128)(2,1)S(1)}, bf16[2,1,1,1,1,1,6,1536]{7,6,5,4,3,2,1,0:T(8,128)(2,1)S(1)}, u32[]{:S(2)}, u32[]{:S(2)}) collective-permute-start(bf16[2,1,1,1,1,1,6,1536]{7,6,5,4,3,2,1,0:T(8,128)(2,1)S(1)} %dynamic-slice_convert_fusion.3), channel_id=1, source_target_pairs={{0,128},{64,192},{128,0},{192,64},{256,384},{320,448},{384,256},{4... | collective-permute-start | bytes 110600 | tf_op jit(solution)/shard_map/ppermute | solution.py:24
  91.4 4.7 %collective-permute-start.7 = (bf16[1,1,1,1,1,1,6,1536]{7,6,5,4,3,2,1,0:T(8,128)(2,1)S(1)}, bf16[1,1,1,1,1,1,6,1536]{7,6,5,4,3,2,1,0:T(8,128)(2,1)S(1)}, u32[]{:S(2)}, u32[]{:S(2)}) collective-permute-start(bf16[1,1,1,1,1,1,6,1536]{7,6,5,4,3,2,1,0:T(8,128)(2,1)S(1)} %dynamic-slice_convert_fusion.4), channel_id=1, source_target_pairs={{0,256},{64,320},{128,384},{192,448},{256,0},{320,64},{384,128},{4... | collective-permute-start | bytes 55304 | tf_op jit(solution)/shard_map/ppermute | solution.py:24
  97.2 3.8 %collective-permute-done.7 = bf16[1,1,1,1,1,1,6,1536]{7,6,5,4,3,2,1,0:T(8,128)(2,1)S(1)} collective-permute-done((bf16[1,1,1,1,1,1,6,1536]{7,6,5,4,3,2,1,0:T(8,128)(2,1)S(1)}, bf16[1,1,1,1,1,1,6,1536]{7,6,5,4,3,2,1,0:T(8,128)(2,1)S(1)}, u32[]{:S(2)}, u32[]{:S(2)}) %collective-permute-start.7) | collective-permute-done | bytes 18464 | tf_op jit(solution)/shard_map/ppermute | solution.py:24
  117.6 5.5 %convolution_add_fusion = f32[2,192,1536]{2,1,0:T(8,128)} fusion(f32[1,256,1536]{2,1,0:T(8,128)} %copy-done.6, f32[1,256,1536]{2,1,0:T(8,128)} %copy-done.5, bf16[384,7680]{1,0:T(8,128)(2,1)} %all-gather.6.cloned.1.call-done, f32[2,192,384]{2,1,0:T(8,128)} %convolution_add_fusion.3, bf16[384,3,1536]{0,2,1:T(8,128)(2,1)S(1)} %bitcast.68, ...), kind=kOutput, calls=%fused_computation.12 | convolution fusion | flops 908623872 | bytes 9633792 | tf_op jit(solution)/shard_map/dot_general | solution.py:135
  130.4 4.8 %collective-permute-start.9 = (f32[1]{0:T(128)}, f32[1]{0:T(128)}, u32[]{:S(2)}, u32[]{:S(2)}) collective-permute-start(f32[1]{0:T(128)} %bitcast.20), channel_id=1, source_target_pairs={{0,16},{8,24},{16,0},{24,8},{32,48},{40,56},{48,32},{56,40},{1,17}... | collective-permute-start | bytes 20 | tf_op jit(solution)/shard_map/ppermute | solution.py:63
  138.4 5.9 %collective-permute-start.11 = (f32[1]{0:T(128)}, f32[1]{0:T(128)}, u32[]{:S(2)}, u32[]{:S(2)}) collective-permute-start(f32[1]{0:T(128)} %bitcast.20), channel_id=1, source_target_pairs={{0,32},{8,40},{16,48},{24,56},{32,0},{40,8},{48,16},{56,24},{1,33}... | collective-permute-start | bytes 20 | tf_op jit(solution)/shard_map/ppermute | solution.py:63
  147.5 5.8 %collective-permute-start.13 = (f32[1]{0:T(128)}, f32[1]{0:T(128)}, u32[]{:S(2)}, u32[]{:S(2)}) collective-permute-start(f32[1]{0:T(128)} %bitcast.20), channel_id=1, source_target_pairs={{0,48},{8,56},{16,32},{24,40},{32,16},{40,24},{48,0},{56,8},{1,49}... | collective-permute-start | bytes 20 | tf_op jit(solution)/shard_map/ppermute | solution.py:63
  161.9 3.7 %collective-permute-start.15 = (f32[1]{0:T(128)}, f32[1]{0:T(128)}, u32[]{:S(2)}, u32[]{:S(2)}) collective-permute-start(f32[1]{0:T(128)} %add.235), channel_id=1, source_target_pairs={{0,64},{64,0},{128,192},{192,128},{256,320},{320,256},{384,448},{4... | collective-permute-start | bytes 20 | tf_op jit(solution)/shard_map/ppermute | solution.py:63
  165.7 5.6 %collective-permute-start.16 = (f32[1]{0:T(128)}, f32[1]{0:T(128)}, u32[]{:S(2)}, u32[]{:S(2)}) collective-permute-start(f32[1]{0:T(128)} %add.235), channel_id=1, source_target_pairs={{0,128},{64,192},{128,0},{192,64},{256,384},{320,448},{384,256},{4... | collective-permute-start | bytes 20 | tf_op jit(solution)/shard_map/ppermute | solution.py:63
  171.3 3.7 %collective-permute-start.17 = (f32[1]{0:T(128)}, f32[1]{0:T(128)}, u32[]{:S(2)}, u32[]{:S(2)}) collective-permute-start(f32[1]{0:T(128)} %add.235), channel_id=1, source_target_pairs={{0,192},{64,128},{128,64},{192,0},{256,448},{320,384},{384,320},{4... | collective-permute-start | bytes 20 | tf_op jit(solution)/shard_map/ppermute | solution.py:63
  175.0 7.7 %collective-permute-start.18 = (f32[1]{0:T(128)}, f32[1]{0:T(128)}, u32[]{:S(2)}, u32[]{:S(2)}) collective-permute-start(f32[1]{0:T(128)} %add.235), channel_id=1, source_target_pairs={{0,256},{64,320},{128,384},{192,448},{256,0},{320,64},{384,128},{4... | collective-permute-start | bytes 20 | tf_op jit(solution)/shard_map/ppermute | solution.py:63
  182.7 4.5 %collective-permute-start.19 = (f32[1]{0:T(128)}, f32[1]{0:T(128)}, u32[]{:S(2)}, u32[]{:S(2)}) collective-permute-start(f32[1]{0:T(128)} %add.235), channel_id=1, source_target_pairs={{0,320},{64,256},{128,448},{192,384},{256,64},{320,0},{384,192},{4... | collective-permute-start | bytes 20 | tf_op jit(solution)/shard_map/ppermute | solution.py:63
  187.3 6.0 %collective-permute-start.20 = (f32[1]{0:T(128)}, f32[1]{0:T(128)}, u32[]{:S(2)}, u32[]{:S(2)}) collective-permute-start(f32[1]{0:T(128)} %add.235), channel_id=1, source_target_pairs={{0,384},{64,448},{128,256},{192,320},{256,128},{320,192},{384,0},{... | collective-permute-start | bytes 20 | tf_op jit(solution)/shard_map/ppermute | solution.py:63
  193.9 5.0 %collective-permute-start.21 = (f32[1]{0:T(128)}, f32[1]{0:T(128)}, u32[]{:S(2)}, u32[]{:S(2)}) collective-permute-start(f32[1]{0:T(128)} %add.235), channel_id=1, source_target_pairs={{0,448},{64,384},{128,320},{192,256},{256,192},{320,128},{384,64},... | collective-permute-start | bytes 20 | tf_op jit(solution)/shard_map/ppermute | solution.py:63
  203.7 8.5 %collective-permute-start.27 = (f32[6,1536]{1,0:T(8,128)S(1)}, f32[6,1536]{1,0:T(8,128)S(1)}, u32[]{:S(2)}, u32[]{:S(2)}) collective-permute-start(f32[6,1536]{1,0:T(8,128)S(1)} %multiply_bitcast_fusion), channel_id=1, source_target_pairs={{0,6},{1,7},{2,4},{3,5},{4,2},{5,3},{6,0},{7,1},{8,14},{9,15},{10,... | collective-permute-start | bytes 110600 | tf_op jit(solution)/shard_map/ppermute | solution.py:63
  212.1 4.3 %collective-permute-start.28 = (f32[6,1536]{1,0:T(8,128)S(1)}, f32[6,1536]{1,0:T(8,128)S(1)}, u32[]{:S(2)}, u32[]{:S(2)}) collective-permute-start(f32[6,1536]{1,0:T(8,128)S(1)} %multiply_bitcast_fusion), channel_id=1, source_target_pairs={{0,7},{1,6},{2,5},{3,4},{4,3},{5,2},{6,1},{7,0},{8,15},{9,14},{10,... | collective-permute-start | bytes 110600 | tf_op jit(solution)/shard_map/ppermute | solution.py:63
  216.4 6.0 %collective-permute-start.25 = (f32[6,1536]{1,0:T(8,128)S(1)}, f32[6,1536]{1,0:T(8,128)S(1)}, u32[]{:S(2)}, u32[]{:S(2)}) collective-permute-start(f32[6,1536]{1,0:T(8,128)S(1)} %multiply_bitcast_fusion), channel_id=1, source_target_pairs={{0,4},{1,5},{2,6},{3,7},{4,0},{5,1},{6,2},{7,3},{8,12},{9,13},{10,... | collective-permute-start | bytes 110600 | tf_op jit(solution)/shard_map/ppermute | solution.py:63
  225.0 6.1 %collective-permute-start.23 = (f32[6,1536]{1,0:T(8,128)S(1)}, f32[6,1536]{1,0:T(8,128)S(1)}, u32[]{:S(2)}, u32[]{:S(2)}) collective-permute-start(f32[6,1536]{1,0:T(8,128)S(1)} %multiply_bitcast_fusion), channel_id=1, source_target_pairs={{0,2},{1,3},{2,0},{3,1},{4,6},{5,7},{6,4},{7,5},{8,10},{9,11},{10,... | collective-permute-start | bytes 110600 | tf_op jit(solution)/shard_map/ppermute | solution.py:63
  (99 shorter events, 80.1 us)
Async XLA Ops:
  7.2 70.6 %all-gather.4.cloned.1.call-start = ((), (), s32[]{:S(2)}) async-start(), calls=%async_computation | async-start | bytes 3317760 | tf_op jit(solution)/shard_map/all_gather | solution.py:87
  27.0 76.3 %all-gather.6.cloned.1.call-start = ((), (), s32[]{:S(2)}) async-start(), calls=%async_computation.1 | async-start | bytes 8847360 | tf_op jit(solution)/shard_map/all_gather | solution.py:101
  37.0 13.6 %collective-permute-start.1 = (bf16[2,2,2,2,1,1,6,1536]{7,6,5,4,3,2,1,0:T(8,128)(2,1)S(1)}, bf16[2,2,2,2,1,1,6,1536]{7,6,5,4,3,2,1,0:T(8,128)(2,1)S(1)}, u32[]{:S(2)}, u32[]{:S(2)}) collective-permute-start(bf16[2,2,2,2,1,1,6,1536]{7,6,5,4,3,2,1,0:T(8,128)(2,1)S(1)} %dynamic-slice_convert_fusion), channel_id=1, source_target_pairs={{0,16},{16,0},{32,48},{48,32},{1,17},{17,1},{33,49},{49,33},{2,18}... | collective-permute-start | bytes 884744 | tf_op jit(solution)/shard_map/ppermute | solution.py:24
  51.9 14.5 %collective-permute-start.2 = (bf16[2,2,2,1,1,1,6,1536]{7,6,5,4,3,2,1,0:T(8,128)(2,1)S(1)}, bf16[2,2,2,1,1,1,6,1536]{7,6,5,4,3,2,1,0:T(8,128)(2,1)}, u32[]{:S(2)}, u32[]{:S(2)}) collective-permute-start(bf16[2,2,2,1,1,1,6,1536]{7,6,5,4,3,2,1,0:T(8,128)(2,1)S(1)} %dynamic-slice_convert_fusion.1), channel_id=1, source_target_pairs={{0,32},{16,48},{32,0},{48,16},{1,33},{17,49},{33,1},{49,17},{2,34}... | collective-permute-start | bytes 442376 | tf_op jit(solution)/shard_map/ppermute | solution.py:24
  56.4 14.3 %collective-permute-start.3 = (bf16[32,3456]{1,0:T(8,128)(2,1)S(1)}, bf16[32,3456]{1,0:T(8,128)(2,1)S(1)}, u32[]{:S(2)}, u32[]{:S(2)}) collective-permute-start(bf16[32,3456]{1,0:T(8,128)(2,1)S(1)} %get-tuple-element.19), channel_id=1, source_target_pairs={{0,8},{8,16},{16,24},{24,32},{32,40},{40,48},{48,56},{56,64},{64,7... | collective-permute-start | bytes 663560 | tf_op jit(solution)/shard_map/ppermute | solution.py:93
  58.3 14.3 %collective-permute-start.4 = (bf16[32,3456]{1,0:T(8,128)(2,1)S(1)}, bf16[32,3456]{1,0:T(8,128)(2,1)S(1)}, u32[]{:S(2)}, u32[]{:S(2)}) collective-permute-start(bf16[32,3456]{1,0:T(8,128)(2,1)S(1)} %get-tuple-element.18), channel_id=1, source_target_pairs={{8,0},{16,8},{24,16},{32,24},{40,32},{48,40},{56,48},{64,56},{72,6... | collective-permute-start | bytes 663560 | tf_op jit(solution)/shard_map/ppermute | solution.py:94
  91.4 9.6 %collective-permute-start.7 = (bf16[1,1,1,1,1,1,6,1536]{7,6,5,4,3,2,1,0:T(8,128)(2,1)S(1)}, bf16[1,1,1,1,1,1,6,1536]{7,6,5,4,3,2,1,0:T(8,128)(2,1)S(1)}, u32[]{:S(2)}, u32[]{:S(2)}) collective-permute-start(bf16[1,1,1,1,1,1,6,1536]{7,6,5,4,3,2,1,0:T(8,128)(2,1)S(1)} %dynamic-slice_convert_fusion.4), channel_id=1, source_target_pairs={{0,256},{64,320},{128,384},{192,448},{256,0},{320,64},{384,128},{4... | collective-permute-start | bytes 55304 | tf_op jit(solution)/shard_map/ppermute | solution.py:24
  127.4 20.1 %collective-permute-start.8 = (f32[1]{0:T(128)}, f32[1]{0:T(128)}, u32[]{:S(2)}, u32[]{:S(2)}) collective-permute-start(f32[1]{0:T(128)} %bitcast.20), channel_id=1, source_target_pairs={{0,8},{8,0},{16,24},{24,16},{32,40},{40,32},{48,56},{56,48},{1,9},... | collective-permute-start | bytes 20 | tf_op jit(solution)/shard_map/ppermute | solution.py:63
  130.4 23.6 %collective-permute-start.9 = (f32[1]{0:T(128)}, f32[1]{0:T(128)}, u32[]{:S(2)}, u32[]{:S(2)}) collective-permute-start(f32[1]{0:T(128)} %bitcast.20), channel_id=1, source_target_pairs={{0,16},{8,24},{16,0},{24,8},{32,48},{40,56},{48,32},{56,40},{1,17}... | collective-permute-start | bytes 20 | tf_op jit(solution)/shard_map/ppermute | solution.py:63
  135.2 22.0 %collective-permute-start.10 = (f32[1]{0:T(128)}, f32[1]{0:T(128)}, u32[]{:S(2)}, u32[]{:S(2)}) collective-permute-start(f32[1]{0:T(128)} %bitcast.20), channel_id=1, source_target_pairs={{0,24},{8,16},{16,8},{24,0},{32,56},{40,48},{48,40},{56,32},{1,25}... | collective-permute-start | bytes 20 | tf_op jit(solution)/shard_map/ppermute | solution.py:63
  138.4 20.1 %collective-permute-start.11 = (f32[1]{0:T(128)}, f32[1]{0:T(128)}, u32[]{:S(2)}, u32[]{:S(2)}) collective-permute-start(f32[1]{0:T(128)} %bitcast.20), channel_id=1, source_target_pairs={{0,32},{8,40},{16,48},{24,56},{32,0},{40,8},{48,16},{56,24},{1,33}... | collective-permute-start | bytes 20 | tf_op jit(solution)/shard_map/ppermute | solution.py:63
  144.3 14.2 %collective-permute-start.12 = (f32[1]{0:T(128)}, f32[1]{0:T(128)}, u32[]{:S(2)}, u32[]{:S(2)}) collective-permute-start(f32[1]{0:T(128)} %bitcast.20), channel_id=1, source_target_pairs={{0,40},{8,32},{16,56},{24,48},{32,8},{40,0},{48,24},{56,16},{1,41}... | collective-permute-start | bytes 20 | tf_op jit(solution)/shard_map/ppermute | solution.py:63
  147.5 12.2 %collective-permute-start.13 = (f32[1]{0:T(128)}, f32[1]{0:T(128)}, u32[]{:S(2)}, u32[]{:S(2)}) collective-permute-start(f32[1]{0:T(128)} %bitcast.20), channel_id=1, source_target_pairs={{0,48},{8,56},{16,32},{24,40},{32,16},{40,24},{48,0},{56,8},{1,49}... | collective-permute-start | bytes 20 | tf_op jit(solution)/shard_map/ppermute | solution.py:63
  161.9 25.3 %collective-permute-start.15 = (f32[1]{0:T(128)}, f32[1]{0:T(128)}, u32[]{:S(2)}, u32[]{:S(2)}) collective-permute-start(f32[1]{0:T(128)} %add.235), channel_id=1, source_target_pairs={{0,64},{64,0},{128,192},{192,128},{256,320},{320,256},{384,448},{4... | collective-permute-start | bytes 20 | tf_op jit(solution)/shard_map/ppermute | solution.py:63
  165.7 28.2 %collective-permute-start.16 = (f32[1]{0:T(128)}, f32[1]{0:T(128)}, u32[]{:S(2)}, u32[]{:S(2)}) collective-permute-start(f32[1]{0:T(128)} %add.235), channel_id=1, source_target_pairs={{0,128},{64,192},{128,0},{192,64},{256,384},{320,448},{384,256},{4... | collective-permute-start | bytes 20 | tf_op jit(solution)/shard_map/ppermute | solution.py:63
  171.3 27.6 %collective-permute-start.17 = (f32[1]{0:T(128)}, f32[1]{0:T(128)}, u32[]{:S(2)}, u32[]{:S(2)}) collective-permute-start(f32[1]{0:T(128)} %add.235), channel_id=1, source_target_pairs={{0,192},{64,128},{128,64},{192,0},{256,448},{320,384},{384,320},{4... | collective-permute-start | bytes 20 | tf_op jit(solution)/shard_map/ppermute | solution.py:63
  175.0 25.2 %collective-permute-start.18 = (f32[1]{0:T(128)}, f32[1]{0:T(128)}, u32[]{:S(2)}, u32[]{:S(2)}) collective-permute-start(f32[1]{0:T(128)} %add.235), channel_id=1, source_target_pairs={{0,256},{64,320},{128,384},{192,448},{256,0},{320,64},{384,128},{4... | collective-permute-start | bytes 20 | tf_op jit(solution)/shard_map/ppermute | solution.py:63
  182.7 17.4 %collective-permute-start.19 = (f32[1]{0:T(128)}, f32[1]{0:T(128)}, u32[]{:S(2)}, u32[]{:S(2)}) collective-permute-start(f32[1]{0:T(128)} %add.235), channel_id=1, source_target_pairs={{0,320},{64,256},{128,448},{192,384},{256,64},{320,0},{384,192},{4... | collective-permute-start | bytes 20 | tf_op jit(solution)/shard_map/ppermute | solution.py:63
  187.3 14.1 %collective-permute-start.20 = (f32[1]{0:T(128)}, f32[1]{0:T(128)}, u32[]{:S(2)}, u32[]{:S(2)}) collective-permute-start(f32[1]{0:T(128)} %add.235), channel_id=1, source_target_pairs={{0,384},{64,448},{128,256},{192,320},{256,128},{320,192},{384,0},{... | collective-permute-start | bytes 20 | tf_op jit(solution)/shard_map/ppermute | solution.py:63
  203.7 27.4 %collective-permute-start.27 = (f32[6,1536]{1,0:T(8,128)S(1)}, f32[6,1536]{1,0:T(8,128)S(1)}, u32[]{:S(2)}, u32[]{:S(2)}) collective-permute-start(f32[6,1536]{1,0:T(8,128)S(1)} %multiply_bitcast_fusion), channel_id=1, source_target_pairs={{0,6},{1,7},{2,4},{3,5},{4,2},{5,3},{6,0},{7,1},{8,14},{9,15},{10,... | collective-permute-start | bytes 110600 | tf_op jit(solution)/shard_map/ppermute | solution.py:63
  212.1 22.1 %collective-permute-start.28 = (f32[6,1536]{1,0:T(8,128)S(1)}, f32[6,1536]{1,0:T(8,128)S(1)}, u32[]{:S(2)}, u32[]{:S(2)}) collective-permute-start(f32[6,1536]{1,0:T(8,128)S(1)} %multiply_bitcast_fusion), channel_id=1, source_target_pairs={{0,7},{1,6},{2,5},{3,4},{4,3},{5,2},{6,1},{7,0},{8,15},{9,14},{10,... | collective-permute-start | bytes 110600 | tf_op jit(solution)/shard_map/ppermute | solution.py:63
  216.4 19.7 %collective-permute-start.25 = (f32[6,1536]{1,0:T(8,128)S(1)}, f32[6,1536]{1,0:T(8,128)S(1)}, u32[]{:S(2)}, u32[]{:S(2)}) collective-permute-start(f32[6,1536]{1,0:T(8,128)S(1)} %multiply_bitcast_fusion), channel_id=1, source_target_pairs={{0,4},{1,5},{2,6},{3,7},{4,0},{5,1},{6,2},{7,3},{8,12},{9,13},{10,... | collective-permute-start | bytes 110600 | tf_op jit(solution)/shard_map/ppermute | solution.py:63
  222.5 13.6 %collective-permute-start.26 = (f32[6,1536]{1,0:T(8,128)S(1)}, f32[6,1536]{1,0:T(8,128)S(1)}, u32[]{:S(2)}, u32[]{:S(2)}) collective-permute-start(f32[6,1536]{1,0:T(8,128)S(1)} %multiply_bitcast_fusion), channel_id=1, source_target_pairs={{0,5},{1,4},{2,7},{3,6},{4,1},{5,0},{6,3},{7,2},{8,13},{9,12},{10,... | collective-permute-start | bytes 110600 | tf_op jit(solution)/shard_map/ppermute | solution.py:63
  225.0 11.2 %collective-permute-start.23 = (f32[6,1536]{1,0:T(8,128)S(1)}, f32[6,1536]{1,0:T(8,128)S(1)}, u32[]{:S(2)}, u32[]{:S(2)}) collective-permute-start(f32[6,1536]{1,0:T(8,128)S(1)} %multiply_bitcast_fusion), channel_id=1, source_target_pairs={{0,2},{1,3},{2,0},{3,1},{4,6},{5,7},{6,4},{7,5},{8,10},{9,11},{10,... | collective-permute-start | bytes 110600 | tf_op jit(solution)/shard_map/ppermute | solution.py:63
  (19 other events, 246.7 us)
Sparse Core Ops, SparseCore 0:
  27.1 50.5 all-gather.3
  79.8 23.3 all-gather.5

commit v11 on v9

--- a/solution.py
+++ b/solution.py
@@ -75,8 +75,10 @@
 
     conv_rows = conv_filters.transpose(2, 0, 1).reshape(shard, -1)
     packed = jnp.concatenate([entry_weight, conv_rows, exit_weight], axis=1)
-    for axis in ("zl", "y"):
-        packed = lax.all_gather(packed, axis, axis=0, tiled=True)
+    packed = lax.all_gather(packed, "zl", axis=0, tiled=True)
+    half = packed.shape[1] // 2
+    halves = [packed[:, :half], packed[:, half:]]
+    halves = [lax.all_gather(h, "y", axis=0, tiled=True) for h in halves]
 
     spacing = DILATION
     edge_in = jnp.concatenate([feats, bottle, jitter], axis=1)
@@ -87,16 +89,18 @@
 
     summed = summed.reshape((2,) * len(DIGITS) + (shard, chans))
     summed = _halve(summed, (("c", 1), ("zl", 1), ("zl", 2)))
-    packed, summed, from_prev, from_next = lax.optimization_barrier(
-        (packed, summed, from_prev, from_next)
+    halves, summed, from_prev, from_next = lax.optimization_barrier(
+        (halves, summed, from_prev, from_next)
     )
-    packed = lax.all_gather(packed, "c", axis=0, tiled=True)
+    halves = [lax.all_gather(h, "c", axis=0, tiled=True) for h in halves]
     summed = _halve(summed, (("y", 1), ("y", 2), ("y", 4)))
-    packed, summed = lax.optimization_barrier((packed, summed))
+    halves, summed = lax.optimization_barrier((halves, summed))
     summed = summed.reshape(shard, chans)
-    w_entry = packed[:, :chans]
-    w_conv = packed[:, chans : 4 * chans].reshape(bot, 3, chans)
-    w_exit = packed[:, 4 * chans :]
+    first, second = halves
+    w_entry = first[:, :chans]
+    w_conv = jnp.concatenate([first[:, chans:], second[:, : 3 * chans - (half - chans)]], axis=1)
+    w_conv = w_conv.reshape(bot, 3, chans)
+    w_exit = second[:, 3 * chans - (half - chans) :]
 
     ext = jnp.concatenate([from_prev, edge_in, from_next], axis=0)
     ext_feats = ext[:, :chans]

time: 194 us -> 251 us (1.29)
  waiting for transfers between devices: 54.3 us -> 109 us
    all_gather x2 -> x4, waiting for transfers between devices: 12.4 us -> 68.9 us  [the longest x2 49.1 us: body(): halves = [lax.all_gather(h, 'y', axis=0, tiled=True) for h in halves]]
    concatenate x0 -> x1, local copies, waits for them, and re-layouts: none -> 3.64 us  [body(): jnp.concatenate([first[:, chans:], second[:, :3 * chans - (half - chans)]...]
    slice x3 -> x5, local copies, waits for them, and re-layouts: 5.63 us -> 2.76 us  [the longest x2 1.47 us: body(): second[:, :3 * chans - (half - chans)]]
    unnamed x24 -> x28, local copies, waits for them, and re-layouts: 6.06 us -> 5.75 us
  transfers between devices with their start and end apart: 13 -> 15, of which waited for: 11 -> 12; matrix products, arithmetic and copies ran while one was open for 5% -> 4% of each run, Pallas kernels for 0% -> 0%
where the time goes in v11:
time: 251 us; the launch traced here: 250 us
  waiting for transfers between devices  109 us (43%)
  blocking collectives  51.2 us (20%)
  starting transfers between devices  36.6 us (15%)
  between operations  15.5 us (6%)
  local copies, waits for them, and re-layouts  13.6 us (5%)
  matrix products  12 us (5%)
  other arithmetic  11.8 us (5%)
    all_gather x2, waiting for transfers between devices, body(): halves = [lax.all_gather(h, 'y', axis=0, tiled=True) for h in halves]  49.1 us
    ppermute x9, waiting for transfers between devices, _swap(): return lax.ppermute(x, axis, [(i, i ^ d) for i in range(n)])  39.6 us
    ppermute x9, starting transfers between devices, _swap(): return lax.ppermute(x, axis, [(i, i ^ d) for i in range(n)])  33.9 us
    psum x3, blocking collectives, body(): gap = lax.psum(gap, axis)  33.3 us
    all_gather x2, waiting for transfers between devices, body(): halves = [lax.all_gather(h, 'c', axis=0, tiled=True) for h in halves]  19.8 us
    all_gather x1, blocking collectives, body(): packed = lax.all_gather(packed, 'zl', axis=0, tiled=True)  17.9 us
    unnamed x28, local copies, waits for them, and re-layouts  5.75 us
    dot_general x1, matrix products, body(): jnp.dot(inner, w_exit, preferred_element_type=jnp.float32)  5.53 us
  transfers between devices with their start and end apart: 15, of which 12 were waited for; matrix products, arithmetic and copies ran while one was open for 4% of the time, Pallas kernels for 0%

profile of v11, /device:TPU:2, one launch (start us, length us, event | category | flops | bytes accessed | tf_op | source)
XLA Modules:
  0.0 249.8 jit_solution(10064112627854914852)
XLA Ops:
  8.2 17.9 %all-gather = bf16[4,6,7680]{2,1,0:T(8,128)(2,1)S(1)} all-gather(bf16[1,6,7680]{2,1,0:T(8,128)(2,1)S(1)} %maximum_bitcast_fusion), channel_id=1, replica_groups=mesh['y'=8,'zl'=4,'c'=2,'zh'=2,'x'=4] {'zl'}, dimensions={0}, use_global_device_ids=true | all-gather | bytes 460800 | tf_op jit(solution)/shard_map/all_gather | solution.py:78
  37.0 4.2 %collective-permute-start.1 = (bf16[2,2,2,2,1,1,6,1536]{7,6,5,4,3,2,1,0:T(8,128)(2,1)S(1)}, bf16[2,2,2,2,1,1,6,1536]{7,6,5,4,3,2,1,0:T(8,128)(2,1)S(1)}, u32[]{:S(2)}, u32[]{:S(2)}) collective-permute-start(bf16[2,2,2,2,1,1,6,1536]{7,6,5,4,3,2,1,0:T(8,128)(2,1)S(1)} %dynamic-slice_convert_fusion), channel_id=1, source_target_pairs={{0,16},{16,0},{32,48},{48,32},{1,17},{17,1},{33,49},{49,33},{2,18}... | collective-permute-start | bytes 884744 | tf_op jit(solution)/shard_map/ppermute | solution.py:24
  41.3 9.4 %collective-permute-done.1 = bf16[2,2,2,2,1,1,6,1536]{7,6,5,4,3,2,1,0:T(8,128)(2,1)S(1)} collective-permute-done((bf16[2,2,2,2,1,1,6,1536]{7,6,5,4,3,2,1,0:T(8,128)(2,1)S(1)}, bf16[2,2,2,2,1,1,6,1536]{7,6,5,4,3,2,1,0:T(8,128)(2,1)S(1)}, u32[]{:S(2)}, u32[]{:S(2)}) %collective-permute-start.1) | collective-permute-done | bytes 294944 | tf_op jit(solution)/shard_map/ppermute | solution.py:24
  51.9 4.4 %collective-permute-start.2 = (bf16[2,2,2,1,1,1,6,1536]{7,6,5,4,3,2,1,0:T(8,128)(2,1)S(1)}, bf16[2,2,2,1,1,1,6,1536]{7,6,5,4,3,2,1,0:T(8,128)(2,1)}, u32[]{:S(2)}, u32[]{:S(2)}) collective-permute-start(bf16[2,2,2,1,1,1,6,1536]{7,6,5,4,3,2,1,0:T(8,128)(2,1)S(1)} %dynamic-slice_convert_fusion.1), channel_id=1, source_target_pairs={{0,32},{16,48},{32,0},{48,16},{1,33},{17,49},{33,1},{49,17},{2,34}... | collective-permute-start | bytes 442376 | tf_op jit(solution)/shard_map/ppermute | solution.py:24
  59.0 6.6 %collective-permute-done.2 = bf16[2,2,2,1,1,1,6,1536]{7,6,5,4,3,2,1,0:T(8,128)(2,1)} collective-permute-done((bf16[2,2,2,1,1,1,6,1536]{7,6,5,4,3,2,1,0:T(8,128)(2,1)S(1)}, bf16[2,2,2,1,1,1,6,1536]{7,6,5,4,3,2,1,0:T(8,128)(2,1)}, u32[]{:S(2)}, u32[]{:S(2)}) %collective-permute-start.2) | collective-permute-done | bytes 147488 | tf_op jit(solution)/shard_map/ppermute | solution.py:24
  66.6 5.6 %all-gather.6.cloned.1.call-done = bf16[192,3840]{1,0:T(8,128)(2,1)} async-done(((bf16[24,3840]{1,0:T(8,128)(2,1)}), bf16[192,3840]{1,0:T(8,128)(2,1)}) %all-gather.6.cloned.1.call-update) | async-done | bytes 1474576 | tf_op jit(solution)/shard_map/all_gather | solution.py:81
  72.2 43.5 %all-gather.8.cloned.1.call-done = bf16[192,3840]{1,0:T(8,128)(2,1)} async-done(((bf16[24,3840]{1,0:T(8,128)(2,1)}), bf16[192,3840]{1,0:T(8,128)(2,1)}) %all-gather.8.cloned.1.call-update) | async-done | bytes 1474576 | tf_op jit(solution)/shard_map/all_gather | solution.py:81
  116.3 3.1 %collective-permute-start.5 = (bf16[2,2,1,1,1,1,6,1536]{7,6,5,4,3,2,1,0:T(8,128)(2,1)S(1)}, bf16[2,2,1,1,1,1,6,1536]{7,6,5,4,3,2,1,0:T(8,128)(2,1)S(1)}, u32[]{:S(2)}, u32[]{:S(2)}) collective-permute-start(bf16[2,2,1,1,1,1,6,1536]{7,6,5,4,3,2,1,0:T(8,128)(2,1)S(1)} %dynamic-slice_convert_fusion.2), channel_id=1, source_target_pairs={{0,64},{64,0},{128,192},{192,128},{256,320},{320,256},{384,448},{4... | collective-permute-start | bytes 221192 | tf_op jit(solution)/shard_map/ppermute | solution.py:24
  119.6 3.3 %collective-permute-done.5 = bf16[2,2,1,1,1,1,6,1536]{7,6,5,4,3,2,1,0:T(8,128)(2,1)S(1)} collective-permute-done((bf16[2,2,1,1,1,1,6,1536]{7,6,5,4,3,2,1,0:T(8,128)(2,1)S(1)}, bf16[2,2,1,1,1,1,6,1536]{7,6,5,4,3,2,1,0:T(8,128)(2,1)S(1)}, u32[]{:S(2)}, u32[]{:S(2)}) %collective-permute-start.5) | collective-permute-done | bytes 73760 | tf_op jit(solution)/shard_map/ppermute | solution.py:24
  122.9 4.0 %collective-permute-start.6 = (bf16[2,1,1,1,1,1,6,1536]{7,6,5,4,3,2,1,0:T(8,128)(2,1)S(1)}, bf16[2,1,1,1,1,1,6,1536]{7,6,5,4,3,2,1,0:T(8,128)(2,1)S(1)}, u32[]{:S(2)}, u32[]{:S(2)}) collective-permute-start(bf16[2,1,1,1,1,1,6,1536]{7,6,5,4,3,2,1,0:T(8,128)(2,1)S(1)} %dynamic-slice_convert_fusion.3), channel_id=1, source_target_pairs={{0,128},{64,192},{128,0},{192,64},{256,384},{320,448},{384,256},{4... | collective-permute-start | bytes 110600 | tf_op jit(solution)/shard_map/ppermute | solution.py:24
  129.8 4.9 %collective-permute-start.7 = (bf16[1,1,1,1,1,1,6,1536]{7,6,5,4,3,2,1,0:T(8,128)(2,1)S(1)}, bf16[1,1,1,1,1,1,6,1536]{7,6,5,4,3,2,1,0:T(8,128)(2,1)S(1)}, u32[]{:S(2)}, u32[]{:S(2)}) collective-permute-start(bf16[1,1,1,1,1,1,6,1536]{7,6,5,4,3,2,1,0:T(8,128)(2,1)S(1)} %dynamic-slice_convert_fusion.4), channel_id=1, source_target_pairs={{0,256},{64,320},{128,384},{192,448},{256,0},{320,64},{384,128},{4... | collective-permute-start | bytes 55304 | tf_op jit(solution)/shard_map/ppermute | solution.py:24
  135.8 3.7 %collective-permute-done.7 = bf16[1,1,1,1,1,1,6,1536]{7,6,5,4,3,2,1,0:T(8,128)(2,1)S(1)} collective-permute-done((bf16[1,1,1,1,1,1,6,1536]{7,6,5,4,3,2,1,0:T(8,128)(2,1)S(1)}, bf16[1,1,1,1,1,1,6,1536]{7,6,5,4,3,2,1,0:T(8,128)(2,1)S(1)}, u32[]{:S(2)}, u32[]{:S(2)}) %collective-permute-start.7) | collective-permute-done | bytes 18464 | tf_op jit(solution)/shard_map/ppermute | solution.py:24
  140.1 19.8 %all-gather.12.cloned.1.call-done = bf16[384,3840]{1,0:T(8,128)(2,1)} async-done(((bf16[192,3840]{1,0:T(8,128)(2,1)}), bf16[384,3840]{1,0:T(8,128)(2,1)}) %all-gather.12.cloned.1.call-update) | async-done | bytes 2949136 | tf_op jit(solution)/shard_map/all_gather | solution.py:95
  162.2 3.6 %copy.31 = bf16[384,4608]{0,1:T(8,128)(2,1)} copy(bf16[384,4608]{1,0:T(8,128)(2,1)S(1)} %pad_maximum_fusion.1) | data formatting | bytes 7077888 | tf_op jit(solution)/shard_map/concatenate | solution.py:101
  174.9 5.5 %convolution_add_fusion = f32[2,192,1536]{2,1,0:T(8,128)} fusion(f32[1,256,1536]{2,1,0:T(8,128)} %copy-done.7, f32[1,256,1536]{2,1,0:T(8,128)} %copy-done.6, bf16[384,3840]{1,0:T(8,128)(2,1)S(1)} %copy-done.1, f32[2,192,384]{2,1,0:T(8,128)} %convolution_add_fusion.3, bf16[384,3,1536]{0,2,1:T(8,128)(2,1)} %bitcast.64, bf16[2,256,1536]{2,1,0:T(8,128)(2,1)} %copy-done.8), kind=kOutput, calls=%fused_computation.13 | convolution fusion | flops 908623872 | bytes 9633792 | tf_op jit(solution)/shard_map/dot_general | solution.py:131
  180.5 3.4 %multiply_reduce_fusion = (f32[]{:T(128)}, bf16[1,192,1536]{2,1,0:T(8,128)(2,1)}) fusion(bf16[1,192,1536]{2,1,0:T(8,128)(2,1)S(1)} %copy-done.11, f32[2,192,1536]{2,1,0:T(8,128)} %convolution_add_fusion), kind=kLoop, calls=%fused_computation.32 | loop fusion | flops 2654207 | bytes 3538948 | tf_op jit(solution)/shard_map/reduce_sum | solution.py:137
  184.4 3.0 %psum.21 = f32[]{:T(128)} all-reduce(f32[]{:T(128)S(6)} %div.40), channel_id=1, replica_groups=mesh['y'=8,'zl'=4,'c'=2,'zh'=2,'x'=4] {'c'}, use_global_device_ids=true, to_apply=%region_1.2 | all-reduce | flops 1 | bytes 8 | tf_op jit(solution)/shard_map/psum | solution.py:140
  187.4 12.8 %psum.22 = f32[]{:T(128)} all-reduce(f32[]{:T(128)} %psum.21), channel_id=1, replica_groups=mesh['y'=8,'zl'=4,'c'=2,'zh'=2,'x'=4] {'zl'}, use_global_device_ids=true, to_apply=%region_2.3 | all-reduce | flops 1 | bytes 8 | tf_op jit(solution)/shard_map/psum | solution.py:140
  200.1 17.6 %psum.23 = f32[]{:T(128)} all-reduce(f32[]{:T(128)} %psum.22), channel_id=1, replica_groups=mesh['y'=8,'zl'=4,'c'=2,'zh'=2,'x'=4] {'y'}, use_global_device_ids=true, to_apply=%region_3.4 | all-reduce | flops 1 | bytes 8 | tf_op jit(solution)/shard_map/psum | solution.py:140
  220.8 4.0 %collective-permute-done.8 = f32[6,1536]{1,0:T(8,128)S(1)} collective-permute-done((f32[6,1536]{1,0:T(8,128)S(1)}, f32[6,1536]{1,0:T(8,128)S(1)}, u32[]{:S(2)}, u32[]{:S(2)}) %collective-permute-start.8) | collective-permute-done | bytes 36896 | tf_op jit(solution)/shard_map/ppermute | solution.py:24
  224.8 3.5 %collective-permute-start.9 = (f32[6,1536]{1,0:T(8,128)S(1)}, f32[6,1536]{1,0:T(8,128)S(1)}, u32[]{:S(2)}, u32[]{:S(2)}) collective-permute-start(f32[6,1536]{1,0:T(8,128)S(1)} %fusion.45), channel_id=1, source_target_pairs={{0,2},{1,3},{2,0},{3,1},{4,6},{5,7},{6,4},{7,5},{8,10},{9,11},{10,... | collective-permute-start | bytes 110600 | tf_op jit(solution)/shard_map/ppermute | solution.py:24
  228.3 3.9 %collective-permute-done.9 = f32[6,1536]{1,0:T(8,128)S(1)} collective-permute-done((f32[6,1536]{1,0:T(8,128)S(1)}, f32[6,1536]{1,0:T(8,128)S(1)}, u32[]{:S(2)}, u32[]{:S(2)}) %collective-permute-start.9) | collective-permute-done | bytes 36896 | tf_op jit(solution)/shard_map/ppermute | solution.py:24
  232.3 5.3 %collective-permute-start.10 = (f32[6,1536]{1,0:T(8,128)S(1)}, f32[6,1536]{1,0:T(8,128)S(1)}, u32[]{:S(2)}, u32[]{:S(2)}) collective-permute-start(f32[6,1536]{1,0:T(8,128)S(1)} %add.182), channel_id=1, source_target_pairs={{0,4},{4,0},{1,5},{5,1},{2,6},{6,2},{3,7},{7,3},{8,12},{12,8},{9,1... | collective-permute-start | bytes 110600 | tf_op jit(solution)/shard_map/ppermute | solution.py:24
  237.6 5.1 %collective-permute-done.10 = f32[6,1536]{1,0:T(8,128)S(1)} collective-permute-done((f32[6,1536]{1,0:T(8,128)S(1)}, f32[6,1536]{1,0:T(8,128)S(1)}, u32[]{:S(2)}, u32[]{:S(2)}) %collective-permute-start.10) | collective-permute-done | bytes 36896 | tf_op jit(solution)/shard_map/ppermute | solution.py:24
  (82 shorter events, 36.2 us)
Async XLA Ops:
  7.2 19.9 %copy-start.5 = (bf16[1,192,384]{2,1,0:T(8,128)(2,1)S(1)}, bf16[1,192,384]{2,1,0:T(8,128)(2,1)}, u32[]{:S(2)}) copy-start(bf16[1,192,384]{2,1,0:T(8,128)(2,1)} %param.8) | copy-start | bytes 442372
  7.2 65.0 %all-gather.6.cloned.1.call-start = ((), (), s32[]{:S(2)}) async-start(), calls=%async_computation | async-start | bytes 1658880 | tf_op jit(solution)/shard_map/all_gather | solution.py:81
  27.0 88.7 %all-gather.8.cloned.1.call-start = ((), (), s32[]{:S(2)}) async-start(), calls=%async_computation.1 | async-start | bytes 1658880 | tf_op jit(solution)/shard_map/all_gather | solution.py:81
  30.3 4.2 %collective-permute-start = (bf16[2,2,2,2,2,1,6,1536]{7,4,6,5,3,2,1,0:T(2,128)(2,1)}, bf16[2,2,2,2,2,1,6,1536]{7,4,6,5,3,2,1,0:T(2,128)(2,1)}, u32[]{:S(2)}, u32[]{:S(2)}) collective-permute-start(bf16[2,2,2,2,2,1,6,1536]{7,4,6,5,3,2,1,0:T(2,128)(2,1)} %copy.42), channel_id=1, source_target_pairs={{0,8},{8,0},{1,9},{9,1},{2,10},{10,2},{3,11},{11,3},{4,12},{12,4},... | collective-permute-start | bytes 1769480 | tf_op jit(solution)/shard_map/ppermute | solution.py:24
  32.2 107.9 %all-gather.10.cloned.1.call-start = ((), (), s32[]{:S(2)}) async-start(), calls=%async_computation.2 | async-start | bytes 4423680 | tf_op jit(solution)/shard_map/all_gather | solution.py:95
  37.0 19.4 %copy-start = (bf16[1,192,1536]{2,1,0:T(8,128)(2,1)S(1)}, bf16[1,192,1536]{2,1,0:T(8,128)(2,1)}, u32[]{:S(2)}) copy-start(bf16[1,192,1536]{2,1,0:T(8,128)(2,1)} %param.9) | copy-start | bytes 1769476
  37.0 19.4 %copy-start.2 = (bf16[1,192,1536]{2,1,0:T(8,128)(2,1)S(1)}, bf16[1,192,1536]{2,1,0:T(8,128)(2,1)}, u32[]{:S(2)}) copy-start(bf16[1,192,1536]{2,1,0:T(8,128)(2,1)} %param.7) | copy-start | bytes 1769476
  37.0 13.6 %collective-permute-start.1 = (bf16[2,2,2,2,1,1,6,1536]{7,6,5,4,3,2,1,0:T(8,128)(2,1)S(1)}, bf16[2,2,2,2,1,1,6,1536]{7,6,5,4,3,2,1,0:T(8,128)(2,1)S(1)}, u32[]{:S(2)}, u32[]{:S(2)}) collective-permute-start(bf16[2,2,2,2,1,1,6,1536]{7,6,5,4,3,2,1,0:T(8,128)(2,1)S(1)} %dynamic-slice_convert_fusion), channel_id=1, source_target_pairs={{0,16},{16,0},{32,48},{48,32},{1,17},{17,1},{33,49},{49,33},{2,18}... | collective-permute-start | bytes 884744 | tf_op jit(solution)/shard_map/ppermute | solution.py:24
  51.9 13.7 %collective-permute-start.2 = (bf16[2,2,2,1,1,1,6,1536]{7,6,5,4,3,2,1,0:T(8,128)(2,1)S(1)}, bf16[2,2,2,1,1,1,6,1536]{7,6,5,4,3,2,1,0:T(8,128)(2,1)}, u32[]{:S(2)}, u32[]{:S(2)}) collective-permute-start(bf16[2,2,2,1,1,1,6,1536]{7,6,5,4,3,2,1,0:T(8,128)(2,1)S(1)} %dynamic-slice_convert_fusion.1), channel_id=1, source_target_pairs={{0,32},{16,48},{32,0},{48,16},{1,33},{17,49},{33,1},{49,17},{2,34}... | collective-permute-start | bytes 442376 | tf_op jit(solution)/shard_map/ppermute | solution.py:24
  56.4 10.2 %collective-permute-start.3 = (bf16[32,3456]{1,0:T(8,128)(2,1)S(1)}, bf16[32,3456]{1,0:T(8,128)(2,1)S(1)}, u32[]{:S(2)}, u32[]{:S(2)}) collective-permute-start(bf16[32,3456]{1,0:T(8,128)(2,1)S(1)} %get-tuple-element.23), channel_id=1, source_target_pairs={{0,8},{8,16},{16,24},{24,32},{32,40},{40,48},{48,56},{56,64},{64,7... | collective-permute-start | bytes 663560 | tf_op jit(solution)/shard_map/ppermute | solution.py:87
  57.7 8.9 %collective-permute-start.4 = (bf16[32,3456]{1,0:T(8,128)(2,1)S(1)}, bf16[32,3456]{1,0:T(8,128)(2,1)S(1)}, u32[]{:S(2)}, u32[]{:S(2)}) collective-permute-start(bf16[32,3456]{1,0:T(8,128)(2,1)S(1)} %get-tuple-element.22), channel_id=1, source_target_pairs={{8,0},{16,8},{24,16},{32,24},{40,32},{48,40},{56,48},{64,56},{72,6... | collective-permute-start | bytes 663560 | tf_op jit(solution)/shard_map/ppermute | solution.py:88
  66.6 68.1 %copy-start.9 = (bf16[32,3456]{1,0:T(8,128)(2,1)}, bf16[32,3456]{1,0:T(8,128)(2,1)S(1)}, u32[]{:S(2)}) copy-start(bf16[32,3456]{1,0:T(8,128)(2,1)S(1)} %collective-permute-done.3) | copy-start | bytes 663556
  66.6 68.1 %copy-start.10 = (bf16[32,3456]{1,0:T(8,128)(2,1)}, bf16[32,3456]{1,0:T(8,128)(2,1)S(1)}, u32[]{:S(2)}) copy-start(bf16[32,3456]{1,0:T(8,128)(2,1)S(1)} %collective-permute-done.4) | copy-start | bytes 663556
  115.7 44.2 %all-gather.12.cloned.1.call-start = ((), (), s32[]{:S(2)}) async-start(), calls=%async_computation.3 | async-start | bytes 4423680 | tf_op jit(solution)/shard_map/all_gather | solution.py:95
  116.3 6.5 %collective-permute-start.5 = (bf16[2,2,1,1,1,1,6,1536]{7,6,5,4,3,2,1,0:T(8,128)(2,1)S(1)}, bf16[2,2,1,1,1,1,6,1536]{7,6,5,4,3,2,1,0:T(8,128)(2,1)S(1)}, u32[]{:S(2)}, u32[]{:S(2)}) collective-permute-start(bf16[2,2,1,1,1,1,6,1536]{7,6,5,4,3,2,1,0:T(8,128)(2,1)S(1)} %dynamic-slice_convert_fusion.2), channel_id=1, source_target_pairs={{0,64},{64,0},{128,192},{192,128},{256,320},{320,256},{384,448},{4... | collective-permute-start | bytes 221192 | tf_op jit(solution)/shard_map/ppermute | solution.py:24
  122.9 6.9 %collective-permute-start.6 = (bf16[2,1,1,1,1,1,6,1536]{7,6,5,4,3,2,1,0:T(8,128)(2,1)S(1)}, bf16[2,1,1,1,1,1,6,1536]{7,6,5,4,3,2,1,0:T(8,128)(2,1)S(1)}, u32[]{:S(2)}, u32[]{:S(2)}) collective-permute-start(bf16[2,1,1,1,1,1,6,1536]{7,6,5,4,3,2,1,0:T(8,128)(2,1)S(1)} %dynamic-slice_convert_fusion.3), channel_id=1, source_target_pairs={{0,128},{64,192},{128,0},{192,64},{256,384},{320,448},{384,256},{4... | collective-permute-start | bytes 110600 | tf_op jit(solution)/shard_map/ppermute | solution.py:24
  129.8 9.7 %collective-permute-start.7 = (bf16[1,1,1,1,1,1,6,1536]{7,6,5,4,3,2,1,0:T(8,128)(2,1)S(1)}, bf16[1,1,1,1,1,1,6,1536]{7,6,5,4,3,2,1,0:T(8,128)(2,1)S(1)}, u32[]{:S(2)}, u32[]{:S(2)}) collective-permute-start(bf16[1,1,1,1,1,1,6,1536]{7,6,5,4,3,2,1,0:T(8,128)(2,1)S(1)} %dynamic-slice_convert_fusion.4), channel_id=1, source_target_pairs={{0,256},{64,320},{128,384},{192,448},{256,0},{320,64},{384,128},{4... | collective-permute-start | bytes 55304 | tf_op jit(solution)/shard_map/ppermute | solution.py:24
  168.4 3.7 %copy-start.4 = (bf16[384,4608]{0,1:T(8,128)(2,1)S(1)}, bf16[384,4608]{0,1:T(8,128)(2,1)}, u32[]{:S(2)}) copy-start(bf16[384,4608]{0,1:T(8,128)(2,1)} %copy.31) | copy-start | bytes 10616836
  170.0 2.9 %copy-start.8 = (bf16[2,256,1536]{2,1,0:T(8,128)(2,1)}, bf16[2,256,1536]{2,1,0:T(8,128)(2,1)S(1)}, u32[]{:S(2)}) copy-start(bf16[2,256,1536]{2,1,0:T(8,128)(2,1)S(1)} %fusion.7) | copy-start | bytes 4718596
  174.9 5.5 %copy-start.11 = (bf16[1,192,1536]{2,1,0:T(8,128)(2,1)S(1)}, bf16[1,192,1536]{2,1,0:T(8,128)(2,1)}, u32[]{:S(2)}) copy-start(bf16[1,192,1536]{2,1,0:T(8,128)(2,1)} %param.10) | copy-start | bytes 1769476
  180.4 37.8 %copy-start.12 = (f32[1,1,1,1,1,1,6,1536]{7,6,5,4,3,2,1,0:T(8,128)S(1)}, f32[1,1,1,1,1,1,6,1536]{7,6,5,4,3,2,1,0:T(8,128)}, u32[]{:S(2)}) copy-start(f32[1,1,1,1,1,1,6,1536]{7,6,5,4,3,2,1,0:T(8,128)} %convert_add_fusion.5) | copy-start | bytes 110596
  218.3 6.4 %collective-permute-start.8 = (f32[6,1536]{1,0:T(8,128)S(1)}, f32[6,1536]{1,0:T(8,128)S(1)}, u32[]{:S(2)}, u32[]{:S(2)}) collective-permute-start(f32[6,1536]{1,0:T(8,128)S(1)} %multiply_bitcast_fusion), channel_id=1, source_target_pairs={{0,1},{1,0},{2,3},{3,2},{4,5},{5,4},{6,7},{7,6},{8,9},{9,8},{10,11... | collective-permute-start | bytes 110600 | tf_op jit(solution)/shard_map/ppermute | solution.py:24
  224.8 7.5 %collective-permute-start.9 = (f32[6,1536]{1,0:T(8,128)S(1)}, f32[6,1536]{1,0:T(8,128)S(1)}, u32[]{:S(2)}, u32[]{:S(2)}) collective-permute-start(f32[6,1536]{1,0:T(8,128)S(1)} %fusion.45), channel_id=1, source_target_pairs={{0,2},{1,3},{2,0},{3,1},{4,6},{5,7},{6,4},{7,5},{8,10},{9,11},{10,... | collective-permute-start | bytes 110600 | tf_op jit(solution)/shard_map/ppermute | solution.py:24
  232.3 10.4 %collective-permute-start.10 = (f32[6,1536]{1,0:T(8,128)S(1)}, f32[6,1536]{1,0:T(8,128)S(1)}, u32[]{:S(2)}, u32[]{:S(2)}) collective-permute-start(f32[6,1536]{1,0:T(8,128)S(1)} %add.182), channel_id=1, source_target_pairs={{0,4},{4,0},{1,5},{5,1},{2,6},{6,2},{3,7},{7,3},{8,12},{12,8},{9,1... | collective-permute-start | bytes 110600 | tf_op jit(solution)/shard_map/ppermute | solution.py:24
  (6 other events, 9.5 us)
Sparse Core Ops, SparseCore 0:
  27.1 45.0 all-gather.5
  74.3 41.3 all-gather.7
  117.8 18.8 all-gather.9
  138.6 21.2 all-gather.11

commit v12 on v9

--- a/solution.py
+++ b/solution.py
@@ -90,9 +90,10 @@
     packed, summed, from_prev, from_next = lax.optimization_barrier(
         (packed, summed, from_prev, from_next)
     )
-    packed = lax.all_gather(packed, "c", axis=0, tiled=True)
+    theirs = _swap(packed, "c", 1)
     summed = _halve(summed, (("y", 1), ("y", 2), ("y", 4)))
-    packed, summed = lax.optimization_barrier((packed, summed))
+    theirs, summed = lax.optimization_barrier((theirs, summed))
+    packed = jnp.concatenate([packed, theirs], axis=0)
     summed = summed.reshape(shard, chans)
     w_entry = packed[:, :chans]
     w_conv = packed[:, chans : 4 * chans].reshape(bot, 3, chans)
@@ -100,12 +101,8 @@
 
     ext = jnp.concatenate([from_prev, edge_in, from_next], axis=0)
     ext_feats = ext[:, :chans]
-    ext_bottle = (
-        ext[:, chans : chans + bot]
-        .reshape(-1, ny, nz, nc, shard)
-        .transpose(0, 3, 1, 2, 4)
-        .reshape(-1, bot)
-    )
+    ext_bottle = ext[:, chans : chans + bot].reshape(-1, ny, nz, nc, shard).transpose(0, 3, 1, 2, 4)
+    ext_bottle = jnp.where(lax.axis_index("c") == 0, ext_bottle, ext_bottle[:, ::-1]).reshape(-1, bot)
     ext_jitter = ext[:, chans + bot :]
 
     baseline = ext_feats.astype(jnp.float32) + jnp.dot(

time: 194 us -> 202 us (1.041)
  local copies, waits for them, and re-layouts: 13.1 us -> 20.7 us
  waiting for transfers between devices: 54.3 us -> 48.7 us
  starting transfers between devices: 34.9 us -> 39.7 us
    ppermute x9 -> x10, starting transfers between devices: 32.1 us -> 37 us  [_swap(): return lax.ppermute(x, axis, [(i, i ^ d) for i in range(n)])]
    concatenate x0 -> x1, local copies, waits for them, and re-layouts: none -> 3.62 us  [body(): packed = jnp.concatenate([packed, theirs], axis=0)]
    ppermute x9 -> x10, waiting for transfers between devices: 41.9 us -> 38.6 us  [_swap(): return lax.ppermute(x, axis, [(i, i ^ d) for i in range(n)])]
    unnamed x24 -> x23, local copies, waits for them, and re-layouts: 6.06 us -> 8.5 us
    slice x3 -> x2, local copies, waits for them, and re-layouts: 5.63 us -> 5.91 us  [body(): w_conv = packed[:, chans:4 * chans].reshape(bot, 3, chans)]
  transfers between devices with their start and end apart: 13 -> 13, of which waited for: 11 -> 10; matrix products, arithmetic and copies ran while one was open for 5% -> 8% of each run, Pallas kernels for 0% -> 0%
where the time goes in v12:
time: 202 us; the launch traced here: 201 us
  blocking collectives  51 us (25%)
  waiting for transfers between devices  48.7 us (24%)
  starting transfers between devices  39.7 us (20%)
  local copies, waits for them, and re-layouts  20.7 us (10%)
  between operations  15.9 us (8%)
  other arithmetic  13.1 us (6%)
  matrix products  11.9 us (6%)
    ppermute x10, waiting for transfers between devices, _swap(): return lax.ppermute(x, axis, [(i, i ^ d) for i in range(n)])  38.6 us
    ppermute x10, starting transfers between devices, _swap(): return lax.ppermute(x, axis, [(i, i ^ d) for i in range(n)])  37 us
    psum x3, blocking collectives, body(): gap = lax.psum(gap, axis)  33 us
    all_gather x1, blocking collectives, body(): packed = lax.all_gather(packed, axis, axis=0, tiled=True)  17.9 us
    all_gather x1, waiting for transfers between devices, body(): packed = lax.all_gather(packed, axis, axis=0, tiled=True)  10 us
    unnamed x23, local copies, waits for them, and re-layouts  8.5 us
    slice x2, local copies, waits for them, and re-layouts, body(): w_conv = packed[:, chans:4 * chans].reshape(bot, 3, chans)  5.91 us
    dot_general x1, matrix products, body(): jnp.dot(inner, w_exit, preferred_element_type=jnp.float32)  5.5 us
  transfers between devices with their start and end apart: 13, of which 10 were waited for; matrix products, arithmetic and copies ran while one was open for 8% of the time, Pallas kernels for 0%

profile of v12, /device:TPU:2, one launch (start us, length us, event | category | flops | bytes accessed | tf_op | source)
XLA Modules:
  0.0 201.0 jit_solution(8276798701286533841)
XLA Ops:
  8.2 17.9 %all-gather = bf16[4,6,7680]{2,1,0:T(8,128)(2,1)S(1)} all-gather(bf16[1,6,7680]{2,1,0:T(8,128)(2,1)S(1)} %maximum_bitcast_fusion), channel_id=1, replica_groups=mesh['y'=8,'zl'=4,'c'=2,'zh'=2,'x'=4] {'zl'}, dimensions={0}, use_global_device_ids=true | all-gather | bytes 460800 | tf_op jit(solution)/shard_map/all_gather | solution.py:79
  38.2 4.1 %collective-permute-start.1 = (bf16[2,2,2,2,1,1,6,1536]{7,6,5,4,3,2,1,0:T(8,128)(2,1)S(1)}, bf16[2,2,2,2,1,1,6,1536]{7,6,5,4,3,2,1,0:T(8,128)(2,1)S(1)}, u32[]{:S(2)}, u32[]{:S(2)}) collective-permute-start(bf16[2,2,2,2,1,1,6,1536]{7,6,5,4,3,2,1,0:T(8,128)(2,1)S(1)} %dynamic-slice_convert_fusion), channel_id=1, source_target_pairs={{0,16},{16,0},{32,48},{48,32},{1,17},{17,1},{33,49},{49,33},{2,18}... | collective-permute-start | bytes 884744 | tf_op jit(solution)/shard_map/ppermute | solution.py:24
  42.3 9.4 %collective-permute-done.1 = bf16[2,2,2,2,1,1,6,1536]{7,6,5,4,3,2,1,0:T(8,128)(2,1)S(1)} collective-permute-done((bf16[2,2,2,2,1,1,6,1536]{7,6,5,4,3,2,1,0:T(8,128)(2,1)S(1)}, bf16[2,2,2,2,1,1,6,1536]{7,6,5,4,3,2,1,0:T(8,128)(2,1)S(1)}, u32[]{:S(2)}, u32[]{:S(2)}) %collective-permute-start.1) | collective-permute-done | bytes 294944 | tf_op jit(solution)/shard_map/ppermute | solution.py:24
  53.0 4.4 %collective-permute-start.2 = (bf16[2,2,2,1,1,1,6,1536]{7,6,5,4,3,2,1,0:T(8,128)(2,1)S(1)}, bf16[2,2,2,1,1,1,6,1536]{7,6,5,4,3,2,1,0:T(8,128)(2,1)}, u32[]{:S(2)}, u32[]{:S(2)}) collective-permute-start(bf16[2,2,2,1,1,1,6,1536]{7,6,5,4,3,2,1,0:T(8,128)(2,1)S(1)} %dynamic-slice_convert_fusion.1), channel_id=1, source_target_pairs={{0,32},{16,48},{32,0},{48,16},{1,33},{17,49},{33,1},{49,17},{2,34}... | collective-permute-start | bytes 442376 | tf_op jit(solution)/shard_map/ppermute | solution.py:24
  60.3 6.4 %collective-permute-done.2 = bf16[2,2,2,1,1,1,6,1536]{7,6,5,4,3,2,1,0:T(8,128)(2,1)} collective-permute-done((bf16[2,2,2,1,1,1,6,1536]{7,6,5,4,3,2,1,0:T(8,128)(2,1)S(1)}, bf16[2,2,2,1,1,1,6,1536]{7,6,5,4,3,2,1,0:T(8,128)(2,1)}, u32[]{:S(2)}, u32[]{:S(2)}) %collective-permute-start.2) | collective-permute-done | bytes 147488 | tf_op jit(solution)/shard_map/ppermute | solution.py:24
  67.8 10.0 %all-gather.3.cloned.1.call-done = bf16[192,7680]{1,0:T(8,128)(2,1)} async-done(((bf16[24,7680]{1,0:T(8,128)(2,1)}), bf16[192,7680]{1,0:T(8,128)(2,1)}) %all-gather.3.cloned.1.call-update) | async-done | bytes 2949136 | tf_op jit(solution)/shard_map/all_gather | solution.py:79
  79.7 3.6 %constant_dynamic-update-slice_fusion.1 = bf16[384,7680]{1,0:T(8,128)(2,1)} fusion(bf16[192,7680]{1,0:T(8,128)(2,1)} %all-gather.3.cloned.1.call-done), kind=kLoop, calls=%fused_computation.69 | loop fusion | bytes 5898240
  83.3 3.4 %collective-permute-start.6 = (bf16[2,2,1,1,1,1,6,1536]{7,6,5,4,3,2,1,0:T(8,128)(2,1)S(1)}, bf16[2,2,1,1,1,1,6,1536]{7,6,5,4,3,2,1,0:T(8,128)(2,1)S(1)}, u32[]{:S(2)}, u32[]{:S(2)}) collective-permute-start(bf16[2,2,1,1,1,1,6,1536]{7,6,5,4,3,2,1,0:T(8,128)(2,1)S(1)} %dynamic-slice_convert_fusion.2), channel_id=1, source_target_pairs={{0,64},{64,0},{128,192},{192,128},{256,320},{320,256},{384,448},{4... | collective-permute-start | bytes 221192 | tf_op jit(solution)/shard_map/ppermute | solution.py:24
  90.4 4.3 %collective-permute-start.7 = (bf16[2,1,1,1,1,1,6,1536]{7,6,5,4,3,2,1,0:T(8,128)(2,1)S(1)}, bf16[2,1,1,1,1,1,6,1536]{7,6,5,4,3,2,1,0:T(8,128)(2,1)S(1)}, u32[]{:S(2)}, u32[]{:S(2)}) collective-permute-start(bf16[2,1,1,1,1,1,6,1536]{7,6,5,4,3,2,1,0:T(8,128)(2,1)S(1)} %dynamic-slice_convert_fusion.3), channel_id=1, source_target_pairs={{0,128},{64,192},{128,0},{192,64},{256,384},{320,448},{384,256},{4... | collective-permute-start | bytes 110600 | tf_op jit(solution)/shard_map/ppermute | solution.py:24
  97.6 5.5 %collective-permute-start.8 = (bf16[1,1,1,1,1,1,6,1536]{7,6,5,4,3,2,1,0:T(8,128)(2,1)S(1)}, bf16[1,1,1,1,1,1,6,1536]{7,6,5,4,3,2,1,0:T(8,128)(2,1)S(1)}, u32[]{:S(2)}, u32[]{:S(2)}) collective-permute-start(bf16[1,1,1,1,1,1,6,1536]{7,6,5,4,3,2,1,0:T(8,128)(2,1)S(1)} %dynamic-slice_convert_fusion.4), channel_id=1, source_target_pairs={{0,256},{64,320},{128,384},{192,448},{256,0},{320,64},{384,128},{4... | collective-permute-start | bytes 55304 | tf_op jit(solution)/shard_map/ppermute | solution.py:24
  104.0 3.3 %collective-permute-done.8 = bf16[1,1,1,1,1,1,6,1536]{7,6,5,4,3,2,1,0:T(8,128)(2,1)S(1)} collective-permute-done((bf16[1,1,1,1,1,1,6,1536]{7,6,5,4,3,2,1,0:T(8,128)(2,1)S(1)}, bf16[1,1,1,1,1,1,6,1536]{7,6,5,4,3,2,1,0:T(8,128)(2,1)S(1)}, u32[]{:S(2)}, u32[]{:S(2)}) %collective-permute-start.8) | collective-permute-done | bytes 18464 | tf_op jit(solution)/shard_map/ppermute | solution.py:24
  107.9 3.6 %constant_dynamic-update-slice_fusion = bf16[384,7680]{1,0:T(8,128)(2,1)} fusion(bf16[384,7680]{1,0:T(8,128)(2,1)} %constant_dynamic-update-slice_fusion.1, bf16[192,7680]{1,0:T(8,128)(2,1)} %collective-permute-done.5), kind=kLoop, calls=%fused_computation.68 | loop fusion | bytes 5898240 | tf_op jit(solution)/shard_map/concatenate | solution.py:96
  113.8 3.7 %copy.31 = bf16[384,4608]{0,1:T(8,128)(2,1)} copy(bf16[384,4608]{1,0:T(8,128)(2,1)S(1)} %slice.73) | data formatting | bytes 7077888 | tf_op jit(solution)/shard_map/slice | solution.py:99
  126.1 5.5 %convolution_add_fusion = f32[2,192,1536]{2,1,0:T(8,128)} fusion(f32[1,256,1536]{2,1,0:T(8,128)} %copy-done.5, f32[1,256,1536]{2,1,0:T(8,128)} %copy-done.4, bf16[384,7680]{1,0:T(8,128)(2,1)} %constant_dynamic-update-slice_fusion, f32[2,192,384]{2,1,0:T(8,128)} %convolution_add_fusion.3, bf16[384,3,1536]{0,2,1:T(8,128)(2,1)S(1)} %bitcast.66, ...), kind=kOutput, calls=%fused_computation.12 | convolution fusion | flops 908623872 | bytes 9633792 | tf_op jit(solution)/shard_map/dot_general | solution.py:124
  131.6 3.6 %multiply_reduce_fusion = (f32[]{:T(128)}, bf16[1,192,1536]{2,1,0:T(8,128)(2,1)}) fusion(bf16[1,192,1536]{2,1,0:T(8,128)(2,1)} %param.10, f32[2,192,1536]{2,1,0:T(8,128)} %convolution_add_fusion), kind=kLoop, calls=%fused_computation.32 | loop fusion | flops 2654207 | bytes 3538948 | tf_op jit(solution)/shard_map/reduce_sum | solution.py:130
  135.8 3.0 %psum.21 = f32[]{:T(128)} all-reduce(f32[]{:T(128)S(6)} %div.40), channel_id=1, replica_groups=mesh['y'=8,'zl'=4,'c'=2,'zh'=2,'x'=4] {'c'}, use_global_device_ids=true, to_apply=%region_1.2 | all-reduce | flops 1 | bytes 8 | tf_op jit(solution)/shard_map/psum | solution.py:133
  138.8 13.6 %psum.22 = f32[]{:T(128)} all-reduce(f32[]{:T(128)} %psum.21), channel_id=1, replica_groups=mesh['y'=8,'zl'=4,'c'=2,'zh'=2,'x'=4] {'zl'}, use_global_device_ids=true, to_apply=%region_2.3 | all-reduce | flops 1 | bytes 8 | tf_op jit(solution)/shard_map/psum | solution.py:133
  152.4 16.4 %psum.23 = f32[]{:T(128)} all-reduce(f32[]{:T(128)} %psum.22), channel_id=1, replica_groups=mesh['y'=8,'zl'=4,'c'=2,'zh'=2,'x'=4] {'y'}, use_global_device_ids=true, to_apply=%region_3.4 | all-reduce | flops 1 | bytes 8 | tf_op jit(solution)/shard_map/psum | solution.py:133
  169.5 2.8 %collective-permute-start.9 = (f32[6,1536]{1,0:T(8,128)S(1)}, f32[6,1536]{1,0:T(8,128)S(1)}, u32[]{:S(2)}, u32[]{:S(2)}) collective-permute-start(f32[6,1536]{1,0:T(8,128)S(1)} %multiply_bitcast_fusion), channel_id=1, source_target_pairs={{0,1},{1,0},{2,3},{3,2},{4,5},{5,4},{6,7},{7,6},{8,9},{9,8},{10,11... | collective-permute-start | bytes 110600 | tf_op jit(solution)/shard_map/ppermute | solution.py:24
  172.3 3.7 %collective-permute-done.9 = f32[6,1536]{1,0:T(8,128)S(1)} collective-permute-done((f32[6,1536]{1,0:T(8,128)S(1)}, f32[6,1536]{1,0:T(8,128)S(1)}, u32[]{:S(2)}, u32[]{:S(2)}) %collective-permute-start.9) | collective-permute-done | bytes 36896 | tf_op jit(solution)/shard_map/ppermute | solution.py:24
  176.0 3.8 %collective-permute-start.10 = (f32[6,1536]{1,0:T(8,128)S(1)}, f32[6,1536]{1,0:T(8,128)S(1)}, u32[]{:S(2)}, u32[]{:S(2)}) collective-permute-start(f32[6,1536]{1,0:T(8,128)S(1)} %fusion.42), channel_id=1, source_target_pairs={{0,2},{1,3},{2,0},{3,1},{4,6},{5,7},{6,4},{7,5},{8,10},{9,11},{10,... | collective-permute-start | bytes 110600 | tf_op jit(solution)/shard_map/ppermute | solution.py:24
  179.8 3.6 %collective-permute-done.10 = f32[6,1536]{1,0:T(8,128)S(1)} collective-permute-done((f32[6,1536]{1,0:T(8,128)S(1)}, f32[6,1536]{1,0:T(8,128)S(1)}, u32[]{:S(2)}, u32[]{:S(2)}) %collective-permute-start.10) | collective-permute-done | bytes 36896 | tf_op jit(solution)/shard_map/ppermute | solution.py:24
  183.5 4.9 %collective-permute-start.11 = (f32[6,1536]{1,0:T(8,128)S(1)}, f32[6,1536]{1,0:T(8,128)S(1)}, u32[]{:S(2)}, u32[]{:S(2)}) collective-permute-start(f32[6,1536]{1,0:T(8,128)S(1)} %add.182), channel_id=1, source_target_pairs={{0,4},{4,0},{1,5},{5,1},{2,6},{6,2},{3,7},{7,3},{8,12},{12,8},{9,1... | collective-permute-start | bytes 110600 | tf_op jit(solution)/shard_map/ppermute | solution.py:24
  188.3 5.2 %collective-permute-done.11 = f32[6,1536]{1,0:T(8,128)S(1)} collective-permute-done((f32[6,1536]{1,0:T(8,128)S(1)}, f32[6,1536]{1,0:T(8,128)S(1)}, u32[]{:S(2)}, u32[]{:S(2)}) %collective-permute-start.11) | collective-permute-done | bytes 36896 | tf_op jit(solution)/shard_map/ppermute | solution.py:24
  (67 shorter events, 39.4 us)
Async XLA Ops:
  7.2 19.9 %copy-start.3 = (bf16[1,192,384]{2,1,0:T(8,128)(2,1)S(1)}, bf16[1,192,384]{2,1,0:T(8,128)(2,1)}, u32[]{:S(2)}) copy-start(bf16[1,192,384]{2,1,0:T(8,128)(2,1)} %param.8) | copy-start | bytes 442372
  7.2 70.6 %all-gather.3.cloned.1.call-start = ((), (), s32[]{:S(2)}) async-start(), calls=%async_computation | async-start | bytes 3317760 | tf_op jit(solution)/shard_map/all_gather | solution.py:79
  30.2 4.2 %collective-permute-start = (bf16[2,2,2,2,2,1,6,1536]{7,4,6,5,3,2,1,0:T(2,128)(2,1)}, bf16[2,2,2,2,2,1,6,1536]{7,4,6,5,3,2,1,0:T(2,128)(2,1)}, u32[]{:S(2)}, u32[]{:S(2)}) collective-permute-start(bf16[2,2,2,2,2,1,6,1536]{7,4,6,5,3,2,1,0:T(2,128)(2,1)} %copy.42), channel_id=1, source_target_pairs={{0,8},{8,0},{1,9},{9,1},{2,10},{10,2},{3,11},{11,3},{4,12},{12,4},... | collective-permute-start | bytes 1769480 | tf_op jit(solution)/shard_map/ppermute | solution.py:24
  36.9 20.5 %copy-start = (bf16[1,192,1536]{2,1,0:T(8,128)(2,1)S(1)}, bf16[1,192,1536]{2,1,0:T(8,128)(2,1)}, u32[]{:S(2)}) copy-start(bf16[1,192,1536]{2,1,0:T(8,128)(2,1)} %param.9) | copy-start | bytes 1769476
  36.9 20.5 %copy-start.1 = (bf16[1,192,1536]{2,1,0:T(8,128)(2,1)S(1)}, bf16[1,192,1536]{2,1,0:T(8,128)(2,1)}, u32[]{:S(2)}) copy-start(bf16[1,192,1536]{2,1,0:T(8,128)(2,1)} %param.7) | copy-start | bytes 1769476
  38.2 13.5 %collective-permute-start.1 = (bf16[2,2,2,2,1,1,6,1536]{7,6,5,4,3,2,1,0:T(8,128)(2,1)S(1)}, bf16[2,2,2,2,1,1,6,1536]{7,6,5,4,3,2,1,0:T(8,128)(2,1)S(1)}, u32[]{:S(2)}, u32[]{:S(2)}) collective-permute-start(bf16[2,2,2,2,1,1,6,1536]{7,6,5,4,3,2,1,0:T(8,128)(2,1)S(1)} %dynamic-slice_convert_fusion), channel_id=1, source_target_pairs={{0,16},{16,0},{32,48},{48,32},{1,17},{17,1},{33,49},{49,33},{2,18}... | collective-permute-start | bytes 884744 | tf_op jit(solution)/shard_map/ppermute | solution.py:24
  53.0 13.7 %collective-permute-start.2 = (bf16[2,2,2,1,1,1,6,1536]{7,6,5,4,3,2,1,0:T(8,128)(2,1)S(1)}, bf16[2,2,2,1,1,1,6,1536]{7,6,5,4,3,2,1,0:T(8,128)(2,1)}, u32[]{:S(2)}, u32[]{:S(2)}) collective-permute-start(bf16[2,2,2,1,1,1,6,1536]{7,6,5,4,3,2,1,0:T(8,128)(2,1)S(1)} %dynamic-slice_convert_fusion.1), channel_id=1, source_target_pairs={{0,32},{16,48},{32,0},{48,16},{1,33},{17,49},{33,1},{49,17},{2,34}... | collective-permute-start | bytes 442376 | tf_op jit(solution)/shard_map/ppermute | solution.py:24
  57.5 10.2 %collective-permute-start.3 = (bf16[32,3456]{1,0:T(8,128)(2,1)S(1)}, bf16[32,3456]{1,0:T(8,128)(2,1)S(1)}, u32[]{:S(2)}, u32[]{:S(2)}) collective-permute-start(bf16[32,3456]{1,0:T(8,128)(2,1)S(1)} %get-tuple-element.19), channel_id=1, source_target_pairs={{0,8},{8,16},{16,24},{24,32},{32,40},{40,48},{48,56},{56,64},{64,7... | collective-permute-start | bytes 663560 | tf_op jit(solution)/shard_map/ppermute | solution.py:85
  58.9 8.8 %collective-permute-start.4 = (bf16[32,3456]{1,0:T(8,128)(2,1)S(1)}, bf16[32,3456]{1,0:T(8,128)(2,1)S(1)}, u32[]{:S(2)}, u32[]{:S(2)}) collective-permute-start(bf16[32,3456]{1,0:T(8,128)(2,1)S(1)} %get-tuple-element.18), channel_id=1, source_target_pairs={{8,0},{16,8},{24,16},{32,24},{40,32},{48,40},{56,48},{64,56},{72,6... | collective-permute-start | bytes 663560 | tf_op jit(solution)/shard_map/ppermute | solution.py:86
  67.7 27.0 %copy-start.7 = (bf16[32,3456]{1,0:T(8,128)(2,1)}, bf16[32,3456]{1,0:T(8,128)(2,1)S(1)}, u32[]{:S(2)}) copy-start(bf16[32,3456]{1,0:T(8,128)(2,1)S(1)} %collective-permute-done.3) | copy-start | bytes 663556
  67.7 27.0 %copy-start.8 = (bf16[32,3456]{1,0:T(8,128)(2,1)}, bf16[32,3456]{1,0:T(8,128)(2,1)S(1)}, u32[]{:S(2)}) copy-start(bf16[32,3456]{1,0:T(8,128)(2,1)S(1)} %collective-permute-done.4) | copy-start | bytes 663556
  77.8 30.1 %collective-permute-start.5 = (bf16[192,7680]{1,0:T(8,128)(2,1)}, bf16[192,7680]{1,0:T(8,128)(2,1)}, u32[]{:S(2)}, u32[]{:S(2)}) collective-permute-start(bf16[192,7680]{1,0:T(8,128)(2,1)} %all-gather.3.cloned.1.call-done), channel_id=1, source_target_pairs={{0,8},{8,0},{1,9},{9,1},{2,10},{10,2},{3,11},{11,3},{4,12},{12,4},... | collective-permute-start | bytes 8847368 | tf_op jit(solution)/shard_map/ppermute | solution.py:24
  83.3 7.1 %collective-permute-start.6 = (bf16[2,2,1,1,1,1,6,1536]{7,6,5,4,3,2,1,0:T(8,128)(2,1)S(1)}, bf16[2,2,1,1,1,1,6,1536]{7,6,5,4,3,2,1,0:T(8,128)(2,1)S(1)}, u32[]{:S(2)}, u32[]{:S(2)}) collective-permute-start(bf16[2,2,1,1,1,1,6,1536]{7,6,5,4,3,2,1,0:T(8,128)(2,1)S(1)} %dynamic-slice_convert_fusion.2), channel_id=1, source_target_pairs={{0,64},{64,0},{128,192},{192,128},{256,320},{320,256},{384,448},{4... | collective-permute-start | bytes 221192 | tf_op jit(solution)/shard_map/ppermute | solution.py:24
  90.4 7.1 %collective-permute-start.7 = (bf16[2,1,1,1,1,1,6,1536]{7,6,5,4,3,2,1,0:T(8,128)(2,1)S(1)}, bf16[2,1,1,1,1,1,6,1536]{7,6,5,4,3,2,1,0:T(8,128)(2,1)S(1)}, u32[]{:S(2)}, u32[]{:S(2)}) collective-permute-start(bf16[2,1,1,1,1,1,6,1536]{7,6,5,4,3,2,1,0:T(8,128)(2,1)S(1)} %dynamic-slice_convert_fusion.3), channel_id=1, source_target_pairs={{0,128},{64,192},{128,0},{192,64},{256,384},{320,448},{384,256},{4... | collective-permute-start | bytes 110600 | tf_op jit(solution)/shard_map/ppermute | solution.py:24
  97.6 9.7 %collective-permute-start.8 = (bf16[1,1,1,1,1,1,6,1536]{7,6,5,4,3,2,1,0:T(8,128)(2,1)S(1)}, bf16[1,1,1,1,1,1,6,1536]{7,6,5,4,3,2,1,0:T(8,128)(2,1)S(1)}, u32[]{:S(2)}, u32[]{:S(2)}) collective-permute-start(bf16[1,1,1,1,1,1,6,1536]{7,6,5,4,3,2,1,0:T(8,128)(2,1)S(1)} %dynamic-slice_convert_fusion.4), channel_id=1, source_target_pairs={{0,256},{64,320},{128,384},{192,448},{256,0},{320,64},{384,128},{4... | collective-permute-start | bytes 55304 | tf_op jit(solution)/shard_map/ppermute | solution.py:24
  120.0 1.2 copy-start.4
  120.0 1.6 copy-start.5
  120.0 3.7 %copy-start.2 = (bf16[384,4608]{0,1:T(8,128)(2,1)S(1)}, bf16[384,4608]{0,1:T(8,128)(2,1)}, u32[]{:S(2)}) copy-start(bf16[384,4608]{0,1:T(8,128)(2,1)} %copy.31) | copy-start | bytes 10616836
  121.6 2.8 %copy-start.6 = (bf16[2,256,1536]{2,1,0:T(8,128)(2,1)}, bf16[2,256,1536]{2,1,0:T(8,128)(2,1)S(1)}, u32[]{:S(2)}) copy-start(bf16[2,256,1536]{2,1,0:T(8,128)(2,1)S(1)} %fusion.7) | copy-start | bytes 4718596
  131.6 37.9 %copy-start.9 = (f32[1,1,1,1,1,1,6,1536]{7,6,5,4,3,2,1,0:T(8,128)S(1)}, f32[1,1,1,1,1,1,6,1536]{7,6,5,4,3,2,1,0:T(8,128)}, u32[]{:S(2)}) copy-start(f32[1,1,1,1,1,1,6,1536]{7,6,5,4,3,2,1,0:T(8,128)} %convert_add_fusion.5) | copy-start | bytes 110596
  169.5 6.4 %collective-permute-start.9 = (f32[6,1536]{1,0:T(8,128)S(1)}, f32[6,1536]{1,0:T(8,128)S(1)}, u32[]{:S(2)}, u32[]{:S(2)}) collective-permute-start(f32[6,1536]{1,0:T(8,128)S(1)} %multiply_bitcast_fusion), channel_id=1, source_target_pairs={{0,1},{1,0},{2,3},{3,2},{4,5},{5,4},{6,7},{7,6},{8,9},{9,8},{10,11... | collective-permute-start | bytes 110600 | tf_op jit(solution)/shard_map/ppermute | solution.py:24
  176.0 7.5 %collective-permute-start.10 = (f32[6,1536]{1,0:T(8,128)S(1)}, f32[6,1536]{1,0:T(8,128)S(1)}, u32[]{:S(2)}, u32[]{:S(2)}) collective-permute-start(f32[6,1536]{1,0:T(8,128)S(1)} %fusion.42), channel_id=1, source_target_pairs={{0,2},{1,3},{2,0},{3,1},{4,6},{5,7},{6,4},{7,5},{8,10},{9,11},{10,... | collective-permute-start | bytes 110600 | tf_op jit(solution)/shard_map/ppermute | solution.py:24
  183.5 10.1 %collective-permute-start.11 = (f32[6,1536]{1,0:T(8,128)S(1)}, f32[6,1536]{1,0:T(8,128)S(1)}, u32[]{:S(2)}, u32[]{:S(2)}) collective-permute-start(f32[6,1536]{1,0:T(8,128)S(1)} %add.182), channel_id=1, source_target_pairs={{0,4},{4,0},{1,5},{5,1},{2,6},{6,2},{3,7},{7,3},{8,12},{12,8},{9,1... | collective-permute-start | bytes 110600 | tf_op jit(solution)/shard_map/ppermute | solution.py:24
Sparse Core Ops, SparseCore 0:
  27.1 50.5 all-gather.2

commit v13 on v12

--- a/solution.py
+++ b/solution.py
@@ -75,8 +75,9 @@
 
     conv_rows = conv_filters.transpose(2, 0, 1).reshape(shard, -1)
     packed = jnp.concatenate([entry_weight, conv_rows, exit_weight], axis=1)
-    for axis in ("zl", "y"):
-        packed = lax.all_gather(packed, axis, axis=0, tiled=True)
+    packed = lax.all_gather(packed, "zl", axis=0, tiled=True)
+    for d in (4, 2, 1):
+        packed = jnp.concatenate([packed, _swap(packed, "y", d)], axis=0)
 
     spacing = DILATION
     edge_in = jnp.concatenate([feats, bottle, jitter], axis=1)
@@ -101,8 +102,11 @@
 
     ext = jnp.concatenate([from_prev, edge_in, from_next], axis=0)
     ext_feats = ext[:, :chans]
-    ext_bottle = ext[:, chans : chans + bot].reshape(-1, ny, nz, nc, shard).transpose(0, 3, 1, 2, 4)
-    ext_bottle = jnp.where(lax.axis_index("c") == 0, ext_bottle, ext_bottle[:, ::-1]).reshape(-1, bot)
+    ys = jnp.array([int(format(p, "03b")[::-1], 2) for p in range(ny)], jnp.int32) ^ lax.axis_index("y")
+    cs = jnp.arange(nc, dtype=jnp.int32) ^ lax.axis_index("c")
+    ext_bottle = ext[:, chans : chans + bot].reshape(-1, ny, nz, nc, shard)
+    ext_bottle = jnp.take(jnp.take(ext_bottle, ys, axis=1), cs, axis=3)
+    ext_bottle = ext_bottle.transpose(0, 3, 1, 2, 4).reshape(-1, bot)
     ext_jitter = ext[:, chans + bot :]
 
     baseline = ext_feats.astype(jnp.float32) + jnp.dot(

time: 202 us -> 235 us (1.16)
  waiting for transfers between devices: 48.7 us -> 77.8 us
  starting transfers between devices: 39.7 us -> 54 us
  between operations: 15.9 us -> 2.64 us
  other arithmetic: 13.1 us -> 18.5 us
  blocking collectives: 51 us -> 47.7 us
    ppermute x10 -> x13, waiting for transfers between devices: 38.6 us -> 77.8 us  [_swap(): return lax.ppermute(x, axis, [(i, i ^ d) for i in range(n)])]
    ppermute x10 -> x13, starting transfers between devices: 37 us -> 49.7 us  [_swap(): return lax.ppermute(x, axis, [(i, i ^ d) for i in range(n)])]
    all_gather x1 -> x0, waiting for transfers between devices: 10 us -> none  [body(): packed = lax.all_gather(packed, axis, axis=0, tiled=True)]
    concatenate x0 -> x3, other arithmetic: none -> 4.13 us  [body(): packed = jnp.concatenate([packed, _swap(packed, 'y', d)], axis=0)]
    psum x3, blocking collectives: 33 us -> 29.8 us  [body(): gap = lax.psum(gap, axis)]
    unnamed x23 -> x33, local copies, waits for them, and re-layouts: 8.5 us -> 5.95 us
  transfers between devices with their start and end apart: 13 -> 15, of which waited for: 10 -> 8; matrix products, arithmetic and copies ran while one was open for 8% -> 9% of each run, Pallas kernels for 0% -> 0%
where the time goes in v13:
time: 235 us; the launch traced here: 234 us
  waiting for transfers between devices  77.8 us (33%)
  starting transfers between devices  54 us (23%)
  blocking collectives  47.7 us (20%)
  local copies, waits for them, and re-layouts  21.5 us (9%)
  other arithmetic  18.5 us (8%)
  matrix products  12 us (5%)
  between operations  2.64 us (1%)
    ppermute x13, waiting for transfers between devices, _swap(): return lax.ppermute(x, axis, [(i, i ^ d) for i in range(n)])  77.8 us
    ppermute x13, starting transfers between devices, _swap(): return lax.ppermute(x, axis, [(i, i ^ d) for i in range(n)])  49.7 us
    psum x3, blocking collectives, body(): gap = lax.psum(gap, axis)  29.8 us
    all_gather x1, blocking collectives, body(): packed = lax.all_gather(packed, 'zl', axis=0, tiled=True)  17.9 us
    unnamed x33, local copies, waits for them, and re-layouts  5.95 us
    slice x2, local copies, waits for them, and re-layouts, body(): w_conv = packed[:, chans:4 * chans].reshape(bot, 3, chans)  5.86 us
    dot_general x1, matrix products, body(): jnp.dot(inner, w_exit, preferred_element_type=jnp.float32)  5.49 us
  transfers between devices with their start and end apart: 15, of which 8 were waited for; matrix products, arithmetic and copies ran while one was open for 9% of the time, Pallas kernels for 0%

profile of v13, /device:TPU:2, one launch (start us, length us, event | category | flops | bytes accessed | tf_op | source)
XLA Modules:
  0.0 234.1 jit_solution(16364318888008466001)
XLA Ops:
  1.6 17.9 %all-gather = bf16[4,6,7680]{2,1,0:T(8,128)(2,1)S(1)} all-gather(bf16[1,6,7680]{2,1,0:T(8,128)(2,1)S(1)} %maximum_bitcast_fusion), channel_id=1, replica_groups=mesh['y'=8,'zl'=4,'c'=2,'zh'=2,'x'=4] {'zl'}, dimensions={0}, use_global_device_ids=true | all-gather | bytes 460800 | tf_op jit(solution)/shard_map/all_gather | solution.py:78
  19.7 7.7 %collective-permute-start = (bf16[24,7680]{1,0:T(8,128)(2,1)S(1)}, bf16[24,7680]{1,0:T(8,128)(2,1)}, u32[]{:S(2)}, u32[]{:S(2)}) collective-permute-start(bf16[24,7680]{1,0:T(8,128)(2,1)S(1)} %reshape.76), channel_id=1, source_target_pairs={{0,256},{64,320},{128,384},{192,448},{256,0},{320,64},{384,128},{4... | collective-permute-start | bytes 1105928 | tf_op jit(solution)/shard_map/ppermute | solution.py:24
  34.2 3.1 %collective-permute-start.6 = (bf16[32,3456]{1,0:T(8,128)(2,1)}, bf16[32,3456]{1,0:T(8,128)(2,1)}, u32[]{:S(2)}, u32[]{:S(2)}) collective-permute-start(bf16[32,3456]{1,0:T(8,128)(2,1)} %get-tuple-element.21), channel_id=1, source_target_pairs={{0,8},{8,16},{16,24},{24,32},{32,40},{40,48},{48,56},{56,64},{64,7... | collective-permute-start | bytes 663560 | tf_op jit(solution)/shard_map/ppermute | solution.py:86
  39.7 7.8 %collective-permute-start.1 = (bf16[48,7680]{1,0:T(8,128)(2,1)S(1)}, bf16[48,7680]{1,0:T(8,128)(2,1)S(1)}, u32[]{:S(2)}, u32[]{:S(2)}) collective-permute-start(bf16[48,7680]{1,0:T(8,128)(2,1)S(1)} %pad_maximum_fusion.5), channel_id=1, source_target_pairs={{0,128},{64,192},{128,0},{192,64},{256,384},{320,448},{384,256},{4... | collective-permute-start | bytes 2211848 | tf_op jit(solution)/shard_map/ppermute | solution.py:24
  50.8 28.7 %collective-permute-done.1 = bf16[48,7680]{1,0:T(8,128)(2,1)S(1)} collective-permute-done((bf16[48,7680]{1,0:T(8,128)(2,1)S(1)}, bf16[48,7680]{1,0:T(8,128)(2,1)S(1)}, u32[]{:S(2)}, u32[]{:S(2)}) %collective-permute-start.1) | collective-permute-done | bytes 737312 | tf_op jit(solution)/shard_map/ppermute | solution.py:24
  83.0 3.3 %collective-permute-start.5 = (bf16[2,2,2,1,1,1,6,1536]{7,6,5,4,3,2,1,0:T(8,128)(2,1)S(1)}, bf16[2,2,2,1,1,1,6,1536]{7,6,5,4,3,2,1,0:T(8,128)(2,1)S(1)}, u32[]{:S(2)}, u32[]{:S(2)}) collective-permute-start(bf16[2,2,2,1,1,1,6,1536]{7,6,5,4,3,2,1,0:T(8,128)(2,1)S(1)} %dynamic-slice_convert_fusion.1), channel_id=1, source_target_pairs={{0,32},{16,48},{32,0},{48,16},{1,33},{17,49},{33,1},{49,17},{2,34}... | collective-permute-start | bytes 442376 | tf_op jit(solution)/shard_map/ppermute | solution.py:24
  86.5 9.5 %collective-permute-done.5 = bf16[2,2,2,1,1,1,6,1536]{7,6,5,4,3,2,1,0:T(8,128)(2,1)S(1)} collective-permute-done((bf16[2,2,2,1,1,1,6,1536]{7,6,5,4,3,2,1,0:T(8,128)(2,1)S(1)}, bf16[2,2,2,1,1,1,6,1536]{7,6,5,4,3,2,1,0:T(8,128)(2,1)S(1)}, u32[]{:S(2)}, u32[]{:S(2)}) %collective-permute-start.5) | collective-permute-done | bytes 147488 | tf_op jit(solution)/shard_map/ppermute | solution.py:24
  96.0 20.9 %collective-permute-done.2 = bf16[96,7680]{1,0:T(8,128)(2,1)} collective-permute-done((bf16[96,7680]{1,0:T(8,128)(2,1)S(1)}, bf16[96,7680]{1,0:T(8,128)(2,1)}, u32[]{:S(2)}, u32[]{:S(2)}) %collective-permute-start.2) | collective-permute-done | bytes 1474592 | tf_op jit(solution)/shard_map/ppermute | solution.py:24
  135.0 5.0 %collective-permute-done.10 = bf16[2,1,1,1,1,1,6,1536]{7,6,5,4,3,2,1,0:T(8,128)(2,1)} collective-permute-done((bf16[2,1,1,1,1,1,6,1536]{7,6,5,4,3,2,1,0:T(8,128)(2,1)}, bf16[2,1,1,1,1,1,6,1536]{7,6,5,4,3,2,1,0:T(8,128)(2,1)}, u32[]{:S(2)}, u32[]{:S(2)}) %collective-permute-start.10) | collective-permute-done | bytes 36896 | tf_op jit(solution)/shard_map/ppermute | solution.py:24
  140.8 4.6 %collective-permute-start.11 = (bf16[1,1,1,1,1,1,6,1536]{7,6,5,4,3,2,1,0:T(8,128)(2,1)S(1)}, bf16[1,1,1,1,1,1,6,1536]{7,6,5,4,3,2,1,0:T(8,128)(2,1)S(1)}, u32[]{:S(2)}, u32[]{:S(2)}) collective-permute-start(bf16[1,1,1,1,1,1,6,1536]{7,6,5,4,3,2,1,0:T(8,128)(2,1)S(1)} %dynamic-slice_convert_fusion.4), channel_id=1, source_target_pairs={{0,256},{64,320},{128,384},{192,448},{256,0},{320,64},{384,128},{4... | collective-permute-start | bytes 55304 | tf_op jit(solution)/shard_map/ppermute | solution.py:24
  146.4 4.0 %collective-permute-done.11 = bf16[1,1,1,1,1,1,6,1536]{7,6,5,4,3,2,1,0:T(8,128)(2,1)S(1)} collective-permute-done((bf16[1,1,1,1,1,1,6,1536]{7,6,5,4,3,2,1,0:T(8,128)(2,1)S(1)}, bf16[1,1,1,1,1,1,6,1536]{7,6,5,4,3,2,1,0:T(8,128)(2,1)S(1)}, u32[]{:S(2)}, u32[]{:S(2)}) %collective-permute-start.11) | collective-permute-done | bytes 18464 | tf_op jit(solution)/shard_map/ppermute | solution.py:24
  151.1 3.6 %constant_dynamic-update-slice_fusion = bf16[384,7680]{1,0:T(8,128)(2,1)} fusion(bf16[384,7680]{1,0:T(8,128)(2,1)} %constant_dynamic-update-slice_fusion.1, bf16[192,7680]{1,0:T(8,128)(2,1)} %collective-permute-done.8), kind=kLoop, calls=%fused_computation.76 | loop fusion | bytes 5898240 | tf_op jit(solution)/shard_map/concatenate | solution.py:97
  157.0 3.6 %copy.45 = bf16[384,4608]{0,1:T(8,128)(2,1)} copy(bf16[384,4608]{1,0:T(8,128)(2,1)S(1)} %slice.77) | data formatting | bytes 7077888 | tf_op jit(solution)/shard_map/slice | solution.py:100
  160.6 2.5 %subtract_bitcast_fusion = (f32[1,256,1536]{2,1,0:T(8,128)S(1)}, f32[1,256,1536]{2,1,0:T(8,128)S(1)}) fusion(bf16[32,3456]{1,0:T(8,128)(2,1)} %collective-permute-done.7, bf16[192,1536]{1,0:T(8,128)(2,1)} %bitcast.61, bf16[192,384]{1,0:T(8,128)(2,1)} %bitcast.72, bf16[192,1536]{1,0:T(8,128)(2,1)} %bitcast.65, bf16[32,3456]{1,0:T(8,128)(2,1)} %collective-permute-done.6, ...), kind=kOutput, calls=%fused_computation.19 | convolution fusion | flops 307888128 | bytes 7077888 | tf_op jit(solution)/shard_map/dot_general | solution.py:112
  169.2 5.5 %convolution_add_fusion = f32[2,192,1536]{2,1,0:T(8,128)} fusion(f32[1,256,1536]{2,1,0:T(8,128)} %copy-done.10, f32[1,256,1536]{2,1,0:T(8,128)} %copy-done.9, bf16[384,7680]{1,0:T(8,128)(2,1)} %constant_dynamic-update-slice_fusion, f32[2,192,384]{2,1,0:T(8,128)} %convolution_add_fusion.3, bf16[384,3,1536]{0,2,1:T(8,128)(2,1)S(1)} %bitcast.71, ...), kind=kOutput, calls=%fused_computation.14 | convolution fusion | flops 908623872 | bytes 9633792 | tf_op jit(solution)/shard_map/dot_general | solution.py:128
  174.7 3.6 %multiply_reduce_fusion = (f32[]{:T(128)}, bf16[1,192,1536]{2,1,0:T(8,128)(2,1)}) fusion(bf16[1,192,1536]{2,1,0:T(8,128)(2,1)} %param.11, f32[2,192,1536]{2,1,0:T(8,128)} %convolution_add_fusion), kind=kLoop, calls=%fused_computation.36 | loop fusion | flops 2654207 | bytes 3538948 | tf_op jit(solution)/shard_map/reduce_sum | solution.py:134
  179.0 3.0 %psum.21 = f32[]{:T(128)} all-reduce(f32[]{:T(128)S(6)} %div.40), channel_id=1, replica_groups=mesh['y'=8,'zl'=4,'c'=2,'zh'=2,'x'=4] {'c'}, use_global_device_ids=true, to_apply=%region_1.2 | all-reduce | flops 1 | bytes 8 | tf_op jit(solution)/shard_map/psum | solution.py:137
  182.0 10.8 %psum.22 = f32[]{:T(128)} all-reduce(f32[]{:T(128)} %psum.21), channel_id=1, replica_groups=mesh['y'=8,'zl'=4,'c'=2,'zh'=2,'x'=4] {'zl'}, use_global_device_ids=true, to_apply=%region_2.3 | all-reduce | flops 1 | bytes 8 | tf_op jit(solution)/shard_map/psum | solution.py:137
  192.7 16.0 %psum.23 = f32[]{:T(128)} all-reduce(f32[]{:T(128)} %psum.22), channel_id=1, replica_groups=mesh['y'=8,'zl'=4,'c'=2,'zh'=2,'x'=4] {'y'}, use_global_device_ids=true, to_apply=%region_3.4 | all-reduce | flops 1 | bytes 8 | tf_op jit(solution)/shard_map/psum | solution.py:137
  209.4 2.4 %collective-permute-start.12 = (f32[6,1536]{1,0:T(8,128)S(1)}, f32[6,1536]{1,0:T(8,128)S(1)}, u32[]{:S(2)}, u32[]{:S(2)}) collective-permute-start(f32[6,1536]{1,0:T(8,128)S(1)} %multiply_bitcast_fusion), channel_id=1, source_target_pairs={{0,1},{1,0},{2,3},{3,2},{4,5},{5,4},{6,7},{7,6},{8,9},{9,8},{10,11... | collective-permute-start | bytes 110600 | tf_op jit(solution)/shard_map/ppermute | solution.py:24
  211.9 3.9 %collective-permute-done.12 = f32[6,1536]{1,0:T(8,128)S(1)} collective-permute-done((f32[6,1536]{1,0:T(8,128)S(1)}, f32[6,1536]{1,0:T(8,128)S(1)}, u32[]{:S(2)}, u32[]{:S(2)}) %collective-permute-start.12) | collective-permute-done | bytes 36896 | tf_op jit(solution)/shard_map/ppermute | solution.py:24
  215.7 3.7 %collective-permute-start.13 = (f32[6,1536]{1,0:T(8,128)S(1)}, f32[6,1536]{1,0:T(8,128)S(1)}, u32[]{:S(2)}, u32[]{:S(2)}) collective-permute-start(f32[6,1536]{1,0:T(8,128)S(1)} %fusion.43), channel_id=1, source_target_pairs={{0,2},{1,3},{2,0},{3,1},{4,6},{5,7},{6,4},{7,5},{8,10},{9,11},{10,... | collective-permute-start | bytes 110600 | tf_op jit(solution)/shard_map/ppermute | solution.py:24
  219.4 3.8 %collective-permute-done.13 = f32[6,1536]{1,0:T(8,128)S(1)} collective-permute-done((f32[6,1536]{1,0:T(8,128)S(1)}, f32[6,1536]{1,0:T(8,128)S(1)}, u32[]{:S(2)}, u32[]{:S(2)}) %collective-permute-start.13) | collective-permute-done | bytes 36896 | tf_op jit(solution)/shard_map/ppermute | solution.py:24
  223.2 8.2 %collective-permute-start.14 = (f32[6,1536]{1,0:T(8,128)S(1)}, f32[6,1536]{1,0:T(8,128)S(1)}, u32[]{:S(2)}, u32[]{:S(2)}) collective-permute-start(f32[6,1536]{1,0:T(8,128)S(1)} %add.204), channel_id=1, source_target_pairs={{0,4},{4,0},{1,5},{5,1},{2,6},{6,2},{3,7},{7,3},{8,12},{12,8},{9,1... | collective-permute-start | bytes 110600 | tf_op jit(solution)/shard_map/ppermute | solution.py:24
  (93 shorter events, 48.2 us)
Async XLA Ops:
  0.6 26.8 %copy-start.6 = (bf16[1,192,384]{2,1,0:T(8,128)(2,1)S(1)}, bf16[1,192,384]{2,1,0:T(8,128)(2,1)}, u32[]{:S(2)}) copy-start(bf16[1,192,384]{2,1,0:T(8,128)(2,1)} %param.9) | copy-start | bytes 442372
  19.7 19.0 %collective-permute-start = (bf16[24,7680]{1,0:T(8,128)(2,1)S(1)}, bf16[24,7680]{1,0:T(8,128)(2,1)}, u32[]{:S(2)}, u32[]{:S(2)}) collective-permute-start(bf16[24,7680]{1,0:T(8,128)(2,1)S(1)} %reshape.76), channel_id=1, source_target_pairs={{0,256},{64,320},{128,384},{192,448},{256,0},{320,64},{384,128},{4... | collective-permute-start | bytes 1105928 | tf_op jit(solution)/shard_map/ppermute | solution.py:24
  30.2 8.5 %copy-start.14 = (s32[8]{0:T(128)S(1)}, s32[8]{0:T(128)}, u32[]{:S(2)}) copy-start(s32[8]{0:T(128)} %constant.196.clone) | copy-start | bytes 100
  31.4 16.1 %collective-permute-start.3 = (bf16[2,2,2,2,2,1,6,1536]{7,4,6,5,3,2,1,0:T(2,128)(2,1)}, bf16[2,2,2,2,2,1,6,1536]{7,4,6,5,3,2,1,0:T(2,128)(2,1)}, u32[]{:S(2)}, u32[]{:S(2)}) collective-permute-start(bf16[2,2,2,2,2,1,6,1536]{7,4,6,5,3,2,1,0:T(2,128)(2,1)} %copy.56), channel_id=1, source_target_pairs={{0,8},{8,0},{1,9},{9,1},{2,10},{10,2},{3,11},{11,3},{4,12},{12,4},... | collective-permute-start | bytes 1769480 | tf_op jit(solution)/shard_map/ppermute | solution.py:24
  34.2 84.5 %collective-permute-start.6 = (bf16[32,3456]{1,0:T(8,128)(2,1)}, bf16[32,3456]{1,0:T(8,128)(2,1)}, u32[]{:S(2)}, u32[]{:S(2)}) collective-permute-start(bf16[32,3456]{1,0:T(8,128)(2,1)} %get-tuple-element.21), channel_id=1, source_target_pairs={{0,8},{8,16},{16,24},{24,32},{32,40},{40,48},{48,56},{56,64},{64,7... | collective-permute-start | bytes 663560 | tf_op jit(solution)/shard_map/ppermute | solution.py:86
  37.3 81.5 %collective-permute-start.7 = (bf16[32,3456]{1,0:T(8,128)(2,1)}, bf16[32,3456]{1,0:T(8,128)(2,1)}, u32[]{:S(2)}, u32[]{:S(2)}) collective-permute-start(bf16[32,3456]{1,0:T(8,128)(2,1)} %get-tuple-element.20), channel_id=1, source_target_pairs={{8,0},{16,8},{24,16},{32,24},{40,32},{48,40},{56,48},{64,56},{72,6... | collective-permute-start | bytes 663560 | tf_op jit(solution)/shard_map/ppermute | solution.py:87
  39.7 39.8 %collective-permute-start.1 = (bf16[48,7680]{1,0:T(8,128)(2,1)S(1)}, bf16[48,7680]{1,0:T(8,128)(2,1)S(1)}, u32[]{:S(2)}, u32[]{:S(2)}) collective-permute-start(bf16[48,7680]{1,0:T(8,128)(2,1)S(1)} %pad_maximum_fusion.5), channel_id=1, source_target_pairs={{0,128},{64,192},{128,0},{192,64},{256,384},{320,448},{384,256},{4... | collective-permute-start | bytes 2211848 | tf_op jit(solution)/shard_map/ppermute | solution.py:24
  48.9 33.9 %collective-permute-start.4 = (bf16[2,2,2,2,1,1,6,1536]{7,6,5,4,3,2,1,0:T(8,128)(2,1)S(1)}, bf16[2,2,2,2,1,1,6,1536]{7,6,5,4,3,2,1,0:T(8,128)(2,1)S(1)}, u32[]{:S(2)}, u32[]{:S(2)}) collective-permute-start(bf16[2,2,2,2,1,1,6,1536]{7,6,5,4,3,2,1,0:T(8,128)(2,1)S(1)} %dynamic-slice_convert_fusion), channel_id=1, source_target_pairs={{0,16},{16,0},{32,48},{48,32},{1,17},{17,1},{33,49},{49,33},{2,18}... | collective-permute-start | bytes 884744 | tf_op jit(solution)/shard_map/ppermute | solution.py:24
  79.5 3.4 %copy-start.5 = (bf16[48,7680]{1,0:T(8,128)(2,1)}, bf16[48,7680]{1,0:T(8,128)(2,1)S(1)}, u32[]{:S(2)}) copy-start(bf16[48,7680]{1,0:T(8,128)(2,1)S(1)} %collective-permute-done.1) | copy-start | bytes 2211844
  80.9 36.1 %collective-permute-start.2 = (bf16[96,7680]{1,0:T(8,128)(2,1)S(1)}, bf16[96,7680]{1,0:T(8,128)(2,1)}, u32[]{:S(2)}, u32[]{:S(2)}) collective-permute-start(bf16[96,7680]{1,0:T(8,128)(2,1)S(1)} %pad_maximum_fusion.3), channel_id=1, source_target_pairs={{0,64},{64,0},{128,192},{192,128},{256,320},{320,256},{384,448},{4... | collective-permute-start | bytes 4423688 | tf_op jit(solution)/shard_map/ppermute | solution.py:24
  83.0 12.9 %collective-permute-start.5 = (bf16[2,2,2,1,1,1,6,1536]{7,6,5,4,3,2,1,0:T(8,128)(2,1)S(1)}, bf16[2,2,2,1,1,1,6,1536]{7,6,5,4,3,2,1,0:T(8,128)(2,1)S(1)}, u32[]{:S(2)}, u32[]{:S(2)}) collective-permute-start(bf16[2,2,2,1,1,1,6,1536]{7,6,5,4,3,2,1,0:T(8,128)(2,1)S(1)} %dynamic-slice_convert_fusion.1), channel_id=1, source_target_pairs={{0,32},{16,48},{32,0},{48,16},{1,33},{17,49},{33,1},{49,17},{2,34}... | collective-permute-start | bytes 442376 | tf_op jit(solution)/shard_map/ppermute | solution.py:24
  96.0 26.4 %copy-start.12 = (f32[2,2,2,1,1,1,6,1536]{7,6,5,4,3,2,1,0:T(8,128)}, f32[2,2,2,1,1,1,6,1536]{7,6,5,4,3,2,1,0:T(8,128)S(1)}, u32[]{:S(2)}) copy-start(f32[2,2,2,1,1,1,6,1536]{7,6,5,4,3,2,1,0:T(8,128)S(1)} %convert_add_fusion.2) | copy-start | bytes 884740
  118.7 6.0 %copy-start.1 = (bf16[1,192,1536]{2,1,0:T(8,128)(2,1)S(1)}, bf16[1,192,1536]{2,1,0:T(8,128)(2,1)}, u32[]{:S(2)}) copy-start(bf16[1,192,1536]{2,1,0:T(8,128)(2,1)} %param.10) | copy-start | bytes 1769476
  118.7 6.0 %copy-start.3 = (bf16[1,192,1536]{2,1,0:T(8,128)(2,1)S(1)}, bf16[1,192,1536]{2,1,0:T(8,128)(2,1)}, u32[]{:S(2)}) copy-start(bf16[1,192,1536]{2,1,0:T(8,128)(2,1)} %param.8) | copy-start | bytes 1769476
  118.7 6.0 %copy-start.8 = (bf16[1,192,384]{2,1,0:T(8,128)(2,1)S(1)}, bf16[1,192,384]{2,1,0:T(8,128)(2,1)}, u32[]{:S(2)}) copy-start(bf16[1,192,384]{2,1,0:T(8,128)(2,1)} %param.9) | copy-start | bytes 442372
  120.5 30.5 %collective-permute-start.8 = (bf16[192,7680]{1,0:T(8,128)(2,1)S(1)}, bf16[192,7680]{1,0:T(8,128)(2,1)}, u32[]{:S(2)}, u32[]{:S(2)}) collective-permute-start(bf16[192,7680]{1,0:T(8,128)(2,1)S(1)} %pad_maximum_fusion.1), channel_id=1, source_target_pairs={{0,8},{8,0},{1,9},{9,1},{2,10},{10,2},{3,11},{11,3},{4,12},{12,4},... | collective-permute-start | bytes 8847368 | tf_op jit(solution)/shard_map/ppermute | solution.py:24
  122.5 8.1 %collective-permute-start.9 = (bf16[2,2,1,1,1,1,6,1536]{7,6,5,4,3,2,1,0:T(8,128)(2,1)S(1)}, bf16[2,2,1,1,1,1,6,1536]{7,6,5,4,3,2,1,0:T(8,128)(2,1)}, u32[]{:S(2)}, u32[]{:S(2)}) collective-permute-start(bf16[2,2,1,1,1,1,6,1536]{7,6,5,4,3,2,1,0:T(8,128)(2,1)S(1)} %dynamic-slice_convert_fusion.2), channel_id=1, source_target_pairs={{0,64},{64,0},{128,192},{192,128},{256,320},{320,256},{384,448},{4... | collective-permute-start | bytes 221192 | tf_op jit(solution)/shard_map/ppermute | solution.py:24
  132.3 7.7 %collective-permute-start.10 = (bf16[2,1,1,1,1,1,6,1536]{7,6,5,4,3,2,1,0:T(8,128)(2,1)}, bf16[2,1,1,1,1,1,6,1536]{7,6,5,4,3,2,1,0:T(8,128)(2,1)}, u32[]{:S(2)}, u32[]{:S(2)}) collective-permute-start(bf16[2,1,1,1,1,1,6,1536]{7,6,5,4,3,2,1,0:T(8,128)(2,1)} %dynamic-slice_convert_fusion.3), channel_id=1, source_target_pairs={{0,128},{64,192},{128,0},{192,64},{256,384},{320,448},{384,256},{4... | collective-permute-start | bytes 110600 | tf_op jit(solution)/shard_map/ppermute | solution.py:24
  140.8 9.6 %collective-permute-start.11 = (bf16[1,1,1,1,1,1,6,1536]{7,6,5,4,3,2,1,0:T(8,128)(2,1)S(1)}, bf16[1,1,1,1,1,1,6,1536]{7,6,5,4,3,2,1,0:T(8,128)(2,1)S(1)}, u32[]{:S(2)}, u32[]{:S(2)}) collective-permute-start(bf16[1,1,1,1,1,1,6,1536]{7,6,5,4,3,2,1,0:T(8,128)(2,1)S(1)} %dynamic-slice_convert_fusion.4), channel_id=1, source_target_pairs={{0,256},{64,320},{128,384},{192,448},{256,0},{320,64},{384,128},{4... | collective-permute-start | bytes 55304 | tf_op jit(solution)/shard_map/ppermute | solution.py:24
  163.1 3.7 %copy-start.4 = (bf16[384,4608]{0,1:T(8,128)(2,1)S(1)}, bf16[384,4608]{0,1:T(8,128)(2,1)}, u32[]{:S(2)}) copy-start(bf16[384,4608]{0,1:T(8,128)(2,1)} %copy.45) | copy-start | bytes 10616836
  174.7 34.7 %copy-start.13 = (f32[1,1,1,1,1,1,6,1536]{7,6,5,4,3,2,1,0:T(8,128)S(1)}, f32[1,1,1,1,1,1,6,1536]{7,6,5,4,3,2,1,0:T(8,128)}, u32[]{:S(2)}) copy-start(f32[1,1,1,1,1,1,6,1536]{7,6,5,4,3,2,1,0:T(8,128)} %convert_add_fusion.5) | copy-start | bytes 110596
  209.4 6.3 %collective-permute-start.12 = (f32[6,1536]{1,0:T(8,128)S(1)}, f32[6,1536]{1,0:T(8,128)S(1)}, u32[]{:S(2)}, u32[]{:S(2)}) collective-permute-start(f32[6,1536]{1,0:T(8,128)S(1)} %multiply_bitcast_fusion), channel_id=1, source_target_pairs={{0,1},{1,0},{2,3},{3,2},{4,5},{5,4},{6,7},{7,6},{8,9},{9,8},{10,11... | collective-permute-start | bytes 110600 | tf_op jit(solution)/shard_map/ppermute | solution.py:24
  215.7 7.5 %collective-permute-start.13 = (f32[6,1536]{1,0:T(8,128)S(1)}, f32[6,1536]{1,0:T(8,128)S(1)}, u32[]{:S(2)}, u32[]{:S(2)}) collective-permute-start(f32[6,1536]{1,0:T(8,128)S(1)} %fusion.43), channel_id=1, source_target_pairs={{0,2},{1,3},{2,0},{3,1},{4,6},{5,7},{6,4},{7,5},{8,10},{9,11},{10,... | collective-permute-start | bytes 110600 | tf_op jit(solution)/shard_map/ppermute | solution.py:24
  223.2 10.3 %collective-permute-start.14 = (f32[6,1536]{1,0:T(8,128)S(1)}, f32[6,1536]{1,0:T(8,128)S(1)}, u32[]{:S(2)}, u32[]{:S(2)}) collective-permute-start(f32[6,1536]{1,0:T(8,128)S(1)} %add.204), channel_id=1, source_target_pairs={{0,4},{4,0},{1,5},{5,1},{2,6},{6,2},{3,7},{7,3},{8,12},{12,8},{9,1... | collective-permute-start | bytes 110600 | tf_op jit(solution)/shard_map/ppermute | solution.py:24
  (6 other events, 15.7 us)

commit v14 on v9

--- a/solution.py
+++ b/solution.py
@@ -86,12 +86,12 @@
     from_next = lax.ppermute(edge_in[:spacing], CTX, pairs_down)
 
     summed = summed.reshape((2,) * len(DIGITS) + (shard, chans))
-    summed = _halve(summed, (("c", 1), ("zl", 1), ("zl", 2)))
+    summed = _halve(summed, (("c", 1), ("y", 1), ("y", 2), ("y", 4)))
     packed, summed, from_prev, from_next = lax.optimization_barrier(
         (packed, summed, from_prev, from_next)
     )
     packed = lax.all_gather(packed, "c", axis=0, tiled=True)
-    summed = _halve(summed, (("y", 1), ("y", 2), ("y", 4)))
+    summed = _halve(summed, (("zl", 1), ("zl", 2)))
     packed, summed = lax.optimization_barrier((packed, summed))
     summed = summed.reshape(shard, chans)
     w_entry = packed[:, :chans]

time: 194 us -> 212 us (1.093)
  waiting for transfers between devices: 54.3 us -> 66.3 us
  starting transfers between devices: 34.9 us -> 41.5 us
    all_gather x1, waiting for transfers between devices: 0.53 us -> 14.5 us  [body(): packed = lax.all_gather(packed, 'c', axis=0, tiled=True)]
    all_gather x1, waiting for transfers between devices: 11.9 us -> 2.57 us  [body(): packed = lax.all_gather(packed, axis, axis=0, tiled=True)]
    ppermute x9, starting transfers between devices: 32.1 us -> 38.9 us  [_swap(): return lax.ppermute(x, axis, [(i, i ^ d) for i in range(n)])]
    ppermute x9, waiting for transfers between devices: 41.9 us -> 47.3 us  [_swap(): return lax.ppermute(x, axis, [(i, i ^ d) for i in range(n)])]
  transfers between devices with their start and end apart: 13 -> 13, of which waited for: 11 -> 12; matrix products, arithmetic and copies ran while one was open for 5% -> 4% of each run, Pallas kernels for 0% -> 0%
where the time goes in v14:
time: 212 us; the launch traced here: 211 us
  waiting for transfers between devices  66.3 us (31%)
  blocking collectives  51.3 us (24%)
  starting transfers between devices  41.5 us (20%)
  between operations  15.9 us (8%)
  local copies, waits for them, and re-layouts  13.1 us (6%)
  matrix products  11.9 us (6%)
  other arithmetic  10.8 us (5%)
    ppermute x9, waiting for transfers between devices, _swap(): return lax.ppermute(x, axis, [(i, i ^ d) for i in range(n)])  47.3 us
    ppermute x9, starting transfers between devices, _swap(): return lax.ppermute(x, axis, [(i, i ^ d) for i in range(n)])  38.9 us
    psum x3, blocking collectives, body(): gap = lax.psum(gap, axis)  33.4 us
    all_gather x1, blocking collectives, body(): packed = lax.all_gather(packed, axis, axis=0, tiled=True)  17.9 us
    all_gather x1, waiting for transfers between devices, body(): packed = lax.all_gather(packed, 'c', axis=0, tiled=True)  14.5 us
    unnamed x24, local copies, waits for them, and re-layouts  6.06 us
    slice x3, local copies, waits for them, and re-layouts, body(): w_conv = packed[:, chans:4 * chans].reshape(bot, 3, chans)  5.63 us
    dot_general x1, matrix products, body(): jnp.dot(inner, w_exit, preferred_element_type=jnp.float32)  5.49 us
  transfers between devices with their start and end apart: 13, of which 12 were waited for; matrix products, arithmetic and copies ran while one was open for 4% of the time, Pallas kernels for 0%

profile of v14, /device:TPU:2, one launch (start us, length us, event | category | flops | bytes accessed | tf_op | source)
XLA Modules:
  0.0 210.9 jit_solution(4876858448249278947)
XLA Ops:
  8.2 17.9 %all-gather = bf16[4,6,7680]{2,1,0:T(8,128)(2,1)S(1)} all-gather(bf16[1,6,7680]{2,1,0:T(8,128)(2,1)S(1)} %maximum_bitcast_fusion), channel_id=1, replica_groups=mesh['y'=8,'zl'=4,'c'=2,'zh'=2,'x'=4] {'zl'}, dimensions={0}, use_global_device_ids=true | all-gather | bytes 460800 | tf_op jit(solution)/shard_map/all_gather | solution.py:79
  37.0 3.5 %collective-permute-start.1 = (bf16[2,2,1,2,2,1,6,1536]{7,6,5,4,3,2,1,0:T(8,128)(2,1)S(1)}, bf16[2,2,1,2,2,1,6,1536]{7,6,5,4,3,2,1,0:T(8,128)(2,1)S(1)}, u32[]{:S(2)}, u32[]{:S(2)}) collective-permute-start(bf16[2,2,1,2,2,1,6,1536]{7,6,5,4,3,2,1,0:T(8,128)(2,1)S(1)} %dynamic-slice_convert_fusion), channel_id=1, source_target_pairs={{0,64},{64,0},{128,192},{192,128},{256,320},{320,256},{384,448},{4... | collective-permute-start | bytes 884744 | tf_op jit(solution)/shard_map/ppermute | solution.py:24
  40.6 14.6 %collective-permute-done.1 = bf16[2,2,1,2,2,1,6,1536]{7,6,5,4,3,2,1,0:T(8,128)(2,1)S(1)} collective-permute-done((bf16[2,2,1,2,2,1,6,1536]{7,6,5,4,3,2,1,0:T(8,128)(2,1)S(1)}, bf16[2,2,1,2,2,1,6,1536]{7,6,5,4,3,2,1,0:T(8,128)(2,1)S(1)}, u32[]{:S(2)}, u32[]{:S(2)}) %collective-permute-start.1) | collective-permute-done | bytes 294944 | tf_op jit(solution)/shard_map/ppermute | solution.py:24
  56.4 4.7 %collective-permute-start.2 = (bf16[2,1,1,2,2,1,6,1536]{7,6,5,4,3,2,1,0:T(8,128)(2,1)S(1)}, bf16[2,1,1,2,2,1,6,1536]{7,6,5,4,3,2,1,0:T(8,128)(2,1)S(1)}, u32[]{:S(2)}, u32[]{:S(2)}) collective-permute-start(bf16[2,1,1,2,2,1,6,1536]{7,6,5,4,3,2,1,0:T(8,128)(2,1)S(1)} %dynamic-slice_convert_fusion.1), channel_id=1, source_target_pairs={{0,128},{64,192},{128,0},{192,64},{256,384},{320,448},{384,256},{4... | collective-permute-start | bytes 442376 | tf_op jit(solution)/shard_map/ppermute | solution.py:24
  61.2 12.8 %collective-permute-done.2 = bf16[2,1,1,2,2,1,6,1536]{7,6,5,4,3,2,1,0:T(8,128)(2,1)S(1)} collective-permute-done((bf16[2,1,1,2,2,1,6,1536]{7,6,5,4,3,2,1,0:T(8,128)(2,1)S(1)}, bf16[2,1,1,2,2,1,6,1536]{7,6,5,4,3,2,1,0:T(8,128)(2,1)S(1)}, u32[]{:S(2)}, u32[]{:S(2)}) %collective-permute-start.2) | collective-permute-done | bytes 147488 | tf_op jit(solution)/shard_map/ppermute | solution.py:24
  74.0 8.2 %collective-permute-start.3 = (bf16[1,1,1,2,2,1,6,1536]{7,6,5,4,3,2,1,0:T(8,128)(2,1)S(1)}, bf16[1,1,1,2,2,1,6,1536]{7,6,5,4,3,2,1,0:T(8,128)(2,1)S(1)}, u32[]{:S(2)}, u32[]{:S(2)}) collective-permute-start(bf16[1,1,1,2,2,1,6,1536]{7,6,5,4,3,2,1,0:T(8,128)(2,1)S(1)} %dynamic-slice_convert_fusion.2), channel_id=1, source_target_pairs={{0,256},{64,320},{128,384},{192,448},{256,0},{320,64},{384,128},{4... | collective-permute-start | bytes 221192 | tf_op jit(solution)/shard_map/ppermute | solution.py:24
  84.9 3.0 %collective-permute-done.3 = bf16[1,1,1,2,2,1,6,1536]{7,6,5,4,3,2,1,0:T(8,128)(2,1)S(1)} collective-permute-done((bf16[1,1,1,2,2,1,6,1536]{7,6,5,4,3,2,1,0:T(8,128)(2,1)S(1)}, bf16[1,1,1,2,2,1,6,1536]{7,6,5,4,3,2,1,0:T(8,128)(2,1)S(1)}, u32[]{:S(2)}, u32[]{:S(2)}) %collective-permute-start.3) | collective-permute-done | bytes 73760 | tf_op jit(solution)/shard_map/ppermute | solution.py:24
  89.8 2.6 %all-gather.4.cloned.1.call-done = bf16[192,7680]{1,0:T(8,128)(2,1)} async-done(((bf16[24,7680]{1,0:T(8,128)(2,1)}), bf16[192,7680]{1,0:T(8,128)(2,1)}) %all-gather.4.cloned.1.call-update) | async-done | bytes 2949136 | tf_op jit(solution)/shard_map/all_gather | solution.py:79
  92.5 3.7 %collective-permute-start.6 = (bf16[1,1,1,2,1,1,6,1536]{7,6,5,4,3,2,1,0:T(8,128)(2,1)S(1)}, bf16[1,1,1,2,1,1,6,1536]{7,6,5,4,3,2,1,0:T(8,128)(2,1)S(1)}, u32[]{:S(2)}, u32[]{:S(2)}) collective-permute-start(bf16[1,1,1,2,1,1,6,1536]{7,6,5,4,3,2,1,0:T(8,128)(2,1)S(1)} %dynamic-slice_convert_fusion.3), channel_id=1, source_target_pairs={{0,16},{16,0},{32,48},{48,32},{1,17},{17,1},{33,49},{49,33},{2,18}... | collective-permute-start | bytes 110600 | tf_op jit(solution)/shard_map/ppermute | solution.py:24
  98.5 5.6 %collective-permute-start.7 = (bf16[1,1,1,1,1,1,6,1536]{7,6,5,4,3,2,1,0:T(8,128)(2,1)S(1)}, bf16[1,1,1,1,1,1,6,1536]{7,6,5,4,3,2,1,0:T(8,128)(2,1)S(1)}, u32[]{:S(2)}, u32[]{:S(2)}) collective-permute-start(bf16[1,1,1,1,1,1,6,1536]{7,6,5,4,3,2,1,0:T(8,128)(2,1)S(1)} %dynamic-slice_convert_fusion.4), channel_id=1, source_target_pairs={{0,32},{16,48},{32,0},{48,16},{1,33},{17,49},{33,1},{49,17},{2,34}... | collective-permute-start | bytes 55304 | tf_op jit(solution)/shard_map/ppermute | solution.py:24
  106.5 14.5 %all-gather.6.cloned.1.call-done = bf16[384,7680]{1,0:T(8,128)(2,1)} async-done(((bf16[192,7680]{1,0:T(8,128)(2,1)}), bf16[384,7680]{1,0:T(8,128)(2,1)}) %all-gather.6.cloned.1.call-update) | async-done | bytes 5898256 | tf_op jit(solution)/shard_map/all_gather | solution.py:93
  123.1 3.6 %copy.31 = bf16[384,4608]{0,1:T(8,128)(2,1)} copy(bf16[384,4608]{1,0:T(8,128)(2,1)S(1)} %slice-done) | data formatting | bytes 7077888 | tf_op jit(solution)/shard_map/slice | solution.py:98
  126.7 2.5 %subtract_bitcast_fusion = (f32[1,256,1536]{2,1,0:T(8,128)S(1)}, f32[1,256,1536]{2,1,0:T(8,128)S(1)}) fusion(bf16[32,3456]{1,0:T(8,128)(2,1)} %copy-done.9, bf16[192,1536]{1,0:T(8,128)(2,1)} %bitcast.56, bf16[192,384]{1,0:T(8,128)(2,1)} %bitcast.67, bf16[192,1536]{1,0:T(8,128)(2,1)} %bitcast.60, bf16[32,3456]{1,0:T(8,128)(2,1)} %copy-done.8, ...), kind=kOutput, calls=%fused_computation.16 | convolution fusion | flops 307888128 | bytes 7077888 | tf_op jit(solution)/shard_map/dot_general | solution.py:111
  135.3 5.5 %convolution_add_fusion = f32[2,192,1536]{2,1,0:T(8,128)} fusion(f32[1,256,1536]{2,1,0:T(8,128)} %copy-done.6, f32[1,256,1536]{2,1,0:T(8,128)} %copy-done.5, bf16[384,7680]{1,0:T(8,128)(2,1)} %all-gather.6.cloned.1.call-done, f32[2,192,384]{2,1,0:T(8,128)} %convolution_add_fusion.3, bf16[384,3,1536]{0,2,1:T(8,128)(2,1)S(1)} %bitcast.66, ...), kind=kOutput, calls=%fused_computation.12 | convolution fusion | flops 908623872 | bytes 9633792 | tf_op jit(solution)/shard_map/dot_general | solution.py:127
  140.8 3.6 %multiply_reduce_fusion = (f32[]{:T(128)}, bf16[1,192,1536]{2,1,0:T(8,128)(2,1)}) fusion(bf16[1,192,1536]{2,1,0:T(8,128)(2,1)} %param.10, f32[2,192,1536]{2,1,0:T(8,128)} %convolution_add_fusion), kind=kLoop, calls=%fused_computation.31 | loop fusion | flops 2654207 | bytes 3538948 | tf_op jit(solution)/shard_map/reduce_sum | solution.py:133
  145.0 3.0 %psum.21 = f32[]{:T(128)} all-reduce(f32[]{:T(128)S(6)} %div.40), channel_id=1, replica_groups=mesh['y'=8,'zl'=4,'c'=2,'zh'=2,'x'=4] {'c'}, use_global_device_ids=true, to_apply=%region_1.2 | all-reduce | flops 1 | bytes 8 | tf_op jit(solution)/shard_map/psum | solution.py:136
  148.0 12.8 %psum.22 = f32[]{:T(128)} all-reduce(f32[]{:T(128)} %psum.21), channel_id=1, replica_groups=mesh['y'=8,'zl'=4,'c'=2,'zh'=2,'x'=4] {'zl'}, use_global_device_ids=true, to_apply=%region_2.3 | all-reduce | flops 1 | bytes 8 | tf_op jit(solution)/shard_map/psum | solution.py:136
  160.8 17.6 %psum.23 = f32[]{:T(128)} all-reduce(f32[]{:T(128)} %psum.22), channel_id=1, replica_groups=mesh['y'=8,'zl'=4,'c'=2,'zh'=2,'x'=4] {'y'}, use_global_device_ids=true, to_apply=%region_3.4 | all-reduce | flops 1 | bytes 8 | tf_op jit(solution)/shard_map/psum | solution.py:136
  179.1 2.5 %collective-permute-start.8 = (f32[6,1536]{1,0:T(8,128)S(1)}, f32[6,1536]{1,0:T(8,128)S(1)}, u32[]{:S(2)}, u32[]{:S(2)}) collective-permute-start(f32[6,1536]{1,0:T(8,128)S(1)} %multiply_bitcast_fusion), channel_id=1, source_target_pairs={{0,1},{1,0},{2,3},{3,2},{4,5},{5,4},{6,7},{7,6},{8,9},{9,8},{10,11... | collective-permute-start | bytes 110600 | tf_op jit(solution)/shard_map/ppermute | solution.py:24
  181.6 4.0 %collective-permute-done.8 = f32[6,1536]{1,0:T(8,128)S(1)} collective-permute-done((f32[6,1536]{1,0:T(8,128)S(1)}, f32[6,1536]{1,0:T(8,128)S(1)}, u32[]{:S(2)}, u32[]{:S(2)}) %collective-permute-start.8) | collective-permute-done | bytes 36896 | tf_op jit(solution)/shard_map/ppermute | solution.py:24
  185.5 3.5 %collective-permute-start.9 = (f32[6,1536]{1,0:T(8,128)S(1)}, f32[6,1536]{1,0:T(8,128)S(1)}, u32[]{:S(2)}, u32[]{:S(2)}) collective-permute-start(f32[6,1536]{1,0:T(8,128)S(1)} %fusion.44), channel_id=1, source_target_pairs={{0,2},{1,3},{2,0},{3,1},{4,6},{5,7},{6,4},{7,5},{8,10},{9,11},{10,... | collective-permute-start | bytes 110600 | tf_op jit(solution)/shard_map/ppermute | solution.py:24
  189.1 3.9 %collective-permute-done.9 = f32[6,1536]{1,0:T(8,128)S(1)} collective-permute-done((f32[6,1536]{1,0:T(8,128)S(1)}, f32[6,1536]{1,0:T(8,128)S(1)}, u32[]{:S(2)}, u32[]{:S(2)}) %collective-permute-start.9) | collective-permute-done | bytes 36896 | tf_op jit(solution)/shard_map/ppermute | solution.py:24
  193.0 5.3 %collective-permute-start.10 = (f32[6,1536]{1,0:T(8,128)S(1)}, f32[6,1536]{1,0:T(8,128)S(1)}, u32[]{:S(2)}, u32[]{:S(2)}) collective-permute-start(f32[6,1536]{1,0:T(8,128)S(1)} %add.182), channel_id=1, source_target_pairs={{0,4},{4,0},{1,5},{5,1},{2,6},{6,2},{3,7},{7,3},{8,12},{12,8},{9,1... | collective-permute-start | bytes 110600 | tf_op jit(solution)/shard_map/ppermute | solution.py:24
  198.3 5.1 %collective-permute-done.10 = f32[6,1536]{1,0:T(8,128)S(1)} collective-permute-done((f32[6,1536]{1,0:T(8,128)S(1)}, f32[6,1536]{1,0:T(8,128)S(1)}, u32[]{:S(2)}, u32[]{:S(2)}) %collective-permute-start.10) | collective-permute-done | bytes 36896 | tf_op jit(solution)/shard_map/ppermute | solution.py:24
  (68 shorter events, 31.0 us)
Async XLA Ops:
  7.2 19.9 %copy-start.4 = (bf16[1,192,384]{2,1,0:T(8,128)(2,1)S(1)}, bf16[1,192,384]{2,1,0:T(8,128)(2,1)}, u32[]{:S(2)}) copy-start(bf16[1,192,384]{2,1,0:T(8,128)(2,1)} %param.8) | copy-start | bytes 442372
  7.2 85.2 %all-gather.4.cloned.1.call-start = ((), (), s32[]{:S(2)}) async-start(), calls=%async_computation | async-start | bytes 3317760 | tf_op jit(solution)/shard_map/all_gather | solution.py:79
  27.0 94.0 %all-gather.6.cloned.1.call-start = ((), (), s32[]{:S(2)}) async-start(), calls=%async_computation.1 | async-start | bytes 8847360 | tf_op jit(solution)/shard_map/all_gather | solution.py:93
  30.3 4.2 %collective-permute-start = (bf16[2,2,2,2,2,1,6,1536]{7,4,6,5,3,2,1,0:T(2,128)(2,1)}, bf16[2,2,2,2,2,1,6,1536]{7,4,6,5,3,2,1,0:T(2,128)(2,1)}, u32[]{:S(2)}, u32[]{:S(2)}) collective-permute-start(bf16[2,2,2,2,2,1,6,1536]{7,4,6,5,3,2,1,0:T(2,128)(2,1)} %copy.42), channel_id=1, source_target_pairs={{0,8},{8,0},{1,9},{9,1},{2,10},{10,2},{3,11},{11,3},{4,12},{12,4},... | collective-permute-start | bytes 1769480 | tf_op jit(solution)/shard_map/ppermute | solution.py:24
  35.8 1.2 copy-start.2
  37.0 18.1 %collective-permute-start.1 = (bf16[2,2,1,2,2,1,6,1536]{7,6,5,4,3,2,1,0:T(8,128)(2,1)S(1)}, bf16[2,2,1,2,2,1,6,1536]{7,6,5,4,3,2,1,0:T(8,128)(2,1)S(1)}, u32[]{:S(2)}, u32[]{:S(2)}) collective-permute-start(bf16[2,2,1,2,2,1,6,1536]{7,6,5,4,3,2,1,0:T(8,128)(2,1)S(1)} %dynamic-slice_convert_fusion), channel_id=1, source_target_pairs={{0,64},{64,0},{128,192},{192,128},{256,320},{320,256},{384,448},{4... | collective-permute-start | bytes 884744 | tf_op jit(solution)/shard_map/ppermute | solution.py:24
  40.5 41.7 %copy-start = (bf16[1,192,1536]{2,1,0:T(8,128)(2,1)S(1)}, bf16[1,192,1536]{2,1,0:T(8,128)(2,1)}, u32[]{:S(2)}) copy-start(bf16[1,192,1536]{2,1,0:T(8,128)(2,1)} %param.9) | copy-start | bytes 1769476
  40.5 41.7 %copy-start.1 = (bf16[1,192,1536]{2,1,0:T(8,128)(2,1)S(1)}, bf16[1,192,1536]{2,1,0:T(8,128)(2,1)}, u32[]{:S(2)}) copy-start(bf16[1,192,1536]{2,1,0:T(8,128)(2,1)} %param.7) | copy-start | bytes 1769476
  56.4 17.5 %collective-permute-start.2 = (bf16[2,1,1,2,2,1,6,1536]{7,6,5,4,3,2,1,0:T(8,128)(2,1)S(1)}, bf16[2,1,1,2,2,1,6,1536]{7,6,5,4,3,2,1,0:T(8,128)(2,1)S(1)}, u32[]{:S(2)}, u32[]{:S(2)}) collective-permute-start(bf16[2,1,1,2,2,1,6,1536]{7,6,5,4,3,2,1,0:T(8,128)(2,1)S(1)} %dynamic-slice_convert_fusion.1), channel_id=1, source_target_pairs={{0,128},{64,192},{128,0},{192,64},{256,384},{320,448},{384,256},{4... | collective-permute-start | bytes 442376 | tf_op jit(solution)/shard_map/ppermute | solution.py:24
  74.0 13.9 %collective-permute-start.3 = (bf16[1,1,1,2,2,1,6,1536]{7,6,5,4,3,2,1,0:T(8,128)(2,1)S(1)}, bf16[1,1,1,2,2,1,6,1536]{7,6,5,4,3,2,1,0:T(8,128)(2,1)S(1)}, u32[]{:S(2)}, u32[]{:S(2)}) collective-permute-start(bf16[1,1,1,2,2,1,6,1536]{7,6,5,4,3,2,1,0:T(8,128)(2,1)S(1)} %dynamic-slice_convert_fusion.2), channel_id=1, source_target_pairs={{0,256},{64,320},{128,384},{192,448},{256,0},{320,64},{384,128},{4... | collective-permute-start | bytes 221192 | tf_op jit(solution)/shard_map/ppermute | solution.py:24
  82.3 5.7 %collective-permute-start.4 = (bf16[32,3456]{1,0:T(8,128)(2,1)S(1)}, bf16[32,3456]{1,0:T(8,128)(2,1)S(1)}, u32[]{:S(2)}, u32[]{:S(2)}) collective-permute-start(bf16[32,3456]{1,0:T(8,128)(2,1)S(1)} %get-tuple-element.19), channel_id=1, source_target_pairs={{0,8},{8,16},{16,24},{24,32},{32,40},{40,48},{48,56},{56,64},{64,7... | collective-permute-start | bytes 663560 | tf_op jit(solution)/shard_map/ppermute | solution.py:85
  83.6 6.2 %collective-permute-start.5 = (bf16[32,3456]{1,0:T(8,128)(2,1)S(1)}, bf16[32,3456]{1,0:T(8,128)(2,1)S(1)}, u32[]{:S(2)}, u32[]{:S(2)}) collective-permute-start(bf16[32,3456]{1,0:T(8,128)(2,1)S(1)} %get-tuple-element.18), channel_id=1, source_target_pairs={{8,0},{16,8},{24,16},{32,24},{40,32},{48,40},{56,48},{64,56},{72,6... | collective-permute-start | bytes 663560 | tf_op jit(solution)/shard_map/ppermute | solution.py:86
  88.0 16.1 %copy-start.8 = (bf16[32,3456]{1,0:T(8,128)(2,1)}, bf16[32,3456]{1,0:T(8,128)(2,1)S(1)}, u32[]{:S(2)}) copy-start(bf16[32,3456]{1,0:T(8,128)(2,1)S(1)} %collective-permute-done.4) | copy-start | bytes 663556
  89.8 14.3 %copy-start.9 = (bf16[32,3456]{1,0:T(8,128)(2,1)}, bf16[32,3456]{1,0:T(8,128)(2,1)S(1)}, u32[]{:S(2)}) copy-start(bf16[32,3456]{1,0:T(8,128)(2,1)S(1)} %collective-permute-done.5) | copy-start | bytes 663556
  92.5 6.0 %collective-permute-start.6 = (bf16[1,1,1,2,1,1,6,1536]{7,6,5,4,3,2,1,0:T(8,128)(2,1)S(1)}, bf16[1,1,1,2,1,1,6,1536]{7,6,5,4,3,2,1,0:T(8,128)(2,1)S(1)}, u32[]{:S(2)}, u32[]{:S(2)}) collective-permute-start(bf16[1,1,1,2,1,1,6,1536]{7,6,5,4,3,2,1,0:T(8,128)(2,1)S(1)} %dynamic-slice_convert_fusion.3), channel_id=1, source_target_pairs={{0,16},{16,0},{32,48},{48,32},{1,17},{17,1},{33,49},{49,33},{2,18}... | collective-permute-start | bytes 110600 | tf_op jit(solution)/shard_map/ppermute | solution.py:24
  98.5 7.4 %collective-permute-start.7 = (bf16[1,1,1,1,1,1,6,1536]{7,6,5,4,3,2,1,0:T(8,128)(2,1)S(1)}, bf16[1,1,1,1,1,1,6,1536]{7,6,5,4,3,2,1,0:T(8,128)(2,1)S(1)}, u32[]{:S(2)}, u32[]{:S(2)}) collective-permute-start(bf16[1,1,1,1,1,1,6,1536]{7,6,5,4,3,2,1,0:T(8,128)(2,1)S(1)} %dynamic-slice_convert_fusion.4), channel_id=1, source_target_pairs={{0,32},{16,48},{32,0},{48,16},{1,33},{17,49},{33,1},{49,17},{2,34}... | collective-permute-start | bytes 55304 | tf_op jit(solution)/shard_map/ppermute | solution.py:24
  121.1 2.0 slice-start
  129.2 1.6 copy-start.6
  129.3 3.7 %copy-start.3 = (bf16[384,4608]{0,1:T(8,128)(2,1)S(1)}, bf16[384,4608]{0,1:T(8,128)(2,1)}, u32[]{:S(2)}) copy-start(bf16[384,4608]{0,1:T(8,128)(2,1)} %copy.31) | copy-start | bytes 10616836
  130.9 2.9 %copy-start.7 = (bf16[2,256,1536]{2,1,0:T(8,128)(2,1)}, bf16[2,256,1536]{2,1,0:T(8,128)(2,1)S(1)}, u32[]{:S(2)}) copy-start(bf16[2,256,1536]{2,1,0:T(8,128)(2,1)S(1)} %fusion.7) | copy-start | bytes 4718596
  140.8 38.2 %copy-start.10 = (f32[1,1,1,1,1,1,6,1536]{7,6,5,4,3,2,1,0:T(8,128)S(1)}, f32[1,1,1,1,1,1,6,1536]{7,6,5,4,3,2,1,0:T(8,128)}, u32[]{:S(2)}) copy-start(f32[1,1,1,1,1,1,6,1536]{7,6,5,4,3,2,1,0:T(8,128)} %convert_add_fusion.5) | copy-start | bytes 110596
  179.1 6.4 %collective-permute-start.8 = (f32[6,1536]{1,0:T(8,128)S(1)}, f32[6,1536]{1,0:T(8,128)S(1)}, u32[]{:S(2)}, u32[]{:S(2)}) collective-permute-start(f32[6,1536]{1,0:T(8,128)S(1)} %multiply_bitcast_fusion), channel_id=1, source_target_pairs={{0,1},{1,0},{2,3},{3,2},{4,5},{5,4},{6,7},{7,6},{8,9},{9,8},{10,11... | collective-permute-start | bytes 110600 | tf_op jit(solution)/shard_map/ppermute | solution.py:24
  185.5 7.5 %collective-permute-start.9 = (f32[6,1536]{1,0:T(8,128)S(1)}, f32[6,1536]{1,0:T(8,128)S(1)}, u32[]{:S(2)}, u32[]{:S(2)}) collective-permute-start(f32[6,1536]{1,0:T(8,128)S(1)} %fusion.44), channel_id=1, source_target_pairs={{0,2},{1,3},{2,0},{3,1},{4,6},{5,7},{6,4},{7,5},{8,10},{9,11},{10,... | collective-permute-start | bytes 110600 | tf_op jit(solution)/shard_map/ppermute | solution.py:24
  193.0 10.4 %collective-permute-start.10 = (f32[6,1536]{1,0:T(8,128)S(1)}, f32[6,1536]{1,0:T(8,128)S(1)}, u32[]{:S(2)}, u32[]{:S(2)}) collective-permute-start(f32[6,1536]{1,0:T(8,128)S(1)} %add.182), channel_id=1, source_target_pairs={{0,4},{4,0},{1,5},{5,1},{2,6},{6,2},{3,7},{7,3},{8,12},{12,8},{9,1... | collective-permute-start | bytes 110600 | tf_op jit(solution)/shard_map/ppermute | solution.py:24
  (1 other events, 1.2 us)
Sparse Core Ops, SparseCore 0:
  27.1 65.2 all-gather.3
  94.5 26.5 all-gather.5

commit v15 on v9

--- a/solution.py
+++ b/solution.py
@@ -131,9 +131,7 @@
     lower = outs[1]
     blended = ((upper + lower) * 0.5).astype(jnp.bfloat16)[None]
     local_gap = jnp.sum((upper - lower) * (upper + lower - 2.0 * goal)) / (rows * n_ctx * chans)
-    gap = local_gap
-    for axis in ("c", "zl", "y"):
-        gap = lax.psum(gap, axis)
+    gap = lax.psum(lax.psum(local_gap, ("zl", "c")), "y")
     factor = gap / (2.0 * NOISE_SCALE)
     estimate = _sum_all(factor * summed, (("x", 1), ("x", 2), ("zh", 1)))
     return (blended, estimate)

time: 194 us -> 195 us (level)
  blocking collectives: 51.3 us -> 53.3 us
    psum x3 -> x2, blocking collectives: 33.4 us -> 35.4 us  [body(): gap = lax.psum(lax.psum(local_gap, ('zl', 'c')), 'y')]
where the time goes in v15:
time: 195 us; the launch traced here: 194 us
  blocking collectives  53.3 us (27%)
  waiting for transfers between devices  52.8 us (27%)
  starting transfers between devices  35.4 us (18%)
  between operations  15.9 us (8%)
  local copies, waits for them, and re-layouts  13.2 us (7%)
  matrix products  11.9 us (6%)
  other arithmetic  11.7 us (6%)
    ppermute x9, waiting for transfers between devices, _swap(): return lax.ppermute(x, axis, [(i, i ^ d) for i in range(n)])  40.4 us
    psum x2, blocking collectives, body(): gap = lax.psum(lax.psum(local_gap, ('zl', 'c')), 'y')  35.4 us
    ppermute x9, starting transfers between devices, _swap(): return lax.ppermute(x, axis, [(i, i ^ d) for i in range(n)])  32.7 us
    all_gather x1, blocking collectives, body(): packed = lax.all_gather(packed, axis, axis=0, tiled=True)  17.9 us
    all_gather x1, waiting for transfers between devices, body(): packed = lax.all_gather(packed, axis, axis=0, tiled=True)  11.9 us
    unnamed x24, local copies, waits for them, and re-layouts  6.05 us
    slice x3, local copies, waits for them, and re-layouts, body(): w_conv = packed[:, chans:4 * chans].reshape(bot, 3, chans)  5.65 us
    dot_general x1, matrix products, body(): jnp.dot(inner, w_exit, preferred_element_type=jnp.float32)  5.5 us
  transfers between devices with their start and end apart: 13, of which 11 were waited for; matrix products, arithmetic and copies ran while one was open for 5% of the time, Pallas kernels for 0%

profile of v15, /device:TPU:2, one launch (start us, length us, event | category | flops | bytes accessed | tf_op | source)
XLA Modules:
  0.0 194.3 jit_solution(4031135510972995357)
XLA Ops:
  8.2 17.9 %all-gather = bf16[4,6,7680]{2,1,0:T(8,128)(2,1)S(1)} all-gather(bf16[1,6,7680]{2,1,0:T(8,128)(2,1)S(1)} %maximum_bitcast_fusion), channel_id=1, replica_groups=mesh['y'=8,'zl'=4,'c'=2,'zh'=2,'x'=4] {'zl'}, dimensions={0}, use_global_device_ids=true | all-gather | bytes 460800 | tf_op jit(solution)/shard_map/all_gather | solution.py:79
  37.0 4.2 %collective-permute-start.1 = (bf16[2,2,2,2,1,1,6,1536]{7,6,5,4,3,2,1,0:T(8,128)(2,1)S(1)}, bf16[2,2,2,2,1,1,6,1536]{7,6,5,4,3,2,1,0:T(8,128)(2,1)S(1)}, u32[]{:S(2)}, u32[]{:S(2)}) collective-permute-start(bf16[2,2,2,2,1,1,6,1536]{7,6,5,4,3,2,1,0:T(8,128)(2,1)S(1)} %dynamic-slice_convert_fusion), channel_id=1, source_target_pairs={{0,16},{16,0},{32,48},{48,32},{1,17},{17,1},{33,49},{49,33},{2,18}... | collective-permute-start | bytes 884744 | tf_op jit(solution)/shard_map/ppermute | solution.py:24
  41.2 9.4 %collective-permute-done.1 = bf16[2,2,2,2,1,1,6,1536]{7,6,5,4,3,2,1,0:T(8,128)(2,1)S(1)} collective-permute-done((bf16[2,2,2,2,1,1,6,1536]{7,6,5,4,3,2,1,0:T(8,128)(2,1)S(1)}, bf16[2,2,2,2,1,1,6,1536]{7,6,5,4,3,2,1,0:T(8,128)(2,1)S(1)}, u32[]{:S(2)}, u32[]{:S(2)}) %collective-permute-start.1) | collective-permute-done | bytes 294944 | tf_op jit(solution)/shard_map/ppermute | solution.py:24
  51.9 4.4 %collective-permute-start.2 = (bf16[2,2,2,1,1,1,6,1536]{7,6,5,4,3,2,1,0:T(8,128)(2,1)S(1)}, bf16[2,2,2,1,1,1,6,1536]{7,6,5,4,3,2,1,0:T(8,128)(2,1)}, u32[]{:S(2)}, u32[]{:S(2)}) collective-permute-start(bf16[2,2,2,1,1,1,6,1536]{7,6,5,4,3,2,1,0:T(8,128)(2,1)S(1)} %dynamic-slice_convert_fusion.1), channel_id=1, source_target_pairs={{0,32},{16,48},{32,0},{48,16},{1,33},{17,49},{33,1},{49,17},{2,34}... | collective-permute-start | bytes 442376 | tf_op jit(solution)/shard_map/ppermute | solution.py:24
  59.1 6.5 %collective-permute-done.2 = bf16[2,2,2,1,1,1,6,1536]{7,6,5,4,3,2,1,0:T(8,128)(2,1)} collective-permute-done((bf16[2,2,2,1,1,1,6,1536]{7,6,5,4,3,2,1,0:T(8,128)(2,1)S(1)}, bf16[2,2,2,1,1,1,6,1536]{7,6,5,4,3,2,1,0:T(8,128)(2,1)}, u32[]{:S(2)}, u32[]{:S(2)}) %collective-permute-start.2) | collective-permute-done | bytes 147488 | tf_op jit(solution)/shard_map/ppermute | solution.py:24
  66.6 11.9 %all-gather.4.cloned.1.call-done = bf16[192,7680]{1,0:T(8,128)(2,1)} async-done(((bf16[24,7680]{1,0:T(8,128)(2,1)}), bf16[192,7680]{1,0:T(8,128)(2,1)}) %all-gather.4.cloned.1.call-update) | async-done | bytes 2949136 | tf_op jit(solution)/shard_map/all_gather | solution.py:79
  78.5 2.7 %collective-permute-start.5 = (bf16[2,2,1,1,1,1,6,1536]{7,6,5,4,3,2,1,0:T(8,128)(2,1)S(1)}, bf16[2,2,1,1,1,1,6,1536]{7,6,5,4,3,2,1,0:T(8,128)(2,1)S(1)}, u32[]{:S(2)}, u32[]{:S(2)}) collective-permute-start(bf16[2,2,1,1,1,1,6,1536]{7,6,5,4,3,2,1,0:T(8,128)(2,1)S(1)} %dynamic-slice_convert_fusion.2), channel_id=1, source_target_pairs={{0,64},{64,0},{128,192},{192,128},{256,320},{320,256},{384,448},{4... | collective-permute-start | bytes 221192 | tf_op jit(solution)/shard_map/ppermute | solution.py:24
  81.4 3.7 %collective-permute-done.5 = bf16[2,2,1,1,1,1,6,1536]{7,6,5,4,3,2,1,0:T(8,128)(2,1)S(1)} collective-permute-done((bf16[2,2,1,1,1,1,6,1536]{7,6,5,4,3,2,1,0:T(8,128)(2,1)S(1)}, bf16[2,2,1,1,1,1,6,1536]{7,6,5,4,3,2,1,0:T(8,128)(2,1)S(1)}, u32[]{:S(2)}, u32[]{:S(2)}) %collective-permute-start.5) | collective-permute-done | bytes 73760 | tf_op jit(solution)/shard_map/ppermute | solution.py:24
  85.1 3.6 %collective-permute-start.6 = (bf16[2,1,1,1,1,1,6,1536]{7,6,5,4,3,2,1,0:T(8,128)(2,1)S(1)}, bf16[2,1,1,1,1,1,6,1536]{7,6,5,4,3,2,1,0:T(8,128)(2,1)S(1)}, u32[]{:S(2)}, u32[]{:S(2)}) collective-permute-start(bf16[2,1,1,1,1,1,6,1536]{7,6,5,4,3,2,1,0:T(8,128)(2,1)S(1)} %dynamic-slice_convert_fusion.3), channel_id=1, source_target_pairs={{0,128},{64,192},{128,0},{192,64},{256,384},{320,448},{384,256},{4... | collective-permute-start | bytes 110600 | tf_op jit(solution)/shard_map/ppermute | solution.py:24
  90.0 2.5 %collective-permute-done.6 = bf16[2,1,1,1,1,1,6,1536]{7,6,5,4,3,2,1,0:T(8,128)(2,1)S(1)} collective-permute-done((bf16[2,1,1,1,1,1,6,1536]{7,6,5,4,3,2,1,0:T(8,128)(2,1)S(1)}, bf16[2,1,1,1,1,1,6,1536]{7,6,5,4,3,2,1,0:T(8,128)(2,1)S(1)}, u32[]{:S(2)}, u32[]{:S(2)}) %collective-permute-start.6) | collective-permute-done | bytes 36896 | tf_op jit(solution)/shard_map/ppermute | solution.py:24
  92.6 4.0 %collective-permute-start.7 = (bf16[1,1,1,1,1,1,6,1536]{7,6,5,4,3,2,1,0:T(8,128)(2,1)S(1)}, bf16[1,1,1,1,1,1,6,1536]{7,6,5,4,3,2,1,0:T(8,128)(2,1)S(1)}, u32[]{:S(2)}, u32[]{:S(2)}) collective-permute-start(bf16[1,1,1,1,1,1,6,1536]{7,6,5,4,3,2,1,0:T(8,128)(2,1)S(1)} %dynamic-slice_convert_fusion.4), channel_id=1, source_target_pairs={{0,256},{64,320},{128,384},{192,448},{256,0},{320,64},{384,128},{4... | collective-permute-start | bytes 55304 | tf_op jit(solution)/shard_map/ppermute | solution.py:24
  97.6 4.6 %collective-permute-done.7 = bf16[1,1,1,1,1,1,6,1536]{7,6,5,4,3,2,1,0:T(8,128)(2,1)S(1)} collective-permute-done((bf16[1,1,1,1,1,1,6,1536]{7,6,5,4,3,2,1,0:T(8,128)(2,1)S(1)}, bf16[1,1,1,1,1,1,6,1536]{7,6,5,4,3,2,1,0:T(8,128)(2,1)S(1)}, u32[]{:S(2)}, u32[]{:S(2)}) %collective-permute-start.7) | collective-permute-done | bytes 18464 | tf_op jit(solution)/shard_map/ppermute | solution.py:24
  105.3 3.7 %copy.31 = bf16[384,4608]{0,1:T(8,128)(2,1)} copy(bf16[384,4608]{1,0:T(8,128)(2,1)S(1)} %slice-done) | data formatting | bytes 7077888 | tf_op jit(solution)/shard_map/slice | solution.py:98
  109.0 2.5 %subtract_bitcast_fusion = (f32[1,256,1536]{2,1,0:T(8,128)S(1)}, f32[1,256,1536]{2,1,0:T(8,128)S(1)}) fusion(bf16[32,3456]{1,0:T(8,128)(2,1)} %copy-done.9, bf16[192,1536]{1,0:T(8,128)(2,1)} %bitcast.56, bf16[192,384]{1,0:T(8,128)(2,1)} %bitcast.67, bf16[192,1536]{1,0:T(8,128)(2,1)} %bitcast.60, bf16[32,3456]{1,0:T(8,128)(2,1)} %copy-done.8, ...), kind=kOutput, calls=%fused_computation.16 | convolution fusion | flops 307888128 | bytes 7077888 | tf_op jit(solution)/shard_map/dot_general | solution.py:111
  117.6 5.5 %convolution_add_fusion = f32[2,192,1536]{2,1,0:T(8,128)} fusion(f32[1,256,1536]{2,1,0:T(8,128)} %copy-done.6, f32[1,256,1536]{2,1,0:T(8,128)} %copy-done.5, bf16[384,7680]{1,0:T(8,128)(2,1)} %all-gather.6.cloned.1.call-done, f32[2,192,384]{2,1,0:T(8,128)} %convolution_add_fusion.3, bf16[384,3,1536]{0,2,1:T(8,128)(2,1)S(1)} %bitcast.66, ...), kind=kOutput, calls=%fused_computation.12 | convolution fusion | flops 908623872 | bytes 9633792 | tf_op jit(solution)/shard_map/dot_general | solution.py:127
  123.1 3.6 %multiply_reduce_fusion = (f32[]{:T(128)}, bf16[1,192,1536]{2,1,0:T(8,128)(2,1)}) fusion(bf16[1,192,1536]{2,1,0:T(8,128)(2,1)} %param.10, f32[2,192,1536]{2,1,0:T(8,128)} %convolution_add_fusion), kind=kLoop, calls=%fused_computation.31 | loop fusion | flops 2654207 | bytes 3538948 | tf_op jit(solution)/shard_map/reduce_sum | solution.py:133
  127.3 17.8 %psum.14 = f32[]{:T(128)} all-reduce(f32[]{:T(128)S(6)} %div.40), channel_id=1, replica_groups=mesh['y'=8,'zl'=4,'c'=2,'zh'=2,'x'=4] {'zl','c'}, use_global_device_ids=true, to_apply=%region_1.2 | all-reduce | flops 1 | bytes 8 | tf_op jit(solution)/shard_map/psum | solution.py:134
  145.2 17.6 %psum.15 = f32[]{:T(128)} all-reduce(f32[]{:T(128)} %psum.14), channel_id=1, replica_groups=mesh['y'=8,'zl'=4,'c'=2,'zh'=2,'x'=4] {'y'}, use_global_device_ids=true, to_apply=%region_2.3 | all-reduce | flops 1 | bytes 8 | tf_op jit(solution)/shard_map/psum | solution.py:134
  163.4 2.5 %collective-permute-start.8 = (f32[6,1536]{1,0:T(8,128)S(1)}, f32[6,1536]{1,0:T(8,128)S(1)}, u32[]{:S(2)}, u32[]{:S(2)}) collective-permute-start(f32[6,1536]{1,0:T(8,128)S(1)} %multiply_bitcast_fusion), channel_id=1, source_target_pairs={{0,1},{1,0},{2,3},{3,2},{4,5},{5,4},{6,7},{7,6},{8,9},{9,8},{10,11... | collective-permute-start | bytes 110600 | tf_op jit(solution)/shard_map/ppermute | solution.py:24
  165.9 3.5 %collective-permute-done.8 = f32[6,1536]{1,0:T(8,128)S(1)} collective-permute-done((f32[6,1536]{1,0:T(8,128)S(1)}, f32[6,1536]{1,0:T(8,128)S(1)}, u32[]{:S(2)}, u32[]{:S(2)}) %collective-permute-start.8) | collective-permute-done | bytes 36896 | tf_op jit(solution)/shard_map/ppermute | solution.py:24
  169.4 4.0 %collective-permute-start.9 = (f32[6,1536]{1,0:T(8,128)S(1)}, f32[6,1536]{1,0:T(8,128)S(1)}, u32[]{:S(2)}, u32[]{:S(2)}) collective-permute-start(f32[6,1536]{1,0:T(8,128)S(1)} %fusion.44), channel_id=1, source_target_pairs={{0,2},{1,3},{2,0},{3,1},{4,6},{5,7},{6,4},{7,5},{8,10},{9,11},{10,... | collective-permute-start | bytes 110600 | tf_op jit(solution)/shard_map/ppermute | solution.py:24
  173.4 3.5 %collective-permute-done.9 = f32[6,1536]{1,0:T(8,128)S(1)} collective-permute-done((f32[6,1536]{1,0:T(8,128)S(1)}, f32[6,1536]{1,0:T(8,128)S(1)}, u32[]{:S(2)}, u32[]{:S(2)}) %collective-permute-start.9) | collective-permute-done | bytes 36896 | tf_op jit(solution)/shard_map/ppermute | solution.py:24
  176.9 5.4 %collective-permute-start.10 = (f32[6,1536]{1,0:T(8,128)S(1)}, f32[6,1536]{1,0:T(8,128)S(1)}, u32[]{:S(2)}, u32[]{:S(2)}) collective-permute-start(f32[6,1536]{1,0:T(8,128)S(1)} %add.180), channel_id=1, source_target_pairs={{0,4},{4,0},{1,5},{5,1},{2,6},{6,2},{3,7},{7,3},{8,12},{12,8},{9,1... | collective-permute-start | bytes 110600 | tf_op jit(solution)/shard_map/ppermute | solution.py:24
  182.3 4.5 %collective-permute-done.10 = f32[6,1536]{1,0:T(8,128)S(1)} collective-permute-done((f32[6,1536]{1,0:T(8,128)S(1)}, f32[6,1536]{1,0:T(8,128)S(1)}, u32[]{:S(2)}, u32[]{:S(2)}) %collective-permute-start.10) | collective-permute-done | bytes 36896 | tf_op jit(solution)/shard_map/ppermute | solution.py:24
  (67 shorter events, 29.0 us)
Async XLA Ops:
  7.2 19.9 %copy-start.4 = (bf16[1,192,384]{2,1,0:T(8,128)(2,1)S(1)}, bf16[1,192,384]{2,1,0:T(8,128)(2,1)}, u32[]{:S(2)}) copy-start(bf16[1,192,384]{2,1,0:T(8,128)(2,1)} %param.8) | copy-start | bytes 442372
  7.2 71.3 %all-gather.4.cloned.1.call-start = ((), (), s32[]{:S(2)}) async-start(), calls=%async_computation | async-start | bytes 3317760 | tf_op jit(solution)/shard_map/all_gather | solution.py:79
  27.0 76.3 %all-gather.6.cloned.1.call-start = ((), (), s32[]{:S(2)}) async-start(), calls=%async_computation.1 | async-start | bytes 8847360 | tf_op jit(solution)/shard_map/all_gather | solution.py:93
  30.3 4.2 %collective-permute-start = (bf16[2,2,2,2,2,1,6,1536]{7,4,6,5,3,2,1,0:T(2,128)(2,1)}, bf16[2,2,2,2,2,1,6,1536]{7,4,6,5,3,2,1,0:T(2,128)(2,1)}, u32[]{:S(2)}, u32[]{:S(2)}) collective-permute-start(bf16[2,2,2,2,2,1,6,1536]{7,4,6,5,3,2,1,0:T(2,128)(2,1)} %copy.42), channel_id=1, source_target_pairs={{0,8},{8,0},{1,9},{9,1},{2,10},{10,2},{3,11},{11,3},{4,12},{12,4},... | collective-permute-start | bytes 1769480 | tf_op jit(solution)/shard_map/ppermute | solution.py:24
  36.9 19.4 %copy-start = (bf16[1,192,1536]{2,1,0:T(8,128)(2,1)S(1)}, bf16[1,192,1536]{2,1,0:T(8,128)(2,1)}, u32[]{:S(2)}) copy-start(bf16[1,192,1536]{2,1,0:T(8,128)(2,1)} %param.9) | copy-start | bytes 1769476
  36.9 19.4 %copy-start.1 = (bf16[1,192,1536]{2,1,0:T(8,128)(2,1)S(1)}, bf16[1,192,1536]{2,1,0:T(8,128)(2,1)}, u32[]{:S(2)}) copy-start(bf16[1,192,1536]{2,1,0:T(8,128)(2,1)} %param.7) | copy-start | bytes 1769476
  37.0 13.6 %collective-permute-start.1 = (bf16[2,2,2,2,1,1,6,1536]{7,6,5,4,3,2,1,0:T(8,128)(2,1)S(1)}, bf16[2,2,2,2,1,1,6,1536]{7,6,5,4,3,2,1,0:T(8,128)(2,1)S(1)}, u32[]{:S(2)}, u32[]{:S(2)}) collective-permute-start(bf16[2,2,2,2,1,1,6,1536]{7,6,5,4,3,2,1,0:T(8,128)(2,1)S(1)} %dynamic-slice_convert_fusion), channel_id=1, source_target_pairs={{0,16},{16,0},{32,48},{48,32},{1,17},{17,1},{33,49},{49,33},{2,18}... | collective-permute-start | bytes 884744 | tf_op jit(solution)/shard_map/ppermute | solution.py:24
  51.9 13.7 %collective-permute-start.2 = (bf16[2,2,2,1,1,1,6,1536]{7,6,5,4,3,2,1,0:T(8,128)(2,1)S(1)}, bf16[2,2,2,1,1,1,6,1536]{7,6,5,4,3,2,1,0:T(8,128)(2,1)}, u32[]{:S(2)}, u32[]{:S(2)}) collective-permute-start(bf16[2,2,2,1,1,1,6,1536]{7,6,5,4,3,2,1,0:T(8,128)(2,1)S(1)} %dynamic-slice_convert_fusion.1), channel_id=1, source_target_pairs={{0,32},{16,48},{32,0},{48,16},{1,33},{17,49},{33,1},{49,17},{2,34}... | collective-permute-start | bytes 442376 | tf_op jit(solution)/shard_map/ppermute | solution.py:24
  56.4 10.2 %collective-permute-start.3 = (bf16[32,3456]{1,0:T(8,128)(2,1)S(1)}, bf16[32,3456]{1,0:T(8,128)(2,1)S(1)}, u32[]{:S(2)}, u32[]{:S(2)}) collective-permute-start(bf16[32,3456]{1,0:T(8,128)(2,1)S(1)} %get-tuple-element.19), channel_id=1, source_target_pairs={{0,8},{8,16},{16,24},{24,32},{32,40},{40,48},{48,56},{56,64},{64,7... | collective-permute-start | bytes 663560 | tf_op jit(solution)/shard_map/ppermute | solution.py:85
  57.8 8.8 %collective-permute-start.4 = (bf16[32,3456]{1,0:T(8,128)(2,1)S(1)}, bf16[32,3456]{1,0:T(8,128)(2,1)S(1)}, u32[]{:S(2)}, u32[]{:S(2)}) collective-permute-start(bf16[32,3456]{1,0:T(8,128)(2,1)S(1)} %get-tuple-element.18), channel_id=1, source_target_pairs={{8,0},{16,8},{24,16},{32,24},{40,32},{48,40},{56,48},{64,56},{72,6... | collective-permute-start | bytes 663560 | tf_op jit(solution)/shard_map/ppermute | solution.py:86
  66.6 30.0 %copy-start.8 = (bf16[32,3456]{1,0:T(8,128)(2,1)}, bf16[32,3456]{1,0:T(8,128)(2,1)S(1)}, u32[]{:S(2)}) copy-start(bf16[32,3456]{1,0:T(8,128)(2,1)S(1)} %collective-permute-done.3) | copy-start | bytes 663556
  66.6 30.0 %copy-start.9 = (bf16[32,3456]{1,0:T(8,128)(2,1)}, bf16[32,3456]{1,0:T(8,128)(2,1)S(1)}, u32[]{:S(2)}) copy-start(bf16[32,3456]{1,0:T(8,128)(2,1)S(1)} %collective-permute-done.4) | copy-start | bytes 663556
  78.5 6.5 %collective-permute-start.5 = (bf16[2,2,1,1,1,1,6,1536]{7,6,5,4,3,2,1,0:T(8,128)(2,1)S(1)}, bf16[2,2,1,1,1,1,6,1536]{7,6,5,4,3,2,1,0:T(8,128)(2,1)S(1)}, u32[]{:S(2)}, u32[]{:S(2)}) collective-permute-start(bf16[2,2,1,1,1,1,6,1536]{7,6,5,4,3,2,1,0:T(8,128)(2,1)S(1)} %dynamic-slice_convert_fusion.2), channel_id=1, source_target_pairs={{0,64},{64,0},{128,192},{192,128},{256,320},{320,256},{384,448},{4... | collective-permute-start | bytes 221192 | tf_op jit(solution)/shard_map/ppermute | solution.py:24
  85.1 7.4 %collective-permute-start.6 = (bf16[2,1,1,1,1,1,6,1536]{7,6,5,4,3,2,1,0:T(8,128)(2,1)S(1)}, bf16[2,1,1,1,1,1,6,1536]{7,6,5,4,3,2,1,0:T(8,128)(2,1)S(1)}, u32[]{:S(2)}, u32[]{:S(2)}) collective-permute-start(bf16[2,1,1,1,1,1,6,1536]{7,6,5,4,3,2,1,0:T(8,128)(2,1)S(1)} %dynamic-slice_convert_fusion.3), channel_id=1, source_target_pairs={{0,128},{64,192},{128,0},{192,64},{256,384},{320,448},{384,256},{4... | collective-permute-start | bytes 110600 | tf_op jit(solution)/shard_map/ppermute | solution.py:24
  92.6 9.6 %collective-permute-start.7 = (bf16[1,1,1,1,1,1,6,1536]{7,6,5,4,3,2,1,0:T(8,128)(2,1)S(1)}, bf16[1,1,1,1,1,1,6,1536]{7,6,5,4,3,2,1,0:T(8,128)(2,1)S(1)}, u32[]{:S(2)}, u32[]{:S(2)}) collective-permute-start(bf16[1,1,1,1,1,1,6,1536]{7,6,5,4,3,2,1,0:T(8,128)(2,1)S(1)} %dynamic-slice_convert_fusion.4), channel_id=1, source_target_pairs={{0,256},{64,320},{128,384},{192,448},{256,0},{320,64},{384,128},{4... | collective-permute-start | bytes 55304 | tf_op jit(solution)/shard_map/ppermute | solution.py:24
  103.3 2.0 %slice-start = ((bf16[384,7680]{1,0:T(8,128)(2,1)}), bf16[384,4608]{1,0:T(8,128)(2,1)S(1)}, s32[]{:S(2)}) async-start(bf16[384,7680]{1,0:T(8,128)(2,1)} %all-gather.6.cloned.1.call-done), calls=%async_computation.2 | async-start | bytes 7077888 | tf_op jit(solution)/shard_map/slice | solution.py:98
  111.5 1.2 copy-start.5
  111.5 1.6 copy-start.6
  111.5 3.7 %copy-start.3 = (bf16[384,4608]{0,1:T(8,128)(2,1)S(1)}, bf16[384,4608]{0,1:T(8,128)(2,1)}, u32[]{:S(2)}) copy-start(bf16[384,4608]{0,1:T(8,128)(2,1)} %copy.31) | copy-start | bytes 10616836
  113.2 2.9 %copy-start.7 = (bf16[2,256,1536]{2,1,0:T(8,128)(2,1)}, bf16[2,256,1536]{2,1,0:T(8,128)(2,1)S(1)}, u32[]{:S(2)}) copy-start(bf16[2,256,1536]{2,1,0:T(8,128)(2,1)S(1)} %fusion.7) | copy-start | bytes 4718596
  123.1 40.3 %copy-start.10 = (f32[1,1,1,1,1,1,6,1536]{7,6,5,4,3,2,1,0:T(8,128)S(1)}, f32[1,1,1,1,1,1,6,1536]{7,6,5,4,3,2,1,0:T(8,128)}, u32[]{:S(2)}) copy-start(f32[1,1,1,1,1,1,6,1536]{7,6,5,4,3,2,1,0:T(8,128)} %convert_add_fusion.5) | copy-start | bytes 110596
  163.4 6.0 %collective-permute-start.8 = (f32[6,1536]{1,0:T(8,128)S(1)}, f32[6,1536]{1,0:T(8,128)S(1)}, u32[]{:S(2)}, u32[]{:S(2)}) collective-permute-start(f32[6,1536]{1,0:T(8,128)S(1)} %multiply_bitcast_fusion), channel_id=1, source_target_pairs={{0,1},{1,0},{2,3},{3,2},{4,5},{5,4},{6,7},{7,6},{8,9},{9,8},{10,11... | collective-permute-start | bytes 110600 | tf_op jit(solution)/shard_map/ppermute | solution.py:24
  169.4 7.5 %collective-permute-start.9 = (f32[6,1536]{1,0:T(8,128)S(1)}, f32[6,1536]{1,0:T(8,128)S(1)}, u32[]{:S(2)}, u32[]{:S(2)}) collective-permute-start(f32[6,1536]{1,0:T(8,128)S(1)} %fusion.44), channel_id=1, source_target_pairs={{0,2},{1,3},{2,0},{3,1},{4,6},{5,7},{6,4},{7,5},{8,10},{9,11},{10,... | collective-permute-start | bytes 110600 | tf_op jit(solution)/shard_map/ppermute | solution.py:24
  176.9 9.9 %collective-permute-start.10 = (f32[6,1536]{1,0:T(8,128)S(1)}, f32[6,1536]{1,0:T(8,128)S(1)}, u32[]{:S(2)}, u32[]{:S(2)}) collective-permute-start(f32[6,1536]{1,0:T(8,128)S(1)} %add.180), channel_id=1, source_target_pairs={{0,4},{4,0},{1,5},{5,1},{2,6},{6,2},{3,7},{7,3},{8,12},{12,8},{9,1... | collective-permute-start | bytes 110600 | tf_op jit(solution)/shard_map/ppermute | solution.py:24
  (1 other events, 1.2 us)
Sparse Core Ops, SparseCore 0:
  27.1 51.2 all-gather.3
  80.6 22.7 all-gather.5
